TPU v7x, 32 devices: a whole 2x2x4 slice. The times are simulated.
32 devices in a mesh: snp: 16 (over z, x, core), smp: 2 (over y).
Axes of the slice: x: 2, y: 2, z: 4, core: 2. Of those that a mesh axis runs over, the one named last changes fastest.
Arguments:
- dosage: float32 [4096, 8192], P('smp', 'snp'), may hold values from 0 to 2
- reach: int32 [16], P('snp'), may hold values from 0 to 3, as said below
Outputs:
- ld_band: float32 [8192, 2048], P(('snp', 'smp'))
Inputs may be any that keep to these rules, and one draw needn't show every extreme that they name: reach equals 3 at the last block.
All inputs are finite; a program needn't handle non-finite values.
Results may differ from a plain program's by a relative error of at most 0.008.
Values may be sent and summed in bfloat16 or wider, within the bound.
No kernel may reach another device: no remote copies, remote signals or barrier semaphores. Data moves between devices by JAX's collectives and lax.ppermute only.
A program may use at most 64 MiB of HBM per device.

v0:
```python
import jax
import jax.numpy as jnp
from jax import lax
from jax.sharding import PartitionSpec as P

TAPS = 4


def shifted(value, axis, steps):
    count = lax.axis_size(axis)
    first, last = (max(0, -steps), min(count, count - steps))
    return lax.ppermute(value, axis, [(source, source + steps) for source in range(first, last)])


def tile_term(standard, neighbour):
    return lax.dot_general(
        standard, neighbour, (((0,), (0,)), ((), ())), preferred_element_type=jnp.float32
    )


def local(dosage, reach):
    rows, width = dosage.shape
    samples = rows * lax.axis_size("smp")
    total = lax.psum(jnp.sum(dosage, axis=0), "smp")
    mean = total / samples
    centered = dosage - mean
    var = lax.psum(jnp.sum(centered * centered, axis=0), "smp") / samples
    standard = (centered * lax.rsqrt(var + 1e-05)).astype(jnp.bfloat16)
    neighbours = [standard]
    previous = standard
    for dist in range(1, TAPS):
        previous = shifted(previous, "snp", 1)
        neighbours.append(previous)
    share = width // lax.axis_size("smp")
    own_reach = reach[0]
    tiles = []
    for dist in range(TAPS):
        neighbour = neighbours[dist]

        def term_one(start, count, neighbour=neighbour):
            return tile_term(standard, neighbour)

        tiles.append(
            lax.psum_scatter(
                term_one(jnp.int32(0), share * lax.axis_size("smp")).astype(jnp.bfloat16),
                "smp",
                scatter_dimension=0,
                tiled=True,
            ).astype(jnp.float32)
        )
    kept = []
    for dist in range(TAPS):
        tile = tiles[dist] / samples
        kept.append(jnp.where(dist <= own_reach, tile, jnp.zeros_like(tile)))
    return jnp.concatenate(kept, axis=1)


def solution(mesh):
    return jax.shard_map(
        local,
        mesh=mesh,
        in_specs=(P("smp", "snp"), P("snp")),
        out_specs=P(("snp", "smp"), None),
        check_vma=False,
    )
```

profile of v0, /device:TPU:0, one launch (start us, length us, event | category | flops | bytes accessed | tf_op | source)
XLA Modules:
  0.0 147.3 jit_solution(3957411592898868847)
XLA Ops:
  6.5 0.0 reduce-scatter.5.cloned.1.call-start
  6.5 2.5 %reduce_sum.18 = f32[512]{0:T(512)S(1)} reduce(f32[2048,512]{1,0:T(8,128)} %param.2, f32[]{:T(128)} %constant.20.clone.1), dimensions={0}, to_apply=%region_0.0 | reduce | flops 1048064 | bytes 4196356 | tf_op jit(solution)/shard_map/reduce_sum | solution.py:24
  9.1 5.9 %psum.14 = f32[512]{0:T(512)S(1)} all-reduce(f32[512]{0:T(512)S(1)} %reduce_sum.18), channel_id=1, replica_groups=mesh['snp'=16,'smp'=2] {'smp'}, use_global_device_ids=true, to_apply=%region_1.0 | all-reduce | flops 512 | bytes 4096 | tf_op jit(solution)/shard_map/psum | solution.py:24
  14.9 2.7 %multiply_reduce_fusion = f32[512]{0:T(512)S(1)} fusion(f32[2048,512]{1,0:T(8,128)} %param.2, f32[512]{0:T(512)S(1)} %broadcast_multiply_fusion), kind=kLoop, calls=%fused_computation.1 | loop fusion | flops 3145216 | bytes 4198400 | tf_op jit(solution)/shard_map/reduce_sum | solution.py:27
  17.6 4.9 %psum.15 = f32[512]{0:T(512)S(1)} all-reduce(f32[512]{0:T(512)S(1)} %multiply_reduce_fusion), channel_id=1, replica_groups=mesh['snp'=16,'smp'=2] {'smp'}, use_global_device_ids=true, to_apply=%region_3.0 | all-reduce | flops 512 | bytes 4096 | tf_op jit(solution)/shard_map/psum | solution.py:27
  22.6 2.8 %multiply_convert_fusion = bf16[2048,512]{1,0:T(8,128)(2,1)S(1)} fusion(f32[2048,512]{1,0:T(8,128)} %param.2, f32[512]{0:T(512)S(1)} %add_rsqrt_fusion, f32[512]{0:T(512)S(1)} %broadcast_multiply_fusion), kind=kLoop, calls=%fused_computation | loop fusion | flops 3145728 | bytes 6295552 | tf_op jit(solution)/shard_map/convert_element_type | solution.py:28
  25.4 2.6 %collective-permute-start = (bf16[2048,512]{1,0:T(8,128)(2,1)S(1)}, bf16[2048,512]{1,0:T(8,128)(2,1)}, u32[]{:S(2)}, u32[]{:S(2)}) collective-permute-start(bf16[2048,512]{1,0:T(8,128)(2,1)S(1)} %multiply_convert_fusion), channel_id=1, source_target_pairs={{0,2},{2,4},{4,6},{6,8},{8,10},{10,12},{12,14},{14,16},{16,18},{18... | collective-permute-start | bytes 6291464 | tf_op jit(solution)/shard_map/ppermute | solution.py:12
  28.0 2.6 %collective-permute-done = bf16[2048,512]{1,0:T(8,128)(2,1)} collective-permute-done((bf16[2048,512]{1,0:T(8,128)(2,1)S(1)}, bf16[2048,512]{1,0:T(8,128)(2,1)}, u32[]{:S(2)}, u32[]{:S(2)}) %collective-permute-start) | collective-permute-done | bytes 2097184 | tf_op jit(solution)/shard_map/ppermute | solution.py:12
  30.6 25.0 %collective-permute-start.1 = (bf16[2048,512]{1,0:T(8,128)(2,1)}, bf16[2048,512]{1,0:T(8,128)(2,1)}, u32[]{:S(2)}, u32[]{:S(2)}) collective-permute-start(bf16[2048,512]{1,0:T(8,128)(2,1)} %collective-permute-done), channel_id=1, source_target_pairs={{0,2},{2,4},{4,6},{6,8},{8,10},{10,12},{12,14},{14,16},{16,18},{18... | collective-permute-start | bytes 6291464 | tf_op jit(solution)/shard_map/ppermute | solution.py:12
  55.6 2.1 %convolution_convert_fusion.3 = bf16[512,512]{1,0:T(8,128)(2,1)} fusion(bf16[2048,512]{1,0:T(8,128)(2,1)S(1)} %multiply_convert_fusion), kind=kOutput, calls=%fused_computation.6 | convolution fusion | flops 1074003968 | bytes 2621440 | tf_op jit(solution)/shard_map/dot_general | solution.py:16
  57.7 0.0 reduce-scatter.5.cloned.1.call-update
  57.7 0.0 reduce-scatter.7.cloned.1.call-start
  57.8 0.6 collective-permute-done.1
  58.4 24.9 %collective-permute-start.2 = (bf16[2048,512]{1,0:T(8,128)(2,1)}, bf16[2048,512]{1,0:T(8,128)(2,1)}, u32[]{:S(2)}, u32[]{:S(2)}) collective-permute-start(bf16[2048,512]{1,0:T(8,128)(2,1)} %collective-permute-done.1), channel_id=1, source_target_pairs={{0,2},{2,4},{4,6},{6,8},{8,10},{10,12},{12,14},{14,16},{16,18},{18... | collective-permute-start | bytes 6291464 | tf_op jit(solution)/shard_map/ppermute | solution.py:12
  83.3 3.7 %convolution_convert_fusion.2 = bf16[512,512]{1,0:T(8,128)(2,1)} fusion(bf16[2048,512]{1,0:T(8,128)(2,1)S(1)} %multiply_convert_fusion, bf16[2048,512]{1,0:T(8,128)(2,1)} %collective-permute-done), kind=kOutput, calls=%fused_computation.5 | convolution fusion | flops 1074003968 | bytes 4718592 | tf_op jit(solution)/shard_map/dot_general | solution.py:16
  87.0 0.0 reduce-scatter.7.cloned.1.call-update
  87.0 0.0 reduce-scatter.9.cloned.1.call-start
  87.1 3.7 %convolution_convert_fusion.1 = bf16[512,512]{1,0:T(8,128)(2,1)} fusion(bf16[2048,512]{1,0:T(8,128)(2,1)S(1)} %multiply_convert_fusion, bf16[2048,512]{1,0:T(8,128)(2,1)} %collective-permute-done.1), kind=kOutput, calls=%fused_computation.4 | convolution fusion | flops 1074003968 | bytes 4718592 | tf_op jit(solution)/shard_map/dot_general | solution.py:16
  90.7 0.0 reduce-scatter.9.cloned.1.call-update
  90.7 0.0 reduce-scatter.11.cloned.1.call-start
  90.8 0.0 collective-permute-done.2
  90.8 3.7 %convolution_convert_fusion = bf16[512,512]{1,0:T(8,128)(2,1)} fusion(bf16[2048,512]{1,0:T(8,128)(2,1)S(1)} %multiply_convert_fusion, bf16[2048,512]{1,0:T(8,128)(2,1)} %collective-permute-done.2), kind=kOutput, calls=%fused_computation.3 | convolution fusion | flops 1074003968 | bytes 4718592 | tf_op jit(solution)/shard_map/dot_general | solution.py:16
  94.5 0.0 reduce-scatter.11.cloned.1.call-update
  95.1 0.0 reduce-scatter.5.cloned.1.call-done
  95.2 1.0 multiply_select_fusion.3
  96.2 8.4 %reduce-scatter.7.cloned.1.call-done = bf16[256,512]{1,0:T(8,128)(2,1)} async-done(((bf16[512,512]{1,0:T(8,128)(2,1)}), bf16[256,512]{1,0:T(8,128)(2,1)}) %reduce-scatter.7.cloned.1.call-update) | async-done | bytes 262160 | tf_op jit(solution)/shard_map/reduce_scatter | solution.py:44
  104.7 1.0 multiply_select_fusion.2
  105.7 15.8 %reduce-scatter.9.cloned.1.call-done = bf16[256,512]{1,0:T(8,128)(2,1)} async-done(((bf16[512,512]{1,0:T(8,128)(2,1)}), bf16[256,512]{1,0:T(8,128)(2,1)}) %reduce-scatter.9.cloned.1.call-update) | async-done | bytes 262160 | tf_op jit(solution)/shard_map/reduce_scatter | solution.py:44
  121.5 1.0 multiply_select_fusion.1
  122.5 15.7 %reduce-scatter.11.cloned.1.call-done = bf16[256,512]{1,0:T(8,128)(2,1)} async-done(((bf16[512,512]{1,0:T(8,128)(2,1)}), bf16[256,512]{1,0:T(8,128)(2,1)}) %reduce-scatter.11.cloned.1.call-update) | async-done | bytes 262160 | tf_op jit(solution)/shard_map/reduce_scatter | solution.py:44
  138.3 1.0 multiply_select_fusion
  139.3 1.5 %pad_maximum_fusion = f32[256,2048]{1,0:T(8,128)} fusion(f32[256,512]{1,0:T(8,128)S(1)} %multiply_select_fusion, f32[256,512]{1,0:T(8,128)S(1)} %multiply_select_fusion.1, f32[256,512]{1,0:T(8,128)S(1)} %multiply_select_fusion.2, f32[256,512]{1,0:T(8,128)S(1)} %multiply_select_fusion.3), kind=kLoop, calls=%fused_computation.2 | loop fusion | flops 1572864 | bytes 4194304 | tf_op jit(solution)/shard_map/concatenate | solution.py:55
  (2 shorter events, 0.0 us)
Async XLA Ops:
  6.5 88.6 %reduce-scatter.5.cloned.1.call-start = ((), (), s32[]{:S(2)}) async-start(), calls=%async_computation.4 | async-start | bytes 786432 | tf_op jit(solution)/shard_map/reduce_scatter | solution.py:44
  25.4 5.2 %collective-permute-start = (bf16[2048,512]{1,0:T(8,128)(2,1)S(1)}, bf16[2048,512]{1,0:T(8,128)(2,1)}, u32[]{:S(2)}, u32[]{:S(2)}) collective-permute-start(bf16[2048,512]{1,0:T(8,128)(2,1)S(1)} %multiply_convert_fusion), channel_id=1, source_target_pairs={{0,2},{2,4},{4,6},{6,8},{8,10},{10,12},{12,14},{14,16},{16,18},{18... | collective-permute-start | bytes 6291464 | tf_op jit(solution)/shard_map/ppermute | solution.py:12
  30.6 27.8 %collective-permute-start.1 = (bf16[2048,512]{1,0:T(8,128)(2,1)}, bf16[2048,512]{1,0:T(8,128)(2,1)}, u32[]{:S(2)}, u32[]{:S(2)}) collective-permute-start(bf16[2048,512]{1,0:T(8,128)(2,1)} %collective-permute-done), channel_id=1, source_target_pairs={{0,2},{2,4},{4,6},{6,8},{8,10},{10,12},{12,14},{14,16},{16,18},{18... | collective-permute-start | bytes 6291464 | tf_op jit(solution)/shard_map/ppermute | solution.py:12
  57.7 46.9 %reduce-scatter.7.cloned.1.call-start = ((), (), s32[]{:S(2)}) async-start(), calls=%async_computation.5 | async-start | bytes 786432 | tf_op jit(solution)/shard_map/reduce_scatter | solution.py:44
  58.4 32.4 %collective-permute-start.2 = (bf16[2048,512]{1,0:T(8,128)(2,1)}, bf16[2048,512]{1,0:T(8,128)(2,1)}, u32[]{:S(2)}, u32[]{:S(2)}) collective-permute-start(bf16[2048,512]{1,0:T(8,128)(2,1)} %collective-permute-done.1), channel_id=1, source_target_pairs={{0,2},{2,4},{4,6},{6,8},{8,10},{10,12},{12,14},{14,16},{16,18},{18... | collective-permute-start | bytes 6291464 | tf_op jit(solution)/shard_map/ppermute | solution.py:12
  87.0 34.5 %reduce-scatter.9.cloned.1.call-start = ((), (), s32[]{:S(2)}) async-start(), calls=%async_computation.6 | async-start | bytes 786432 | tf_op jit(solution)/shard_map/reduce_scatter | solution.py:44
  90.7 47.5 %reduce-scatter.11.cloned.1.call-start = ((), (), s32[]{:S(2)}) async-start(), calls=%async_computation.7 | async-start | bytes 786432 | tf_op jit(solution)/shard_map/reduce_scatter | solution.py:44
Sparse Core Ops, SparseCore 0:
  57.8 16.6 reduce-scatter.4
  87.1 17.4 reduce-scatter.6
  106.9 14.5 reduce-scatter.8
  123.7 14.5 reduce-scatter.10
where the time goes:
time: 148 us; the launch traced here: 147 us
  starting transfers between devices  52.7 us (36%)
  waiting for transfers between devices  43.2 us (29%)
  between operations  13.8 us (9%)
  other arithmetic  13.6 us (9%)
  matrix products  13.1 us (9%)
  blocking collectives  10.8 us (7%)
    ppermute x3, starting transfers between devices, shifted(): lax.ppermute(value, axis, [(source, source + steps) for source in range(f...  52.6 us
    reduce_scatter x4, waiting for transfers between devices, local(): lax.psum_scatter(term_one(jnp.int32(0), share * lax.axis_size('smp')).ast...  40 us
    dot_general x4, matrix products, tile_term(): lax.dot_general(standard, neighbour, (((0,), (0,)), ((), ())), preferred_...  13.1 us
    psum x1, blocking collectives, local(): total = lax.psum(jnp.sum(dosage, axis=0), 'smp')  5.86 us
    psum x1, blocking collectives, local(): var = lax.psum(jnp.sum(centered * centered, axis=0), 'smp') / samples  4.94 us
    select_n x4, other arithmetic, local(): kept.append(jnp.where(dist <= own_reach, tile, jnp.zeros_like(tile)))  4.09 us
    ppermute x3, waiting for transfers between devices, shifted(): lax.ppermute(value, axis, [(source, source + steps) for source in range(f...  3.15 us
  transfers between devices with their start and end apart: 7, of which 5 were waited for; matrix products, arithmetic and copies ran while one was open for 11% of the time, Pallas kernels for 0%

commit v1 on v0

v1 whole, which is shorter than its diff:
```python
import jax
import jax.numpy as jnp
from jax import lax
from jax.sharding import PartitionSpec as P

TAPS = 4


def shifted(value, axis, steps):
    count = lax.axis_size(axis)
    first, last = (max(0, -steps), min(count, count - steps))
    return lax.ppermute(value, axis, [(source, source + steps) for source in range(first, last)])


def rotated(value, axis, steps):
    count = lax.axis_size(axis)
    return lax.ppermute(value, axis, [(source, (source + steps) % count) for source in range(count)])


def tile_term(standard, neighbour):
    return lax.dot_general(
        standard, neighbour, (((0,), (0,)), ((), ())), preferred_element_type=jnp.float32
    )


def local(dosage, reach):
    rows, width = dosage.shape
    n_smp = lax.axis_size("smp")
    samples = rows * n_smp
    me = lax.axis_index("smp")

    part_mean = jnp.sum(dosage, axis=0) / rows
    deviation = dosage - part_mean
    part_m2 = jnp.sum(deviation * deviation, axis=0)
    stats = jnp.stack([part_mean, part_m2])
    gathered = [stats] + [rotated(stats, "smp", s) for s in range(1, n_smp)]
    mean = gathered[0][0]
    for g in gathered[1:]:
        mean = mean + g[0]
    mean = mean / n_smp
    m2 = gathered[0][1]
    spread = (gathered[0][0] - mean) ** 2
    for g in gathered[1:]:
        m2 = m2 + g[1]
        spread = spread + (g[0] - mean) ** 2
    var = (m2 + rows * spread) / samples
    standard = ((dosage - mean) * lax.rsqrt(var + 1e-05)).astype(jnp.bfloat16)

    neighbours = [standard]
    previous = standard
    for dist in range(1, TAPS):
        previous = shifted(previous, "snp", 1)
        neighbours.append(previous)

    share = width // n_smp
    own_reach = reach[0]
    kept = []
    for dist in range(TAPS):
        partial = tile_term(standard, neighbours[dist]).astype(jnp.bfloat16)
        pieces = partial.reshape(n_smp, share, width)
        total = lax.dynamic_index_in_dim(pieces, me, 0, keepdims=False).astype(jnp.float32)
        for s in range(1, n_smp):
            outgoing = lax.dynamic_index_in_dim(pieces, (me + s) % n_smp, 0, keepdims=False)
            total = total + rotated(outgoing, "smp", s).astype(jnp.float32)
        tile = total / samples
        kept.append(jnp.where(dist <= own_reach, tile, jnp.zeros_like(tile)))
    return jnp.concatenate(kept, axis=1)


def solution(mesh):
    return jax.shard_map(
        local,
        mesh=mesh,
        in_specs=(P("smp", "snp"), P("snp")),
        out_specs=P(("snp", "smp"), None),
        check_vma=False,
    )
```

time: 148 us -> 108 us (0.73)
  the two profiles are of different devices: /device:TPU:0 before, /device:TPU:3 now
where the time goes in v1:
time: 108 us
  waiting for transfers between devices  66.4 us (61%)
  starting transfers between devices  21.1 us (20%)
  matrix products  9.84 us (9%)
  other arithmetic  7.9 us (7%)
  local copies, waits for them, and re-layouts  1.43 us (1%)
    ppermute x3, waiting for transfers between devices, shifted(): lax.ppermute(value, axis, [(source, source + steps) for source in range(f...  54.3 us
    ppermute x3, starting transfers between devices, shifted(): lax.ppermute(value, axis, [(source, source + steps) for source in range(f...  15.5 us
    ppermute x5, waiting for transfers between devices, rotated(): lax.ppermute(value, axis, [(source, (source + steps) % count) for source...  12.1 us
    dot_general x4, matrix products, tile_term(): lax.dot_general(standard, neighbour, (((0,), (0,)), ((), ())), preferred_...  9.84 us
    ppermute x5, starting transfers between devices, rotated(): lax.ppermute(value, axis, [(source, (source + steps) % count) for source...  5.52 us
    reduce_sum x1, other arithmetic, local(): part_m2 = jnp.sum(deviation * deviation, axis=0)  2.85 us
    reduce_sum x1, other arithmetic, local(): part_mean = jnp.sum(dosage, axis=0) / rows  2.52 us
  transfers between devices with their start and end apart: 8, of which 6 were waited for; matrix products, arithmetic and copies ran while one was open for 10% of the time, Pallas kernels for 0%

profile of v1, /device:TPU:3, one launch (start us, length us, event | category | flops | bytes accessed | tf_op | source)
XLA Modules:
  0.0 107.5 jit_solution(696317675881719940)
XLA Ops:
  0.0 2.5 %reduce_sum.18 = f32[512]{0:T(512)S(1)} reduce(f32[2048,512]{1,0:T(8,128)} %param.2, f32[]{:T(128)} %constant.59.clone.1), dimensions={0}, to_apply=%region_0.0 | reduce | flops 1048064 | bytes 4196356 | tf_op jit(solution)/shard_map/reduce_sum | solution.py:32
  2.5 0.0 copy-start
  2.5 2.9 %multiply_reduce_fusion = f32[512]{0:T(512)S(1)} fusion(f32[2048,512]{1,0:T(8,128)} %param.2, f32[512]{0:T(512)S(1)} %broadcast_multiply_fusion), kind=kLoop, calls=%fused_computation.1 | loop fusion | flops 3145216 | bytes 4198400 | tf_op jit(solution)/shard_map/reduce_sum | solution.py:34
  5.4 1.3 %collective-permute-start = (f32[2,512]{1,0:T(2,128)S(1)}, f32[2,512]{1,0:T(2,128)S(1)}, u32[]{:S(2)}, u32[]{:S(2)}) collective-permute-start(f32[2,512]{1,0:T(2,128)S(1)} %pad_maximum_fusion.1), channel_id=1, source_target_pairs={{0,1},{1,0},{2,3},{3,2},{4,5},{5,4},{6,7},{7,6},{8,9},{9,8},{10,11... | collective-permute-start | bytes 12296 | tf_op jit(solution)/shard_map/ppermute | solution.py:17
  6.7 1.2 %collective-permute-done = f32[2,512]{1,0:T(2,128)S(1)} collective-permute-done((f32[2,512]{1,0:T(2,128)S(1)}, f32[2,512]{1,0:T(2,128)S(1)}, u32[]{:S(2)}, u32[]{:S(2)}) %collective-permute-start) | collective-permute-done | bytes 4128 | tf_op jit(solution)/shard_map/ppermute | solution.py:17
  7.9 0.0 copy-done
  7.9 0.6 multiply_convert_fusion
  8.5 4.9 %collective-permute-start.2 = (bf16[2048,512]{1,0:T(8,128)(2,1)S(1)}, bf16[2048,512]{1,0:T(8,128)(2,1)S(1)}, u32[]{:S(2)}, u32[]{:S(2)}) collective-permute-start(bf16[2048,512]{1,0:T(8,128)(2,1)S(1)} %multiply_convert_fusion), channel_id=1, source_target_pairs={{0,2},{2,4},{4,6},{6,8},{8,10},{10,12},{12,14},{14,16},{16,18},{18... | collective-permute-start | bytes 6291464 | tf_op jit(solution)/shard_map/ppermute | solution.py:12
  13.4 23.0 %collective-permute-done.2 = bf16[2048,512]{1,0:T(8,128)(2,1)S(1)} collective-permute-done((bf16[2048,512]{1,0:T(8,128)(2,1)S(1)}, bf16[2048,512]{1,0:T(8,128)(2,1)S(1)}, u32[]{:S(2)}, u32[]{:S(2)}) %collective-permute-start.2) | collective-permute-done | bytes 2097184 | tf_op jit(solution)/shard_map/ppermute | solution.py:12
  36.4 0.0 copy-start.1
  36.4 1.3 %copy-done.1 = bf16[2048,512]{1,0:T(8,128)(2,1)} copy-done((bf16[2048,512]{1,0:T(8,128)(2,1)}, bf16[2048,512]{1,0:T(8,128)(2,1)S(1)}, u32[]{:S(2)}) %copy-start.1) | copy-done | bytes 2097176
  37.7 5.3 %collective-permute-start.4 = (bf16[2048,512]{1,0:T(8,128)(2,1)S(1)}, bf16[2048,512]{1,0:T(8,128)(2,1)}, u32[]{:S(2)}, u32[]{:S(2)}) collective-permute-start(bf16[2048,512]{1,0:T(8,128)(2,1)S(1)} %collective-permute-done.2), channel_id=1, source_target_pairs={{0,2},{2,4},{4,6},{6,8},{8,10},{10,12},{12,14},{14,16},{16,18},{18... | collective-permute-start | bytes 6291464 | tf_op jit(solution)/shard_map/ppermute | solution.py:12
  43.0 23.0 %collective-permute-done.4 = bf16[2048,512]{1,0:T(8,128)(2,1)} collective-permute-done((bf16[2048,512]{1,0:T(8,128)(2,1)S(1)}, bf16[2048,512]{1,0:T(8,128)(2,1)}, u32[]{:S(2)}, u32[]{:S(2)}) %collective-permute-start.4) | collective-permute-done | bytes 2097184 | tf_op jit(solution)/shard_map/ppermute | solution.py:12
  66.0 5.4 %collective-permute-start.6 = (bf16[2048,512]{1,0:T(8,128)(2,1)}, bf16[2048,512]{1,0:T(8,128)(2,1)}, u32[]{:S(2)}, u32[]{:S(2)}) collective-permute-start(bf16[2048,512]{1,0:T(8,128)(2,1)} %collective-permute-done.4), channel_id=1, source_target_pairs={{0,2},{2,4},{4,6},{6,8},{8,10},{10,12},{12,14},{14,16},{16,18},{18... | collective-permute-start | bytes 6291464 | tf_op jit(solution)/shard_map/ppermute | solution.py:12
  71.4 1.3 %convolution_convert_fusion.3 = bf16[512,512]{1,0:T(8,128)(2,1)S(1)} fusion(bf16[2048,512]{1,0:T(8,128)(2,1)S(1)} %multiply_convert_fusion), kind=kOutput, calls=%fused_computation.6 | convolution fusion | flops 1074003968 | bytes 2621440 | tf_op jit(solution)/shard_map/dot_general | solution.py:21
  72.7 1.3 %collective-permute-start.1 = (bf16[256,512]{1,0:T(8,128)(2,1)S(1)}, bf16[256,512]{1,0:T(8,128)(2,1)S(1)}, u32[]{:S(2)}, u32[]{:S(2)}) collective-permute-start(bf16[256,512]{1,0:T(8,128)(2,1)S(1)} %dynamic-slice_bitcast_fusion.3), channel_id=1, source_target_pairs={{0,1},{1,0},{2,3},{3,2},{4,5},{5,4},{6,7},{7,6},{8,9},{9,8},{10,11... | collective-permute-start | bytes 786440 | tf_op jit(solution)/shard_map/ppermute | solution.py:17
  74.6 4.0 %collective-permute-done.1 = bf16[256,512]{1,0:T(8,128)(2,1)S(1)} collective-permute-done((bf16[256,512]{1,0:T(8,128)(2,1)S(1)}, bf16[256,512]{1,0:T(8,128)(2,1)S(1)}, u32[]{:S(2)}, u32[]{:S(2)}) %collective-permute-start.1) | collective-permute-done | bytes 262176 | tf_op jit(solution)/shard_map/ppermute | solution.py:17
  78.7 0.1 fusion.7
  78.8 2.9 %convolution_convert_fusion.2 = bf16[512,512]{1,0:T(8,128)(2,1)S(1)} fusion(bf16[2048,512]{1,0:T(8,128)(2,1)S(1)} %multiply_convert_fusion, bf16[2048,512]{1,0:T(8,128)(2,1)} %copy-done.1), kind=kOutput, calls=%fused_computation.5 | convolution fusion | flops 1074003968 | bytes 4718592 | tf_op jit(solution)/shard_map/dot_general | solution.py:21
  81.7 1.3 %collective-permute-start.3 = (bf16[256,512]{1,0:T(8,128)(2,1)S(1)}, bf16[256,512]{1,0:T(8,128)(2,1)S(1)}, u32[]{:S(2)}, u32[]{:S(2)}) collective-permute-start(bf16[256,512]{1,0:T(8,128)(2,1)S(1)} %dynamic-slice_bitcast_fusion.2), channel_id=1, source_target_pairs={{0,1},{1,0},{2,3},{3,2},{4,5},{5,4},{6,7},{7,6},{8,9},{9,8},{10,11... | collective-permute-start | bytes 786440 | tf_op jit(solution)/shard_map/ppermute | solution.py:17
  83.0 2.9 %convolution_convert_fusion.1 = bf16[512,512]{1,0:T(8,128)(2,1)S(1)} fusion(bf16[2048,512]{1,0:T(8,128)(2,1)S(1)} %multiply_convert_fusion, bf16[2048,512]{1,0:T(8,128)(2,1)} %collective-permute-done.4), kind=kOutput, calls=%fused_computation.4 | convolution fusion | flops 1074003968 | bytes 4718592 | tf_op jit(solution)/shard_map/dot_general | solution.py:21
  85.9 0.3 collective-permute-start.5
  86.2 8.4 %collective-permute-done.6 = bf16[2048,512]{1,0:T(8,128)(2,1)} collective-permute-done((bf16[2048,512]{1,0:T(8,128)(2,1)}, bf16[2048,512]{1,0:T(8,128)(2,1)}, u32[]{:S(2)}, u32[]{:S(2)}) %collective-permute-start.6) | collective-permute-done | bytes 2097184 | tf_op jit(solution)/shard_map/ppermute | solution.py:12
  94.6 2.9 %convolution_convert_fusion = bf16[512,512]{1,0:T(8,128)(2,1)S(1)} fusion(bf16[2048,512]{1,0:T(8,128)(2,1)S(1)} %multiply_convert_fusion, bf16[2048,512]{1,0:T(8,128)(2,1)} %collective-permute-done.6), kind=kOutput, calls=%fused_computation.3 | convolution fusion | flops 1074003968 | bytes 4718592 | tf_op jit(solution)/shard_map/dot_general | solution.py:21
  97.5 1.3 %collective-permute-start.7 = (bf16[256,512]{1,0:T(8,128)(2,1)S(1)}, bf16[256,512]{1,0:T(8,128)(2,1)S(1)}, u32[]{:S(2)}, u32[]{:S(2)}) collective-permute-start(bf16[256,512]{1,0:T(8,128)(2,1)S(1)} %dynamic-slice_bitcast_fusion), channel_id=1, source_target_pairs={{0,1},{1,0},{2,3},{3,2},{4,5},{5,4},{6,7},{7,6},{8,9},{9,8},{10,11... | collective-permute-start | bytes 786440 | tf_op jit(solution)/shard_map/ppermute | solution.py:17
  98.8 0.0 collective-permute-done.3
  98.8 0.1 fusion.5
  98.9 0.0 collective-permute-done.5
  98.9 0.1 fusion.3
  99.1 6.8 %collective-permute-done.7 = bf16[256,512]{1,0:T(8,128)(2,1)S(1)} collective-permute-done((bf16[256,512]{1,0:T(8,128)(2,1)S(1)}, bf16[256,512]{1,0:T(8,128)(2,1)S(1)}, u32[]{:S(2)}, u32[]{:S(2)}) %collective-permute-start.7) | collective-permute-done | bytes 262176 | tf_op jit(solution)/shard_map/ppermute | solution.py:17
  105.9 0.1 fusion.1
  106.0 1.5 %pad_maximum_fusion = f32[256,2048]{1,0:T(8,128)} fusion(f32[256,512]{1,0:T(8,128)S(1)} %fusion.1, f32[256,512]{1,0:T(8,128)S(1)} %fusion.3, f32[256,512]{1,0:T(8,128)S(1)} %fusion.5, f32[256,512]{1,0:T(8,128)S(1)} %fusion.7), kind=kLoop, calls=%fused_computation.2 | loop fusion | flops 1572864 | bytes 4194304 | tf_op jit(solution)/shard_map/concatenate | solution.py:67
  (7 shorter events, 0.1 us)
Async XLA Ops:
  2.5 5.4 %copy-start = (f32[2048,512]{1,0:T(8,128)S(1)}, f32[2048,512]{1,0:T(8,128)}, u32[]{:S(2)}) copy-start(f32[2048,512]{1,0:T(8,128)} %param.2) | copy-start | bytes 12582916
  5.4 2.5 %collective-permute-start = (f32[2,512]{1,0:T(2,128)S(1)}, f32[2,512]{1,0:T(2,128)S(1)}, u32[]{:S(2)}, u32[]{:S(2)}) collective-permute-start(f32[2,512]{1,0:T(2,128)S(1)} %pad_maximum_fusion.1), channel_id=1, source_target_pairs={{0,1},{1,0},{2,3},{3,2},{4,5},{5,4},{6,7},{7,6},{8,9},{9,8},{10,11... | collective-permute-start | bytes 12296 | tf_op jit(solution)/shard_map/ppermute | solution.py:17
  8.5 27.9 %collective-permute-start.2 = (bf16[2048,512]{1,0:T(8,128)(2,1)S(1)}, bf16[2048,512]{1,0:T(8,128)(2,1)S(1)}, u32[]{:S(2)}, u32[]{:S(2)}) collective-permute-start(bf16[2048,512]{1,0:T(8,128)(2,1)S(1)} %multiply_convert_fusion), channel_id=1, source_target_pairs={{0,2},{2,4},{4,6},{6,8},{8,10},{10,12},{12,14},{14,16},{16,18},{18... | collective-permute-start | bytes 6291464 | tf_op jit(solution)/shard_map/ppermute | solution.py:12
  36.4 1.3 %copy-start.1 = (bf16[2048,512]{1,0:T(8,128)(2,1)}, bf16[2048,512]{1,0:T(8,128)(2,1)S(1)}, u32[]{:S(2)}) copy-start(bf16[2048,512]{1,0:T(8,128)(2,1)S(1)} %collective-permute-done.2) | copy-start | bytes 6291460
  37.7 28.2 %collective-permute-start.4 = (bf16[2048,512]{1,0:T(8,128)(2,1)S(1)}, bf16[2048,512]{1,0:T(8,128)(2,1)}, u32[]{:S(2)}, u32[]{:S(2)}) collective-permute-start(bf16[2048,512]{1,0:T(8,128)(2,1)S(1)} %collective-permute-done.2), channel_id=1, source_target_pairs={{0,2},{2,4},{4,6},{6,8},{8,10},{10,12},{12,14},{14,16},{16,18},{18... | collective-permute-start | bytes 6291464 | tf_op jit(solution)/shard_map/ppermute | solution.py:12
  66.0 28.7 %collective-permute-start.6 = (bf16[2048,512]{1,0:T(8,128)(2,1)}, bf16[2048,512]{1,0:T(8,128)(2,1)}, u32[]{:S(2)}, u32[]{:S(2)}) collective-permute-start(bf16[2048,512]{1,0:T(8,128)(2,1)} %collective-permute-done.4), channel_id=1, source_target_pairs={{0,2},{2,4},{4,6},{6,8},{8,10},{10,12},{12,14},{14,16},{16,18},{18... | collective-permute-start | bytes 6291464 | tf_op jit(solution)/shard_map/ppermute | solution.py:12
  72.7 6.0 %collective-permute-start.1 = (bf16[256,512]{1,0:T(8,128)(2,1)S(1)}, bf16[256,512]{1,0:T(8,128)(2,1)S(1)}, u32[]{:S(2)}, u32[]{:S(2)}) collective-permute-start(bf16[256,512]{1,0:T(8,128)(2,1)S(1)} %dynamic-slice_bitcast_fusion.3), channel_id=1, source_target_pairs={{0,1},{1,0},{2,3},{3,2},{4,5},{5,4},{6,7},{7,6},{8,9},{9,8},{10,11... | collective-permute-start | bytes 786440 | tf_op jit(solution)/shard_map/ppermute | solution.py:17
  81.7 17.1 %collective-permute-start.3 = (bf16[256,512]{1,0:T(8,128)(2,1)S(1)}, bf16[256,512]{1,0:T(8,128)(2,1)S(1)}, u32[]{:S(2)}, u32[]{:S(2)}) collective-permute-start(bf16[256,512]{1,0:T(8,128)(2,1)S(1)} %dynamic-slice_bitcast_fusion.2), channel_id=1, source_target_pairs={{0,1},{1,0},{2,3},{3,2},{4,5},{5,4},{6,7},{7,6},{8,9},{9,8},{10,11... | collective-permute-start | bytes 786440 | tf_op jit(solution)/shard_map/ppermute | solution.py:17
  85.9 13.0 %collective-permute-start.5 = (bf16[256,512]{1,0:T(8,128)(2,1)S(1)}, bf16[256,512]{1,0:T(8,128)(2,1)S(1)}, u32[]{:S(2)}, u32[]{:S(2)}) collective-permute-start(bf16[256,512]{1,0:T(8,128)(2,1)S(1)} %dynamic-slice_bitcast_fusion.1), channel_id=1, source_target_pairs={{0,1},{1,0},{2,3},{3,2},{4,5},{5,4},{6,7},{7,6},{8,9},{9,8},{10,11... | collective-permute-start | bytes 786440 | tf_op jit(solution)/shard_map/ppermute | solution.py:17
  97.5 8.4 %collective-permute-start.7 = (bf16[256,512]{1,0:T(8,128)(2,1)S(1)}, bf16[256,512]{1,0:T(8,128)(2,1)S(1)}, u32[]{:S(2)}, u32[]{:S(2)}) collective-permute-start(bf16[256,512]{1,0:T(8,128)(2,1)S(1)} %dynamic-slice_bitcast_fusion), channel_id=1, source_target_pairs={{0,1},{1,0},{2,3},{3,2},{4,5},{5,4},{6,7},{7,6},{8,9},{9,8},{10,11... | collective-permute-start | bytes 786440 | tf_op jit(solution)/shard_map/ppermute | solution.py:17

commit v2 on v1

--- a/solution.py
+++ b/solution.py
@@ -4,6 +4,7 @@
 from jax.sharding import PartitionSpec as P
 
 TAPS = 4
+CHUNKS = 2
 
 
 def shifted(value, axis, steps):
@@ -15,6 +16,32 @@
 def rotated(value, axis, steps):
     count = lax.axis_size(axis)
     return lax.ppermute(value, axis, [(source, (source + steps) % count) for source in range(count)])
+
+
+def chained(piece):
+    out = []
+    previous = piece
+    for dist in range(1, TAPS):
+        previous = shifted(previous, "snp", 1)
+        out.append(previous)
+    return out
+
+
+def relayed(piece, count):
+    def send(value, pairs):
+        pairs = [(s, t) for s, t in pairs if 0 <= s < count and 0 <= t < count]
+        return lax.ppermute(value, "snp", pairs)
+
+    groups = range(0, count, 4)
+    near = send(piece, [(b + i, b + i + 1) for b in groups for i in range(3)])
+    far = send(piece, [p for b in groups for p in ((b, b + 3), (b + 1, b + 4), (b + 3, b + 6))])
+    back = send(piece, [(b + 2, b) for b in groups])
+    hop_a = send(back, [(b, b + 4) for b in groups])
+    hop_b = send(far, [p for b in groups for p in ((b + 3, b + 2), (b + 2, b + 1))])
+    hop_c = send(near, [(b + 2, b + 3) for b in groups])
+    last_a = send(hop_b, [(b + 1, b) for b in groups])
+    last_b = send(hop_a, [(b, b + 1) for b in groups])
+    return [near + last_a, hop_a + hop_b + hop_c, far + last_b]
 
 
 def tile_term(standard, neighbour):
@@ -46,17 +73,25 @@
     var = (m2 + rows * spread) / samples
     standard = ((dosage - mean) * lax.rsqrt(var + 1e-05)).astype(jnp.bfloat16)
 
-    neighbours = [standard]
-    previous = standard
-    for dist in range(1, TAPS):
-        previous = shifted(previous, "snp", 1)
-        neighbours.append(previous)
+    chunks = CHUNKS if rows % (CHUNKS * 16) == 0 else 1
+    step = rows // chunks
+    pieces_of = [standard[c * step:(c + 1) * step] for c in range(chunks)]
+    if lax.axis_size("snp") % 4 == 0:
+        delivered = [relayed(piece, lax.axis_size("snp")) for piece in pieces_of]
+    else:
+        delivered = [chained(piece) for piece in pieces_of]
 
     share = width // n_smp
     own_reach = reach[0]
     kept = []
     for dist in range(TAPS):
-        partial = tile_term(standard, neighbours[dist]).astype(jnp.bfloat16)
+        if dist == 0:
+            partial = tile_term(standard, standard)
+        else:
+            partial = tile_term(pieces_of[0], delivered[0][dist - 1])
+            for c in range(1, chunks):
+                partial = partial + tile_term(pieces_of[c], delivered[c][dist - 1])
+        partial = partial.astype(jnp.bfloat16)
         pieces = partial.reshape(n_smp, share, width)
         total = lax.dynamic_index_in_dim(pieces, me, 0, keepdims=False).astype(jnp.float32)
         for s in range(1, n_smp):

time: 108 us -> 103 us (0.954)
  the two profiles are of different devices: /device:TPU:3 before, /device:TPU:0 now
where the time goes in v2:
time: 103 us; the launch traced here: 101 us
  starting transfers between devices  45.7 us (44%)
  waiting for transfers between devices  29.8 us (29%)
  matrix products  14.5 us (14%)
  other arithmetic  9.94 us (10%)
    ppermute x16, starting transfers between devices, send(): return lax.ppermute(value, 'snp', pairs)  38 us
    ppermute x16, waiting for transfers between devices, send(): return lax.ppermute(value, 'snp', pairs)  18.6 us
    dot_general x7, matrix products, tile_term(): lax.dot_general(standard, neighbour, (((0,), (0,)), ((), ())), preferred_...  14.5 us
    ppermute x5, waiting for transfers between devices, rotated(): lax.ppermute(value, axis, [(source, (source + steps) % count) for source...  11.1 us
    ppermute x5, starting transfers between devices, rotated(): lax.ppermute(value, axis, [(source, (source + steps) % count) for source...  7.63 us
    convert_element_type x1, other arithmetic, local(): standard = ((dosage - mean) * lax.rsqrt(var + 1e-05)).astype(jnp.bfloat16)  2.78 us
    reduce_sum x1, other arithmetic, local(): part_m2 = jnp.sum(deviation * deviation, axis=0)  2.7 us
    reduce_sum x1, other arithmetic, local(): part_mean = jnp.sum(dosage, axis=0) / rows  2.52 us
  transfers between devices with their start and end apart: 21, of which 7 were waited for; matrix products, arithmetic and copies ran while one was open for 15% of the time, Pallas kernels for 0%

profile of v2, /device:TPU:0, one launch (start us, length us, event | category | flops | bytes accessed | tf_op | source)
XLA Modules:
  0.0 101.0 jit_solution(13565136987194847674)
XLA Ops:
  0.0 2.5 %reduce_sum.18 = f32[512]{0:T(512)S(1)} reduce(f32[2048,512]{1,0:T(8,128)} %param.2, f32[]{:T(128)} %constant.59.clone.1), dimensions={0}, to_apply=%region_0.0 | reduce | flops 1048064 | bytes 4196356 | tf_op jit(solution)/shard_map/reduce_sum | solution.py:59
  2.5 2.7 %multiply_reduce_fusion = f32[512]{0:T(512)S(1)} fusion(f32[2048,512]{1,0:T(8,128)} %param.2, f32[512]{0:T(512)S(1)} %broadcast_multiply_fusion), kind=kLoop, calls=%fused_computation.1 | loop fusion | flops 3145216 | bytes 4198400 | tf_op jit(solution)/shard_map/reduce_sum | solution.py:61
  5.2 3.0 %collective-permute-start = (f32[2,512]{1,0:T(2,128)S(1)}, f32[2,512]{1,0:T(2,128)S(1)}, u32[]{:S(2)}, u32[]{:S(2)}) collective-permute-start(f32[2,512]{1,0:T(2,128)S(1)} %pad_maximum_fusion.1), channel_id=1, source_target_pairs={{0,1},{1,0},{2,3},{3,2},{4,5},{5,4},{6,7},{7,6},{8,9},{9,8},{10,11... | collective-permute-start | bytes 12296 | tf_op jit(solution)/shard_map/ppermute | solution.py:18
  8.3 1.6 %collective-permute-done = f32[2,512]{1,0:T(2,128)S(1)} collective-permute-done((f32[2,512]{1,0:T(2,128)S(1)}, f32[2,512]{1,0:T(2,128)S(1)}, u32[]{:S(2)}, u32[]{:S(2)}) %collective-permute-start) | collective-permute-done | bytes 4128 | tf_op jit(solution)/shard_map/ppermute | solution.py:18
  9.9 2.8 %multiply_convert_fusion = bf16[2048,512]{1,0:T(8,128)(2,1)S(1)} fusion(f32[2048,512]{1,0:T(8,128)} %param.2, f32[512]{0:T(512)S(1)} %bitcast.47, f32[512]{0:T(512)S(1)} %bitcast.46), kind=kLoop, calls=%fused_computation | loop fusion | flops 3145728 | bytes 6295552 | tf_op jit(solution)/shard_map/convert_element_type | solution.py:74
  12.7 0.1 fusion.29
  12.8 3.2 %collective-permute-start.7 = (bf16[1024,512]{1,0:T(8,128)(2,1)S(1)}, bf16[1024,512]{1,0:T(8,128)(2,1)}, u32[]{:S(2)}, u32[]{:S(2)}) collective-permute-start(bf16[1024,512]{1,0:T(8,128)(2,1)S(1)} %get-tuple-element.6), channel_id=1, source_target_pairs={{0,6},{2,8},{6,12},{8,14},{10,16},{14,20},{16,22},{18,24},{22,28},... | collective-permute-start | bytes 3145736 | tf_op jit(solution)/shard_map/ppermute | solution.py:33
  16.0 1.3 %collective-permute-start.14 = (bf16[1024,512]{1,0:T(8,128)(2,1)S(1)}, bf16[1024,512]{1,0:T(8,128)(2,1)S(1)}, u32[]{:S(2)}, u32[]{:S(2)}) collective-permute-start(bf16[1024,512]{1,0:T(8,128)(2,1)S(1)} %get-tuple-element.6), channel_id=1, source_target_pairs={{4,0},{12,8},{20,16},{28,24},{5,1},{13,9},{21,17},{29,25}} | collective-permute-start | bytes 3145736 | tf_op jit(solution)/shard_map/ppermute | solution.py:33
  17.2 1.3 %convolution_convert_fusion = bf16[512,512]{1,0:T(8,128)(2,1)S(1)} fusion(bf16[2048,512]{1,0:T(8,128)(2,1)S(1)} %multiply_convert_fusion), kind=kOutput, calls=%fused_computation.9 | convolution fusion | flops 1074003968 | bytes 2621440 | tf_op jit(solution)/shard_map/dot_general | solution.py:48
  18.6 1.6 %collective-permute-start.1 = (bf16[256,512]{1,0:T(8,128)(2,1)S(1)}, bf16[256,512]{1,0:T(8,128)(2,1)S(1)}, u32[]{:S(2)}, u32[]{:S(2)}) collective-permute-start(bf16[256,512]{1,0:T(8,128)(2,1)S(1)} %dynamic-slice_bitcast_fusion.3), channel_id=1, source_target_pairs={{0,1},{1,0},{2,3},{3,2},{4,5},{5,4},{6,7},{7,6},{8,9},{9,8},{10,11... | collective-permute-start | bytes 786440 | tf_op jit(solution)/shard_map/ppermute | solution.py:18
  20.1 1.3 %collective-permute-start.11 = (bf16[1024,512]{1,0:T(8,128)(2,1)S(1)}, bf16[1024,512]{1,0:T(8,128)(2,1)}, u32[]{:S(2)}, u32[]{:S(2)}) collective-permute-start(bf16[1024,512]{1,0:T(8,128)(2,1)S(1)} %get-tuple-element.5), channel_id=1, source_target_pairs={{4,0},{12,8},{20,16},{28,24},{5,1},{13,9},{21,17},{29,25}} | collective-permute-start | bytes 3145736 | tf_op jit(solution)/shard_map/ppermute | solution.py:33
  21.4 4.4 %collective-permute-start.6 = (bf16[1024,512]{1,0:T(8,128)(2,1)S(1)}, bf16[1024,512]{1,0:T(8,128)(2,1)}, u32[]{:S(2)}, u32[]{:S(2)}) collective-permute-start(bf16[1024,512]{1,0:T(8,128)(2,1)S(1)} %get-tuple-element.6), channel_id=1, source_target_pairs={{0,2},{2,4},{4,6},{8,10},{10,12},{12,14},{16,18},{18,20},{20,22},{... | collective-permute-start | bytes 3145736 | tf_op jit(solution)/shard_map/ppermute | solution.py:33
  25.8 1.7 %collective-permute-done.1 = bf16[256,512]{1,0:T(8,128)(2,1)S(1)} collective-permute-done((bf16[256,512]{1,0:T(8,128)(2,1)S(1)}, bf16[256,512]{1,0:T(8,128)(2,1)S(1)}, u32[]{:S(2)}, u32[]{:S(2)}) %collective-permute-start.1) | collective-permute-done | bytes 262176 | tf_op jit(solution)/shard_map/ppermute | solution.py:18
  27.5 2.3 %collective-permute-start.3 = (bf16[1024,512]{1,0:T(8,128)(2,1)S(1)}, bf16[1024,512]{1,0:T(8,128)(2,1)}, u32[]{:S(2)}, u32[]{:S(2)}) collective-permute-start(bf16[1024,512]{1,0:T(8,128)(2,1)S(1)} %get-tuple-element.5), channel_id=1, source_target_pairs={{0,6},{2,8},{6,12},{8,14},{10,16},{14,20},{16,22},{18,24},{22,28},... | collective-permute-start | bytes 3145736 | tf_op jit(solution)/shard_map/ppermute | solution.py:33
  29.8 0.0 collective-permute-done.7
  29.8 3.7 %collective-permute-start.2 = (bf16[1024,512]{1,0:T(8,128)(2,1)S(1)}, bf16[1024,512]{1,0:T(8,128)(2,1)}, u32[]{:S(2)}, u32[]{:S(2)}) collective-permute-start(bf16[1024,512]{1,0:T(8,128)(2,1)S(1)} %get-tuple-element.5), channel_id=1, source_target_pairs={{0,2},{2,4},{4,6},{8,10},{10,12},{12,14},{16,18},{18,20},{20,22},{... | collective-permute-start | bytes 3145736 | tf_op jit(solution)/shard_map/ppermute | solution.py:33
  33.5 0.0 collective-permute-done.14
  33.5 4.5 %collective-permute-start.15 = (bf16[1024,512]{1,0:T(8,128)(2,1)S(1)}, bf16[1024,512]{1,0:T(8,128)(2,1)}, u32[]{:S(2)}, u32[]{:S(2)}) collective-permute-start(bf16[1024,512]{1,0:T(8,128)(2,1)S(1)} %collective-permute-done.14), channel_id=1, source_target_pairs={{0,8},{8,16},{16,24},{1,9},{9,17},{17,25}} | collective-permute-start | bytes 3145736 | tf_op jit(solution)/shard_map/ppermute | solution.py:33
  38.0 6.0 %collective-permute-done.11 = bf16[1024,512]{1,0:T(8,128)(2,1)} collective-permute-done((bf16[1024,512]{1,0:T(8,128)(2,1)S(1)}, bf16[1024,512]{1,0:T(8,128)(2,1)}, u32[]{:S(2)}, u32[]{:S(2)}) %collective-permute-start.11) | collective-permute-done | bytes 1048608 | tf_op jit(solution)/shard_map/ppermute | solution.py:33
  44.0 3.7 %collective-permute-start.12 = (bf16[1024,512]{1,0:T(8,128)(2,1)}, bf16[1024,512]{1,0:T(8,128)(2,1)}, u32[]{:S(2)}, u32[]{:S(2)}) collective-permute-start(bf16[1024,512]{1,0:T(8,128)(2,1)} %collective-permute-done.11), channel_id=1, source_target_pairs={{0,8},{8,16},{16,24},{1,9},{9,17},{17,25}} | collective-permute-start | bytes 3145736 | tf_op jit(solution)/shard_map/ppermute | solution.py:33
  47.7 0.0 collective-permute-done.6
  47.7 1.6 %collective-permute-start.16 = (bf16[1024,512]{1,0:T(8,128)(2,1)}, bf16[1024,512]{1,0:T(8,128)(2,1)}, u32[]{:S(2)}, u32[]{:S(2)}) collective-permute-start(bf16[1024,512]{1,0:T(8,128)(2,1)} %collective-permute-done.6), channel_id=1, source_target_pairs={{4,6},{12,14},{20,22},{28,30},{5,7},{13,15},{21,23},{29,31}} | collective-permute-start | bytes 3145736 | tf_op jit(solution)/shard_map/ppermute | solution.py:33
  49.4 3.0 %collective-permute-done.3 = bf16[1024,512]{1,0:T(8,128)(2,1)} collective-permute-done((bf16[1024,512]{1,0:T(8,128)(2,1)S(1)}, bf16[1024,512]{1,0:T(8,128)(2,1)}, u32[]{:S(2)}, u32[]{:S(2)}) %collective-permute-start.3) | collective-permute-done | bytes 1048608 | tf_op jit(solution)/shard_map/ppermute | solution.py:33
  52.4 1.7 %collective-permute-start.8 = (bf16[1024,512]{1,0:T(8,128)(2,1)}, bf16[1024,512]{1,0:T(8,128)(2,1)}, u32[]{:S(2)}, u32[]{:S(2)}) collective-permute-start(bf16[1024,512]{1,0:T(8,128)(2,1)} %collective-permute-done.7), channel_id=1, source_target_pairs={{6,4},{4,2},{14,12},{12,10},{22,20},{20,18},{30,28},{28,26},{7,5},... | collective-permute-start | bytes 3145736 | tf_op jit(solution)/shard_map/ppermute | solution.py:33
  54.1 1.6 %collective-permute-start.13 = (bf16[1024,512]{1,0:T(8,128)(2,1)}, bf16[1024,512]{1,0:T(8,128)(2,1)}, u32[]{:S(2)}, u32[]{:S(2)}) collective-permute-start(bf16[1024,512]{1,0:T(8,128)(2,1)} %collective-permute-done.2), channel_id=1, source_target_pairs={{4,6},{12,14},{20,22},{28,30},{5,7},{13,15},{21,23},{29,31}} | collective-permute-start | bytes 3145736 | tf_op jit(solution)/shard_map/ppermute | solution.py:33
  55.7 0.0 collective-permute-done.15
  55.7 1.7 %collective-permute-start.4 = (bf16[1024,512]{1,0:T(8,128)(2,1)}, bf16[1024,512]{1,0:T(8,128)(2,1)}, u32[]{:S(2)}, u32[]{:S(2)}) collective-permute-start(bf16[1024,512]{1,0:T(8,128)(2,1)} %collective-permute-done.3), channel_id=1, source_target_pairs={{6,4},{4,2},{14,12},{12,10},{22,20},{20,18},{30,28},{28,26},{7,5},... | collective-permute-start | bytes 3145736 | tf_op jit(solution)/shard_map/ppermute | solution.py:33
  58.0 5.7 %collective-permute-done.12 = bf16[1024,512]{1,0:T(8,128)(2,1)} collective-permute-done((bf16[1024,512]{1,0:T(8,128)(2,1)}, bf16[1024,512]{1,0:T(8,128)(2,1)}, u32[]{:S(2)}, u32[]{:S(2)}) %collective-permute-start.12) | collective-permute-done | bytes 1048608 | tf_op jit(solution)/shard_map/ppermute | solution.py:33
  63.8 3.2 %collective-permute-start.19 = (bf16[1024,512]{1,0:T(8,128)(2,1)}, bf16[1024,512]{1,0:T(8,128)(2,1)S(1)}, u32[]{:S(2)}, u32[]{:S(2)}) collective-permute-start(bf16[1024,512]{1,0:T(8,128)(2,1)} %collective-permute-done.15), channel_id=1, source_target_pairs={{0,2},{8,10},{16,18},{24,26},{1,3},{9,11},{17,19},{25,27}} | collective-permute-start | bytes 3145736 | tf_op jit(solution)/shard_map/ppermute | solution.py:33
  67.0 0.1 fusion.21
  67.1 1.4 %collective-permute-start.18 = (bf16[1024,512]{1,0:T(8,128)(2,1)}, bf16[1024,512]{1,0:T(8,128)(2,1)S(1)}, u32[]{:S(2)}, u32[]{:S(2)}) collective-permute-start(bf16[1024,512]{1,0:T(8,128)(2,1)} %collective-permute-done.12), channel_id=1, source_target_pairs={{0,2},{8,10},{16,18},{24,26},{1,3},{9,11},{17,19},{25,27}} | collective-permute-start | bytes 3145736 | tf_op jit(solution)/shard_map/ppermute | solution.py:33
  68.5 1.3 %collective-permute-start.9 = (bf16[1024,512]{1,0:T(8,128)(2,1)}, bf16[1024,512]{1,0:T(8,128)(2,1)S(1)}, u32[]{:S(2)}, u32[]{:S(2)}) collective-permute-start(bf16[1024,512]{1,0:T(8,128)(2,1)} %collective-permute-done.8), channel_id=1, source_target_pairs={{2,0},{10,8},{18,16},{26,24},{3,1},{11,9},{19,17},{27,25}} | collective-permute-start | bytes 3145736 | tf_op jit(solution)/shard_map/ppermute | solution.py:33
  69.8 2.6 %fusion.6 = f32[512,512]{1,0:T(8,128)S(1)} fusion(bf16[1024,512]{1,0:T(8,128)(2,1)} %collective-permute-done.16, bf16[1024,512]{1,0:T(8,128)(2,1)} %collective-permute-done.15, bf16[1024,512]{1,0:T(8,128)(2,1)} %collective-permute-done.8, bf16[2048,512]{1,0:T(8,128)(2,1)S(1)} %multiply_convert_fusion), kind=kOutput, calls=%fused_computation.13 | convolution fusion | flops 537919488 | bytes 5242880 | tf_op jit(solution)/shard_map/dot_general | solution.py:48
  72.4 2.6 %fusion.1 = bf16[512,512]{1,0:T(8,128)(2,1)S(1)} fusion(f32[512,512]{1,0:T(8,128)S(1)} %fusion.6, bf16[1024,512]{1,0:T(8,128)(2,1)} %collective-permute-done.13, bf16[1024,512]{1,0:T(8,128)(2,1)} %collective-permute-done.12, bf16[1024,512]{1,0:T(8,128)(2,1)} %collective-permute-done.4, bf16[2048,512]{1,0:T(8,128)(2,1)S(1)} %multiply_convert_fusion), kind=kOutput, calls=%fused_computation.7 | convolution fusion | flops 538443776 | bytes 5767168 | tf_op jit(solution)/shard_map/dot_general | solution.py:48
  75.1 1.3 %collective-permute-start.17 = (bf16[256,512]{1,0:T(8,128)(2,1)S(1)}, bf16[256,512]{1,0:T(8,128)(2,1)S(1)}, u32[]{:S(2)}, u32[]{:S(2)}) collective-permute-start(bf16[256,512]{1,0:T(8,128)(2,1)S(1)} %dynamic-slice_bitcast_fusion.1), channel_id=1, source_target_pairs={{0,1},{1,0},{2,3},{3,2},{4,5},{5,4},{6,7},{7,6},{8,9},{9,8},{10,11... | collective-permute-start | bytes 786440 | tf_op jit(solution)/shard_map/ppermute | solution.py:18
  76.4 1.3 %collective-permute-start.5 = (bf16[1024,512]{1,0:T(8,128)(2,1)}, bf16[1024,512]{1,0:T(8,128)(2,1)S(1)}, u32[]{:S(2)}, u32[]{:S(2)}) collective-permute-start(bf16[1024,512]{1,0:T(8,128)(2,1)} %collective-permute-done.4), channel_id=1, source_target_pairs={{2,0},{10,8},{18,16},{26,24},{3,1},{11,9},{19,17},{27,25}} | collective-permute-start | bytes 3145736 | tf_op jit(solution)/shard_map/ppermute | solution.py:33
  77.7 2.0 %fusion.3 = f32[512,512]{1,0:T(8,128)S(1)} fusion(bf16[1024,512]{1,0:T(8,128)(2,1)} %collective-permute-done.7, bf16[1024,512]{1,0:T(8,128)(2,1)S(1)} %collective-permute-done.19, bf16[2048,512]{1,0:T(8,128)(2,1)S(1)} %multiply_convert_fusion), kind=kOutput, calls=%fused_computation.10 | convolution fusion | flops 537395200 | bytes 4194304 | tf_op jit(solution)/shard_map/dot_general | solution.py:48
  79.7 2.0 %fusion.2 = bf16[512,512]{1,0:T(8,128)(2,1)S(1)} fusion(f32[512,512]{1,0:T(8,128)S(1)} %fusion.3, bf16[1024,512]{1,0:T(8,128)(2,1)} %collective-permute-done.3, bf16[1024,512]{1,0:T(8,128)(2,1)S(1)} %collective-permute-done.18, bf16[2048,512]{1,0:T(8,128)(2,1)S(1)} %multiply_convert_fusion), kind=kOutput, calls=%fused_computation.8 | convolution fusion | flops 537919488 | bytes 4718592 | tf_op jit(solution)/shard_map/dot_general | solution.py:48
  81.7 0.9 collective-permute-start.20
  82.6 2.0 %fusion.11 = f32[512,512]{1,0:T(8,128)S(1)} fusion(bf16[1024,512]{1,0:T(8,128)(2,1)} %collective-permute-done.6, bf16[1024,512]{1,0:T(8,128)(2,1)S(1)} %collective-permute-done.9, bf16[2048,512]{1,0:T(8,128)(2,1)S(1)} %multiply_convert_fusion), kind=kOutput, calls=%fused_computation.18 | convolution fusion | flops 537395200 | bytes 4194304 | tf_op jit(solution)/shard_map/dot_general | solution.py:48
  84.6 3.8 %collective-permute-done.5 = bf16[1024,512]{1,0:T(8,128)(2,1)S(1)} collective-permute-done((bf16[1024,512]{1,0:T(8,128)(2,1)}, bf16[1024,512]{1,0:T(8,128)(2,1)S(1)}, u32[]{:S(2)}, u32[]{:S(2)}) %collective-permute-start.5) | collective-permute-done | bytes 1048608 | tf_op jit(solution)/shard_map/ppermute | solution.py:33
  88.4 2.0 %fusion = bf16[512,512]{1,0:T(8,128)(2,1)S(1)} fusion(f32[512,512]{1,0:T(8,128)S(1)} %fusion.11, bf16[1024,512]{1,0:T(8,128)(2,1)} %collective-permute-done.2, bf16[1024,512]{1,0:T(8,128)(2,1)S(1)} %collective-permute-done.5, bf16[2048,512]{1,0:T(8,128)(2,1)S(1)} %multiply_convert_fusion), kind=kOutput, calls=%fused_computation.6 | convolution fusion | flops 537919488 | bytes 4718592 | tf_op jit(solution)/shard_map/dot_general | solution.py:48
  90.5 0.9 collective-permute-start.10
  91.3 0.1 fusion.17
  91.5 0.1 fusion.15
  91.6 7.8 %collective-permute-done.10 = bf16[256,512]{1,0:T(8,128)(2,1)S(1)} collective-permute-done((bf16[256,512]{1,0:T(8,128)(2,1)S(1)}, bf16[256,512]{1,0:T(8,128)(2,1)S(1)}, u32[]{:S(2)}, u32[]{:S(2)}) %collective-permute-start.10) | collective-permute-done | bytes 262176 | tf_op jit(solution)/shard_map/ppermute | solution.py:18
  99.4 0.1 fusion.19
  99.5 1.5 %pad_maximum_fusion = f32[256,2048]{1,0:T(8,128)} fusion(f32[256,512]{1,0:T(8,128)S(1)} %fusion.15, f32[256,512]{1,0:T(8,128)S(1)} %fusion.17, f32[256,512]{1,0:T(8,128)S(1)} %fusion.19, f32[256,512]{1,0:T(8,128)S(1)} %fusion.21), kind=kLoop, calls=%fused_computation.2 | loop fusion | flops 1572864 | bytes 4194304 | tf_op jit(solution)/shard_map/concatenate | solution.py:102
  (17 shorter events, 0.2 us)
Async XLA Ops:
  5.2 4.6 %collective-permute-start = (f32[2,512]{1,0:T(2,128)S(1)}, f32[2,512]{1,0:T(2,128)S(1)}, u32[]{:S(2)}, u32[]{:S(2)}) collective-permute-start(f32[2,512]{1,0:T(2,128)S(1)} %pad_maximum_fusion.1), channel_id=1, source_target_pairs={{0,1},{1,0},{2,3},{3,2},{4,5},{5,4},{6,7},{7,6},{8,9},{9,8},{10,11... | collective-permute-start | bytes 12296 | tf_op jit(solution)/shard_map/ppermute | solution.py:18
  12.8 17.0 %collective-permute-start.7 = (bf16[1024,512]{1,0:T(8,128)(2,1)S(1)}, bf16[1024,512]{1,0:T(8,128)(2,1)}, u32[]{:S(2)}, u32[]{:S(2)}) collective-permute-start(bf16[1024,512]{1,0:T(8,128)(2,1)S(1)} %get-tuple-element.6), channel_id=1, source_target_pairs={{0,6},{2,8},{6,12},{8,14},{10,16},{14,20},{16,22},{18,24},{22,28},... | collective-permute-start | bytes 3145736 | tf_op jit(solution)/shard_map/ppermute | solution.py:33
  16.0 17.6 %collective-permute-start.14 = (bf16[1024,512]{1,0:T(8,128)(2,1)S(1)}, bf16[1024,512]{1,0:T(8,128)(2,1)S(1)}, u32[]{:S(2)}, u32[]{:S(2)}) collective-permute-start(bf16[1024,512]{1,0:T(8,128)(2,1)S(1)} %get-tuple-element.6), channel_id=1, source_target_pairs={{4,0},{12,8},{20,16},{28,24},{5,1},{13,9},{21,17},{29,25}} | collective-permute-start | bytes 3145736 | tf_op jit(solution)/shard_map/ppermute | solution.py:33
  18.6 9.0 %collective-permute-start.1 = (bf16[256,512]{1,0:T(8,128)(2,1)S(1)}, bf16[256,512]{1,0:T(8,128)(2,1)S(1)}, u32[]{:S(2)}, u32[]{:S(2)}) collective-permute-start(bf16[256,512]{1,0:T(8,128)(2,1)S(1)} %dynamic-slice_bitcast_fusion.3), channel_id=1, source_target_pairs={{0,1},{1,0},{2,3},{3,2},{4,5},{5,4},{6,7},{7,6},{8,9},{9,8},{10,11... | collective-permute-start | bytes 786440 | tf_op jit(solution)/shard_map/ppermute | solution.py:18
  20.1 23.8 %collective-permute-start.11 = (bf16[1024,512]{1,0:T(8,128)(2,1)S(1)}, bf16[1024,512]{1,0:T(8,128)(2,1)}, u32[]{:S(2)}, u32[]{:S(2)}) collective-permute-start(bf16[1024,512]{1,0:T(8,128)(2,1)S(1)} %get-tuple-element.5), channel_id=1, source_target_pairs={{4,0},{12,8},{20,16},{28,24},{5,1},{13,9},{21,17},{29,25}} | collective-permute-start | bytes 3145736 | tf_op jit(solution)/shard_map/ppermute | solution.py:33
  21.4 26.3 %collective-permute-start.6 = (bf16[1024,512]{1,0:T(8,128)(2,1)S(1)}, bf16[1024,512]{1,0:T(8,128)(2,1)}, u32[]{:S(2)}, u32[]{:S(2)}) collective-permute-start(bf16[1024,512]{1,0:T(8,128)(2,1)S(1)} %get-tuple-element.6), channel_id=1, source_target_pairs={{0,2},{2,4},{4,6},{8,10},{10,12},{12,14},{16,18},{18,20},{20,22},{... | collective-permute-start | bytes 3145736 | tf_op jit(solution)/shard_map/ppermute | solution.py:33
  27.5 24.9 %collective-permute-start.3 = (bf16[1024,512]{1,0:T(8,128)(2,1)S(1)}, bf16[1024,512]{1,0:T(8,128)(2,1)}, u32[]{:S(2)}, u32[]{:S(2)}) collective-permute-start(bf16[1024,512]{1,0:T(8,128)(2,1)S(1)} %get-tuple-element.5), channel_id=1, source_target_pairs={{0,6},{2,8},{6,12},{8,14},{10,16},{14,20},{16,22},{18,24},{22,28},... | collective-permute-start | bytes 3145736 | tf_op jit(solution)/shard_map/ppermute | solution.py:33
  29.8 24.3 %collective-permute-start.2 = (bf16[1024,512]{1,0:T(8,128)(2,1)S(1)}, bf16[1024,512]{1,0:T(8,128)(2,1)}, u32[]{:S(2)}, u32[]{:S(2)}) collective-permute-start(bf16[1024,512]{1,0:T(8,128)(2,1)S(1)} %get-tuple-element.5), channel_id=1, source_target_pairs={{0,2},{2,4},{4,6},{8,10},{10,12},{12,14},{16,18},{18,20},{20,22},{... | collective-permute-start | bytes 3145736 | tf_op jit(solution)/shard_map/ppermute | solution.py:33
  33.5 22.2 %collective-permute-start.15 = (bf16[1024,512]{1,0:T(8,128)(2,1)S(1)}, bf16[1024,512]{1,0:T(8,128)(2,1)}, u32[]{:S(2)}, u32[]{:S(2)}) collective-permute-start(bf16[1024,512]{1,0:T(8,128)(2,1)S(1)} %collective-permute-done.14), channel_id=1, source_target_pairs={{0,8},{8,16},{16,24},{1,9},{9,17},{17,25}} | collective-permute-start | bytes 3145736 | tf_op jit(solution)/shard_map/ppermute | solution.py:33
  44.0 19.8 %collective-permute-start.12 = (bf16[1024,512]{1,0:T(8,128)(2,1)}, bf16[1024,512]{1,0:T(8,128)(2,1)}, u32[]{:S(2)}, u32[]{:S(2)}) collective-permute-start(bf16[1024,512]{1,0:T(8,128)(2,1)} %collective-permute-done.11), channel_id=1, source_target_pairs={{0,8},{8,16},{16,24},{1,9},{9,17},{17,25}} | collective-permute-start | bytes 3145736 | tf_op jit(solution)/shard_map/ppermute | solution.py:33
  47.7 19.4 %collective-permute-start.16 = (bf16[1024,512]{1,0:T(8,128)(2,1)}, bf16[1024,512]{1,0:T(8,128)(2,1)}, u32[]{:S(2)}, u32[]{:S(2)}) collective-permute-start(bf16[1024,512]{1,0:T(8,128)(2,1)} %collective-permute-done.6), channel_id=1, source_target_pairs={{4,6},{12,14},{20,22},{28,30},{5,7},{13,15},{21,23},{29,31}} | collective-permute-start | bytes 3145736 | tf_op jit(solution)/shard_map/ppermute | solution.py:33
  52.4 16.1 %collective-permute-start.8 = (bf16[1024,512]{1,0:T(8,128)(2,1)}, bf16[1024,512]{1,0:T(8,128)(2,1)}, u32[]{:S(2)}, u32[]{:S(2)}) collective-permute-start(bf16[1024,512]{1,0:T(8,128)(2,1)} %collective-permute-done.7), channel_id=1, source_target_pairs={{6,4},{4,2},{14,12},{12,10},{22,20},{20,18},{30,28},{28,26},{7,5},... | collective-permute-start | bytes 3145736 | tf_op jit(solution)/shard_map/ppermute | solution.py:33
  54.1 18.3 %collective-permute-start.13 = (bf16[1024,512]{1,0:T(8,128)(2,1)}, bf16[1024,512]{1,0:T(8,128)(2,1)}, u32[]{:S(2)}, u32[]{:S(2)}) collective-permute-start(bf16[1024,512]{1,0:T(8,128)(2,1)} %collective-permute-done.2), channel_id=1, source_target_pairs={{4,6},{12,14},{20,22},{28,30},{5,7},{13,15},{21,23},{29,31}} | collective-permute-start | bytes 3145736 | tf_op jit(solution)/shard_map/ppermute | solution.py:33
  55.7 16.7 %collective-permute-start.4 = (bf16[1024,512]{1,0:T(8,128)(2,1)}, bf16[1024,512]{1,0:T(8,128)(2,1)}, u32[]{:S(2)}, u32[]{:S(2)}) collective-permute-start(bf16[1024,512]{1,0:T(8,128)(2,1)} %collective-permute-done.3), channel_id=1, source_target_pairs={{6,4},{4,2},{14,12},{12,10},{22,20},{20,18},{30,28},{28,26},{7,5},... | collective-permute-start | bytes 3145736 | tf_op jit(solution)/shard_map/ppermute | solution.py:33
  63.8 13.9 %collective-permute-start.19 = (bf16[1024,512]{1,0:T(8,128)(2,1)}, bf16[1024,512]{1,0:T(8,128)(2,1)S(1)}, u32[]{:S(2)}, u32[]{:S(2)}) collective-permute-start(bf16[1024,512]{1,0:T(8,128)(2,1)} %collective-permute-done.15), channel_id=1, source_target_pairs={{0,2},{8,10},{16,18},{24,26},{1,3},{9,11},{17,19},{25,27}} | collective-permute-start | bytes 3145736 | tf_op jit(solution)/shard_map/ppermute | solution.py:33
  67.1 12.6 %collective-permute-start.18 = (bf16[1024,512]{1,0:T(8,128)(2,1)}, bf16[1024,512]{1,0:T(8,128)(2,1)S(1)}, u32[]{:S(2)}, u32[]{:S(2)}) collective-permute-start(bf16[1024,512]{1,0:T(8,128)(2,1)} %collective-permute-done.12), channel_id=1, source_target_pairs={{0,2},{8,10},{16,18},{24,26},{1,3},{9,11},{17,19},{25,27}} | collective-permute-start | bytes 3145736 | tf_op jit(solution)/shard_map/ppermute | solution.py:33
  68.5 14.1 %collective-permute-start.9 = (bf16[1024,512]{1,0:T(8,128)(2,1)}, bf16[1024,512]{1,0:T(8,128)(2,1)S(1)}, u32[]{:S(2)}, u32[]{:S(2)}) collective-permute-start(bf16[1024,512]{1,0:T(8,128)(2,1)} %collective-permute-done.8), channel_id=1, source_target_pairs={{2,0},{10,8},{18,16},{26,24},{3,1},{11,9},{19,17},{27,25}} | collective-permute-start | bytes 3145736 | tf_op jit(solution)/shard_map/ppermute | solution.py:33
  75.1 16.3 %collective-permute-start.17 = (bf16[256,512]{1,0:T(8,128)(2,1)S(1)}, bf16[256,512]{1,0:T(8,128)(2,1)S(1)}, u32[]{:S(2)}, u32[]{:S(2)}) collective-permute-start(bf16[256,512]{1,0:T(8,128)(2,1)S(1)} %dynamic-slice_bitcast_fusion.1), channel_id=1, source_target_pairs={{0,1},{1,0},{2,3},{3,2},{4,5},{5,4},{6,7},{7,6},{8,9},{9,8},{10,11... | collective-permute-start | bytes 786440 | tf_op jit(solution)/shard_map/ppermute | solution.py:18
  76.4 12.1 %collective-permute-start.5 = (bf16[1024,512]{1,0:T(8,128)(2,1)}, bf16[1024,512]{1,0:T(8,128)(2,1)S(1)}, u32[]{:S(2)}, u32[]{:S(2)}) collective-permute-start(bf16[1024,512]{1,0:T(8,128)(2,1)} %collective-permute-done.4), channel_id=1, source_target_pairs={{2,0},{10,8},{18,16},{26,24},{3,1},{11,9},{19,17},{27,25}} | collective-permute-start | bytes 3145736 | tf_op jit(solution)/shard_map/ppermute | solution.py:33
  81.7 9.7 %collective-permute-start.20 = (bf16[256,512]{1,0:T(8,128)(2,1)S(1)}, bf16[256,512]{1,0:T(8,128)(2,1)S(1)}, u32[]{:S(2)}, u32[]{:S(2)}) collective-permute-start(bf16[256,512]{1,0:T(8,128)(2,1)S(1)} %dynamic-slice_bitcast_fusion), channel_id=1, source_target_pairs={{0,1},{1,0},{2,3},{3,2},{4,5},{5,4},{6,7},{7,6},{8,9},{9,8},{10,11... | collective-permute-start | bytes 786440 | tf_op jit(solution)/shard_map/ppermute | solution.py:18
  90.5 8.9 %collective-permute-start.10 = (bf16[256,512]{1,0:T(8,128)(2,1)S(1)}, bf16[256,512]{1,0:T(8,128)(2,1)S(1)}, u32[]{:S(2)}, u32[]{:S(2)}) collective-permute-start(bf16[256,512]{1,0:T(8,128)(2,1)S(1)} %dynamic-slice_bitcast_fusion.2), channel_id=1, source_target_pairs={{0,1},{1,0},{2,3},{3,2},{4,5},{5,4},{6,7},{7,6},{8,9},{9,8},{10,11... | collective-permute-start | bytes 786440 | tf_op jit(solution)/shard_map/ppermute | solution.py:18

commit v3 on v2

--- a/solution.py
+++ b/solution.py
@@ -4,7 +4,7 @@
 from jax.sharding import PartitionSpec as P
 
 TAPS = 4
-CHUNKS = 2
+CHUNKS = 1
 
 
 def shifted(value, axis, steps):
@@ -33,15 +33,22 @@
         return lax.ppermute(value, "snp", pairs)
 
     groups = range(0, count, 4)
-    near = send(piece, [(b + i, b + i + 1) for b in groups for i in range(3)])
-    far = send(piece, [p for b in groups for p in ((b, b + 3), (b + 1, b + 4), (b + 3, b + 6))])
+    cross_one = send(piece, [(b + 1, b + 2) for b in groups])
+    cross_three = send(piece, [(b, b + 3) for b in groups])
+    up_three = send(piece, [p for b in groups for p in ((b + 1, b + 4), (b + 3, b + 6))])
     back = send(piece, [(b + 2, b) for b in groups])
-    hop_a = send(back, [(b, b + 4) for b in groups])
-    hop_b = send(far, [p for b in groups for p in ((b + 3, b + 2), (b + 2, b + 1))])
-    hop_c = send(near, [(b + 2, b + 3) for b in groups])
-    last_a = send(hop_b, [(b + 1, b) for b in groups])
-    last_b = send(hop_a, [(b, b + 1) for b in groups])
-    return [near + last_a, hop_a + hop_b + hop_c, far + last_b]
+    inner_one = send(piece, [p for b in groups for p in ((b, b + 1), (b + 2, b + 3))])
+    up_two = send(back, [(b, b + 4) for b in groups])
+    back_two = send(up_three, [(b + 2, b + 1) for b in groups])
+    swap_a = send(cross_one, [(b + 2, b + 3) for b in groups])
+    swap_b = send(cross_three, [(b + 3, b + 2) for b in groups])
+    last_one = send(back_two, [(b + 1, b) for b in groups])
+    last_three = send(up_two, [(b, b + 1) for b in groups])
+    return [
+        inner_one + cross_one + last_one,
+        up_two + back_two + swap_a + swap_b,
+        cross_three + up_three + last_three,
+    ]
 
 
 def tile_term(standard, neighbour):

time: 103 us -> 113 us (1.097); the launches traced: 101 us -> 112 us
  waiting for transfers between devices: 29.8 us -> 46.7 us
  starting transfers between devices: 45.7 us -> 42.6 us
  other arithmetic: 9.94 us -> 7.89 us
    ppermute x16 -> x11, waiting for transfers between devices: 18.6 us -> 33.7 us  [send(): return lax.ppermute(value, 'snp', pairs)]
    ppermute x16 -> x11, starting transfers between devices: 38 us -> 33.2 us  [send(): return lax.ppermute(value, 'snp', pairs)]
    convert_element_type x1, other arithmetic: 2.78 us -> 0.59 us  [local(): standard = ((dosage - mean) * lax.rsqrt(var + 1e-05)).astype(jnp.bfloat16)]
    ppermute x5, waiting for transfers between devices: 11.1 us -> 13 us  [rotated(): lax.ppermute(value, axis, [(source, (source + steps) % count) for source...]
    ppermute x5, starting transfers between devices: 7.63 us -> 9.36 us  [rotated(): lax.ppermute(value, axis, [(source, (source + steps) % count) for source...]
    dot_general x7 -> x4, matrix products: 14.5 us -> 14.3 us  [tile_term(): lax.dot_general(standard, neighbour, (((0,), (0,)), ((), ())), preferred_...]
  transfers between devices with their start and end apart: 21 -> 16, of which waited for: 7 -> 6; matrix products, arithmetic and copies ran while one was open for 15% -> 13% of each run, Pallas kernels for 0% -> 0%
where the time goes in v3:
time: 113 us; the launch traced here: 112 us
  waiting for transfers between devices  46.7 us (41%)
  starting transfers between devices  42.6 us (38%)
  matrix products  14.3 us (13%)
  other arithmetic  7.89 us (7%)
    ppermute x11, waiting for transfers between devices, send(): return lax.ppermute(value, 'snp', pairs)  33.7 us
    ppermute x11, starting transfers between devices, send(): return lax.ppermute(value, 'snp', pairs)  33.2 us
    dot_general x4, matrix products, tile_term(): lax.dot_general(standard, neighbour, (((0,), (0,)), ((), ())), preferred_...  14.3 us
    ppermute x5, waiting for transfers between devices, rotated(): lax.ppermute(value, axis, [(source, (source + steps) % count) for source...  13 us
    ppermute x5, starting transfers between devices, rotated(): lax.ppermute(value, axis, [(source, (source + steps) % count) for source...  9.36 us
    reduce_sum x1, other arithmetic, local(): part_m2 = jnp.sum(deviation * deviation, axis=0)  2.86 us
    reduce_sum x1, other arithmetic, local(): part_mean = jnp.sum(dosage, axis=0) / rows  2.52 us
  transfers between devices with their start and end apart: 16, of which 6 were waited for; matrix products, arithmetic and copies ran while one was open for 13% of the time, Pallas kernels for 0%

profile of v3, /device:TPU:0, one launch (start us, length us, event | category | flops | bytes accessed | tf_op | source)
XLA Modules:
  0.0 112.5 jit_solution(10102657552889395288)
XLA Ops:
  0.0 2.5 %reduce_sum.18 = f32[512]{0:T(512)S(1)} reduce(f32[2048,512]{1,0:T(8,128)} %param.2, f32[]{:T(128)} %constant.59.clone.1), dimensions={0}, to_apply=%region_0.0 | reduce | flops 1048064 | bytes 4196356 | tf_op jit(solution)/shard_map/reduce_sum | solution.py:66
  2.5 0.0 copy-start
  2.5 2.9 %multiply_reduce_fusion = f32[512]{0:T(512)S(1)} fusion(f32[2048,512]{1,0:T(8,128)} %param.2, f32[512]{0:T(512)S(1)} %broadcast_multiply_fusion), kind=kLoop, calls=%fused_computation.1 | loop fusion | flops 3145216 | bytes 4198400 | tf_op jit(solution)/shard_map/reduce_sum | solution.py:68
  5.4 3.0 %collective-permute-start = (f32[2,512]{1,0:T(2,128)S(1)}, f32[2,512]{1,0:T(2,128)S(1)}, u32[]{:S(2)}, u32[]{:S(2)}) collective-permute-start(f32[2,512]{1,0:T(2,128)S(1)} %pad_maximum_fusion.1), channel_id=1, source_target_pairs={{0,1},{1,0},{2,3},{3,2},{4,5},{5,4},{6,7},{7,6},{8,9},{9,8},{10,11... | collective-permute-start | bytes 12296 | tf_op jit(solution)/shard_map/ppermute | solution.py:18
  8.4 1.6 %collective-permute-done = f32[2,512]{1,0:T(2,128)S(1)} collective-permute-done((f32[2,512]{1,0:T(2,128)S(1)}, f32[2,512]{1,0:T(2,128)S(1)}, u32[]{:S(2)}, u32[]{:S(2)}) %collective-permute-start) | collective-permute-done | bytes 4128 | tf_op jit(solution)/shard_map/ppermute | solution.py:18
  10.0 0.0 copy-done
  10.0 0.6 multiply_convert_fusion
  10.6 1.3 %collective-permute-start.8 = (bf16[2048,512]{1,0:T(8,128)(2,1)S(1)}, bf16[2048,512]{1,0:T(8,128)(2,1)}, u32[]{:S(2)}, u32[]{:S(2)}) collective-permute-start(bf16[2048,512]{1,0:T(8,128)(2,1)S(1)} %multiply_convert_fusion), channel_id=1, source_target_pairs={{4,0},{12,8},{20,16},{28,24},{5,1},{13,9},{21,17},{29,25}} | collective-permute-start | bytes 6291464 | tf_op jit(solution)/shard_map/ppermute | solution.py:33
  11.9 2.0 %collective-permute-start.4 = (bf16[2048,512]{1,0:T(8,128)(2,1)S(1)}, bf16[2048,512]{1,0:T(8,128)(2,1)}, u32[]{:S(2)}, u32[]{:S(2)}) collective-permute-start(bf16[2048,512]{1,0:T(8,128)(2,1)S(1)} %multiply_convert_fusion), channel_id=1, source_target_pairs={{2,8},{6,12},{10,16},{14,20},{18,24},{22,28},{3,9},{7,13},{11,17},... | collective-permute-start | bytes 6291464 | tf_op jit(solution)/shard_map/ppermute | solution.py:33
  13.9 10.2 %collective-permute-start.11 = (bf16[2048,512]{1,0:T(8,128)(2,1)S(1)}, bf16[2048,512]{1,0:T(8,128)(2,1)}, u32[]{:S(2)}, u32[]{:S(2)}) collective-permute-start(bf16[2048,512]{1,0:T(8,128)(2,1)S(1)} %multiply_convert_fusion), channel_id=1, source_target_pairs={{0,6},{8,14},{16,22},{24,30},{1,7},{9,15},{17,23},{25,31}} | collective-permute-start | bytes 6291464 | tf_op jit(solution)/shard_map/ppermute | solution.py:33
  24.1 2.0 %collective-permute-start.3 = (bf16[2048,512]{1,0:T(8,128)(2,1)S(1)}, bf16[2048,512]{1,0:T(8,128)(2,1)}, u32[]{:S(2)}, u32[]{:S(2)}) collective-permute-start(bf16[2048,512]{1,0:T(8,128)(2,1)S(1)} %multiply_convert_fusion), channel_id=1, source_target_pairs={{2,4},{10,12},{18,20},{26,28},{3,5},{11,13},{19,21},{27,29}} | collective-permute-start | bytes 6291464 | tf_op jit(solution)/shard_map/ppermute | solution.py:33
  26.1 12.6 %collective-permute-done.8 = bf16[2048,512]{1,0:T(8,128)(2,1)} collective-permute-done((bf16[2048,512]{1,0:T(8,128)(2,1)S(1)}, bf16[2048,512]{1,0:T(8,128)(2,1)}, u32[]{:S(2)}, u32[]{:S(2)}) %collective-permute-start.8) | collective-permute-done | bytes 2097184 | tf_op jit(solution)/shard_map/ppermute | solution.py:33
  38.7 5.3 %collective-permute-start.9 = (bf16[2048,512]{1,0:T(8,128)(2,1)}, bf16[2048,512]{1,0:T(8,128)(2,1)}, u32[]{:S(2)}, u32[]{:S(2)}) collective-permute-start(bf16[2048,512]{1,0:T(8,128)(2,1)} %collective-permute-done.8), channel_id=1, source_target_pairs={{0,8},{8,16},{16,24},{1,9},{9,17},{17,25}} | collective-permute-start | bytes 6291464 | tf_op jit(solution)/shard_map/ppermute | solution.py:33
  44.0 0.0 collective-permute-done.4
  44.0 2.0 %collective-permute-start.5 = (bf16[2048,512]{1,0:T(8,128)(2,1)}, bf16[2048,512]{1,0:T(8,128)(2,1)}, u32[]{:S(2)}, u32[]{:S(2)}) collective-permute-start(bf16[2048,512]{1,0:T(8,128)(2,1)} %collective-permute-done.4), channel_id=1, source_target_pairs={{4,2},{12,10},{20,18},{28,26},{5,3},{13,11},{21,19},{29,27}} | collective-permute-start | bytes 6291464 | tf_op jit(solution)/shard_map/ppermute | solution.py:33
  46.0 21.2 %collective-permute-done.11 = bf16[2048,512]{1,0:T(8,128)(2,1)} collective-permute-done((bf16[2048,512]{1,0:T(8,128)(2,1)S(1)}, bf16[2048,512]{1,0:T(8,128)(2,1)}, u32[]{:S(2)}, u32[]{:S(2)}) %collective-permute-start.11) | collective-permute-done | bytes 2097184 | tf_op jit(solution)/shard_map/ppermute | solution.py:33
  67.2 2.0 %collective-permute-start.12 = (bf16[2048,512]{1,0:T(8,128)(2,1)}, bf16[2048,512]{1,0:T(8,128)(2,1)}, u32[]{:S(2)}, u32[]{:S(2)}) collective-permute-start(bf16[2048,512]{1,0:T(8,128)(2,1)} %collective-permute-done.11), channel_id=1, source_target_pairs={{6,4},{14,12},{22,20},{30,28},{7,5},{15,13},{23,21},{31,29}} | collective-permute-start | bytes 6291464 | tf_op jit(solution)/shard_map/ppermute | solution.py:33
  69.2 0.0 collective-permute-done.3
  69.2 2.0 %collective-permute-start.10 = (bf16[2048,512]{1,0:T(8,128)(2,1)}, bf16[2048,512]{1,0:T(8,128)(2,1)}, u32[]{:S(2)}, u32[]{:S(2)}) collective-permute-start(bf16[2048,512]{1,0:T(8,128)(2,1)} %collective-permute-done.3), channel_id=1, source_target_pairs={{4,6},{12,14},{20,22},{28,30},{5,7},{13,15},{21,23},{29,31}} | collective-permute-start | bytes 6291464 | tf_op jit(solution)/shard_map/ppermute | solution.py:33
  71.1 0.0 collective-permute-done.9
  71.1 2.6 %collective-permute-start.14 = (bf16[2048,512]{1,0:T(8,128)(2,1)}, bf16[2048,512]{1,0:T(8,128)(2,1)}, u32[]{:S(2)}, u32[]{:S(2)}) collective-permute-start(bf16[2048,512]{1,0:T(8,128)(2,1)} %collective-permute-done.9), channel_id=1, source_target_pairs={{0,2},{8,10},{16,18},{24,26},{1,3},{9,11},{17,19},{25,27}} | collective-permute-start | bytes 6291464 | tf_op jit(solution)/shard_map/ppermute | solution.py:33
  73.7 1.3 %convolution_convert_fusion = bf16[512,512]{1,0:T(8,128)(2,1)S(1)} fusion(bf16[2048,512]{1,0:T(8,128)(2,1)S(1)} %multiply_convert_fusion), kind=kOutput, calls=%fused_computation.16 | convolution fusion | flops 1074003968 | bytes 2621440 | tf_op jit(solution)/shard_map/dot_general | solution.py:55
  75.0 2.1 %collective-permute-start.1 = (bf16[256,512]{1,0:T(8,128)(2,1)S(1)}, bf16[256,512]{1,0:T(8,128)(2,1)S(1)}, u32[]{:S(2)}, u32[]{:S(2)}) collective-permute-start(bf16[256,512]{1,0:T(8,128)(2,1)S(1)} %dynamic-slice_bitcast_fusion.3), channel_id=1, source_target_pairs={{0,1},{1,0},{2,3},{3,2},{4,5},{5,4},{6,7},{7,6},{8,9},{9,8},{10,11... | collective-permute-start | bytes 786440 | tf_op jit(solution)/shard_map/ppermute | solution.py:18
  77.1 4.4 %collective-permute-done.1 = bf16[256,512]{1,0:T(8,128)(2,1)S(1)} collective-permute-done((bf16[256,512]{1,0:T(8,128)(2,1)S(1)}, bf16[256,512]{1,0:T(8,128)(2,1)S(1)}, u32[]{:S(2)}, u32[]{:S(2)}) %collective-permute-start.1) | collective-permute-done | bytes 262176 | tf_op jit(solution)/shard_map/ppermute | solution.py:18
  81.5 2.6 %collective-permute-start.2 = (bf16[2048,512]{1,0:T(8,128)(2,1)S(1)}, bf16[2048,512]{1,0:T(8,128)(2,1)}, u32[]{:S(2)}, u32[]{:S(2)}) collective-permute-start(bf16[2048,512]{1,0:T(8,128)(2,1)S(1)} %multiply_convert_fusion), channel_id=1, source_target_pairs={{0,2},{4,6},{8,10},{12,14},{16,18},{20,22},{24,26},{28,30},{1,3},{... | collective-permute-start | bytes 6291464 | tf_op jit(solution)/shard_map/ppermute | solution.py:33
  84.1 0.0 collective-permute-done.5
  84.1 1.3 %collective-permute-start.6 = (bf16[2048,512]{1,0:T(8,128)(2,1)}, bf16[2048,512]{1,0:T(8,128)(2,1)}, u32[]{:S(2)}, u32[]{:S(2)}) collective-permute-start(bf16[2048,512]{1,0:T(8,128)(2,1)} %collective-permute-done.5), channel_id=1, source_target_pairs={{2,0},{10,8},{18,16},{26,24},{3,1},{11,9},{19,17},{27,25}} | collective-permute-start | bytes 6291464 | tf_op jit(solution)/shard_map/ppermute | solution.py:33
  86.0 0.1 fusion.26
  86.1 0.0 collective-permute-done.12
  86.2 0.0 collective-permute-done.10
  86.2 4.7 %fusion.13 = bf16[512,512]{1,0:T(8,128)(2,1)S(1)} fusion(bf16[2048,512]{1,0:T(8,128)(2,1)S(1)} %multiply_convert_fusion, bf16[2048,512]{1,0:T(8,128)(2,1)} %collective-permute-done.12, bf16[2048,512]{1,0:T(8,128)(2,1)} %collective-permute-done.10, bf16[2048,512]{1,0:T(8,128)(2,1)} %collective-permute-done.9, bf16[2048,512]{1,0:T(8,128)(2,1)} %collective-permute-done.5), kind=kOutput, calls=%fused_computation.14 | convolution fusion | flops 1077149696 | bytes 11010048 | tf_op jit(solution)/shard_map/dot_general | solution.py:55
  91.0 2.1 %collective-permute-start.13 = (bf16[256,512]{1,0:T(8,128)(2,1)S(1)}, bf16[256,512]{1,0:T(8,128)(2,1)S(1)}, u32[]{:S(2)}, u32[]{:S(2)}) collective-permute-start(bf16[256,512]{1,0:T(8,128)(2,1)S(1)} %dynamic-slice_bitcast_fusion.1), channel_id=1, source_target_pairs={{0,1},{1,0},{2,3},{3,2},{4,5},{5,4},{6,7},{7,6},{8,9},{9,8},{10,11... | collective-permute-start | bytes 786440 | tf_op jit(solution)/shard_map/ppermute | solution.py:18
  93.0 0.0 collective-permute-done.14
  93.0 4.1 %fusion.16 = bf16[512,512]{1,0:T(8,128)(2,1)S(1)} fusion(bf16[2048,512]{1,0:T(8,128)(2,1)S(1)} %multiply_convert_fusion, bf16[2048,512]{1,0:T(8,128)(2,1)} %collective-permute-done.14, bf16[2048,512]{1,0:T(8,128)(2,1)} %collective-permute-done.11, bf16[2048,512]{1,0:T(8,128)(2,1)} %collective-permute-done.4), kind=kOutput, calls=%fused_computation.15 | convolution fusion | flops 1076101120 | bytes 8912896 | tf_op jit(solution)/shard_map/dot_general | solution.py:55
  97.2 0.1 collective-permute-start.15
  97.3 0.0 collective-permute-done.2
  97.3 0.0 collective-permute-done.6
  97.3 4.1 %fusion.10 = bf16[512,512]{1,0:T(8,128)(2,1)S(1)} fusion(bf16[2048,512]{1,0:T(8,128)(2,1)S(1)} %multiply_convert_fusion, bf16[2048,512]{1,0:T(8,128)(2,1)} %collective-permute-done.6, bf16[2048,512]{1,0:T(8,128)(2,1)} %collective-permute-done.2, bf16[2048,512]{1,0:T(8,128)(2,1)} %collective-permute-done.3), kind=kOutput, calls=%fused_computation.13 | convolution fusion | flops 1076101120 | bytes 8912896 | tf_op jit(solution)/shard_map/dot_general | solution.py:55
  101.5 2.1 %collective-permute-start.7 = (bf16[256,512]{1,0:T(8,128)(2,1)S(1)}, bf16[256,512]{1,0:T(8,128)(2,1)S(1)}, u32[]{:S(2)}, u32[]{:S(2)}) collective-permute-start(bf16[256,512]{1,0:T(8,128)(2,1)S(1)} %dynamic-slice_bitcast_fusion.2), channel_id=1, source_target_pairs={{0,1},{1,0},{2,3},{3,2},{4,5},{5,4},{6,7},{7,6},{8,9},{9,8},{10,11... | collective-permute-start | bytes 786440 | tf_op jit(solution)/shard_map/ppermute | solution.py:18
  103.6 0.0 collective-permute-done.13
  103.6 0.1 fusion.22
  103.7 1.6 %collective-permute-done.15 = bf16[256,512]{1,0:T(8,128)(2,1)S(1)} collective-permute-done((bf16[256,512]{1,0:T(8,128)(2,1)S(1)}, bf16[256,512]{1,0:T(8,128)(2,1)S(1)}, u32[]{:S(2)}, u32[]{:S(2)}) %collective-permute-start.15) | collective-permute-done | bytes 262176 | tf_op jit(solution)/shard_map/ppermute | solution.py:18
  105.2 0.1 fusion.20
  105.4 5.5 %collective-permute-done.7 = bf16[256,512]{1,0:T(8,128)(2,1)S(1)} collective-permute-done((bf16[256,512]{1,0:T(8,128)(2,1)S(1)}, bf16[256,512]{1,0:T(8,128)(2,1)S(1)}, u32[]{:S(2)}, u32[]{:S(2)}) %collective-permute-start.7) | collective-permute-done | bytes 262176 | tf_op jit(solution)/shard_map/ppermute | solution.py:18
  110.9 0.1 fusion.24
  111.0 1.5 %pad_maximum_fusion = f32[256,2048]{1,0:T(8,128)} fusion(f32[256,512]{1,0:T(8,128)S(1)} %fusion.20, f32[256,512]{1,0:T(8,128)S(1)} %fusion.22, f32[256,512]{1,0:T(8,128)S(1)} %fusion.24, f32[256,512]{1,0:T(8,128)S(1)} %fusion.26), kind=kLoop, calls=%fused_computation.2 | loop fusion | flops 1572864 | bytes 4194304 | tf_op jit(solution)/shard_map/concatenate | solution.py:109
  (7 shorter events, 0.1 us)
Async XLA Ops:
  2.5 7.5 %copy-start = (f32[2048,512]{1,0:T(8,128)S(1)}, f32[2048,512]{1,0:T(8,128)}, u32[]{:S(2)}) copy-start(f32[2048,512]{1,0:T(8,128)} %param.2) | copy-start | bytes 12582916
  5.4 4.6 %collective-permute-start = (f32[2,512]{1,0:T(2,128)S(1)}, f32[2,512]{1,0:T(2,128)S(1)}, u32[]{:S(2)}, u32[]{:S(2)}) collective-permute-start(f32[2,512]{1,0:T(2,128)S(1)} %pad_maximum_fusion.1), channel_id=1, source_target_pairs={{0,1},{1,0},{2,3},{3,2},{4,5},{5,4},{6,7},{7,6},{8,9},{9,8},{10,11... | collective-permute-start | bytes 12296 | tf_op jit(solution)/shard_map/ppermute | solution.py:18
  10.6 28.0 %collective-permute-start.8 = (bf16[2048,512]{1,0:T(8,128)(2,1)S(1)}, bf16[2048,512]{1,0:T(8,128)(2,1)}, u32[]{:S(2)}, u32[]{:S(2)}) collective-permute-start(bf16[2048,512]{1,0:T(8,128)(2,1)S(1)} %multiply_convert_fusion), channel_id=1, source_target_pairs={{4,0},{12,8},{20,16},{28,24},{5,1},{13,9},{21,17},{29,25}} | collective-permute-start | bytes 6291464 | tf_op jit(solution)/shard_map/ppermute | solution.py:33
  11.9 32.1 %collective-permute-start.4 = (bf16[2048,512]{1,0:T(8,128)(2,1)S(1)}, bf16[2048,512]{1,0:T(8,128)(2,1)}, u32[]{:S(2)}, u32[]{:S(2)}) collective-permute-start(bf16[2048,512]{1,0:T(8,128)(2,1)S(1)} %multiply_convert_fusion), channel_id=1, source_target_pairs={{2,8},{6,12},{10,16},{14,20},{18,24},{22,28},{3,9},{7,13},{11,17},... | collective-permute-start | bytes 6291464 | tf_op jit(solution)/shard_map/ppermute | solution.py:33
  13.9 53.2 %collective-permute-start.11 = (bf16[2048,512]{1,0:T(8,128)(2,1)S(1)}, bf16[2048,512]{1,0:T(8,128)(2,1)}, u32[]{:S(2)}, u32[]{:S(2)}) collective-permute-start(bf16[2048,512]{1,0:T(8,128)(2,1)S(1)} %multiply_convert_fusion), channel_id=1, source_target_pairs={{0,6},{8,14},{16,22},{24,30},{1,7},{9,15},{17,23},{25,31}} | collective-permute-start | bytes 6291464 | tf_op jit(solution)/shard_map/ppermute | solution.py:33
  24.1 45.0 %collective-permute-start.3 = (bf16[2048,512]{1,0:T(8,128)(2,1)S(1)}, bf16[2048,512]{1,0:T(8,128)(2,1)}, u32[]{:S(2)}, u32[]{:S(2)}) collective-permute-start(bf16[2048,512]{1,0:T(8,128)(2,1)S(1)} %multiply_convert_fusion), channel_id=1, source_target_pairs={{2,4},{10,12},{18,20},{26,28},{3,5},{11,13},{19,21},{27,29}} | collective-permute-start | bytes 6291464 | tf_op jit(solution)/shard_map/ppermute | solution.py:33
  38.7 32.5 %collective-permute-start.9 = (bf16[2048,512]{1,0:T(8,128)(2,1)}, bf16[2048,512]{1,0:T(8,128)(2,1)}, u32[]{:S(2)}, u32[]{:S(2)}) collective-permute-start(bf16[2048,512]{1,0:T(8,128)(2,1)} %collective-permute-done.8), channel_id=1, source_target_pairs={{0,8},{8,16},{16,24},{1,9},{9,17},{17,25}} | collective-permute-start | bytes 6291464 | tf_op jit(solution)/shard_map/ppermute | solution.py:33
  44.0 40.1 %collective-permute-start.5 = (bf16[2048,512]{1,0:T(8,128)(2,1)}, bf16[2048,512]{1,0:T(8,128)(2,1)}, u32[]{:S(2)}, u32[]{:S(2)}) collective-permute-start(bf16[2048,512]{1,0:T(8,128)(2,1)} %collective-permute-done.4), channel_id=1, source_target_pairs={{4,2},{12,10},{20,18},{28,26},{5,3},{13,11},{21,19},{29,27}} | collective-permute-start | bytes 6291464 | tf_op jit(solution)/shard_map/ppermute | solution.py:33
  67.2 19.0 %collective-permute-start.12 = (bf16[2048,512]{1,0:T(8,128)(2,1)}, bf16[2048,512]{1,0:T(8,128)(2,1)}, u32[]{:S(2)}, u32[]{:S(2)}) collective-permute-start(bf16[2048,512]{1,0:T(8,128)(2,1)} %collective-permute-done.11), channel_id=1, source_target_pairs={{6,4},{14,12},{22,20},{30,28},{7,5},{15,13},{23,21},{31,29}} | collective-permute-start | bytes 6291464 | tf_op jit(solution)/shard_map/ppermute | solution.py:33
  69.2 17.0 %collective-permute-start.10 = (bf16[2048,512]{1,0:T(8,128)(2,1)}, bf16[2048,512]{1,0:T(8,128)(2,1)}, u32[]{:S(2)}, u32[]{:S(2)}) collective-permute-start(bf16[2048,512]{1,0:T(8,128)(2,1)} %collective-permute-done.3), channel_id=1, source_target_pairs={{4,6},{12,14},{20,22},{28,30},{5,7},{13,15},{21,23},{29,31}} | collective-permute-start | bytes 6291464 | tf_op jit(solution)/shard_map/ppermute | solution.py:33
  71.1 21.9 %collective-permute-start.14 = (bf16[2048,512]{1,0:T(8,128)(2,1)}, bf16[2048,512]{1,0:T(8,128)(2,1)}, u32[]{:S(2)}, u32[]{:S(2)}) collective-permute-start(bf16[2048,512]{1,0:T(8,128)(2,1)} %collective-permute-done.9), channel_id=1, source_target_pairs={{0,2},{8,10},{16,18},{24,26},{1,3},{9,11},{17,19},{25,27}} | collective-permute-start | bytes 6291464 | tf_op jit(solution)/shard_map/ppermute | solution.py:33
  75.0 6.4 %collective-permute-start.1 = (bf16[256,512]{1,0:T(8,128)(2,1)S(1)}, bf16[256,512]{1,0:T(8,128)(2,1)S(1)}, u32[]{:S(2)}, u32[]{:S(2)}) collective-permute-start(bf16[256,512]{1,0:T(8,128)(2,1)S(1)} %dynamic-slice_bitcast_fusion.3), channel_id=1, source_target_pairs={{0,1},{1,0},{2,3},{3,2},{4,5},{5,4},{6,7},{7,6},{8,9},{9,8},{10,11... | collective-permute-start | bytes 786440 | tf_op jit(solution)/shard_map/ppermute | solution.py:18
  81.5 15.8 %collective-permute-start.2 = (bf16[2048,512]{1,0:T(8,128)(2,1)S(1)}, bf16[2048,512]{1,0:T(8,128)(2,1)}, u32[]{:S(2)}, u32[]{:S(2)}) collective-permute-start(bf16[2048,512]{1,0:T(8,128)(2,1)S(1)} %multiply_convert_fusion), channel_id=1, source_target_pairs={{0,2},{4,6},{8,10},{12,14},{16,18},{20,22},{24,26},{28,30},{1,3},{... | collective-permute-start | bytes 6291464 | tf_op jit(solution)/shard_map/ppermute | solution.py:33
  84.1 13.2 %collective-permute-start.6 = (bf16[2048,512]{1,0:T(8,128)(2,1)}, bf16[2048,512]{1,0:T(8,128)(2,1)}, u32[]{:S(2)}, u32[]{:S(2)}) collective-permute-start(bf16[2048,512]{1,0:T(8,128)(2,1)} %collective-permute-done.5), channel_id=1, source_target_pairs={{2,0},{10,8},{18,16},{26,24},{3,1},{11,9},{19,17},{27,25}} | collective-permute-start | bytes 6291464 | tf_op jit(solution)/shard_map/ppermute | solution.py:33
  91.0 12.6 %collective-permute-start.13 = (bf16[256,512]{1,0:T(8,128)(2,1)S(1)}, bf16[256,512]{1,0:T(8,128)(2,1)S(1)}, u32[]{:S(2)}, u32[]{:S(2)}) collective-permute-start(bf16[256,512]{1,0:T(8,128)(2,1)S(1)} %dynamic-slice_bitcast_fusion.1), channel_id=1, source_target_pairs={{0,1},{1,0},{2,3},{3,2},{4,5},{5,4},{6,7},{7,6},{8,9},{9,8},{10,11... | collective-permute-start | bytes 786440 | tf_op jit(solution)/shard_map/ppermute | solution.py:18
  97.2 8.0 %collective-permute-start.15 = (bf16[256,512]{1,0:T(8,128)(2,1)S(1)}, bf16[256,512]{1,0:T(8,128)(2,1)S(1)}, u32[]{:S(2)}, u32[]{:S(2)}) collective-permute-start(bf16[256,512]{1,0:T(8,128)(2,1)S(1)} %dynamic-slice_bitcast_fusion), channel_id=1, source_target_pairs={{0,1},{1,0},{2,3},{3,2},{4,5},{5,4},{6,7},{7,6},{8,9},{9,8},{10,11... | collective-permute-start | bytes 786440 | tf_op jit(solution)/shard_map/ppermute | solution.py:18
  101.5 9.3 %collective-permute-start.7 = (bf16[256,512]{1,0:T(8,128)(2,1)S(1)}, bf16[256,512]{1,0:T(8,128)(2,1)S(1)}, u32[]{:S(2)}, u32[]{:S(2)}) collective-permute-start(bf16[256,512]{1,0:T(8,128)(2,1)S(1)} %dynamic-slice_bitcast_fusion.2), channel_id=1, source_target_pairs={{0,1},{1,0},{2,3},{3,2},{4,5},{5,4},{6,7},{7,6},{8,9},{9,8},{10,11... | collective-permute-start | bytes 786440 | tf_op jit(solution)/shard_map/ppermute | solution.py:18

commit v4 on v3

--- a/solution.py
+++ b/solution.py
@@ -4,7 +4,6 @@
 from jax.sharding import PartitionSpec as P
 
 TAPS = 4
-CHUNKS = 1
 
 
 def shifted(value, axis, steps):
@@ -38,17 +37,20 @@
     up_three = send(piece, [p for b in groups for p in ((b + 1, b + 4), (b + 3, b + 6))])
     back = send(piece, [(b + 2, b) for b in groups])
     inner_one = send(piece, [p for b in groups for p in ((b, b + 1), (b + 2, b + 3))])
+    inner_back = send(piece, [(b + 3, b + 2) for b in groups])
     up_two = send(back, [(b, b + 4) for b in groups])
     back_two = send(up_three, [(b + 2, b + 1) for b in groups])
-    swap_a = send(cross_one, [(b + 2, b + 3) for b in groups])
-    swap_b = send(cross_three, [(b + 3, b + 2) for b in groups])
     last_one = send(back_two, [(b + 1, b) for b in groups])
     last_three = send(up_two, [(b, b + 1) for b in groups])
-    return [
-        inner_one + cross_one + last_one,
-        up_two + back_two + swap_a + swap_b,
-        cross_three + up_three + last_three,
-    ]
+    early = [inner_one + last_one, up_two + back_two, up_three + last_three]
+    late = cross_one + cross_three
+    partner = inner_back + inner_one
+    return early, late, partner
+
+
+def swap_partner(value, count):
+    pairs = [p for b in range(0, count, 4) for p in ((b + 2, b + 3), (b + 3, b + 2))]
+    return lax.ppermute(value, "snp", [(s, t) for s, t in pairs if t < count])
 
 
 def tile_term(standard, neighbour):
@@ -80,26 +82,29 @@
     var = (m2 + rows * spread) / samples
     standard = ((dosage - mean) * lax.rsqrt(var + 1e-05)).astype(jnp.bfloat16)
 
-    chunks = CHUNKS if rows % (CHUNKS * 16) == 0 else 1
-    step = rows // chunks
-    pieces_of = [standard[c * step:(c + 1) * step] for c in range(chunks)]
-    if lax.axis_size("snp") % 4 == 0:
-        delivered = [relayed(piece, lax.axis_size("snp")) for piece in pieces_of]
-    else:
-        delivered = [chained(piece) for piece in pieces_of]
-
+    count = lax.axis_size("snp")
     share = width // n_smp
     own_reach = reach[0]
+    if count % 4 == 0:
+        early, late, partner = relayed(standard, count)
+        place = lax.axis_index("snp") % 4
+        own_late = tile_term(standard, late)
+        for_partner = swap_partner(tile_term(partner, late).astype(jnp.bfloat16), count)
+        partials = [tile_term(standard, standard).astype(jnp.bfloat16)]
+        partials.append(
+            (tile_term(standard, early[0]) + jnp.where(place == 2, own_late, 0.0)).astype(jnp.bfloat16)
+        )
+        partials.append(tile_term(standard, early[1]).astype(jnp.bfloat16) + for_partner)
+        partials.append(
+            (tile_term(standard, early[2]) + jnp.where(place == 3, own_late, 0.0)).astype(jnp.bfloat16)
+        )
+    else:
+        neighbours = [standard] + chained(standard)
+        partials = [tile_term(standard, nb).astype(jnp.bfloat16) for nb in neighbours]
+
     kept = []
     for dist in range(TAPS):
-        if dist == 0:
-            partial = tile_term(standard, standard)
-        else:
-            partial = tile_term(pieces_of[0], delivered[0][dist - 1])
-            for c in range(1, chunks):
-                partial = partial + tile_term(pieces_of[c], delivered[c][dist - 1])
-        partial = partial.astype(jnp.bfloat16)
-        pieces = partial.reshape(n_smp, share, width)
+        pieces = partials[dist].reshape(n_smp, share, width)
         total = lax.dynamic_index_in_dim(pieces, me, 0, keepdims=False).astype(jnp.float32)
         for s in range(1, n_smp):
             outgoing = lax.dynamic_index_in_dim(pieces, (me + s) % n_smp, 0, keepdims=False)

time: 113 us -> 104 us (0.920)
  waiting for transfers between devices: 46.7 us -> 21.1 us
  starting transfers between devices: 42.6 us -> 54.5 us
  matrix products: 14.3 us -> 17.8 us
  local copies, waits for them, and re-layouts: 0.11 us -> 1.43 us
    ppermute x11 -> x10, waiting for transfers between devices: 33.7 us -> 11.8 us  [send(): return lax.ppermute(value, 'snp', pairs)]
    ppermute x11 -> x10, starting transfers between devices: 33.2 us -> 45.5 us  [send(): return lax.ppermute(value, 'snp', pairs)]
    ppermute x5, waiting for transfers between devices: 13 us -> 9.35 us  [rotated(): lax.ppermute(value, axis, [(source, (source + steps) % count) for source...]
    dot_general x4 -> x6, matrix products: 14.3 us -> 17.8 us  [tile_term(): lax.dot_general(standard, neighbour, (((0,), (0,)), ((), ())), preferred_...]
    unnamed x2 -> x6, local copies, waits for them, and re-layouts: 0.01 us -> 1.33 us
  transfers between devices with their start and end apart: 16 -> 16, of which waited for: 6 -> 5; matrix products, arithmetic and copies ran while one was open for 13% -> 18% of each run, Pallas kernels for 0% -> 0%
where the time goes in v4:
time: 104 us
  starting transfers between devices  54.5 us (52%)
  waiting for transfers between devices  21.1 us (20%)
  matrix products  17.8 us (17%)
  other arithmetic  7.9 us (8%)
  local copies, waits for them, and re-layouts  1.43 us (1%)
    ppermute x10, starting transfers between devices, send(): return lax.ppermute(value, 'snp', pairs)  45.5 us
    dot_general x6, matrix products, tile_term(): lax.dot_general(standard, neighbour, (((0,), (0,)), ((), ())), preferred_...  17.8 us
    ppermute x10, waiting for transfers between devices, send(): return lax.ppermute(value, 'snp', pairs)  11.8 us
    ppermute x5, waiting for transfers between devices, rotated(): lax.ppermute(value, axis, [(source, (source + steps) % count) for source...  9.35 us
    ppermute x5, starting transfers between devices, rotated(): lax.ppermute(value, axis, [(source, (source + steps) % count) for source...  8.29 us
    reduce_sum x1, other arithmetic, local(): part_m2 = jnp.sum(deviation * deviation, axis=0)  2.85 us
    reduce_sum x1, other arithmetic, local(): part_mean = jnp.sum(dosage, axis=0) / rows  2.52 us
  transfers between devices with their start and end apart: 16, of which 5 were waited for; matrix products, arithmetic and copies ran while one was open for 18% of the time, Pallas kernels for 0%

profile of v4, /device:TPU:0, one launch (start us, length us, event | category | flops | bytes accessed | tf_op | source)
XLA Modules:
  0.0 103.7 jit_solution(1410279743501798729)
XLA Ops:
  0.0 2.5 %reduce_sum.18 = f32[512]{0:T(512)S(1)} reduce(f32[2048,512]{1,0:T(8,128)} %param.2, f32[]{:T(128)} %constant.70.clone.1), dimensions={0}, to_apply=%region_0.0 | reduce | flops 1048064 | bytes 4196356 | tf_op jit(solution)/shard_map/reduce_sum | solution.py:68
  2.5 2.9 %multiply_reduce_fusion = f32[512]{0:T(512)S(1)} fusion(f32[2048,512]{1,0:T(8,128)} %param.2, f32[512]{0:T(512)S(1)} %broadcast_multiply_fusion), kind=kLoop, calls=%fused_computation.1 | loop fusion | flops 3145216 | bytes 4198400 | tf_op jit(solution)/shard_map/reduce_sum | solution.py:70
  5.4 3.0 %collective-permute-start = (f32[2,512]{1,0:T(2,128)S(1)}, f32[2,512]{1,0:T(2,128)S(1)}, u32[]{:S(2)}, u32[]{:S(2)}) collective-permute-start(f32[2,512]{1,0:T(2,128)S(1)} %pad_maximum_fusion.1), channel_id=1, source_target_pairs={{0,1},{1,0},{2,3},{3,2},{4,5},{5,4},{6,7},{7,6},{8,9},{9,8},{10,11... | collective-permute-start | bytes 12296 | tf_op jit(solution)/shard_map/ppermute | solution.py:17
  8.4 1.6 %collective-permute-done = f32[2,512]{1,0:T(2,128)S(1)} collective-permute-done((f32[2,512]{1,0:T(2,128)S(1)}, f32[2,512]{1,0:T(2,128)S(1)}, u32[]{:S(2)}, u32[]{:S(2)}) %collective-permute-start) | collective-permute-done | bytes 4128 | tf_op jit(solution)/shard_map/ppermute | solution.py:17
  10.0 0.6 multiply_convert_fusion
  10.6 2.0 %collective-permute-start.3 = (bf16[2048,512]{1,0:T(8,128)(2,1)S(1)}, bf16[2048,512]{1,0:T(8,128)(2,1)}, u32[]{:S(2)}, u32[]{:S(2)}) collective-permute-start(bf16[2048,512]{1,0:T(8,128)(2,1)S(1)} %multiply_convert_fusion), channel_id=1, source_target_pairs={{2,8},{6,12},{10,16},{14,20},{18,24},{22,28},{3,9},{7,13},{11,17},... | collective-permute-start | bytes 6291464 | tf_op jit(solution)/shard_map/ppermute | solution.py:32
  12.6 1.3 %collective-permute-start.9 = (bf16[2048,512]{1,0:T(8,128)(2,1)S(1)}, bf16[2048,512]{1,0:T(8,128)(2,1)}, u32[]{:S(2)}, u32[]{:S(2)}) collective-permute-start(bf16[2048,512]{1,0:T(8,128)(2,1)S(1)} %multiply_convert_fusion), channel_id=1, source_target_pairs={{4,0},{12,8},{20,16},{28,24},{5,1},{13,9},{21,17},{29,25}} | collective-permute-start | bytes 6291464 | tf_op jit(solution)/shard_map/ppermute | solution.py:32
  13.9 0.8 collective-permute-start.6
  14.7 0.0 collective-permute-done.3
  14.7 2.0 %collective-permute-start.4 = (bf16[2048,512]{1,0:T(8,128)(2,1)}, bf16[2048,512]{1,0:T(8,128)(2,1)}, u32[]{:S(2)}, u32[]{:S(2)}) collective-permute-start(bf16[2048,512]{1,0:T(8,128)(2,1)} %collective-permute-done.3), channel_id=1, source_target_pairs={{4,2},{12,10},{20,18},{28,26},{5,3},{13,11},{21,19},{29,27}} | collective-permute-start | bytes 6291464 | tf_op jit(solution)/shard_map/ppermute | solution.py:32
  16.8 27.3 %collective-permute-start.7 = (bf16[2048,512]{1,0:T(8,128)(2,1)S(1)}, bf16[2048,512]{1,0:T(8,128)(2,1)}, u32[]{:S(2)}, u32[]{:S(2)}) collective-permute-start(bf16[2048,512]{1,0:T(8,128)(2,1)S(1)} %multiply_convert_fusion), channel_id=1, source_target_pairs={{0,6},{8,14},{16,22},{24,30},{1,7},{9,15},{17,23},{25,31}} | collective-permute-start | bytes 6291464 | tf_op jit(solution)/shard_map/ppermute | solution.py:32
  44.0 0.0 collective-permute-done.9
  44.0 4.8 %collective-permute-start.10 = (bf16[2048,512]{1,0:T(8,128)(2,1)}, bf16[2048,512]{1,0:T(8,128)(2,1)}, u32[]{:S(2)}, u32[]{:S(2)}) collective-permute-start(bf16[2048,512]{1,0:T(8,128)(2,1)} %collective-permute-done.9), channel_id=1, source_target_pairs={{0,8},{8,16},{16,24},{1,9},{9,17},{17,25}} | collective-permute-start | bytes 6291464 | tf_op jit(solution)/shard_map/ppermute | solution.py:32
  48.8 2.7 %collective-permute-start.2 = (bf16[2048,512]{1,0:T(8,128)(2,1)S(1)}, bf16[2048,512]{1,0:T(8,128)(2,1)}, u32[]{:S(2)}, u32[]{:S(2)}) collective-permute-start(bf16[2048,512]{1,0:T(8,128)(2,1)S(1)} %multiply_convert_fusion), channel_id=1, source_target_pairs={{0,2},{4,6},{8,10},{12,14},{16,18},{20,22},{24,26},{28,30},{1,3},{... | collective-permute-start | bytes 6291464 | tf_op jit(solution)/shard_map/ppermute | solution.py:32
  51.5 0.0 collective-permute-done.6
  51.5 1.3 %copy-done.1 = bf16[2048,512]{1,0:T(8,128)(2,1)} copy-done((bf16[2048,512]{1,0:T(8,128)(2,1)}, bf16[2048,512]{1,0:T(8,128)(2,1)S(1)}, u32[]{:S(2)}) %copy-start.1) | copy-done | bytes 2097176
  52.8 2.0 %collective-permute-start.11 = (bf16[2048,512]{1,0:T(8,128)(2,1)S(1)}, bf16[2048,512]{1,0:T(8,128)(2,1)}, u32[]{:S(2)}, u32[]{:S(2)}) collective-permute-start(bf16[2048,512]{1,0:T(8,128)(2,1)S(1)} %multiply_convert_fusion), channel_id=1, source_target_pairs={{6,4},{14,12},{22,20},{30,28},{7,5},{15,13},{23,21},{31,29}} | collective-permute-start | bytes 6291464 | tf_op jit(solution)/shard_map/ppermute | solution.py:32
  55.5 0.0 copy-start.2
  55.5 1.3 %convolution_convert_fusion = bf16[512,512]{1,0:T(8,128)(2,1)S(1)} fusion(bf16[2048,512]{1,0:T(8,128)(2,1)S(1)} %multiply_convert_fusion), kind=kOutput, calls=%fused_computation.17 | convolution fusion | flops 1074003968 | bytes 2621440 | tf_op jit(solution)/shard_map/dot_general | solution.py:57
  56.8 0.0 collective-permute-done.4
  56.8 1.3 %collective-permute-start.5 = (bf16[2048,512]{1,0:T(8,128)(2,1)}, bf16[2048,512]{1,0:T(8,128)(2,1)S(1)}, u32[]{:S(2)}, u32[]{:S(2)}) collective-permute-start(bf16[2048,512]{1,0:T(8,128)(2,1)} %collective-permute-done.4), channel_id=1, source_target_pairs={{2,0},{10,8},{18,16},{26,24},{3,1},{11,9},{19,17},{27,25}} | collective-permute-start | bytes 6291464 | tf_op jit(solution)/shard_map/ppermute | solution.py:32
  58.1 8.1 %collective-permute-done.7 = bf16[2048,512]{1,0:T(8,128)(2,1)} collective-permute-done((bf16[2048,512]{1,0:T(8,128)(2,1)S(1)}, bf16[2048,512]{1,0:T(8,128)(2,1)}, u32[]{:S(2)}, u32[]{:S(2)}) %collective-permute-start.7) | collective-permute-done | bytes 2097184 | tf_op jit(solution)/shard_map/ppermute | solution.py:32
  66.2 1.5 %collective-permute-start.1 = (bf16[256,512]{1,0:T(8,128)(2,1)S(1)}, bf16[256,512]{1,0:T(8,128)(2,1)S(1)}, u32[]{:S(2)}, u32[]{:S(2)}) collective-permute-start(bf16[256,512]{1,0:T(8,128)(2,1)S(1)} %dynamic-slice_bitcast_fusion.3), channel_id=1, source_target_pairs={{0,1},{1,0},{2,3},{3,2},{4,5},{5,4},{6,7},{7,6},{8,9},{9,8},{10,11... | collective-permute-start | bytes 786440 | tf_op jit(solution)/shard_map/ppermute | solution.py:17
  67.8 3.6 %collective-permute-done.10 = bf16[2048,512]{1,0:T(8,128)(2,1)} collective-permute-done((bf16[2048,512]{1,0:T(8,128)(2,1)}, bf16[2048,512]{1,0:T(8,128)(2,1)}, u32[]{:S(2)}, u32[]{:S(2)}) %collective-permute-start.10) | collective-permute-done | bytes 2097184 | tf_op jit(solution)/shard_map/ppermute | solution.py:32
  71.4 1.4 %collective-permute-start.14 = (bf16[2048,512]{1,0:T(8,128)(2,1)}, bf16[2048,512]{1,0:T(8,128)(2,1)S(1)}, u32[]{:S(2)}, u32[]{:S(2)}) collective-permute-start(bf16[2048,512]{1,0:T(8,128)(2,1)} %collective-permute-done.10), channel_id=1, source_target_pairs={{0,2},{8,10},{16,18},{24,26},{1,3},{9,11},{17,19},{25,27}} | collective-permute-start | bytes 6291464 | tf_op jit(solution)/shard_map/ppermute | solution.py:32
  72.8 0.0 collective-permute-done.2
  72.8 0.0 collective-permute-done.11
  72.8 4.2 %fusion.23 = bf16[512,512]{1,0:T(8,128)(2,1)S(1)} fusion(bf16[2048,512]{1,0:T(8,128)(2,1)} %collective-permute-done.11, bf16[2048,512]{1,0:T(8,128)(2,1)} %collective-permute-done.2, bf16[2048,512]{1,0:T(8,128)(2,1)S(1)} %copy-done.2, bf16[2048,512]{1,0:T(8,128)(2,1)} %collective-permute-done.7), kind=kOutput, calls=%fused_computation.16 | convolution fusion | flops 1076101120 | bytes 8912896 | tf_op jit(solution)/shard_map/dot_general | solution.py:57
  77.1 0.7 collective-permute-start.12
  77.8 0.0 collective-permute-done.1
  77.8 0.1 fusion.39
  77.9 2.9 %fusion.30 = f32[512,512]{1,0:T(8,128)S(1)} fusion(bf16[2048,512]{1,0:T(8,128)(2,1)S(1)} %multiply_convert_fusion, bf16[2048,512]{1,0:T(8,128)(2,1)S(1)} %copy-done.2, bf16[2048,512]{1,0:T(8,128)(2,1)} %collective-permute-done.7), kind=kOutput, calls=%fused_computation.20 | convolution fusion | flops 1074790400 | bytes 7340032 | tf_op jit(solution)/shard_map/dot_general | solution.py:57
  80.8 0.0 collective-permute-done.12
  80.8 3.5 %fusion.26 = bf16[512,512]{1,0:T(8,128)(2,1)S(1)} fusion(bf16[512,512]{1,0:T(8,128)(2,1)S(1)} %collective-permute-done.12, bf16[2048,512]{1,0:T(8,128)(2,1)S(1)} %multiply_convert_fusion, bf16[2048,512]{1,0:T(8,128)(2,1)} %collective-permute-done.10, bf16[2048,512]{1,0:T(8,128)(2,1)} %collective-permute-done.4), kind=kOutput, calls=%fused_computation.18 | convolution fusion | flops 1075314688 | bytes 7340032 | tf_op jit(solution)/shard_map/dot_general | solution.py:57
  84.4 1.6 %collective-permute-start.13 = (bf16[256,512]{1,0:T(8,128)(2,1)S(1)}, bf16[256,512]{1,0:T(8,128)(2,1)S(1)}, u32[]{:S(2)}, u32[]{:S(2)}) collective-permute-start(bf16[256,512]{1,0:T(8,128)(2,1)S(1)} %dynamic-slice_bitcast_fusion.1), channel_id=1, source_target_pairs={{0,1},{1,0},{2,3},{3,2},{4,5},{5,4},{6,7},{7,6},{8,9},{9,8},{10,11... | collective-permute-start | bytes 786440 | tf_op jit(solution)/shard_map/ppermute | solution.py:17
  86.0 0.0 collective-permute-done.5
  86.0 2.9 %fusion.17 = bf16[512,512]{1,0:T(8,128)(2,1)S(1)} fusion(bf16[2048,512]{1,0:T(8,128)(2,1)S(1)} %multiply_convert_fusion, bf16[2048,512]{1,0:T(8,128)(2,1)} %collective-permute-done.2, bf16[2048,512]{1,0:T(8,128)(2,1)S(1)} %collective-permute-done.5, f32[512,512]{1,0:T(8,128)S(1)} %fusion.30, pred[]{:T(512)S(6)} %eq.12), kind=kOutput, calls=%fused_computation.14 | convolution fusion | flops 1075576832 | bytes 7864321 | tf_op jit(solution)/shard_map/dot_general | solution.py:57
  88.9 0.6 collective-permute-start.8
  89.5 0.0 collective-permute-done.14
  89.5 2.9 %fusion.14 = bf16[512,512]{1,0:T(8,128)(2,1)S(1)} fusion(bf16[2048,512]{1,0:T(8,128)(2,1)S(1)} %multiply_convert_fusion, bf16[2048,512]{1,0:T(8,128)(2,1)} %collective-permute-done.3, bf16[2048,512]{1,0:T(8,128)(2,1)S(1)} %collective-permute-done.14, f32[512,512]{1,0:T(8,128)S(1)} %fusion.30, pred[]{:T(512)S(6)} %eq.13), kind=kOutput, calls=%fused_computation.13 | convolution fusion | flops 1075576832 | bytes 7864321 | tf_op jit(solution)/shard_map/dot_general | solution.py:57
  92.5 1.6 %collective-permute-start.15 = (bf16[256,512]{1,0:T(8,128)(2,1)S(1)}, bf16[256,512]{1,0:T(8,128)(2,1)S(1)}, u32[]{:S(2)}, u32[]{:S(2)}) collective-permute-start(bf16[256,512]{1,0:T(8,128)(2,1)S(1)} %dynamic-slice_bitcast_fusion), channel_id=1, source_target_pairs={{0,1},{1,0},{2,3},{3,2},{4,5},{5,4},{6,7},{7,6},{8,9},{9,8},{10,11... | collective-permute-start | bytes 786440 | tf_op jit(solution)/shard_map/ppermute | solution.py:17
  94.1 0.0 collective-permute-done.13
  94.1 0.1 fusion.35
  94.2 4.7 %collective-permute-done.8 = bf16[256,512]{1,0:T(8,128)(2,1)S(1)} collective-permute-done((bf16[256,512]{1,0:T(8,128)(2,1)S(1)}, bf16[256,512]{1,0:T(8,128)(2,1)S(1)}, u32[]{:S(2)}, u32[]{:S(2)}) %collective-permute-start.8) | collective-permute-done | bytes 262176 | tf_op jit(solution)/shard_map/ppermute | solution.py:17
  98.9 0.1 fusion.37
  99.0 3.1 %collective-permute-done.15 = bf16[256,512]{1,0:T(8,128)(2,1)S(1)} collective-permute-done((bf16[256,512]{1,0:T(8,128)(2,1)S(1)}, bf16[256,512]{1,0:T(8,128)(2,1)S(1)}, u32[]{:S(2)}, u32[]{:S(2)}) %collective-permute-start.15) | collective-permute-done | bytes 262176 | tf_op jit(solution)/shard_map/ppermute | solution.py:17
  102.1 0.1 fusion.33
  102.2 1.5 %pad_maximum_fusion = f32[256,2048]{1,0:T(8,128)} fusion(f32[256,512]{1,0:T(8,128)S(1)} %fusion.33, f32[256,512]{1,0:T(8,128)S(1)} %fusion.35, f32[256,512]{1,0:T(8,128)S(1)} %fusion.37, f32[256,512]{1,0:T(8,128)S(1)} %fusion.39), kind=kLoop, calls=%fused_computation.2 | loop fusion | flops 1572864 | bytes 4194304 | tf_op jit(solution)/shard_map/concatenate | solution.py:114
  (11 shorter events, 0.1 us)
Async XLA Ops:
  2.5 7.5 %copy-start = (f32[2048,512]{1,0:T(8,128)S(1)}, f32[2048,512]{1,0:T(8,128)}, u32[]{:S(2)}) copy-start(f32[2048,512]{1,0:T(8,128)} %param.2) | copy-start | bytes 12582916
  5.4 4.6 %collective-permute-start = (f32[2,512]{1,0:T(2,128)S(1)}, f32[2,512]{1,0:T(2,128)S(1)}, u32[]{:S(2)}, u32[]{:S(2)}) collective-permute-start(f32[2,512]{1,0:T(2,128)S(1)} %pad_maximum_fusion.1), channel_id=1, source_target_pairs={{0,1},{1,0},{2,3},{3,2},{4,5},{5,4},{6,7},{7,6},{8,9},{9,8},{10,11... | collective-permute-start | bytes 12296 | tf_op jit(solution)/shard_map/ppermute | solution.py:17
  10.6 4.1 %collective-permute-start.3 = (bf16[2048,512]{1,0:T(8,128)(2,1)S(1)}, bf16[2048,512]{1,0:T(8,128)(2,1)}, u32[]{:S(2)}, u32[]{:S(2)}) collective-permute-start(bf16[2048,512]{1,0:T(8,128)(2,1)S(1)} %multiply_convert_fusion), channel_id=1, source_target_pairs={{2,8},{6,12},{10,16},{14,20},{18,24},{22,28},{3,9},{7,13},{11,17},... | collective-permute-start | bytes 6291464 | tf_op jit(solution)/shard_map/ppermute | solution.py:32
  12.6 31.4 %collective-permute-start.9 = (bf16[2048,512]{1,0:T(8,128)(2,1)S(1)}, bf16[2048,512]{1,0:T(8,128)(2,1)}, u32[]{:S(2)}, u32[]{:S(2)}) collective-permute-start(bf16[2048,512]{1,0:T(8,128)(2,1)S(1)} %multiply_convert_fusion), channel_id=1, source_target_pairs={{4,0},{12,8},{20,16},{28,24},{5,1},{13,9},{21,17},{29,25}} | collective-permute-start | bytes 6291464 | tf_op jit(solution)/shard_map/ppermute | solution.py:32
  13.9 37.6 %collective-permute-start.6 = (bf16[2048,512]{1,0:T(8,128)(2,1)S(1)}, bf16[2048,512]{1,0:T(8,128)(2,1)S(1)}, u32[]{:S(2)}, u32[]{:S(2)}) collective-permute-start(bf16[2048,512]{1,0:T(8,128)(2,1)S(1)} %multiply_convert_fusion), channel_id=1, source_target_pairs={{2,4},{10,12},{18,20},{26,28},{3,5},{11,13},{19,21},{27,29}} | collective-permute-start | bytes 6291464 | tf_op jit(solution)/shard_map/ppermute | solution.py:32
  14.7 42.0 %collective-permute-start.4 = (bf16[2048,512]{1,0:T(8,128)(2,1)}, bf16[2048,512]{1,0:T(8,128)(2,1)}, u32[]{:S(2)}, u32[]{:S(2)}) collective-permute-start(bf16[2048,512]{1,0:T(8,128)(2,1)} %collective-permute-done.3), channel_id=1, source_target_pairs={{4,2},{12,10},{20,18},{28,26},{5,3},{13,11},{21,19},{29,27}} | collective-permute-start | bytes 6291464 | tf_op jit(solution)/shard_map/ppermute | solution.py:32
  16.8 49.5 %collective-permute-start.7 = (bf16[2048,512]{1,0:T(8,128)(2,1)S(1)}, bf16[2048,512]{1,0:T(8,128)(2,1)}, u32[]{:S(2)}, u32[]{:S(2)}) collective-permute-start(bf16[2048,512]{1,0:T(8,128)(2,1)S(1)} %multiply_convert_fusion), channel_id=1, source_target_pairs={{0,6},{8,14},{16,22},{24,30},{1,7},{9,15},{17,23},{25,31}} | collective-permute-start | bytes 6291464 | tf_op jit(solution)/shard_map/ppermute | solution.py:32
  44.0 27.3 %collective-permute-start.10 = (bf16[2048,512]{1,0:T(8,128)(2,1)}, bf16[2048,512]{1,0:T(8,128)(2,1)}, u32[]{:S(2)}, u32[]{:S(2)}) collective-permute-start(bf16[2048,512]{1,0:T(8,128)(2,1)} %collective-permute-done.9), channel_id=1, source_target_pairs={{0,8},{8,16},{16,24},{1,9},{9,17},{17,25}} | collective-permute-start | bytes 6291464 | tf_op jit(solution)/shard_map/ppermute | solution.py:32
  48.8 24.0 %collective-permute-start.2 = (bf16[2048,512]{1,0:T(8,128)(2,1)S(1)}, bf16[2048,512]{1,0:T(8,128)(2,1)}, u32[]{:S(2)}, u32[]{:S(2)}) collective-permute-start(bf16[2048,512]{1,0:T(8,128)(2,1)S(1)} %multiply_convert_fusion), channel_id=1, source_target_pairs={{0,2},{4,6},{8,10},{12,14},{16,18},{20,22},{24,26},{28,30},{1,3},{... | collective-permute-start | bytes 6291464 | tf_op jit(solution)/shard_map/ppermute | solution.py:32
  51.5 1.3 %copy-start.1 = (bf16[2048,512]{1,0:T(8,128)(2,1)}, bf16[2048,512]{1,0:T(8,128)(2,1)S(1)}, u32[]{:S(2)}) copy-start(bf16[2048,512]{1,0:T(8,128)(2,1)S(1)} %collective-permute-done.6) | copy-start | bytes 6291460
  52.8 20.0 %collective-permute-start.11 = (bf16[2048,512]{1,0:T(8,128)(2,1)S(1)}, bf16[2048,512]{1,0:T(8,128)(2,1)}, u32[]{:S(2)}, u32[]{:S(2)}) collective-permute-start(bf16[2048,512]{1,0:T(8,128)(2,1)S(1)} %multiply_convert_fusion), channel_id=1, source_target_pairs={{6,4},{14,12},{22,20},{30,28},{7,5},{15,13},{23,21},{31,29}} | collective-permute-start | bytes 6291464 | tf_op jit(solution)/shard_map/ppermute | solution.py:32
  55.5 17.3 %copy-start.2 = (bf16[2048,512]{1,0:T(8,128)(2,1)S(1)}, bf16[2048,512]{1,0:T(8,128)(2,1)}, u32[]{:S(2)}) copy-start(bf16[2048,512]{1,0:T(8,128)(2,1)} %copy-done.1) | copy-start | bytes 6291460
  56.8 29.2 %collective-permute-start.5 = (bf16[2048,512]{1,0:T(8,128)(2,1)}, bf16[2048,512]{1,0:T(8,128)(2,1)S(1)}, u32[]{:S(2)}, u32[]{:S(2)}) collective-permute-start(bf16[2048,512]{1,0:T(8,128)(2,1)} %collective-permute-done.4), channel_id=1, source_target_pairs={{2,0},{10,8},{18,16},{26,24},{3,1},{11,9},{19,17},{27,25}} | collective-permute-start | bytes 6291464 | tf_op jit(solution)/shard_map/ppermute | solution.py:32
  66.2 11.5 %collective-permute-start.1 = (bf16[256,512]{1,0:T(8,128)(2,1)S(1)}, bf16[256,512]{1,0:T(8,128)(2,1)S(1)}, u32[]{:S(2)}, u32[]{:S(2)}) collective-permute-start(bf16[256,512]{1,0:T(8,128)(2,1)S(1)} %dynamic-slice_bitcast_fusion.3), channel_id=1, source_target_pairs={{0,1},{1,0},{2,3},{3,2},{4,5},{5,4},{6,7},{7,6},{8,9},{9,8},{10,11... | collective-permute-start | bytes 786440 | tf_op jit(solution)/shard_map/ppermute | solution.py:17
  71.4 18.1 %collective-permute-start.14 = (bf16[2048,512]{1,0:T(8,128)(2,1)}, bf16[2048,512]{1,0:T(8,128)(2,1)S(1)}, u32[]{:S(2)}, u32[]{:S(2)}) collective-permute-start(bf16[2048,512]{1,0:T(8,128)(2,1)} %collective-permute-done.10), channel_id=1, source_target_pairs={{0,2},{8,10},{16,18},{24,26},{1,3},{9,11},{17,19},{25,27}} | collective-permute-start | bytes 6291464 | tf_op jit(solution)/shard_map/ppermute | solution.py:32
  77.1 3.8 %collective-permute-start.12 = (bf16[512,512]{1,0:T(8,128)(2,1)S(1)}, bf16[512,512]{1,0:T(8,128)(2,1)S(1)}, u32[]{:S(2)}, u32[]{:S(2)}) collective-permute-start(bf16[512,512]{1,0:T(8,128)(2,1)S(1)} %fusion.23), channel_id=1, source_target_pairs={{4,6},{6,4},{12,14},{14,12},{20,22},{22,20},{28,30},{30,28},{5,7},... | collective-permute-start | bytes 1572872 | tf_op jit(solution)/shard_map/ppermute | solution.py:53
  84.4 9.7 %collective-permute-start.13 = (bf16[256,512]{1,0:T(8,128)(2,1)S(1)}, bf16[256,512]{1,0:T(8,128)(2,1)S(1)}, u32[]{:S(2)}, u32[]{:S(2)}) collective-permute-start(bf16[256,512]{1,0:T(8,128)(2,1)S(1)} %dynamic-slice_bitcast_fusion.1), channel_id=1, source_target_pairs={{0,1},{1,0},{2,3},{3,2},{4,5},{5,4},{6,7},{7,6},{8,9},{9,8},{10,11... | collective-permute-start | bytes 786440 | tf_op jit(solution)/shard_map/ppermute | solution.py:17
  88.9 9.9 %collective-permute-start.8 = (bf16[256,512]{1,0:T(8,128)(2,1)S(1)}, bf16[256,512]{1,0:T(8,128)(2,1)S(1)}, u32[]{:S(2)}, u32[]{:S(2)}) collective-permute-start(bf16[256,512]{1,0:T(8,128)(2,1)S(1)} %dynamic-slice_bitcast_fusion.2), channel_id=1, source_target_pairs={{0,1},{1,0},{2,3},{3,2},{4,5},{5,4},{6,7},{7,6},{8,9},{9,8},{10,11... | collective-permute-start | bytes 786440 | tf_op jit(solution)/shard_map/ppermute | solution.py:17
  92.5 9.6 %collective-permute-start.15 = (bf16[256,512]{1,0:T(8,128)(2,1)S(1)}, bf16[256,512]{1,0:T(8,128)(2,1)S(1)}, u32[]{:S(2)}, u32[]{:S(2)}) collective-permute-start(bf16[256,512]{1,0:T(8,128)(2,1)S(1)} %dynamic-slice_bitcast_fusion), channel_id=1, source_target_pairs={{0,1},{1,0},{2,3},{3,2},{4,5},{5,4},{6,7},{7,6},{8,9},{9,8},{10,11... | collective-permute-start | bytes 786440 | tf_op jit(solution)/shard_map/ppermute | solution.py:17

commit v5 on v1

--- a/solution.py
+++ b/solution.py
@@ -15,6 +15,39 @@
 def rotated(value, axis, steps):
     count = lax.axis_size(axis)
     return lax.ppermute(value, axis, [(source, (source + steps) % count) for source in range(count)])
+
+
+def chained(piece):
+    out = []
+    previous = piece
+    for dist in range(1, TAPS):
+        previous = shifted(previous, "snp", 1)
+        out.append(previous)
+    return out
+
+
+def relayed(standard, count, place):
+    def send(value, pairs):
+        pairs = [(s, t) for s, t in pairs if 0 <= s < count and 0 <= t < count]
+        return lax.ppermute(value, "snp", pairs)
+
+    def pairs_of(*steps):
+        return [(b + s, b + t) for b in range(0, count, 4) for s, t in steps]
+
+    cross = send(standard, pairs_of((1, 2), (0, 3)))
+    fast_a = send(standard, pairs_of((0, 1), (2, 3), (1, 4), (3, 6)))
+    fast_b = send(standard, pairs_of((2, 1), (3, 2), (1, 0)))
+    relay = send(jnp.where(place == 1, fast_b, fast_a), pairs_of((1, 4), (2, 1)))
+    lhs = jnp.where(place % 2 == 0, fast_b, fast_a)
+    rhs = jnp.where(place < 2, relay, cross)
+    handed = send(tile_term(lhs, rhs).astype(jnp.bfloat16), pairs_of((0, 1), (1, 0), (2, 3), (3, 2)))
+    with_a = tile_term(standard, fast_a).astype(jnp.bfloat16)
+    with_relay = tile_term(standard, relay).astype(jnp.bfloat16)
+    with_cross = tile_term(standard, cross).astype(jnp.bfloat16)
+    one = jnp.where(place == 0, handed, jnp.where(place == 2, with_cross, with_a))
+    two = jnp.where(place < 2, with_relay, handed)
+    three = jnp.where(place == 1, handed, jnp.where(place == 3, with_cross, with_a))
+    return [one, two, three]
 
 
 def tile_term(standard, neighbour):
@@ -46,23 +79,28 @@
     var = (m2 + rows * spread) / samples
     standard = ((dosage - mean) * lax.rsqrt(var + 1e-05)).astype(jnp.bfloat16)
 
-    neighbours = [standard]
-    previous = standard
-    for dist in range(1, TAPS):
-        previous = shifted(previous, "snp", 1)
-        neighbours.append(previous)
-
+    count = lax.axis_size("snp")
     share = width // n_smp
     own_reach = reach[0]
+    first = tile_term(standard, standard).astype(jnp.bfloat16)
+    if count % 4 == 0:
+        rest = relayed(standard, count, lax.axis_index("snp") % 4)
+    else:
+        rest = [tile_term(standard, nb).astype(jnp.bfloat16) for nb in chained(standard)]
+
+    def exchanged(partial):
+        pieces = partial.reshape(partial.shape[:-2] + (n_smp, share, width))
+        axis = pieces.ndim - 3
+        total = lax.dynamic_index_in_dim(pieces, me, axis, keepdims=False).astype(jnp.float32)
+        for s in range(1, n_smp):
+            outgoing = lax.dynamic_index_in_dim(pieces, (me + s) % n_smp, axis, keepdims=False)
+            total = total + rotated(outgoing, "smp", s).astype(jnp.float32)
+        return total
+
+    totals = [exchanged(first)] + list(exchanged(jnp.stack(rest)))
     kept = []
     for dist in range(TAPS):
-        partial = tile_term(standard, neighbours[dist]).astype(jnp.bfloat16)
-        pieces = partial.reshape(n_smp, share, width)
-        total = lax.dynamic_index_in_dim(pieces, me, 0, keepdims=False).astype(jnp.float32)
-        for s in range(1, n_smp):
-            outgoing = lax.dynamic_index_in_dim(pieces, (me + s) % n_smp, 0, keepdims=False)
-            total = total + rotated(outgoing, "smp", s).astype(jnp.float32)
-        tile = total / samples
+        tile = totals[dist] / samples
         kept.append(jnp.where(dist <= own_reach, tile, jnp.zeros_like(tile)))
     return jnp.concatenate(kept, axis=1)
 

time: 108 us -> 114 us (1.056)
  the two profiles are of different devices: /device:TPU:3 before, /device:TPU:0 now
where the time goes in v5:
time: 114 us
  waiting for transfers between devices  61.3 us (54%)
  starting transfers between devices  25.8 us (23%)
  matrix products  13.4 us (12%)
  other arithmetic  12.7 us (11%)
    ppermute x5, waiting for transfers between devices, send(): return lax.ppermute(value, 'snp', pairs)  38.7 us
    ppermute x3, waiting for transfers between devices, rotated(): lax.ppermute(value, axis, [(source, (source + steps) % count) for source...  22.6 us
    ppermute x5, starting transfers between devices, send(): return lax.ppermute(value, 'snp', pairs)  20.6 us
    dot_general x5, matrix products, tile_term(): lax.dot_general(standard, neighbour, (((0,), (0,)), ((), ())), preferred_...  13.4 us
    ppermute x3, starting transfers between devices, rotated(): lax.ppermute(value, axis, [(source, (source + steps) % count) for source...  5.18 us
    select_n x1, other arithmetic, relayed(): jnp.where(place == 1, fast_b, fast_a)  3.13 us
    reduce_sum x1, other arithmetic, local(): part_m2 = jnp.sum(deviation * deviation, axis=0)  2.85 us
    reduce_sum x1, other arithmetic, local(): part_mean = jnp.sum(dosage, axis=0) / rows  2.52 us
  transfers between devices with their start and end apart: 8, of which 3 were waited for; matrix products, arithmetic and copies ran while one was open for 6% of the time, Pallas kernels for 0%

profile of v5, /device:TPU:0, one launch (start us, length us, event | category | flops | bytes accessed | tf_op | source)
XLA Modules:
  0.0 114.1 jit_solution(16168983105602108101)
XLA Ops:
  0.0 2.5 %reduce_sum.18 = f32[512]{0:T(512)S(1)} reduce(f32[2048,512]{1,0:T(8,128)} %param.2, f32[]{:T(128)} %constant.64.clone.1), dimensions={0}, to_apply=%region_0.0 | reduce | flops 1048064 | bytes 4196356 | tf_op jit(solution)/shard_map/reduce_sum | solution.py:65
  2.5 0.0 copy-start
  2.5 2.9 %multiply_reduce_fusion = f32[512]{0:T(512)S(1)} fusion(f32[2048,512]{1,0:T(8,128)} %param.2, f32[512]{0:T(512)S(1)} %broadcast_multiply_fusion), kind=kLoop, calls=%fused_computation.1 | loop fusion | flops 3145216 | bytes 4198400 | tf_op jit(solution)/shard_map/reduce_sum | solution.py:67
  5.4 3.0 %collective-permute-start = (f32[2,512]{1,0:T(2,128)S(1)}, f32[2,512]{1,0:T(2,128)S(1)}, u32[]{:S(2)}, u32[]{:S(2)}) collective-permute-start(f32[2,512]{1,0:T(2,128)S(1)} %pad_maximum_fusion.2), channel_id=1, source_target_pairs={{0,1},{1,0},{2,3},{3,2},{4,5},{5,4},{6,7},{7,6},{8,9},{9,8},{10,11... | collective-permute-start | bytes 12296 | tf_op jit(solution)/shard_map/ppermute | solution.py:17
  8.4 1.6 %collective-permute-done = f32[2,512]{1,0:T(2,128)S(1)} collective-permute-done((f32[2,512]{1,0:T(2,128)S(1)}, f32[2,512]{1,0:T(2,128)S(1)}, u32[]{:S(2)}, u32[]{:S(2)}) %collective-permute-start) | collective-permute-done | bytes 4128 | tf_op jit(solution)/shard_map/ppermute | solution.py:17
  10.0 0.0 copy-done
  10.0 0.6 multiply_convert_fusion
  10.6 2.6 %collective-permute-start.3 = (bf16[2048,512]{1,0:T(8,128)(2,1)S(1)}, bf16[2048,512]{1,0:T(8,128)(2,1)}, u32[]{:S(2)}, u32[]{:S(2)}) collective-permute-start(bf16[2048,512]{1,0:T(8,128)(2,1)S(1)} %multiply_convert_fusion), channel_id=1, source_target_pairs={{0,2},{4,6},{2,8},{6,12},{8,10},{12,14},{10,16},{14,20},{16,18},{2... | collective-permute-start | bytes 6291464 | tf_op jit(solution)/shard_map/ppermute | solution.py:32
  13.3 1.3 %collective-permute-start.2 = (bf16[2048,512]{1,0:T(8,128)(2,1)S(1)}, bf16[2048,512]{1,0:T(8,128)(2,1)}, u32[]{:S(2)}, u32[]{:S(2)}) collective-permute-start(bf16[2048,512]{1,0:T(8,128)(2,1)S(1)} %multiply_convert_fusion), channel_id=1, source_target_pairs={{4,2},{6,4},{2,0},{12,10},{14,12},{10,8},{20,18},{22,20},{18,16},{... | collective-permute-start | bytes 6291464 | tf_op jit(solution)/shard_map/ppermute | solution.py:32
  14.6 7.2 %collective-permute-start.5 = (bf16[2048,512]{1,0:T(8,128)(2,1)S(1)}, bf16[2048,512]{1,0:T(8,128)(2,1)}, u32[]{:S(2)}, u32[]{:S(2)}) collective-permute-start(bf16[2048,512]{1,0:T(8,128)(2,1)S(1)} %multiply_convert_fusion), channel_id=1, source_target_pairs={{2,4},{0,6},{10,12},{8,14},{18,20},{16,22},{26,28},{24,30},{3,5},{... | collective-permute-start | bytes 6291464 | tf_op jit(solution)/shard_map/ppermute | solution.py:32
  21.8 0.0 collective-permute-done.3
  21.8 0.0 collective-permute-done.2
  21.8 3.1 %broadcast_select_fusion = bf16[2048,512]{1,0:T(8,128)(2,1)} fusion(bf16[2048,512]{1,0:T(8,128)(2,1)} %collective-permute-done.2, bf16[2048,512]{1,0:T(8,128)(2,1)} %collective-permute-done.3, pred[]{:T(512)S(6)} %eq.23), kind=kLoop, calls=%fused_computation.6 | loop fusion | flops 1048576 | bytes 6291457 | tf_op jit(solution)/shard_map/jit(_where)/select_n | solution.py:40
  25.0 2.0 %collective-permute-start.4 = (bf16[2048,512]{1,0:T(8,128)(2,1)}, bf16[2048,512]{1,0:T(8,128)(2,1)}, u32[]{:S(2)}, u32[]{:S(2)}) collective-permute-start(bf16[2048,512]{1,0:T(8,128)(2,1)} %broadcast_select_fusion), channel_id=1, source_target_pairs={{2,8},{4,2},{10,16},{12,10},{18,24},{20,18},{28,26},{3,9},{5,3},{1... | collective-permute-start | bytes 6291464 | tf_op jit(solution)/shard_map/ppermute | solution.py:32
  27.0 38.7 %collective-permute-done.5 = bf16[2048,512]{1,0:T(8,128)(2,1)} collective-permute-done((bf16[2048,512]{1,0:T(8,128)(2,1)S(1)}, bf16[2048,512]{1,0:T(8,128)(2,1)}, u32[]{:S(2)}, u32[]{:S(2)}) %collective-permute-start.5) | collective-permute-done | bytes 2097184 | tf_op jit(solution)/shard_map/ppermute | solution.py:32
  65.7 0.0 collective-permute-done.4
  65.7 3.5 %fusion.5 = bf16[512,512]{1,0:T(8,128)(2,1)S(1)} fusion(bf16[2048,512]{1,0:T(8,128)(2,1)} %collective-permute-done.4, bf16[2048,512]{1,0:T(8,128)(2,1)} %collective-permute-done.5, pred[]{:T(512)S(6)} %lt.35, bf16[2048,512]{1,0:T(8,128)(2,1)} %collective-permute-done.2, bf16[2048,512]{1,0:T(8,128)(2,1)} %collective-permute-done.3, pred[]{:T(512)S(6)} %eq.22), kind=kOutput, calls=%fused_computation.11 | convolution fusion | flops 1076101120 | bytes 8912898 | tf_op jit(solution)/shard_map/dot_general | solution.py:54
  69.2 7.4 %collective-permute-start.6 = (bf16[512,512]{1,0:T(8,128)(2,1)S(1)}, bf16[512,512]{1,0:T(8,128)(2,1)S(1)}, u32[]{:S(2)}, u32[]{:S(2)}) collective-permute-start(bf16[512,512]{1,0:T(8,128)(2,1)S(1)} %fusion.5), channel_id=1, source_target_pairs={{0,2},{2,0},{4,6},{6,4},{8,10},{10,8},{12,14},{14,12},{16,18},{18,... | collective-permute-start | bytes 1572872 | tf_op jit(solution)/shard_map/ppermute | solution.py:32
  76.6 2.9 %convolution_convert_fusion.1 = bf16[512,512]{1,0:T(8,128)(2,1)S(1)} fusion(bf16[2048,512]{1,0:T(8,128)(2,1)S(1)} %multiply_convert_fusion, bf16[2048,512]{1,0:T(8,128)(2,1)} %collective-permute-done.3), kind=kOutput, calls=%fused_computation.13 | convolution fusion | flops 1074003968 | bytes 4718592 | tf_op jit(solution)/shard_map/dot_general | solution.py:54
  79.5 0.0 collective-permute-done.6
  79.5 2.9 %fusion.10 = bf16[512,512]{1,0:T(8,128)(2,1)S(1)} fusion(bf16[512,512]{1,0:T(8,128)(2,1)S(1)} %collective-permute-done.6, bf16[2048,512]{1,0:T(8,128)(2,1)S(1)} %multiply_convert_fusion, bf16[2048,512]{1,0:T(8,128)(2,1)} %collective-permute-done.4, pred[]{:T(512)S(6)} %lt.35), kind=kOutput, calls=%fused_computation.16 | convolution fusion | flops 1074266112 | bytes 5242881 | tf_op jit(solution)/shard_map/dot_general | solution.py:54
  82.4 2.9 %select_select_fusion.1 = (bf16[512,512]{1,0:T(8,128)(2,1)S(1)}, bf16[512,512]{1,0:T(8,128)(2,1)S(1)}) fusion(bf16[512,512]{1,0:T(8,128)(2,1)S(1)} %collective-permute-done.6, bf16[512,512]{1,0:T(8,128)(2,1)S(1)} %convolution_convert_fusion.1, pred[]{:T(512)S(6)} %eq.24, pred[]{:T(512)S(6)} %eq.21, pred[]{:T(512)S(6)} %eq.25, pred[]{:T(512)S(6)} %eq.23, ...), kind=kOutput, calls=%fused_computation.31 | convolution fusion | flops 1075052544 | bytes 6291460 | tf_op jit(solution)/shard_map/dot_general | solution.py:54
  85.2 0.2 pad_maximum_fusion.1
  85.4 0.0 copy-start.1
  85.4 0.1 dynamic-slice_bitcast_fusion
  85.5 1.6 %collective-permute-start.7 = (bf16[3,256,512]{2,1,0:T(8,128)(2,1)S(1)}, bf16[3,256,512]{2,1,0:T(8,128)(2,1)}, u32[]{:S(2)}, u32[]{:S(2)}) collective-permute-start(bf16[3,256,512]{2,1,0:T(8,128)(2,1)S(1)} %dynamic-slice_bitcast_fusion), channel_id=1, source_target_pairs={{0,1},{1,0},{2,3},{3,2},{4,5},{5,4},{6,7},{7,6},{8,9},{9,8},{10,11... | collective-permute-start | bytes 2359304 | tf_op jit(solution)/shard_map/ppermute | solution.py:17
  87.1 1.3 %convolution_convert_fusion.3 = bf16[512,512]{1,0:T(8,128)(2,1)S(1)} fusion(bf16[2048,512]{1,0:T(8,128)(2,1)S(1)} %multiply_convert_fusion), kind=kOutput, calls=%fused_computation.15 | convolution fusion | flops 1074003968 | bytes 2621440 | tf_op jit(solution)/shard_map/dot_general | solution.py:54
  88.4 0.0 copy-done.1
  88.4 0.6 collective-permute-start.1
  89.6 21.0 %collective-permute-done.1 = bf16[256,512]{1,0:T(8,128)(2,1)S(1)} collective-permute-done((bf16[256,512]{1,0:T(8,128)(2,1)S(1)}, bf16[256,512]{1,0:T(8,128)(2,1)S(1)}, u32[]{:S(2)}, u32[]{:S(2)}) %collective-permute-start.1) | collective-permute-done | bytes 262176 | tf_op jit(solution)/shard_map/ppermute | solution.py:17
  110.7 0.1 fusion.18
  110.8 0.0 collective-permute-done.7
  110.8 1.6 %convert_add_fusion = f32[3,256,512]{2,1,0:T(8,128)S(1)} fusion(bf16[3,256,512]{2,1,0:T(8,128)(2,1)} %collective-permute-done.7, bf16[3,2,256,512]{3,2,0,1:T(8,128)(2,1)} %copy-done.1, s32[]{:T(128)S(6)} %select_n.115), kind=kLoop, calls=%fused_computation.10 | loop fusion | flops 1179648 | bytes 3145732 | tf_op jit(solution)/shard_map/add | solution.py:97
  112.4 0.2 fusion.16
  112.6 1.5 %pad_maximum_fusion = f32[256,2048]{1,0:T(8,128)} fusion(f32[256,512]{1,0:T(8,128)S(1)} %get-tuple-element.6, f32[256,512]{1,0:T(8,128)S(1)} %get-tuple-element.7, f32[256,512]{1,0:T(8,128)S(1)} %get-tuple-element.5, f32[256,512]{1,0:T(8,128)S(1)} %fusion.18), kind=kLoop, calls=%fused_computation.2 | loop fusion | flops 1572864 | bytes 4194304 | tf_op jit(solution)/shard_map/concatenate | solution.py:105
  (4 shorter events, 0.1 us)
Async XLA Ops:
  2.5 7.5 %copy-start = (f32[2048,512]{1,0:T(8,128)S(1)}, f32[2048,512]{1,0:T(8,128)}, u32[]{:S(2)}) copy-start(f32[2048,512]{1,0:T(8,128)} %param.2) | copy-start | bytes 12582916
  5.4 4.6 %collective-permute-start = (f32[2,512]{1,0:T(2,128)S(1)}, f32[2,512]{1,0:T(2,128)S(1)}, u32[]{:S(2)}, u32[]{:S(2)}) collective-permute-start(f32[2,512]{1,0:T(2,128)S(1)} %pad_maximum_fusion.2), channel_id=1, source_target_pairs={{0,1},{1,0},{2,3},{3,2},{4,5},{5,4},{6,7},{7,6},{8,9},{9,8},{10,11... | collective-permute-start | bytes 12296 | tf_op jit(solution)/shard_map/ppermute | solution.py:17
  10.6 11.2 %collective-permute-start.3 = (bf16[2048,512]{1,0:T(8,128)(2,1)S(1)}, bf16[2048,512]{1,0:T(8,128)(2,1)}, u32[]{:S(2)}, u32[]{:S(2)}) collective-permute-start(bf16[2048,512]{1,0:T(8,128)(2,1)S(1)} %multiply_convert_fusion), channel_id=1, source_target_pairs={{0,2},{4,6},{2,8},{6,12},{8,10},{12,14},{10,16},{14,20},{16,18},{2... | collective-permute-start | bytes 6291464 | tf_op jit(solution)/shard_map/ppermute | solution.py:32
  13.3 8.6 %collective-permute-start.2 = (bf16[2048,512]{1,0:T(8,128)(2,1)S(1)}, bf16[2048,512]{1,0:T(8,128)(2,1)}, u32[]{:S(2)}, u32[]{:S(2)}) collective-permute-start(bf16[2048,512]{1,0:T(8,128)(2,1)S(1)} %multiply_convert_fusion), channel_id=1, source_target_pairs={{4,2},{6,4},{2,0},{12,10},{14,12},{10,8},{20,18},{22,20},{18,16},{... | collective-permute-start | bytes 6291464 | tf_op jit(solution)/shard_map/ppermute | solution.py:32
  14.6 51.1 %collective-permute-start.5 = (bf16[2048,512]{1,0:T(8,128)(2,1)S(1)}, bf16[2048,512]{1,0:T(8,128)(2,1)}, u32[]{:S(2)}, u32[]{:S(2)}) collective-permute-start(bf16[2048,512]{1,0:T(8,128)(2,1)S(1)} %multiply_convert_fusion), channel_id=1, source_target_pairs={{2,4},{0,6},{10,12},{8,14},{18,20},{16,22},{26,28},{24,30},{3,5},{... | collective-permute-start | bytes 6291464 | tf_op jit(solution)/shard_map/ppermute | solution.py:32
  25.0 40.7 %collective-permute-start.4 = (bf16[2048,512]{1,0:T(8,128)(2,1)}, bf16[2048,512]{1,0:T(8,128)(2,1)}, u32[]{:S(2)}, u32[]{:S(2)}) collective-permute-start(bf16[2048,512]{1,0:T(8,128)(2,1)} %broadcast_select_fusion), channel_id=1, source_target_pairs={{2,8},{4,2},{10,16},{12,10},{18,24},{20,18},{28,26},{3,9},{5,3},{1... | collective-permute-start | bytes 6291464 | tf_op jit(solution)/shard_map/ppermute | solution.py:32
  69.2 10.3 %collective-permute-start.6 = (bf16[512,512]{1,0:T(8,128)(2,1)S(1)}, bf16[512,512]{1,0:T(8,128)(2,1)S(1)}, u32[]{:S(2)}, u32[]{:S(2)}) collective-permute-start(bf16[512,512]{1,0:T(8,128)(2,1)S(1)} %fusion.5), channel_id=1, source_target_pairs={{0,2},{2,0},{4,6},{6,4},{8,10},{10,8},{12,14},{14,12},{16,18},{18,... | collective-permute-start | bytes 1572872 | tf_op jit(solution)/shard_map/ppermute | solution.py:32
  85.4 2.9 %copy-start.1 = (bf16[3,2,256,512]{3,2,0,1:T(8,128)(2,1)}, bf16[3,2,256,512]{3,2,0,1:T(8,128)(2,1)S(1)}, u32[]{:S(2)}) copy-start(bf16[3,2,256,512]{3,2,0,1:T(8,128)(2,1)S(1)} %pad_maximum_fusion.1) | copy-start | bytes 4718596
  85.5 25.3 %collective-permute-start.7 = (bf16[3,256,512]{2,1,0:T(8,128)(2,1)S(1)}, bf16[3,256,512]{2,1,0:T(8,128)(2,1)}, u32[]{:S(2)}, u32[]{:S(2)}) collective-permute-start(bf16[3,256,512]{2,1,0:T(8,128)(2,1)S(1)} %dynamic-slice_bitcast_fusion), channel_id=1, source_target_pairs={{0,1},{1,0},{2,3},{3,2},{4,5},{5,4},{6,7},{7,6},{8,9},{9,8},{10,11... | collective-permute-start | bytes 2359304 | tf_op jit(solution)/shard_map/ppermute | solution.py:17
  88.4 22.3 %collective-permute-start.1 = (bf16[256,512]{1,0:T(8,128)(2,1)S(1)}, bf16[256,512]{1,0:T(8,128)(2,1)S(1)}, u32[]{:S(2)}, u32[]{:S(2)}) collective-permute-start(bf16[256,512]{1,0:T(8,128)(2,1)S(1)} %dynamic-slice_bitcast_fusion.1), channel_id=1, source_target_pairs={{0,1},{1,0},{2,3},{3,2},{4,5},{5,4},{6,7},{7,6},{8,9},{9,8},{10,11... | collective-permute-start | bytes 786440 | tf_op jit(solution)/shard_map/ppermute | solution.py:17

commit v6 on v5

--- a/solution.py
+++ b/solution.py
@@ -37,7 +37,7 @@
     cross = send(standard, pairs_of((1, 2), (0, 3)))
     fast_a = send(standard, pairs_of((0, 1), (2, 3), (1, 4), (3, 6)))
     fast_b = send(standard, pairs_of((2, 1), (3, 2), (1, 0)))
-    relay = send(jnp.where(place == 1, fast_b, fast_a), pairs_of((1, 4), (2, 1)))
+    relay = send(fast_b, pairs_of((1, 4))) + send(fast_a, pairs_of((2, 1)))
     lhs = jnp.where(place % 2 == 0, fast_b, fast_a)
     rhs = jnp.where(place < 2, relay, cross)
     handed = send(tile_term(lhs, rhs).astype(jnp.bfloat16), pairs_of((0, 1), (1, 0), (2, 3), (3, 2)))
@@ -97,7 +97,7 @@
             total = total + rotated(outgoing, "smp", s).astype(jnp.float32)
         return total
 
-    totals = [exchanged(first)] + list(exchanged(jnp.stack(rest)))
+    totals = list(exchanged(jnp.stack([first] + rest)))
     kept = []
     for dist in range(TAPS):
         tile = totals[dist] / samples

time: 114 us -> 112 us (0.982)
  other arithmetic: 12.7 us -> 8.34 us
  starting transfers between devices: 25.8 us -> 21.7 us
  waiting for transfers between devices: 61.3 us -> 64.5 us
  matrix products: 13.4 us -> 14.9 us
    ppermute x5 -> x6, starting transfers between devices: 20.6 us -> 17.1 us  [send(): return lax.ppermute(value, 'snp', pairs)]
    select_n x1 -> x0, other arithmetic: 3.13 us -> none  [relayed(): jnp.where(place == 1, fast_b, fast_a)]
    ppermute x3 -> x2, waiting for transfers between devices: 22.6 us -> 24.7 us  [rotated(): lax.ppermute(value, axis, [(source, (source + steps) % count) for source...]
    dot_general x5, matrix products: 13.4 us -> 14.9 us  [tile_term(): lax.dot_general(standard, neighbour, (((0,), (0,)), ((), ())), preferred_...]
    add x1, other arithmetic: 1.61 us -> 0.33 us  [exchanged(): total = total + rotated(outgoing, 'smp', s).astype(jnp.float32)]
    ppermute x5 -> x6, waiting for transfers between devices: 38.7 us -> 39.8 us  [send(): return lax.ppermute(value, 'snp', pairs)]
    ppermute x3 -> x2, starting transfers between devices: 5.18 us -> 4.54 us  [rotated(): lax.ppermute(value, axis, [(source, (source + steps) % count) for source...]
  transfers between devices with their start and end apart: 8 -> 8, of which waited for: 3 -> 3; matrix products, arithmetic and copies ran while one was open for 6% -> 4% of each run, Pallas kernels for 0% -> 0%
where the time goes in v6:
time: 112 us; the launch traced here: 111 us
  waiting for transfers between devices  64.5 us (58%)
  starting transfers between devices  21.7 us (19%)
  matrix products  14.9 us (13%)
  other arithmetic  8.34 us (7%)
    ppermute x6, waiting for transfers between devices, send(): return lax.ppermute(value, 'snp', pairs)  39.8 us
    ppermute x2, waiting for transfers between devices, rotated(): lax.ppermute(value, axis, [(source, (source + steps) % count) for source...  24.7 us
    ppermute x6, starting transfers between devices, send(): return lax.ppermute(value, 'snp', pairs)  17.1 us
    dot_general x5, matrix products, tile_term(): lax.dot_general(standard, neighbour, (((0,), (0,)), ((), ())), preferred_...  14.9 us
    ppermute x2, starting transfers between devices, rotated(): lax.ppermute(value, axis, [(source, (source + steps) % count) for source...  4.54 us
    reduce_sum x1, other arithmetic, local(): part_m2 = jnp.sum(deviation * deviation, axis=0)  2.86 us
    reduce_sum x1, other arithmetic, local(): part_mean = jnp.sum(dosage, axis=0) / rows  2.52 us
  transfers between devices with their start and end apart: 8, of which 3 were waited for; matrix products, arithmetic and copies ran while one was open for 4% of the time, Pallas kernels for 0%

profile of v6, /device:TPU:0, one launch (start us, length us, event | category | flops | bytes accessed | tf_op | source)
XLA Modules:
  0.0 111.2 jit_solution(8849713278771319103)
XLA Ops:
  0.0 2.5 %reduce_sum.18 = f32[512]{0:T(512)S(1)} reduce(f32[2048,512]{1,0:T(8,128)} %param.2, f32[]{:T(128)} %constant.56.clone.1), dimensions={0}, to_apply=%region_0.0 | reduce | flops 1048064 | bytes 4196356 | tf_op jit(solution)/shard_map/reduce_sum | solution.py:65
  2.5 0.0 copy-start
  2.5 2.9 %multiply_reduce_fusion = f32[512]{0:T(512)S(1)} fusion(f32[2048,512]{1,0:T(8,128)} %param.2, f32[512]{0:T(512)S(1)} %broadcast_multiply_fusion), kind=kLoop, calls=%fused_computation.1 | loop fusion | flops 3145216 | bytes 4198400 | tf_op jit(solution)/shard_map/reduce_sum | solution.py:67
  5.4 3.0 %collective-permute-start = (f32[2,512]{1,0:T(2,128)S(1)}, f32[2,512]{1,0:T(2,128)S(1)}, u32[]{:S(2)}, u32[]{:S(2)}) collective-permute-start(f32[2,512]{1,0:T(2,128)S(1)} %pad_maximum_fusion.2), channel_id=1, source_target_pairs={{0,1},{1,0},{2,3},{3,2},{4,5},{5,4},{6,7},{7,6},{8,9},{9,8},{10,11... | collective-permute-start | bytes 12296 | tf_op jit(solution)/shard_map/ppermute | solution.py:17
  8.4 1.6 %collective-permute-done = f32[2,512]{1,0:T(2,128)S(1)} collective-permute-done((f32[2,512]{1,0:T(2,128)S(1)}, f32[2,512]{1,0:T(2,128)S(1)}, u32[]{:S(2)}, u32[]{:S(2)}) %collective-permute-start) | collective-permute-done | bytes 4128 | tf_op jit(solution)/shard_map/ppermute | solution.py:17
  10.0 0.0 copy-done
  10.0 0.6 multiply_convert_fusion
  10.6 2.6 %collective-permute-start.2 = (bf16[2048,512]{1,0:T(8,128)(2,1)S(1)}, bf16[2048,512]{1,0:T(8,128)(2,1)}, u32[]{:S(2)}, u32[]{:S(2)}) collective-permute-start(bf16[2048,512]{1,0:T(8,128)(2,1)S(1)} %multiply_convert_fusion), channel_id=1, source_target_pairs={{0,2},{4,6},{2,8},{6,12},{8,10},{12,14},{10,16},{14,20},{16,18},{2... | collective-permute-start | bytes 6291464 | tf_op jit(solution)/shard_map/ppermute | solution.py:32
  13.3 1.3 %collective-permute-start.1 = (bf16[2048,512]{1,0:T(8,128)(2,1)S(1)}, bf16[2048,512]{1,0:T(8,128)(2,1)}, u32[]{:S(2)}, u32[]{:S(2)}) collective-permute-start(bf16[2048,512]{1,0:T(8,128)(2,1)S(1)} %multiply_convert_fusion), channel_id=1, source_target_pairs={{4,2},{6,4},{2,0},{12,10},{14,12},{10,8},{20,18},{22,20},{18,16},{... | collective-permute-start | bytes 6291464 | tf_op jit(solution)/shard_map/ppermute | solution.py:32
  14.5 7.3 %collective-permute-start.5 = (bf16[2048,512]{1,0:T(8,128)(2,1)S(1)}, bf16[2048,512]{1,0:T(8,128)(2,1)}, u32[]{:S(2)}, u32[]{:S(2)}) collective-permute-start(bf16[2048,512]{1,0:T(8,128)(2,1)S(1)} %multiply_convert_fusion), channel_id=1, source_target_pairs={{2,4},{0,6},{10,12},{8,14},{18,20},{16,22},{26,28},{24,30},{3,5},{... | collective-permute-start | bytes 6291464 | tf_op jit(solution)/shard_map/ppermute | solution.py:32
  21.8 0.0 collective-permute-done.2
  21.8 2.0 %collective-permute-start.4 = (bf16[2048,512]{1,0:T(8,128)(2,1)}, bf16[2048,512]{1,0:T(8,128)(2,1)}, u32[]{:S(2)}, u32[]{:S(2)}) collective-permute-start(bf16[2048,512]{1,0:T(8,128)(2,1)} %collective-permute-done.2), channel_id=1, source_target_pairs={{4,2},{12,10},{20,18},{28,26},{5,3},{13,11},{21,19},{29,27}} | collective-permute-start | bytes 6291464 | tf_op jit(solution)/shard_map/ppermute | solution.py:32
  23.9 0.0 collective-permute-done.1
  23.9 2.0 %collective-permute-start.3 = (bf16[2048,512]{1,0:T(8,128)(2,1)}, bf16[2048,512]{1,0:T(8,128)(2,1)}, u32[]{:S(2)}, u32[]{:S(2)}) collective-permute-start(bf16[2048,512]{1,0:T(8,128)(2,1)} %collective-permute-done.1), channel_id=1, source_target_pairs={{2,8},{10,16},{18,24},{3,9},{11,17},{19,25}} | collective-permute-start | bytes 6291464 | tf_op jit(solution)/shard_map/ppermute | solution.py:32
  25.9 39.8 %collective-permute-done.5 = bf16[2048,512]{1,0:T(8,128)(2,1)} collective-permute-done((bf16[2048,512]{1,0:T(8,128)(2,1)S(1)}, bf16[2048,512]{1,0:T(8,128)(2,1)}, u32[]{:S(2)}, u32[]{:S(2)}) %collective-permute-start.5) | collective-permute-done | bytes 2097184 | tf_op jit(solution)/shard_map/ppermute | solution.py:32
  65.6 0.0 collective-permute-done.4
  65.6 0.0 collective-permute-done.3
  65.6 4.4 %fusion.5 = bf16[512,512]{1,0:T(8,128)(2,1)S(1)} fusion(bf16[2048,512]{1,0:T(8,128)(2,1)} %collective-permute-done.5, pred[]{:T(512)S(6)} %lt.27, bf16[2048,512]{1,0:T(8,128)(2,1)} %collective-permute-done.1, bf16[2048,512]{1,0:T(8,128)(2,1)} %collective-permute-done.2, pred[]{:T(512)S(6)} %eq.20, bf16[2048,512]{1,0:T(8,128)(2,1)} %collective-permute-done.3, ...), kind=kOutput, calls=%fused_computation.10 | convolution fusion | flops 1077149696 | bytes 11010050 | tf_op jit(solution)/shard_map/dot_general | solution.py:54
  70.1 1.9 %collective-permute-start.6 = (bf16[512,512]{1,0:T(8,128)(2,1)S(1)}, bf16[512,512]{1,0:T(8,128)(2,1)S(1)}, u32[]{:S(2)}, u32[]{:S(2)}) collective-permute-start(bf16[512,512]{1,0:T(8,128)(2,1)S(1)} %fusion.5), channel_id=1, source_target_pairs={{0,2},{2,0},{4,6},{6,4},{8,10},{10,8},{12,14},{14,12},{16,18},{18,... | collective-permute-start | bytes 1572872 | tf_op jit(solution)/shard_map/ppermute | solution.py:32
  72.0 1.3 %convolution_convert_fusion.3 = bf16[512,512]{1,0:T(8,128)(2,1)S(1)} fusion(bf16[2048,512]{1,0:T(8,128)(2,1)S(1)} %multiply_convert_fusion), kind=kOutput, calls=%fused_computation.14 | convolution fusion | flops 1074003968 | bytes 2621440 | tf_op jit(solution)/shard_map/dot_general | solution.py:54
  73.3 2.9 %convolution_convert_fusion.1 = bf16[512,512]{1,0:T(8,128)(2,1)S(1)} fusion(bf16[2048,512]{1,0:T(8,128)(2,1)S(1)} %multiply_convert_fusion, bf16[2048,512]{1,0:T(8,128)(2,1)} %collective-permute-done.2), kind=kOutput, calls=%fused_computation.12 | convolution fusion | flops 1074003968 | bytes 4718592 | tf_op jit(solution)/shard_map/dot_general | solution.py:54
  76.1 0.0 collective-permute-done.6
  76.1 3.5 %fusion.10 = bf16[512,512]{1,0:T(8,128)(2,1)S(1)} fusion(bf16[512,512]{1,0:T(8,128)(2,1)S(1)} %collective-permute-done.6, bf16[2048,512]{1,0:T(8,128)(2,1)S(1)} %multiply_convert_fusion, bf16[2048,512]{1,0:T(8,128)(2,1)} %collective-permute-done.3, bf16[2048,512]{1,0:T(8,128)(2,1)} %collective-permute-done.4, pred[]{:T(512)S(6)} %lt.27), kind=kOutput, calls=%fused_computation.15 | convolution fusion | flops 1075314688 | bytes 7340033 | tf_op jit(solution)/shard_map/dot_general | solution.py:54
  79.6 2.9 %select_select_fusion.1 = (bf16[512,512]{1,0:T(8,128)(2,1)S(1)}, bf16[512,512]{1,0:T(8,128)(2,1)S(1)}) fusion(bf16[512,512]{1,0:T(8,128)(2,1)S(1)} %collective-permute-done.6, bf16[512,512]{1,0:T(8,128)(2,1)S(1)} %convolution_convert_fusion.1, pred[]{:T(512)S(6)} %eq.21, pred[]{:T(512)S(6)} %eq.19, pred[]{:T(512)S(6)} %eq.23, pred[]{:T(512)S(6)} %eq.22, ...), kind=kOutput, calls=%fused_computation.32 | convolution fusion | flops 1075052544 | bytes 6291460 | tf_op jit(solution)/shard_map/dot_general | solution.py:54
  82.5 0.3 pad_maximum_fusion
  82.8 1.0 dynamic-slice_bitcast_fusion
  83.8 1.5 %collective-permute-start.7 = (bf16[4,256,512]{2,1,0:T(8,128)(2,1)}, bf16[4,256,512]{2,1,0:T(8,128)(2,1)S(1)}, u32[]{:S(2)}, u32[]{:S(2)}) collective-permute-start(bf16[4,256,512]{2,1,0:T(8,128)(2,1)} %dynamic-slice_bitcast_fusion), channel_id=1, source_target_pairs={{0,1},{1,0},{2,3},{3,2},{4,5},{5,4},{6,7},{7,6},{8,9},{9,8},{10,11... | collective-permute-start | bytes 3145736 | tf_op jit(solution)/shard_map/ppermute | solution.py:17
  86.0 23.1 %collective-permute-done.7 = bf16[4,256,512]{2,1,0:T(8,128)(2,1)S(1)} collective-permute-done((bf16[4,256,512]{2,1,0:T(8,128)(2,1)}, bf16[4,256,512]{2,1,0:T(8,128)(2,1)S(1)}, u32[]{:S(2)}, u32[]{:S(2)}) %collective-permute-start.7) | collective-permute-done | bytes 1048608 | tf_op jit(solution)/shard_map/ppermute | solution.py:17
  109.1 0.3 convert_add_fusion
  109.5 0.3 fusion.20
  109.7 1.5 %pad_maximum_fusion.1 = f32[256,2048]{1,0:T(8,128)} fusion(f32[256,512]{1,0:T(8,128)S(1)} %get-tuple-element.6, f32[256,512]{1,0:T(8,128)S(1)} %get-tuple-element.7, f32[256,512]{1,0:T(8,128)S(1)} %get-tuple-element.8, f32[256,512]{1,0:T(8,128)S(1)} %get-tuple-element.5), kind=kLoop, calls=%fused_computation.3 | loop fusion | flops 1572864 | bytes 4194304 | tf_op jit(solution)/shard_map/concatenate | solution.py:105
  (3 shorter events, 0.0 us)
Async XLA Ops:
  2.5 7.5 %copy-start = (f32[2048,512]{1,0:T(8,128)S(1)}, f32[2048,512]{1,0:T(8,128)}, u32[]{:S(2)}) copy-start(f32[2048,512]{1,0:T(8,128)} %param.2) | copy-start | bytes 12582916
  5.4 4.6 %collective-permute-start = (f32[2,512]{1,0:T(2,128)S(1)}, f32[2,512]{1,0:T(2,128)S(1)}, u32[]{:S(2)}, u32[]{:S(2)}) collective-permute-start(f32[2,512]{1,0:T(2,128)S(1)} %pad_maximum_fusion.2), channel_id=1, source_target_pairs={{0,1},{1,0},{2,3},{3,2},{4,5},{5,4},{6,7},{7,6},{8,9},{9,8},{10,11... | collective-permute-start | bytes 12296 | tf_op jit(solution)/shard_map/ppermute | solution.py:17
  10.6 11.2 %collective-permute-start.2 = (bf16[2048,512]{1,0:T(8,128)(2,1)S(1)}, bf16[2048,512]{1,0:T(8,128)(2,1)}, u32[]{:S(2)}, u32[]{:S(2)}) collective-permute-start(bf16[2048,512]{1,0:T(8,128)(2,1)S(1)} %multiply_convert_fusion), channel_id=1, source_target_pairs={{0,2},{4,6},{2,8},{6,12},{8,10},{12,14},{10,16},{14,20},{16,18},{2... | collective-permute-start | bytes 6291464 | tf_op jit(solution)/shard_map/ppermute | solution.py:32
  13.3 10.6 %collective-permute-start.1 = (bf16[2048,512]{1,0:T(8,128)(2,1)S(1)}, bf16[2048,512]{1,0:T(8,128)(2,1)}, u32[]{:S(2)}, u32[]{:S(2)}) collective-permute-start(bf16[2048,512]{1,0:T(8,128)(2,1)S(1)} %multiply_convert_fusion), channel_id=1, source_target_pairs={{4,2},{6,4},{2,0},{12,10},{14,12},{10,8},{20,18},{22,20},{18,16},{... | collective-permute-start | bytes 6291464 | tf_op jit(solution)/shard_map/ppermute | solution.py:32
  14.5 51.1 %collective-permute-start.5 = (bf16[2048,512]{1,0:T(8,128)(2,1)S(1)}, bf16[2048,512]{1,0:T(8,128)(2,1)}, u32[]{:S(2)}, u32[]{:S(2)}) collective-permute-start(bf16[2048,512]{1,0:T(8,128)(2,1)S(1)} %multiply_convert_fusion), channel_id=1, source_target_pairs={{2,4},{0,6},{10,12},{8,14},{18,20},{16,22},{26,28},{24,30},{3,5},{... | collective-permute-start | bytes 6291464 | tf_op jit(solution)/shard_map/ppermute | solution.py:32
  21.8 43.8 %collective-permute-start.4 = (bf16[2048,512]{1,0:T(8,128)(2,1)}, bf16[2048,512]{1,0:T(8,128)(2,1)}, u32[]{:S(2)}, u32[]{:S(2)}) collective-permute-start(bf16[2048,512]{1,0:T(8,128)(2,1)} %collective-permute-done.2), channel_id=1, source_target_pairs={{4,2},{12,10},{20,18},{28,26},{5,3},{13,11},{21,19},{29,27}} | collective-permute-start | bytes 6291464 | tf_op jit(solution)/shard_map/ppermute | solution.py:32
  23.9 41.8 %collective-permute-start.3 = (bf16[2048,512]{1,0:T(8,128)(2,1)}, bf16[2048,512]{1,0:T(8,128)(2,1)}, u32[]{:S(2)}, u32[]{:S(2)}) collective-permute-start(bf16[2048,512]{1,0:T(8,128)(2,1)} %collective-permute-done.1), channel_id=1, source_target_pairs={{2,8},{10,16},{18,24},{3,9},{11,17},{19,25}} | collective-permute-start | bytes 6291464 | tf_op jit(solution)/shard_map/ppermute | solution.py:32
  70.1 6.1 %collective-permute-start.6 = (bf16[512,512]{1,0:T(8,128)(2,1)S(1)}, bf16[512,512]{1,0:T(8,128)(2,1)S(1)}, u32[]{:S(2)}, u32[]{:S(2)}) collective-permute-start(bf16[512,512]{1,0:T(8,128)(2,1)S(1)} %fusion.5), channel_id=1, source_target_pairs={{0,2},{2,0},{4,6},{6,4},{8,10},{10,8},{12,14},{14,12},{16,18},{18,... | collective-permute-start | bytes 1572872 | tf_op jit(solution)/shard_map/ppermute | solution.py:32
  83.8 25.3 %collective-permute-start.7 = (bf16[4,256,512]{2,1,0:T(8,128)(2,1)}, bf16[4,256,512]{2,1,0:T(8,128)(2,1)S(1)}, u32[]{:S(2)}, u32[]{:S(2)}) collective-permute-start(bf16[4,256,512]{2,1,0:T(8,128)(2,1)} %dynamic-slice_bitcast_fusion), channel_id=1, source_target_pairs={{0,1},{1,0},{2,3},{3,2},{4,5},{5,4},{6,7},{7,6},{8,9},{9,8},{10,11... | collective-permute-start | bytes 3145736 | tf_op jit(solution)/shard_map/ppermute | solution.py:17

commit v7 on v6

--- a/solution.py
+++ b/solution.py
@@ -44,10 +44,7 @@
     with_a = tile_term(standard, fast_a).astype(jnp.bfloat16)
     with_relay = tile_term(standard, relay).astype(jnp.bfloat16)
     with_cross = tile_term(standard, cross).astype(jnp.bfloat16)
-    one = jnp.where(place == 0, handed, jnp.where(place == 2, with_cross, with_a))
-    two = jnp.where(place < 2, with_relay, handed)
-    three = jnp.where(place == 1, handed, jnp.where(place == 3, with_cross, with_a))
-    return [one, two, three]
+    return with_a, jnp.where(place < 2, with_relay, with_cross), handed
 
 
 def tile_term(standard, neighbour):
@@ -83,10 +80,6 @@
     share = width // n_smp
     own_reach = reach[0]
     first = tile_term(standard, standard).astype(jnp.bfloat16)
-    if count % 4 == 0:
-        rest = relayed(standard, count, lax.axis_index("snp") % 4)
-    else:
-        rest = [tile_term(standard, nb).astype(jnp.bfloat16) for nb in chained(standard)]
 
     def exchanged(partial):
         pieces = partial.reshape(partial.shape[:-2] + (n_smp, share, width))
@@ -97,7 +90,20 @@
             total = total + rotated(outgoing, "smp", s).astype(jnp.float32)
         return total
 
-    totals = list(exchanged(jnp.stack([first] + rest)))
+    if count % 4 == 0:
+        place = lax.axis_index("snp") % 4
+        with_a, own_late, handed = relayed(standard, count, place)
+        early = exchanged(jnp.stack([first, with_a]))
+        late = exchanged(jnp.stack([own_late, handed]))
+        totals = [
+            early[0],
+            jnp.where(place == 0, late[1], jnp.where(place == 2, late[0], early[1])),
+            jnp.where(place < 2, late[0], late[1]),
+            jnp.where(place == 1, late[1], jnp.where(place == 3, late[0], early[1])),
+        ]
+    else:
+        rest = [tile_term(standard, nb).astype(jnp.bfloat16) for nb in chained(standard)]
+        totals = list(exchanged(jnp.stack([first] + rest)))
     kept = []
     for dist in range(TAPS):
         tile = totals[dist] / samples

time: 112 us -> 95.3 us (0.85)
  waiting for transfers between devices: 64.5 us -> 45.7 us
  other arithmetic: 8.34 us -> 11.2 us
    ppermute x2 -> x3, waiting for transfers between devices: 24.7 us -> 12.5 us  [rotated(): lax.ppermute(value, axis, [(source, (source + steps) % count) for source...]
    ppermute x6, waiting for transfers between devices: 39.8 us -> 33.3 us  [send(): return lax.ppermute(value, 'snp', pairs)]
    add x1 -> x2, other arithmetic: 0.33 us -> 2.48 us  [exchanged(): total = total + rotated(outgoing, 'smp', s).astype(jnp.float32)]
    ppermute x6, starting transfers between devices: 17.1 us -> 15.3 us  [send(): return lax.ppermute(value, 'snp', pairs)]
    ppermute x2 -> x3, starting transfers between devices: 4.54 us -> 6.12 us  [rotated(): lax.ppermute(value, axis, [(source, (source + steps) % count) for source...]
  transfers between devices with their start and end apart: 8 -> 9, of which waited for: 3 -> 3; matrix products, arithmetic and copies ran while one was open for 4% -> 18% of each run, Pallas kernels for 0% -> 0%
where the time goes in v7:
time: 95.3 us; the launch traced here: 94.9 us
  waiting for transfers between devices  45.7 us (48%)
  starting transfers between devices  21.4 us (22%)
  matrix products  14.9 us (16%)
  other arithmetic  11.2 us (12%)
    ppermute x6, waiting for transfers between devices, send(): return lax.ppermute(value, 'snp', pairs)  33.3 us
    ppermute x6, starting transfers between devices, send(): return lax.ppermute(value, 'snp', pairs)  15.3 us
    dot_general x5, matrix products, tile_term(): lax.dot_general(standard, neighbour, (((0,), (0,)), ((), ())), preferred_...  14.9 us
    ppermute x3, waiting for transfers between devices, rotated(): lax.ppermute(value, axis, [(source, (source + steps) % count) for source...  12.5 us
    ppermute x3, starting transfers between devices, rotated(): lax.ppermute(value, axis, [(source, (source + steps) % count) for source...  6.12 us
    reduce_sum x1, other arithmetic, local(): part_m2 = jnp.sum(deviation * deviation, axis=0)  2.85 us
    reduce_sum x1, other arithmetic, local(): part_mean = jnp.sum(dosage, axis=0) / rows  2.52 us
    add x2, other arithmetic, exchanged(): total = total + rotated(outgoing, 'smp', s).astype(jnp.float32)  2.48 us
  transfers between devices with their start and end apart: 9, of which 3 were waited for; matrix products, arithmetic and copies ran while one was open for 18% of the time, Pallas kernels for 0%

profile of v7, /device:TPU:0, one launch (start us, length us, event | category | flops | bytes accessed | tf_op | source)
XLA Modules:
  0.0 94.9 jit_solution(175045564153523476)
XLA Ops:
  0.0 2.5 %reduce_sum.18 = f32[512]{0:T(512)S(1)} reduce(f32[2048,512]{1,0:T(8,128)} %param.2, f32[]{:T(128)} %constant.62.clone.1), dimensions={0}, to_apply=%region_0.0 | reduce | flops 1048064 | bytes 4196356 | tf_op jit(solution)/shard_map/reduce_sum | solution.py:62
  2.5 0.0 copy-start
  2.5 2.9 %multiply_reduce_fusion = f32[512]{0:T(512)S(1)} fusion(f32[2048,512]{1,0:T(8,128)} %param.2, f32[512]{0:T(512)S(1)} %broadcast_multiply_fusion), kind=kLoop, calls=%fused_computation.1 | loop fusion | flops 3145216 | bytes 4198400 | tf_op jit(solution)/shard_map/reduce_sum | solution.py:64
  5.4 3.0 %collective-permute-start = (f32[2,512]{1,0:T(2,128)S(1)}, f32[2,512]{1,0:T(2,128)S(1)}, u32[]{:S(2)}, u32[]{:S(2)}) collective-permute-start(f32[2,512]{1,0:T(2,128)S(1)} %pad_maximum_fusion.1), channel_id=1, source_target_pairs={{0,1},{1,0},{2,3},{3,2},{4,5},{5,4},{6,7},{7,6},{8,9},{9,8},{10,11... | collective-permute-start | bytes 12296 | tf_op jit(solution)/shard_map/ppermute | solution.py:17
  8.4 1.6 %collective-permute-done = f32[2,512]{1,0:T(2,128)S(1)} collective-permute-done((f32[2,512]{1,0:T(2,128)S(1)}, f32[2,512]{1,0:T(2,128)S(1)}, u32[]{:S(2)}, u32[]{:S(2)}) %collective-permute-start) | collective-permute-done | bytes 4128 | tf_op jit(solution)/shard_map/ppermute | solution.py:17
  10.0 0.0 copy-done
  10.0 0.6 multiply_convert_fusion
  10.6 2.6 %collective-permute-start.1 = (bf16[2048,512]{1,0:T(8,128)(2,1)S(1)}, bf16[2048,512]{1,0:T(8,128)(2,1)}, u32[]{:S(2)}, u32[]{:S(2)}) collective-permute-start(bf16[2048,512]{1,0:T(8,128)(2,1)S(1)} %multiply_convert_fusion), channel_id=1, source_target_pairs={{0,2},{4,6},{2,8},{6,12},{8,10},{12,14},{10,16},{14,20},{16,18},{2... | collective-permute-start | bytes 6291464 | tf_op jit(solution)/shard_map/ppermute | solution.py:32
  13.3 1.3 %collective-permute-start.3 = (bf16[2048,512]{1,0:T(8,128)(2,1)S(1)}, bf16[2048,512]{1,0:T(8,128)(2,1)}, u32[]{:S(2)}, u32[]{:S(2)}) collective-permute-start(bf16[2048,512]{1,0:T(8,128)(2,1)S(1)} %multiply_convert_fusion), channel_id=1, source_target_pairs={{4,2},{6,4},{2,0},{12,10},{14,12},{10,8},{20,18},{22,20},{18,16},{... | collective-permute-start | bytes 6291464 | tf_op jit(solution)/shard_map/ppermute | solution.py:32
  14.6 7.3 %collective-permute-start.6 = (bf16[2048,512]{1,0:T(8,128)(2,1)S(1)}, bf16[2048,512]{1,0:T(8,128)(2,1)}, u32[]{:S(2)}, u32[]{:S(2)}) collective-permute-start(bf16[2048,512]{1,0:T(8,128)(2,1)S(1)} %multiply_convert_fusion), channel_id=1, source_target_pairs={{2,4},{0,6},{10,12},{8,14},{18,20},{16,22},{26,28},{24,30},{3,5},{... | collective-permute-start | bytes 6291464 | tf_op jit(solution)/shard_map/ppermute | solution.py:32
  21.8 0.0 collective-permute-done.1
  21.8 2.0 %collective-permute-start.5 = (bf16[2048,512]{1,0:T(8,128)(2,1)}, bf16[2048,512]{1,0:T(8,128)(2,1)}, u32[]{:S(2)}, u32[]{:S(2)}) collective-permute-start(bf16[2048,512]{1,0:T(8,128)(2,1)} %collective-permute-done.1), channel_id=1, source_target_pairs={{4,2},{12,10},{20,18},{28,26},{5,3},{13,11},{21,19},{29,27}} | collective-permute-start | bytes 6291464 | tf_op jit(solution)/shard_map/ppermute | solution.py:32
  23.9 0.0 collective-permute-done.3
  23.9 2.0 %collective-permute-start.4 = (bf16[2048,512]{1,0:T(8,128)(2,1)}, bf16[2048,512]{1,0:T(8,128)(2,1)}, u32[]{:S(2)}, u32[]{:S(2)}) collective-permute-start(bf16[2048,512]{1,0:T(8,128)(2,1)} %collective-permute-done.3), channel_id=1, source_target_pairs={{2,8},{10,16},{18,24},{3,9},{11,17},{19,25}} | collective-permute-start | bytes 6291464 | tf_op jit(solution)/shard_map/ppermute | solution.py:32
  25.9 1.3 %convolution_convert_fusion.3 = bf16[512,512]{1,0:T(8,128)(2,1)S(1)} fusion(bf16[2048,512]{1,0:T(8,128)(2,1)S(1)} %multiply_convert_fusion), kind=kOutput, calls=%fused_computation.12 | convolution fusion | flops 1074003968 | bytes 2621440 | tf_op jit(solution)/shard_map/dot_general | solution.py:51
  27.1 2.9 %convolution_convert_fusion.2 = bf16[512,512]{1,0:T(8,128)(2,1)S(1)} fusion(bf16[2048,512]{1,0:T(8,128)(2,1)S(1)} %multiply_convert_fusion, bf16[2048,512]{1,0:T(8,128)(2,1)} %collective-permute-done.1), kind=kOutput, calls=%fused_computation.11 | convolution fusion | flops 1074003968 | bytes 4718592 | tf_op jit(solution)/shard_map/dot_general | solution.py:51
  30.0 0.8 fusion.18
  30.9 1.5 %collective-permute-start.2 = (bf16[2,256,512]{2,1,0:T(8,128)(2,1)}, bf16[2,256,512]{2,1,0:T(8,128)(2,1)}, u32[]{:S(2)}, u32[]{:S(2)}) collective-permute-start(bf16[2,256,512]{2,1,0:T(8,128)(2,1)} %fusion.18), channel_id=1, source_target_pairs={{0,1},{1,0},{2,3},{3,2},{4,5},{5,4},{6,7},{7,6},{8,9},{9,8},{10,11... | collective-permute-start | bytes 1572872 | tf_op jit(solution)/shard_map/ppermute | solution.py:17
  32.4 33.3 %collective-permute-done.6 = bf16[2048,512]{1,0:T(8,128)(2,1)} collective-permute-done((bf16[2048,512]{1,0:T(8,128)(2,1)S(1)}, bf16[2048,512]{1,0:T(8,128)(2,1)}, u32[]{:S(2)}, u32[]{:S(2)}) %collective-permute-start.6) | collective-permute-done | bytes 2097184 | tf_op jit(solution)/shard_map/ppermute | solution.py:32
  65.6 2.9 %convolution_convert_fusion = bf16[512,512]{1,0:T(8,128)(2,1)S(1)} fusion(bf16[2048,512]{1,0:T(8,128)(2,1)S(1)} %multiply_convert_fusion, bf16[2048,512]{1,0:T(8,128)(2,1)} %collective-permute-done.6), kind=kOutput, calls=%fused_computation.9 | convolution fusion | flops 1074003968 | bytes 4718592 | tf_op jit(solution)/shard_map/dot_general | solution.py:51
  68.5 0.0 collective-permute-done.5
  68.5 0.0 collective-permute-done.4
  68.5 4.4 %fusion.5 = bf16[512,512]{1,0:T(8,128)(2,1)S(1)} fusion(bf16[2048,512]{1,0:T(8,128)(2,1)} %collective-permute-done.6, pred[]{:T(512)S(6)} %lt.34, bf16[2048,512]{1,0:T(8,128)(2,1)} %collective-permute-done.3, bf16[2048,512]{1,0:T(8,128)(2,1)} %collective-permute-done.1, pred[]{:T(512)S(6)} %eq.21, bf16[2048,512]{1,0:T(8,128)(2,1)} %collective-permute-done.4, ...), kind=kOutput, calls=%fused_computation.8 | convolution fusion | flops 1077149696 | bytes 11010050 | tf_op jit(solution)/shard_map/dot_general | solution.py:51
  73.0 0.1 collective-permute-start.7
  73.0 3.5 %fusion.10 = bf16[512,512]{1,0:T(8,128)(2,1)S(1)} fusion(bf16[512,512]{1,0:T(8,128)(2,1)S(1)} %convolution_convert_fusion, bf16[2048,512]{1,0:T(8,128)(2,1)S(1)} %multiply_convert_fusion, bf16[2048,512]{1,0:T(8,128)(2,1)} %collective-permute-done.4, bf16[2048,512]{1,0:T(8,128)(2,1)} %collective-permute-done.5, pred[]{:T(512)S(6)} %lt.34), kind=kOutput, calls=%fused_computation.21 | convolution fusion | flops 1075314688 | bytes 7340033 | tf_op jit(solution)/shard_map/dot_general | solution.py:51
  76.5 0.0 copy-start.3
  76.6 0.0 collective-permute-done.7
  76.6 0.0 copy-start.1
  76.6 0.9 copy-done.1
  77.4 0.1 fusion.14
  77.5 0.0 copy-done.3
  77.5 1.6 %collective-permute-start.8 = (bf16[2,256,512]{2,1,0:T(8,128)(2,1)S(1)}, bf16[2,256,512]{2,1,0:T(8,128)(2,1)}, u32[]{:S(2)}, u32[]{:S(2)}) collective-permute-start(bf16[2,256,512]{2,1,0:T(8,128)(2,1)S(1)} %fusion.14), channel_id=1, source_target_pairs={{0,1},{1,0},{2,3},{3,2},{4,5},{5,4},{6,7},{7,6},{8,9},{9,8},{10,11... | collective-permute-start | bytes 1572872 | tf_op jit(solution)/shard_map/ppermute | solution.py:17
  79.7 0.0 copy-start.2
  79.8 0.0 copy-start.4
  79.8 0.0 collective-permute-done.2
  79.8 1.3 %convert_add_fusion.1 = f32[2,256,512]{2,1,0:T(8,128)S(1)} fusion(bf16[2,256,512]{2,1,0:T(8,128)(2,1)} %collective-permute-done.2, s32[]{:T(128)S(6)} %select_n.108, bf16[1,2,256,512]{3,2,0,1:T(8,128)(2,1)S(1)} %bitcast.66, bf16[1,2,256,512]{3,2,0,1:T(8,128)(2,1)S(1)} %bitcast.68), kind=kLoop, calls=%fused_computation.23 | loop fusion | flops 1048576 | bytes 2621444 | tf_op jit(solution)/shard_map/add | solution.py:90
  81.1 0.1 fusion.22
  81.1 10.9 %collective-permute-done.8 = bf16[2,256,512]{2,1,0:T(8,128)(2,1)} collective-permute-done((bf16[2,256,512]{2,1,0:T(8,128)(2,1)S(1)}, bf16[2,256,512]{2,1,0:T(8,128)(2,1)}, u32[]{:S(2)}, u32[]{:S(2)}) %collective-permute-start.8) | collective-permute-done | bytes 524320 | tf_op jit(solution)/shard_map/ppermute | solution.py:17
  92.0 0.0 copy-done.2
  92.0 0.0 copy-done.4
  92.0 1.2 %convert_add_fusion = f32[2,256,512]{2,1,0:T(8,128)S(1)} fusion(bf16[2,256,512]{2,1,0:T(8,128)(2,1)} %collective-permute-done.8, s32[]{:T(128)S(6)} %select_n.108, bf16[1,2,256,512]{3,2,0,1:T(8,128)(2,1)S(1)} %bitcast.72, bf16[1,2,256,512]{3,2,0,1:T(8,128)(2,1)S(1)} %bitcast.70), kind=kLoop, calls=%fused_computation.22 | loop fusion | flops 1048576 | bytes 2621444 | tf_op jit(solution)/shard_map/add | solution.py:90
  93.2 0.2 multiply_select_fusion.2
  93.5 1.5 %pad_maximum_fusion = f32[256,2048]{1,0:T(8,128)} fusion(f32[256,512]{1,0:T(8,128)S(1)} %get-tuple-element.6, f32[256,512]{1,0:T(8,128)S(1)} %get-tuple-element.7, f32[256,512]{1,0:T(8,128)S(1)} %get-tuple-element.5, f32[256,512]{1,0:T(8,128)S(1)} %fusion.22), kind=kLoop, calls=%fused_computation.2 | loop fusion | flops 1572864 | bytes 4194304 | tf_op jit(solution)/shard_map/concatenate | solution.py:111
  (3 shorter events, 0.0 us)
Async XLA Ops:
  2.5 7.5 %copy-start = (f32[2048,512]{1,0:T(8,128)S(1)}, f32[2048,512]{1,0:T(8,128)}, u32[]{:S(2)}) copy-start(f32[2048,512]{1,0:T(8,128)} %param.2) | copy-start | bytes 12582916
  5.4 4.6 %collective-permute-start = (f32[2,512]{1,0:T(2,128)S(1)}, f32[2,512]{1,0:T(2,128)S(1)}, u32[]{:S(2)}, u32[]{:S(2)}) collective-permute-start(f32[2,512]{1,0:T(2,128)S(1)} %pad_maximum_fusion.1), channel_id=1, source_target_pairs={{0,1},{1,0},{2,3},{3,2},{4,5},{5,4},{6,7},{7,6},{8,9},{9,8},{10,11... | collective-permute-start | bytes 12296 | tf_op jit(solution)/shard_map/ppermute | solution.py:17
  10.6 11.2 %collective-permute-start.1 = (bf16[2048,512]{1,0:T(8,128)(2,1)S(1)}, bf16[2048,512]{1,0:T(8,128)(2,1)}, u32[]{:S(2)}, u32[]{:S(2)}) collective-permute-start(bf16[2048,512]{1,0:T(8,128)(2,1)S(1)} %multiply_convert_fusion), channel_id=1, source_target_pairs={{0,2},{4,6},{2,8},{6,12},{8,10},{12,14},{10,16},{14,20},{16,18},{2... | collective-permute-start | bytes 6291464 | tf_op jit(solution)/shard_map/ppermute | solution.py:32
  13.3 10.6 %collective-permute-start.3 = (bf16[2048,512]{1,0:T(8,128)(2,1)S(1)}, bf16[2048,512]{1,0:T(8,128)(2,1)}, u32[]{:S(2)}, u32[]{:S(2)}) collective-permute-start(bf16[2048,512]{1,0:T(8,128)(2,1)S(1)} %multiply_convert_fusion), channel_id=1, source_target_pairs={{4,2},{6,4},{2,0},{12,10},{14,12},{10,8},{20,18},{22,20},{18,16},{... | collective-permute-start | bytes 6291464 | tf_op jit(solution)/shard_map/ppermute | solution.py:32
  14.6 51.1 %collective-permute-start.6 = (bf16[2048,512]{1,0:T(8,128)(2,1)S(1)}, bf16[2048,512]{1,0:T(8,128)(2,1)}, u32[]{:S(2)}, u32[]{:S(2)}) collective-permute-start(bf16[2048,512]{1,0:T(8,128)(2,1)S(1)} %multiply_convert_fusion), channel_id=1, source_target_pairs={{2,4},{0,6},{10,12},{8,14},{18,20},{16,22},{26,28},{24,30},{3,5},{... | collective-permute-start | bytes 6291464 | tf_op jit(solution)/shard_map/ppermute | solution.py:32
  21.8 46.7 %collective-permute-start.5 = (bf16[2048,512]{1,0:T(8,128)(2,1)}, bf16[2048,512]{1,0:T(8,128)(2,1)}, u32[]{:S(2)}, u32[]{:S(2)}) collective-permute-start(bf16[2048,512]{1,0:T(8,128)(2,1)} %collective-permute-done.1), channel_id=1, source_target_pairs={{4,2},{12,10},{20,18},{28,26},{5,3},{13,11},{21,19},{29,27}} | collective-permute-start | bytes 6291464 | tf_op jit(solution)/shard_map/ppermute | solution.py:32
  23.9 44.7 %collective-permute-start.4 = (bf16[2048,512]{1,0:T(8,128)(2,1)}, bf16[2048,512]{1,0:T(8,128)(2,1)}, u32[]{:S(2)}, u32[]{:S(2)}) collective-permute-start(bf16[2048,512]{1,0:T(8,128)(2,1)} %collective-permute-done.3), channel_id=1, source_target_pairs={{2,8},{10,16},{18,24},{3,9},{11,17},{19,25}} | collective-permute-start | bytes 6291464 | tf_op jit(solution)/shard_map/ppermute | solution.py:32
  30.9 48.9 %collective-permute-start.2 = (bf16[2,256,512]{2,1,0:T(8,128)(2,1)}, bf16[2,256,512]{2,1,0:T(8,128)(2,1)}, u32[]{:S(2)}, u32[]{:S(2)}) collective-permute-start(bf16[2,256,512]{2,1,0:T(8,128)(2,1)} %fusion.18), channel_id=1, source_target_pairs={{0,1},{1,0},{2,3},{3,2},{4,5},{5,4},{6,7},{7,6},{8,9},{9,8},{10,11... | collective-permute-start | bytes 1572872 | tf_op jit(solution)/shard_map/ppermute | solution.py:17
  73.0 3.6 %collective-permute-start.7 = (bf16[512,512]{1,0:T(8,128)(2,1)S(1)}, bf16[512,512]{1,0:T(8,128)(2,1)S(1)}, u32[]{:S(2)}, u32[]{:S(2)}) collective-permute-start(bf16[512,512]{1,0:T(8,128)(2,1)S(1)} %fusion.5), channel_id=1, source_target_pairs={{0,2},{2,0},{4,6},{6,4},{8,10},{10,8},{12,14},{14,12},{16,18},{18,... | collective-permute-start | bytes 1572872 | tf_op jit(solution)/shard_map/ppermute | solution.py:32
  76.5 1.0 %copy-start.3 = (bf16[512,512]{1,0:T(8,128)(2,1)}, bf16[512,512]{1,0:T(8,128)(2,1)S(1)}, u32[]{:S(2)}) copy-start(bf16[512,512]{1,0:T(8,128)(2,1)S(1)} %fusion.10) | copy-start | bytes 1572868
  76.6 0.9 copy-start.1
  77.5 14.5 %collective-permute-start.8 = (bf16[2,256,512]{2,1,0:T(8,128)(2,1)S(1)}, bf16[2,256,512]{2,1,0:T(8,128)(2,1)}, u32[]{:S(2)}, u32[]{:S(2)}) collective-permute-start(bf16[2,256,512]{2,1,0:T(8,128)(2,1)S(1)} %fusion.14), channel_id=1, source_target_pairs={{0,1},{1,0},{2,3},{3,2},{4,5},{5,4},{6,7},{7,6},{8,9},{9,8},{10,11... | collective-permute-start | bytes 1572872 | tf_op jit(solution)/shard_map/ppermute | solution.py:17
  79.7 12.3 %copy-start.2 = (bf16[512,512]{1,0:T(8,128)(2,1)S(1)}, bf16[512,512]{1,0:T(8,128)(2,1)}, u32[]{:S(2)}) copy-start(bf16[512,512]{1,0:T(8,128)(2,1)} %copy-done.1) | copy-start | bytes 1572868
  79.8 12.2 %copy-start.4 = (bf16[512,512]{1,0:T(8,128)(2,1)S(1)}, bf16[512,512]{1,0:T(8,128)(2,1)}, u32[]{:S(2)}) copy-start(bf16[512,512]{1,0:T(8,128)(2,1)} %copy-done.3) | copy-start | bytes 1572868

commit v8 on v7

--- a/solution.py
+++ b/solution.py
@@ -39,12 +39,11 @@
     fast_b = send(standard, pairs_of((2, 1), (3, 2), (1, 0)))
     relay = send(fast_b, pairs_of((1, 4))) + send(fast_a, pairs_of((2, 1)))
     lhs = jnp.where(place % 2 == 0, fast_b, fast_a)
-    rhs = jnp.where(place < 2, relay, cross)
+    rhs = relay + cross
     handed = send(tile_term(lhs, rhs).astype(jnp.bfloat16), pairs_of((0, 1), (1, 0), (2, 3), (3, 2)))
     with_a = tile_term(standard, fast_a).astype(jnp.bfloat16)
-    with_relay = tile_term(standard, relay).astype(jnp.bfloat16)
-    with_cross = tile_term(standard, cross).astype(jnp.bfloat16)
-    return with_a, jnp.where(place < 2, with_relay, with_cross), handed
+    own_late = tile_term(standard, rhs).astype(jnp.bfloat16)
+    return with_a, own_late, handed
 
 
 def tile_term(standard, neighbour):
@@ -94,7 +93,7 @@
         place = lax.axis_index("snp") % 4
         with_a, own_late, handed = relayed(standard, count, place)
         early = exchanged(jnp.stack([first, with_a]))
-        late = exchanged(jnp.stack([own_late, handed]))
+        late = [exchanged(own_late), exchanged(handed)]
         totals = [
             early[0],
             jnp.where(place == 0, late[1], jnp.where(place == 2, late[0], early[1])),

time: 95.3 us -> 92.7 us (0.973)
  other arithmetic: 11.2 us -> 8.07 us
  starting transfers between devices: 21.4 us -> 23.8 us
  matrix products: 14.9 us -> 13.3 us
    add x2 -> x1, other arithmetic: 2.48 us -> 0.16 us  [exchanged(): total = total + rotated(outgoing, 'smp', s).astype(jnp.float32)]
    ppermute x6, starting transfers between devices: 15.3 us -> 17.1 us  [send(): return lax.ppermute(value, 'snp', pairs)]
    dot_general x5 -> x4, matrix products: 14.9 us -> 13.3 us  [tile_term(): lax.dot_general(standard, neighbour, (((0,), (0,)), ((), ())), preferred_...]
    ppermute x3 -> x4, starting transfers between devices: 6.12 us -> 6.77 us  [rotated(): lax.ppermute(value, axis, [(source, (source + steps) % count) for source...]
    ppermute x3 -> x4, waiting for transfers between devices: 12.5 us -> 13.1 us  [rotated(): lax.ppermute(value, axis, [(source, (source + steps) % count) for source...]
  transfers between devices with their start and end apart: 9 -> 10, of which waited for: 3 -> 4; matrix products, arithmetic and copies ran while one was open for 18% -> 15% of each run, Pallas kernels for 0% -> 0%
where the time goes in v8:
time: 92.7 us; the launch traced here: 92.5 us
  waiting for transfers between devices  46.4 us (50%)
  starting transfers between devices  23.8 us (26%)
  matrix products  13.3 us (14%)
  other arithmetic  8.07 us (9%)
    ppermute x6, waiting for transfers between devices, send(): return lax.ppermute(value, 'snp', pairs)  33.3 us
    ppermute x6, starting transfers between devices, send(): return lax.ppermute(value, 'snp', pairs)  17.1 us
    dot_general x4, matrix products, tile_term(): lax.dot_general(standard, neighbour, (((0,), (0,)), ((), ())), preferred_...  13.3 us
    ppermute x4, waiting for transfers between devices, rotated(): lax.ppermute(value, axis, [(source, (source + steps) % count) for source...  13.1 us
    ppermute x4, starting transfers between devices, rotated(): lax.ppermute(value, axis, [(source, (source + steps) % count) for source...  6.77 us
    reduce_sum x1, other arithmetic, local(): part_m2 = jnp.sum(deviation * deviation, axis=0)  2.86 us
    reduce_sum x1, other arithmetic, local(): part_mean = jnp.sum(dosage, axis=0) / rows  2.52 us
  transfers between devices with their start and end apart: 10, of which 4 were waited for; matrix products, arithmetic and copies ran while one was open for 15% of the time, Pallas kernels for 0%

profile of v8, /device:TPU:0, one launch (start us, length us, event | category | flops | bytes accessed | tf_op | source)
XLA Modules:
  0.0 92.5 jit_solution(9988185361296252072)
XLA Ops:
  0.0 2.5 %reduce_sum.18 = f32[512]{0:T(512)S(1)} reduce(f32[2048,512]{1,0:T(8,128)} %param.2, f32[]{:T(128)} %constant.70.clone.1), dimensions={0}, to_apply=%region_0.0 | reduce | flops 1048064 | bytes 4196356 | tf_op jit(solution)/shard_map/reduce_sum | solution.py:61
  2.5 0.0 copy-start
  2.5 2.9 %multiply_reduce_fusion = f32[512]{0:T(512)S(1)} fusion(f32[2048,512]{1,0:T(8,128)} %param.2, f32[512]{0:T(512)S(1)} %broadcast_multiply_fusion), kind=kLoop, calls=%fused_computation.1 | loop fusion | flops 3145216 | bytes 4198400 | tf_op jit(solution)/shard_map/reduce_sum | solution.py:63
  5.4 3.0 %collective-permute-start = (f32[2,512]{1,0:T(2,128)S(1)}, f32[2,512]{1,0:T(2,128)S(1)}, u32[]{:S(2)}, u32[]{:S(2)}) collective-permute-start(f32[2,512]{1,0:T(2,128)S(1)} %pad_maximum_fusion.1), channel_id=1, source_target_pairs={{0,1},{1,0},{2,3},{3,2},{4,5},{5,4},{6,7},{7,6},{8,9},{9,8},{10,11... | collective-permute-start | bytes 12296 | tf_op jit(solution)/shard_map/ppermute | solution.py:17
  8.4 1.6 %collective-permute-done = f32[2,512]{1,0:T(2,128)S(1)} collective-permute-done((f32[2,512]{1,0:T(2,128)S(1)}, f32[2,512]{1,0:T(2,128)S(1)}, u32[]{:S(2)}, u32[]{:S(2)}) %collective-permute-start) | collective-permute-done | bytes 4128 | tf_op jit(solution)/shard_map/ppermute | solution.py:17
  10.0 0.0 copy-done
  10.0 0.6 multiply_convert_fusion
  10.6 2.6 %collective-permute-start.1 = (bf16[2048,512]{1,0:T(8,128)(2,1)S(1)}, bf16[2048,512]{1,0:T(8,128)(2,1)}, u32[]{:S(2)}, u32[]{:S(2)}) collective-permute-start(bf16[2048,512]{1,0:T(8,128)(2,1)S(1)} %multiply_convert_fusion), channel_id=1, source_target_pairs={{0,2},{4,6},{2,8},{6,12},{8,10},{12,14},{10,16},{14,20},{16,18},{2... | collective-permute-start | bytes 6291464 | tf_op jit(solution)/shard_map/ppermute | solution.py:32
  13.3 1.3 %collective-permute-start.3 = (bf16[2048,512]{1,0:T(8,128)(2,1)S(1)}, bf16[2048,512]{1,0:T(8,128)(2,1)}, u32[]{:S(2)}, u32[]{:S(2)}) collective-permute-start(bf16[2048,512]{1,0:T(8,128)(2,1)S(1)} %multiply_convert_fusion), channel_id=1, source_target_pairs={{4,2},{6,4},{2,0},{12,10},{14,12},{10,8},{20,18},{22,20},{18,16},{... | collective-permute-start | bytes 6291464 | tf_op jit(solution)/shard_map/ppermute | solution.py:32
  14.6 7.3 %collective-permute-start.6 = (bf16[2048,512]{1,0:T(8,128)(2,1)S(1)}, bf16[2048,512]{1,0:T(8,128)(2,1)}, u32[]{:S(2)}, u32[]{:S(2)}) collective-permute-start(bf16[2048,512]{1,0:T(8,128)(2,1)S(1)} %multiply_convert_fusion), channel_id=1, source_target_pairs={{2,4},{0,6},{10,12},{8,14},{18,20},{16,22},{26,28},{24,30},{3,5},{... | collective-permute-start | bytes 6291464 | tf_op jit(solution)/shard_map/ppermute | solution.py:32
  21.8 0.0 collective-permute-done.1
  21.8 2.0 %collective-permute-start.5 = (bf16[2048,512]{1,0:T(8,128)(2,1)}, bf16[2048,512]{1,0:T(8,128)(2,1)}, u32[]{:S(2)}, u32[]{:S(2)}) collective-permute-start(bf16[2048,512]{1,0:T(8,128)(2,1)} %collective-permute-done.1), channel_id=1, source_target_pairs={{4,2},{12,10},{20,18},{28,26},{5,3},{13,11},{21,19},{29,27}} | collective-permute-start | bytes 6291464 | tf_op jit(solution)/shard_map/ppermute | solution.py:32
  23.9 0.0 collective-permute-done.3
  23.9 2.0 %collective-permute-start.4 = (bf16[2048,512]{1,0:T(8,128)(2,1)}, bf16[2048,512]{1,0:T(8,128)(2,1)}, u32[]{:S(2)}, u32[]{:S(2)}) collective-permute-start(bf16[2048,512]{1,0:T(8,128)(2,1)} %collective-permute-done.3), channel_id=1, source_target_pairs={{2,8},{10,16},{18,24},{3,9},{11,17},{19,25}} | collective-permute-start | bytes 6291464 | tf_op jit(solution)/shard_map/ppermute | solution.py:32
  26.5 1.3 %convolution_convert_fusion.2 = bf16[512,512]{1,0:T(8,128)(2,1)S(1)} fusion(bf16[2048,512]{1,0:T(8,128)(2,1)S(1)} %multiply_convert_fusion), kind=kOutput, calls=%fused_computation.10 | convolution fusion | flops 1074003968 | bytes 2621440 | tf_op jit(solution)/shard_map/dot_general | solution.py:50
  27.8 2.9 %convolution_convert_fusion.1 = bf16[512,512]{1,0:T(8,128)(2,1)S(1)} fusion(bf16[2048,512]{1,0:T(8,128)(2,1)S(1)} %multiply_convert_fusion, bf16[2048,512]{1,0:T(8,128)(2,1)} %collective-permute-done.1), kind=kOutput, calls=%fused_computation.9 | convolution fusion | flops 1074003968 | bytes 4718592 | tf_op jit(solution)/shard_map/dot_general | solution.py:50
  30.7 0.1 fusion.7
  30.8 1.6 %collective-permute-start.2 = (bf16[2,256,512]{2,1,0:T(8,128)(2,1)S(1)}, bf16[2,256,512]{2,1,0:T(8,128)(2,1)S(1)}, u32[]{:S(2)}, u32[]{:S(2)}) collective-permute-start(bf16[2,256,512]{2,1,0:T(8,128)(2,1)S(1)} %fusion.7), channel_id=1, source_target_pairs={{0,1},{1,0},{2,3},{3,2},{4,5},{5,4},{6,7},{7,6},{8,9},{9,8},{10,11... | collective-permute-start | bytes 1572872 | tf_op jit(solution)/shard_map/ppermute | solution.py:17
  32.3 33.3 %collective-permute-done.6 = bf16[2048,512]{1,0:T(8,128)(2,1)} collective-permute-done((bf16[2048,512]{1,0:T(8,128)(2,1)S(1)}, bf16[2048,512]{1,0:T(8,128)(2,1)}, u32[]{:S(2)}, u32[]{:S(2)}) %collective-permute-start.6) | collective-permute-done | bytes 2097184 | tf_op jit(solution)/shard_map/ppermute | solution.py:32
  65.6 0.0 collective-permute-done.5
  65.6 0.0 collective-permute-done.4
  65.6 5.1 %fusion.3 = bf16[512,512]{1,0:T(8,128)(2,1)S(1)} fusion(bf16[2048,512]{1,0:T(8,128)(2,1)} %collective-permute-done.3, bf16[2048,512]{1,0:T(8,128)(2,1)} %collective-permute-done.1, pred[]{:T(512)S(6)} %eq.22, bf16[2048,512]{1,0:T(8,128)(2,1)} %collective-permute-done.6, bf16[2048,512]{1,0:T(8,128)(2,1)} %collective-permute-done.4, ...), kind=kOutput, calls=%fused_computation.7 | convolution fusion | flops 1077149696 | bytes 11010049 | tf_op jit(solution)/shard_map/dot_general | solution.py:50
  70.7 1.9 %collective-permute-start.7 = (bf16[512,512]{1,0:T(8,128)(2,1)S(1)}, bf16[512,512]{1,0:T(8,128)(2,1)S(1)}, u32[]{:S(2)}, u32[]{:S(2)}) collective-permute-start(bf16[512,512]{1,0:T(8,128)(2,1)S(1)} %fusion.3), channel_id=1, source_target_pairs={{0,2},{2,0},{4,6},{6,4},{8,10},{10,8},{12,14},{14,12},{16,18},{18,... | collective-permute-start | bytes 1572872 | tf_op jit(solution)/shard_map/ppermute | solution.py:32
  72.6 4.1 %convolution_convert_fusion = bf16[512,512]{1,0:T(8,128)(2,1)S(1)} fusion(bf16[2048,512]{1,0:T(8,128)(2,1)S(1)} %multiply_convert_fusion, bf16[2048,512]{1,0:T(8,128)(2,1)} %collective-permute-done.6, bf16[2048,512]{1,0:T(8,128)(2,1)} %collective-permute-done.4, bf16[2048,512]{1,0:T(8,128)(2,1)} %collective-permute-done.5), kind=kOutput, calls=%fused_computation.8 | convolution fusion | flops 1076101120 | bytes 8912896 | tf_op jit(solution)/shard_map/dot_general | solution.py:50
  76.8 1.6 %collective-permute-start.9 = (bf16[256,512]{1,0:T(8,128)(2,1)S(1)}, bf16[256,512]{1,0:T(8,128)(2,1)S(1)}, u32[]{:S(2)}, u32[]{:S(2)}) collective-permute-start(bf16[256,512]{1,0:T(8,128)(2,1)S(1)} %dynamic-slice_bitcast_fusion), channel_id=1, source_target_pairs={{0,1},{1,0},{2,3},{3,2},{4,5},{5,4},{6,7},{7,6},{8,9},{9,8},{10,11... | collective-permute-start | bytes 786440 | tf_op jit(solution)/shard_map/ppermute | solution.py:17
  78.4 0.0 collective-permute-done.7
  78.4 0.5 collective-permute-start.8
  78.9 0.0 collective-permute-done.2
  78.9 0.2 convert_add_fusion
  79.1 0.1 fusion.11
  79.2 6.8 %collective-permute-done.9 = bf16[256,512]{1,0:T(8,128)(2,1)S(1)} collective-permute-done((bf16[256,512]{1,0:T(8,128)(2,1)S(1)}, bf16[256,512]{1,0:T(8,128)(2,1)S(1)}, u32[]{:S(2)}, u32[]{:S(2)}) %collective-permute-start.9) | collective-permute-done | bytes 262176 | tf_op jit(solution)/shard_map/ppermute | solution.py:17
  86.0 4.7 %collective-permute-done.8 = bf16[256,512]{1,0:T(8,128)(2,1)S(1)} collective-permute-done((bf16[256,512]{1,0:T(8,128)(2,1)S(1)}, bf16[256,512]{1,0:T(8,128)(2,1)S(1)}, u32[]{:S(2)}, u32[]{:S(2)}) %collective-permute-start.8) | collective-permute-done | bytes 262176 | tf_op jit(solution)/shard_map/ppermute | solution.py:17
  90.7 0.3 multiply_select_fusion.2
  91.0 1.5 %pad_maximum_fusion = f32[256,2048]{1,0:T(8,128)} fusion(f32[256,512]{1,0:T(8,128)S(1)} %get-tuple-element.6, f32[256,512]{1,0:T(8,128)S(1)} %get-tuple-element.7, f32[256,512]{1,0:T(8,128)S(1)} %get-tuple-element.5, f32[256,512]{1,0:T(8,128)S(1)} %fusion.11), kind=kLoop, calls=%fused_computation.2 | loop fusion | flops 1572864 | bytes 4194304 | tf_op jit(solution)/shard_map/concatenate | solution.py:110
  (5 shorter events, 0.1 us)
Async XLA Ops:
  2.5 7.5 %copy-start = (f32[2048,512]{1,0:T(8,128)S(1)}, f32[2048,512]{1,0:T(8,128)}, u32[]{:S(2)}) copy-start(f32[2048,512]{1,0:T(8,128)} %param.2) | copy-start | bytes 12582916
  5.4 4.6 %collective-permute-start = (f32[2,512]{1,0:T(2,128)S(1)}, f32[2,512]{1,0:T(2,128)S(1)}, u32[]{:S(2)}, u32[]{:S(2)}) collective-permute-start(f32[2,512]{1,0:T(2,128)S(1)} %pad_maximum_fusion.1), channel_id=1, source_target_pairs={{0,1},{1,0},{2,3},{3,2},{4,5},{5,4},{6,7},{7,6},{8,9},{9,8},{10,11... | collective-permute-start | bytes 12296 | tf_op jit(solution)/shard_map/ppermute | solution.py:17
  10.6 11.2 %collective-permute-start.1 = (bf16[2048,512]{1,0:T(8,128)(2,1)S(1)}, bf16[2048,512]{1,0:T(8,128)(2,1)}, u32[]{:S(2)}, u32[]{:S(2)}) collective-permute-start(bf16[2048,512]{1,0:T(8,128)(2,1)S(1)} %multiply_convert_fusion), channel_id=1, source_target_pairs={{0,2},{4,6},{2,8},{6,12},{8,10},{12,14},{10,16},{14,20},{16,18},{2... | collective-permute-start | bytes 6291464 | tf_op jit(solution)/shard_map/ppermute | solution.py:32
  13.3 10.6 %collective-permute-start.3 = (bf16[2048,512]{1,0:T(8,128)(2,1)S(1)}, bf16[2048,512]{1,0:T(8,128)(2,1)}, u32[]{:S(2)}, u32[]{:S(2)}) collective-permute-start(bf16[2048,512]{1,0:T(8,128)(2,1)S(1)} %multiply_convert_fusion), channel_id=1, source_target_pairs={{4,2},{6,4},{2,0},{12,10},{14,12},{10,8},{20,18},{22,20},{18,16},{... | collective-permute-start | bytes 6291464 | tf_op jit(solution)/shard_map/ppermute | solution.py:32
  14.6 51.1 %collective-permute-start.6 = (bf16[2048,512]{1,0:T(8,128)(2,1)S(1)}, bf16[2048,512]{1,0:T(8,128)(2,1)}, u32[]{:S(2)}, u32[]{:S(2)}) collective-permute-start(bf16[2048,512]{1,0:T(8,128)(2,1)S(1)} %multiply_convert_fusion), channel_id=1, source_target_pairs={{2,4},{0,6},{10,12},{8,14},{18,20},{16,22},{26,28},{24,30},{3,5},{... | collective-permute-start | bytes 6291464 | tf_op jit(solution)/shard_map/ppermute | solution.py:32
  21.8 43.8 %collective-permute-start.5 = (bf16[2048,512]{1,0:T(8,128)(2,1)}, bf16[2048,512]{1,0:T(8,128)(2,1)}, u32[]{:S(2)}, u32[]{:S(2)}) collective-permute-start(bf16[2048,512]{1,0:T(8,128)(2,1)} %collective-permute-done.1), channel_id=1, source_target_pairs={{4,2},{12,10},{20,18},{28,26},{5,3},{13,11},{21,19},{29,27}} | collective-permute-start | bytes 6291464 | tf_op jit(solution)/shard_map/ppermute | solution.py:32
  23.9 41.8 %collective-permute-start.4 = (bf16[2048,512]{1,0:T(8,128)(2,1)}, bf16[2048,512]{1,0:T(8,128)(2,1)}, u32[]{:S(2)}, u32[]{:S(2)}) collective-permute-start(bf16[2048,512]{1,0:T(8,128)(2,1)} %collective-permute-done.3), channel_id=1, source_target_pairs={{2,8},{10,16},{18,24},{3,9},{11,17},{19,25}} | collective-permute-start | bytes 6291464 | tf_op jit(solution)/shard_map/ppermute | solution.py:32
  30.8 48.2 %collective-permute-start.2 = (bf16[2,256,512]{2,1,0:T(8,128)(2,1)S(1)}, bf16[2,256,512]{2,1,0:T(8,128)(2,1)S(1)}, u32[]{:S(2)}, u32[]{:S(2)}) collective-permute-start(bf16[2,256,512]{2,1,0:T(8,128)(2,1)S(1)} %fusion.7), channel_id=1, source_target_pairs={{0,1},{1,0},{2,3},{3,2},{4,5},{5,4},{6,7},{7,6},{8,9},{9,8},{10,11... | collective-permute-start | bytes 1572872 | tf_op jit(solution)/shard_map/ppermute | solution.py:17
  70.7 7.7 %collective-permute-start.7 = (bf16[512,512]{1,0:T(8,128)(2,1)S(1)}, bf16[512,512]{1,0:T(8,128)(2,1)S(1)}, u32[]{:S(2)}, u32[]{:S(2)}) collective-permute-start(bf16[512,512]{1,0:T(8,128)(2,1)S(1)} %fusion.3), channel_id=1, source_target_pairs={{0,2},{2,0},{4,6},{6,4},{8,10},{10,8},{12,14},{14,12},{16,18},{18,... | collective-permute-start | bytes 1572872 | tf_op jit(solution)/shard_map/ppermute | solution.py:32
  76.8 9.2 %collective-permute-start.9 = (bf16[256,512]{1,0:T(8,128)(2,1)S(1)}, bf16[256,512]{1,0:T(8,128)(2,1)S(1)}, u32[]{:S(2)}, u32[]{:S(2)}) collective-permute-start(bf16[256,512]{1,0:T(8,128)(2,1)S(1)} %dynamic-slice_bitcast_fusion), channel_id=1, source_target_pairs={{0,1},{1,0},{2,3},{3,2},{4,5},{5,4},{6,7},{7,6},{8,9},{9,8},{10,11... | collective-permute-start | bytes 786440 | tf_op jit(solution)/shard_map/ppermute | solution.py:17
  78.4 12.3 %collective-permute-start.8 = (bf16[256,512]{1,0:T(8,128)(2,1)S(1)}, bf16[256,512]{1,0:T(8,128)(2,1)S(1)}, u32[]{:S(2)}, u32[]{:S(2)}) collective-permute-start(bf16[256,512]{1,0:T(8,128)(2,1)S(1)} %dynamic-slice_bitcast_fusion.1), channel_id=1, source_target_pairs={{0,1},{1,0},{2,3},{3,2},{4,5},{5,4},{6,7},{7,6},{8,9},{9,8},{10,11... | collective-permute-start | bytes 786440 | tf_op jit(solution)/shard_map/ppermute | solution.py:17

commit v9 on v8

--- a/solution.py
+++ b/solution.py
@@ -38,11 +38,11 @@
     fast_a = send(standard, pairs_of((0, 1), (2, 3), (1, 4), (3, 6)))
     fast_b = send(standard, pairs_of((2, 1), (3, 2), (1, 0)))
     relay = send(fast_b, pairs_of((1, 4))) + send(fast_a, pairs_of((2, 1)))
-    lhs = jnp.where(place % 2 == 0, fast_b, fast_a)
-    rhs = relay + cross
+    lhs = lax.optimization_barrier(jnp.where(place % 2 == 0, fast_b, fast_a))
+    rhs = lax.optimization_barrier(relay + cross)
     handed = send(tile_term(lhs, rhs).astype(jnp.bfloat16), pairs_of((0, 1), (1, 0), (2, 3), (3, 2)))
+    own_late = tile_term(standard, rhs).astype(jnp.bfloat16)
     with_a = tile_term(standard, fast_a).astype(jnp.bfloat16)
-    own_late = tile_term(standard, rhs).astype(jnp.bfloat16)
     return with_a, own_late, handed
 
 

time: 92.7 us -> 90.8 us (0.980)
  matrix products: 13.3 us -> 6.68 us
  other arithmetic: 8.07 us -> 13.1 us
  waiting for transfers between devices: 46.4 us -> 44.3 us
  starting transfers between devices: 23.8 us -> 25.7 us
    dot_general x4, matrix products: 13.3 us -> 6.68 us  [tile_term(): lax.dot_general(standard, neighbour, (((0,), (0,)), ((), ())), preferred_...]
    add x0 -> x1, other arithmetic: none -> 3.16 us  [relayed(): rhs = lax.optimization_barrier(relay + cross)]
    ppermute x6, waiting for transfers between devices: 33.3 us -> 31.2 us  [send(): return lax.ppermute(value, 'snp', pairs)]
    ppermute x6, starting transfers between devices: 17.1 us -> 18.9 us  [send(): return lax.ppermute(value, 'snp', pairs)]
    select_n x0 -> x1, other arithmetic: none -> 1.81 us  [relayed(): lhs = lax.optimization_barrier(jnp.where(place % 2 == 0, fast_b, fast_a))]
  transfers between devices with their start and end apart: 10 -> 10, of which waited for: 4 -> 4; matrix products, arithmetic and copies ran while one was open for 15% -> 13% of each run, Pallas kernels for 0% -> 0%
where the time goes in v9:
time: 90.8 us; the launch traced here: 90.5 us
  waiting for transfers between devices  44.3 us (49%)
  starting transfers between devices  25.7 us (28%)
  other arithmetic  13.1 us (14%)
  matrix products  6.68 us (7%)
    ppermute x6, waiting for transfers between devices, send(): return lax.ppermute(value, 'snp', pairs)  31.2 us
    ppermute x6, starting transfers between devices, send(): return lax.ppermute(value, 'snp', pairs)  18.9 us
    ppermute x4, waiting for transfers between devices, rotated(): lax.ppermute(value, axis, [(source, (source + steps) % count) for source...  13.1 us
    ppermute x4, starting transfers between devices, rotated(): lax.ppermute(value, axis, [(source, (source + steps) % count) for source...  6.77 us
    dot_general x4, matrix products, tile_term(): lax.dot_general(standard, neighbour, (((0,), (0,)), ((), ())), preferred_...  6.68 us
    add x1, other arithmetic, relayed(): rhs = lax.optimization_barrier(relay + cross)  3.16 us
    reduce_sum x1, other arithmetic, local(): part_m2 = jnp.sum(deviation * deviation, axis=0)  2.85 us
    reduce_sum x1, other arithmetic, local(): part_mean = jnp.sum(dosage, axis=0) / rows  2.52 us
  transfers between devices with their start and end apart: 10, of which 4 were waited for; matrix products, arithmetic and copies ran while one was open for 13% of the time, Pallas kernels for 0%

profile of v9, /device:TPU:0, one launch (start us, length us, event | category | flops | bytes accessed | tf_op | source)
XLA Modules:
  0.0 90.5 jit_solution(5737980201317331260)
XLA Ops:
  0.0 2.5 %reduce_sum.18 = f32[512]{0:T(512)S(1)} reduce(f32[2048,512]{1,0:T(8,128)} %param.2, f32[]{:T(128)} %constant.70.clone.1), dimensions={0}, to_apply=%region_0.0 | reduce | flops 1048064 | bytes 4196356 | tf_op jit(solution)/shard_map/reduce_sum | solution.py:61
  2.5 0.0 copy-start
  2.5 2.9 %multiply_reduce_fusion = f32[512]{0:T(512)S(1)} fusion(f32[2048,512]{1,0:T(8,128)} %param.2, f32[512]{0:T(512)S(1)} %broadcast_multiply_fusion), kind=kLoop, calls=%fused_computation.1 | loop fusion | flops 3145216 | bytes 4198400 | tf_op jit(solution)/shard_map/reduce_sum | solution.py:63
  5.4 3.0 %collective-permute-start = (f32[2,512]{1,0:T(2,128)S(1)}, f32[2,512]{1,0:T(2,128)S(1)}, u32[]{:S(2)}, u32[]{:S(2)}) collective-permute-start(f32[2,512]{1,0:T(2,128)S(1)} %pad_maximum_fusion.1), channel_id=1, source_target_pairs={{0,1},{1,0},{2,3},{3,2},{4,5},{5,4},{6,7},{7,6},{8,9},{9,8},{10,11... | collective-permute-start | bytes 12296 | tf_op jit(solution)/shard_map/ppermute | solution.py:17
  8.4 1.6 %collective-permute-done = f32[2,512]{1,0:T(2,128)S(1)} collective-permute-done((f32[2,512]{1,0:T(2,128)S(1)}, f32[2,512]{1,0:T(2,128)S(1)}, u32[]{:S(2)}, u32[]{:S(2)}) %collective-permute-start) | collective-permute-done | bytes 4128 | tf_op jit(solution)/shard_map/ppermute | solution.py:17
  10.0 0.0 copy-done
  10.0 0.6 multiply_convert_fusion
  10.6 1.3 %collective-permute-start.3 = (bf16[2048,512]{1,0:T(8,128)(2,1)S(1)}, bf16[2048,512]{1,0:T(8,128)(2,1)}, u32[]{:S(2)}, u32[]{:S(2)}) collective-permute-start(bf16[2048,512]{1,0:T(8,128)(2,1)S(1)} %multiply_convert_fusion), channel_id=1, source_target_pairs={{4,2},{6,4},{2,0},{12,10},{14,12},{10,8},{20,18},{22,20},{18,16},{... | collective-permute-start | bytes 6291464 | tf_op jit(solution)/shard_map/ppermute | solution.py:32
  11.9 4.4 %collective-permute-start.1 = (bf16[2048,512]{1,0:T(8,128)(2,1)S(1)}, bf16[2048,512]{1,0:T(8,128)(2,1)}, u32[]{:S(2)}, u32[]{:S(2)}) collective-permute-start(bf16[2048,512]{1,0:T(8,128)(2,1)S(1)} %multiply_convert_fusion), channel_id=1, source_target_pairs={{0,2},{4,6},{2,8},{6,12},{8,10},{12,14},{10,16},{14,20},{16,18},{2... | collective-permute-start | bytes 6291464 | tf_op jit(solution)/shard_map/ppermute | solution.py:32
  16.3 4.8 %collective-permute-start.6 = (bf16[2048,512]{1,0:T(8,128)(2,1)S(1)}, bf16[2048,512]{1,0:T(8,128)(2,1)}, u32[]{:S(2)}, u32[]{:S(2)}) collective-permute-start(bf16[2048,512]{1,0:T(8,128)(2,1)S(1)} %multiply_convert_fusion), channel_id=1, source_target_pairs={{2,4},{0,6},{10,12},{8,14},{18,20},{16,22},{26,28},{24,30},{3,5},{... | collective-permute-start | bytes 6291464 | tf_op jit(solution)/shard_map/ppermute | solution.py:32
  21.1 0.0 collective-permute-done.3
  21.1 2.0 %collective-permute-start.4 = (bf16[2048,512]{1,0:T(8,128)(2,1)}, bf16[2048,512]{1,0:T(8,128)(2,1)}, u32[]{:S(2)}, u32[]{:S(2)}) collective-permute-start(bf16[2048,512]{1,0:T(8,128)(2,1)} %collective-permute-done.3), channel_id=1, source_target_pairs={{2,8},{10,16},{18,24},{3,9},{11,17},{19,25}} | collective-permute-start | bytes 6291464 | tf_op jit(solution)/shard_map/ppermute | solution.py:32
  23.1 0.0 collective-permute-done.1
  23.1 2.0 %collective-permute-start.5 = (bf16[2048,512]{1,0:T(8,128)(2,1)}, bf16[2048,512]{1,0:T(8,128)(2,1)}, u32[]{:S(2)}, u32[]{:S(2)}) collective-permute-start(bf16[2048,512]{1,0:T(8,128)(2,1)} %collective-permute-done.1), channel_id=1, source_target_pairs={{4,2},{12,10},{20,18},{28,26},{5,3},{13,11},{21,19},{29,27}} | collective-permute-start | bytes 6291464 | tf_op jit(solution)/shard_map/ppermute | solution.py:32
  25.8 1.3 %convolution_convert_fusion.3 = bf16[512,512]{1,0:T(8,128)(2,1)S(1)} fusion(bf16[2048,512]{1,0:T(8,128)(2,1)S(1)} %multiply_convert_fusion), kind=kOutput, calls=%fused_computation.8 | convolution fusion | flops 1074003968 | bytes 2621440 | tf_op jit(solution)/shard_map/dot_general | solution.py:50
  27.1 2.9 %convolution_convert_fusion.2 = bf16[512,512]{1,0:T(8,128)(2,1)S(1)} fusion(bf16[2048,512]{1,0:T(8,128)(2,1)S(1)} %multiply_convert_fusion, bf16[2048,512]{1,0:T(8,128)(2,1)} %collective-permute-done.1), kind=kOutput, calls=%fused_computation.7 | convolution fusion | flops 1074003968 | bytes 4718592 | tf_op jit(solution)/shard_map/dot_general | solution.py:50
  30.0 0.1 fusion.1
  30.0 1.6 %collective-permute-start.2 = (bf16[2,256,512]{2,1,0:T(8,128)(2,1)S(1)}, bf16[2,256,512]{2,1,0:T(8,128)(2,1)S(1)}, u32[]{:S(2)}, u32[]{:S(2)}) collective-permute-start(bf16[2,256,512]{2,1,0:T(8,128)(2,1)S(1)} %fusion.1), channel_id=1, source_target_pairs={{0,1},{1,0},{2,3},{3,2},{4,5},{5,4},{6,7},{7,6},{8,9},{9,8},{10,11... | collective-permute-start | bytes 1572872 | tf_op jit(solution)/shard_map/ppermute | solution.py:17
  31.6 1.8 %broadcast_select_fusion = bf16[2048,512]{1,0:T(8,128)(2,1)S(1)} fusion(bf16[2048,512]{1,0:T(8,128)(2,1)} %collective-permute-done.3, bf16[2048,512]{1,0:T(8,128)(2,1)} %collective-permute-done.1, pred[]{:T(512)S(6)} %eq.22), kind=kLoop, calls=%fused_computation.4 | loop fusion | flops 1048576 | bytes 6291457 | tf_op jit(solution)/shard_map/jit(_where)/select_n | solution.py:41
  33.4 31.2 %collective-permute-done.6 = bf16[2048,512]{1,0:T(8,128)(2,1)} collective-permute-done((bf16[2048,512]{1,0:T(8,128)(2,1)S(1)}, bf16[2048,512]{1,0:T(8,128)(2,1)}, u32[]{:S(2)}, u32[]{:S(2)}) %collective-permute-start.6) | collective-permute-done | bytes 2097184 | tf_op jit(solution)/shard_map/ppermute | solution.py:32
  64.6 0.0 collective-permute-done.4
  64.6 0.0 collective-permute-done.5
  64.6 3.2 %add_add_fusion = bf16[2048,512]{1,0:T(8,128)(2,1)S(1)} fusion(bf16[2048,512]{1,0:T(8,128)(2,1)} %collective-permute-done.6, bf16[2048,512]{1,0:T(8,128)(2,1)} %collective-permute-done.4, bf16[2048,512]{1,0:T(8,128)(2,1)} %collective-permute-done.5), kind=kLoop, calls=%fused_computation.3 | loop fusion | flops 2097152 | bytes 8388608 | tf_op jit(solution)/shard_map/add | solution.py:42
  67.8 1.3 %convolution_convert_fusion.1 = bf16[512,512]{1,0:T(8,128)(2,1)S(1)} fusion(bf16[2048,512]{1,0:T(8,128)(2,1)S(1)} %broadcast_select_fusion, bf16[2048,512]{1,0:T(8,128)(2,1)S(1)} %add_add_fusion), kind=kOutput, calls=%fused_computation.6 | convolution fusion | flops 1074003968 | bytes 4718592 | tf_op jit(solution)/shard_map/dot_general | solution.py:50
  69.1 4.4 %collective-permute-start.7 = (bf16[512,512]{1,0:T(8,128)(2,1)S(1)}, bf16[512,512]{1,0:T(8,128)(2,1)S(1)}, u32[]{:S(2)}, u32[]{:S(2)}) collective-permute-start(bf16[512,512]{1,0:T(8,128)(2,1)S(1)} %convolution_convert_fusion.1), channel_id=1, source_target_pairs={{0,2},{2,0},{4,6},{6,4},{8,10},{10,8},{12,14},{14,12},{16,18},{18,... | collective-permute-start | bytes 1572872 | tf_op jit(solution)/shard_map/ppermute | solution.py:32
  73.5 1.3 %convolution_convert_fusion = bf16[512,512]{1,0:T(8,128)(2,1)S(1)} fusion(bf16[2048,512]{1,0:T(8,128)(2,1)S(1)} %multiply_convert_fusion, bf16[2048,512]{1,0:T(8,128)(2,1)S(1)} %add_add_fusion), kind=kOutput, calls=%fused_computation.5 | convolution fusion | flops 1074003968 | bytes 4718592 | tf_op jit(solution)/shard_map/dot_general | solution.py:50
  74.8 1.6 %collective-permute-start.9 = (bf16[256,512]{1,0:T(8,128)(2,1)S(1)}, bf16[256,512]{1,0:T(8,128)(2,1)S(1)}, u32[]{:S(2)}, u32[]{:S(2)}) collective-permute-start(bf16[256,512]{1,0:T(8,128)(2,1)S(1)} %dynamic-slice_bitcast_fusion), channel_id=1, source_target_pairs={{0,1},{1,0},{2,3},{3,2},{4,5},{5,4},{6,7},{7,6},{8,9},{9,8},{10,11... | collective-permute-start | bytes 786440 | tf_op jit(solution)/shard_map/ppermute | solution.py:17
  76.4 0.0 collective-permute-done.7
  76.4 0.6 collective-permute-start.8
  77.0 0.0 collective-permute-done.2
  77.0 0.2 convert_add_fusion
  77.2 0.1 fusion.5
  77.2 6.8 %collective-permute-done.9 = bf16[256,512]{1,0:T(8,128)(2,1)S(1)} collective-permute-done((bf16[256,512]{1,0:T(8,128)(2,1)S(1)}, bf16[256,512]{1,0:T(8,128)(2,1)S(1)}, u32[]{:S(2)}, u32[]{:S(2)}) %collective-permute-start.9) | collective-permute-done | bytes 262176 | tf_op jit(solution)/shard_map/ppermute | solution.py:17
  84.0 4.7 %collective-permute-done.8 = bf16[256,512]{1,0:T(8,128)(2,1)S(1)} collective-permute-done((bf16[256,512]{1,0:T(8,128)(2,1)S(1)}, bf16[256,512]{1,0:T(8,128)(2,1)S(1)}, u32[]{:S(2)}, u32[]{:S(2)}) %collective-permute-start.8) | collective-permute-done | bytes 262176 | tf_op jit(solution)/shard_map/ppermute | solution.py:17
  88.7 0.3 multiply_select_fusion.2
  89.0 1.5 %pad_maximum_fusion = f32[256,2048]{1,0:T(8,128)} fusion(f32[256,512]{1,0:T(8,128)S(1)} %get-tuple-element.6, f32[256,512]{1,0:T(8,128)S(1)} %get-tuple-element.7, f32[256,512]{1,0:T(8,128)S(1)} %get-tuple-element.5, f32[256,512]{1,0:T(8,128)S(1)} %fusion.5), kind=kLoop, calls=%fused_computation.2 | loop fusion | flops 1572864 | bytes 4194304 | tf_op jit(solution)/shard_map/concatenate | solution.py:110
  (5 shorter events, 0.1 us)
Async XLA Ops:
  2.5 7.5 %copy-start = (f32[2048,512]{1,0:T(8,128)S(1)}, f32[2048,512]{1,0:T(8,128)}, u32[]{:S(2)}) copy-start(f32[2048,512]{1,0:T(8,128)} %param.2) | copy-start | bytes 12582916
  5.4 4.6 %collective-permute-start = (f32[2,512]{1,0:T(2,128)S(1)}, f32[2,512]{1,0:T(2,128)S(1)}, u32[]{:S(2)}, u32[]{:S(2)}) collective-permute-start(f32[2,512]{1,0:T(2,128)S(1)} %pad_maximum_fusion.1), channel_id=1, source_target_pairs={{0,1},{1,0},{2,3},{3,2},{4,5},{5,4},{6,7},{7,6},{8,9},{9,8},{10,11... | collective-permute-start | bytes 12296 | tf_op jit(solution)/shard_map/ppermute | solution.py:17
  10.6 10.5 %collective-permute-start.3 = (bf16[2048,512]{1,0:T(8,128)(2,1)S(1)}, bf16[2048,512]{1,0:T(8,128)(2,1)}, u32[]{:S(2)}, u32[]{:S(2)}) collective-permute-start(bf16[2048,512]{1,0:T(8,128)(2,1)S(1)} %multiply_convert_fusion), channel_id=1, source_target_pairs={{4,2},{6,4},{2,0},{12,10},{14,12},{10,8},{20,18},{22,20},{18,16},{... | collective-permute-start | bytes 6291464 | tf_op jit(solution)/shard_map/ppermute | solution.py:32
  11.9 11.2 %collective-permute-start.1 = (bf16[2048,512]{1,0:T(8,128)(2,1)S(1)}, bf16[2048,512]{1,0:T(8,128)(2,1)}, u32[]{:S(2)}, u32[]{:S(2)}) collective-permute-start(bf16[2048,512]{1,0:T(8,128)(2,1)S(1)} %multiply_convert_fusion), channel_id=1, source_target_pairs={{0,2},{4,6},{2,8},{6,12},{8,10},{12,14},{10,16},{14,20},{16,18},{2... | collective-permute-start | bytes 6291464 | tf_op jit(solution)/shard_map/ppermute | solution.py:32
  16.3 48.3 %collective-permute-start.6 = (bf16[2048,512]{1,0:T(8,128)(2,1)S(1)}, bf16[2048,512]{1,0:T(8,128)(2,1)}, u32[]{:S(2)}, u32[]{:S(2)}) collective-permute-start(bf16[2048,512]{1,0:T(8,128)(2,1)S(1)} %multiply_convert_fusion), channel_id=1, source_target_pairs={{2,4},{0,6},{10,12},{8,14},{18,20},{16,22},{26,28},{24,30},{3,5},{... | collective-permute-start | bytes 6291464 | tf_op jit(solution)/shard_map/ppermute | solution.py:32
  21.1 43.5 %collective-permute-start.4 = (bf16[2048,512]{1,0:T(8,128)(2,1)}, bf16[2048,512]{1,0:T(8,128)(2,1)}, u32[]{:S(2)}, u32[]{:S(2)}) collective-permute-start(bf16[2048,512]{1,0:T(8,128)(2,1)} %collective-permute-done.3), channel_id=1, source_target_pairs={{2,8},{10,16},{18,24},{3,9},{11,17},{19,25}} | collective-permute-start | bytes 6291464 | tf_op jit(solution)/shard_map/ppermute | solution.py:32
  23.1 41.5 %collective-permute-start.5 = (bf16[2048,512]{1,0:T(8,128)(2,1)}, bf16[2048,512]{1,0:T(8,128)(2,1)}, u32[]{:S(2)}, u32[]{:S(2)}) collective-permute-start(bf16[2048,512]{1,0:T(8,128)(2,1)} %collective-permute-done.1), channel_id=1, source_target_pairs={{4,2},{12,10},{20,18},{28,26},{5,3},{13,11},{21,19},{29,27}} | collective-permute-start | bytes 6291464 | tf_op jit(solution)/shard_map/ppermute | solution.py:32
  30.0 46.9 %collective-permute-start.2 = (bf16[2,256,512]{2,1,0:T(8,128)(2,1)S(1)}, bf16[2,256,512]{2,1,0:T(8,128)(2,1)S(1)}, u32[]{:S(2)}, u32[]{:S(2)}) collective-permute-start(bf16[2,256,512]{2,1,0:T(8,128)(2,1)S(1)} %fusion.1), channel_id=1, source_target_pairs={{0,1},{1,0},{2,3},{3,2},{4,5},{5,4},{6,7},{7,6},{8,9},{9,8},{10,11... | collective-permute-start | bytes 1572872 | tf_op jit(solution)/shard_map/ppermute | solution.py:17
  69.1 7.3 %collective-permute-start.7 = (bf16[512,512]{1,0:T(8,128)(2,1)S(1)}, bf16[512,512]{1,0:T(8,128)(2,1)S(1)}, u32[]{:S(2)}, u32[]{:S(2)}) collective-permute-start(bf16[512,512]{1,0:T(8,128)(2,1)S(1)} %convolution_convert_fusion.1), channel_id=1, source_target_pairs={{0,2},{2,0},{4,6},{6,4},{8,10},{10,8},{12,14},{14,12},{16,18},{18,... | collective-permute-start | bytes 1572872 | tf_op jit(solution)/shard_map/ppermute | solution.py:32
  74.8 9.2 %collective-permute-start.9 = (bf16[256,512]{1,0:T(8,128)(2,1)S(1)}, bf16[256,512]{1,0:T(8,128)(2,1)S(1)}, u32[]{:S(2)}, u32[]{:S(2)}) collective-permute-start(bf16[256,512]{1,0:T(8,128)(2,1)S(1)} %dynamic-slice_bitcast_fusion), channel_id=1, source_target_pairs={{0,1},{1,0},{2,3},{3,2},{4,5},{5,4},{6,7},{7,6},{8,9},{9,8},{10,11... | collective-permute-start | bytes 786440 | tf_op jit(solution)/shard_map/ppermute | solution.py:17
  76.4 12.3 %collective-permute-start.8 = (bf16[256,512]{1,0:T(8,128)(2,1)S(1)}, bf16[256,512]{1,0:T(8,128)(2,1)S(1)}, u32[]{:S(2)}, u32[]{:S(2)}) collective-permute-start(bf16[256,512]{1,0:T(8,128)(2,1)S(1)} %dynamic-slice_bitcast_fusion.1), channel_id=1, source_target_pairs={{0,1},{1,0},{2,3},{3,2},{4,5},{5,4},{6,7},{7,6},{8,9},{9,8},{10,11... | collective-permute-start | bytes 786440 | tf_op jit(solution)/shard_map/ppermute | solution.py:17

commit v10 on v9

--- a/solution.py
+++ b/solution.py
@@ -58,9 +58,12 @@
     samples = rows * n_smp
     me = lax.axis_index("smp")
 
-    part_mean = jnp.sum(dosage, axis=0) / rows
-    deviation = dosage - part_mean
-    part_m2 = jnp.sum(deviation * deviation, axis=0)
+    origin = dosage[0]
+    shifted_dosage = dosage - origin
+    part_sum = jnp.sum(shifted_dosage, axis=0)
+    part_square = jnp.sum(shifted_dosage * shifted_dosage, axis=0)
+    part_mean = origin + part_sum / rows
+    part_m2 = part_square - part_sum * (part_sum / rows)
     stats = jnp.stack([part_mean, part_m2])
     gathered = [stats] + [rotated(stats, "smp", s) for s in range(1, n_smp)]
     mean = gathered[0][0]

time: 90.8 us -> 89.6 us (0.987)
  other arithmetic: 13.1 us -> 10.6 us
  local copies, waits for them, and re-layouts: 0.05 us -> 1.27 us
    reduce_sum x2 -> x1, other arithmetic: 5.37 us -> 2.94 us  [local(): part_square = jnp.sum(shifted_dosage * shifted_dosage, axis=0)]
where the time goes in v10:
time: 89.6 us; the launch traced here: 89.3 us
  waiting for transfers between devices  44.3 us (49%)
  starting transfers between devices  25.6 us (29%)
  other arithmetic  10.6 us (12%)
  matrix products  6.68 us (7%)
  local copies, waits for them, and re-layouts  1.27 us (1%)
    ppermute x6, waiting for transfers between devices, send(): return lax.ppermute(value, 'snp', pairs)  31.2 us
    ppermute x6, starting transfers between devices, send(): return lax.ppermute(value, 'snp', pairs)  18.9 us
    ppermute x4, waiting for transfers between devices, rotated(): lax.ppermute(value, axis, [(source, (source + steps) % count) for source...  13.1 us
    ppermute x4, starting transfers between devices, rotated(): lax.ppermute(value, axis, [(source, (source + steps) % count) for source...  6.78 us
    dot_general x4, matrix products, tile_term(): lax.dot_general(standard, neighbour, (((0,), (0,)), ((), ())), preferred_...  6.68 us
    add x1, other arithmetic, relayed(): rhs = lax.optimization_barrier(relay + cross)  3.16 us
    reduce_sum x1, other arithmetic, local(): part_square = jnp.sum(shifted_dosage * shifted_dosage, axis=0)  2.94 us
    select_n x1, other arithmetic, relayed(): lhs = lax.optimization_barrier(jnp.where(place % 2 == 0, fast_b, fast_a))  1.81 us
  transfers between devices with their start and end apart: 10, of which 4 were waited for; matrix products, arithmetic and copies ran while one was open for 13% of the time, Pallas kernels for 0%

profile of v10, /device:TPU:0, one launch (start us, length us, event | category | flops | bytes accessed | tf_op | source)
XLA Modules:
  0.0 89.3 jit_solution(13404225424806002324)
XLA Ops:
  0.0 0.7 slice.17
  0.7 0.0 copy-start
  0.7 2.9 %multiply_reduce_fusion = (f32[512]{0:T(512)S(1)}, f32[512]{0:T(512)S(1)}) fusion(f32[2048,512]{1,0:T(8,128)} %param.2, f32[512]{0:T(512)S(1)} %bitcast.64), kind=kLoop, calls=%fused_computation.1 | loop fusion | flops 4193280 | bytes 4200448 | tf_op jit(solution)/shard_map/reduce_sum | solution.py:64
  3.7 0.5 copy-done
  4.2 3.0 %collective-permute-start = (f32[2,512]{1,0:T(2,128)S(1)}, f32[2,512]{1,0:T(2,128)S(1)}, u32[]{:S(2)}, u32[]{:S(2)}) collective-permute-start(f32[2,512]{1,0:T(2,128)S(1)} %pad_maximum_fusion.1), channel_id=1, source_target_pairs={{0,1},{1,0},{2,3},{3,2},{4,5},{5,4},{6,7},{7,6},{8,9},{9,8},{10,11... | collective-permute-start | bytes 12296 | tf_op jit(solution)/shard_map/ppermute | solution.py:17
  7.2 1.6 %collective-permute-done = f32[2,512]{1,0:T(2,128)S(1)} collective-permute-done((f32[2,512]{1,0:T(2,128)S(1)}, f32[2,512]{1,0:T(2,128)S(1)}, u32[]{:S(2)}, u32[]{:S(2)}) %collective-permute-start) | collective-permute-done | bytes 4128 | tf_op jit(solution)/shard_map/ppermute | solution.py:17
  8.8 0.6 multiply_convert_fusion
  9.4 1.3 %collective-permute-start.3 = (bf16[2048,512]{1,0:T(8,128)(2,1)S(1)}, bf16[2048,512]{1,0:T(8,128)(2,1)}, u32[]{:S(2)}, u32[]{:S(2)}) collective-permute-start(bf16[2048,512]{1,0:T(8,128)(2,1)S(1)} %multiply_convert_fusion), channel_id=1, source_target_pairs={{4,2},{6,4},{2,0},{12,10},{14,12},{10,8},{20,18},{22,20},{18,16},{... | collective-permute-start | bytes 6291464 | tf_op jit(solution)/shard_map/ppermute | solution.py:32
  10.7 4.4 %collective-permute-start.1 = (bf16[2048,512]{1,0:T(8,128)(2,1)S(1)}, bf16[2048,512]{1,0:T(8,128)(2,1)}, u32[]{:S(2)}, u32[]{:S(2)}) collective-permute-start(bf16[2048,512]{1,0:T(8,128)(2,1)S(1)} %multiply_convert_fusion), channel_id=1, source_target_pairs={{0,2},{4,6},{2,8},{6,12},{8,10},{12,14},{10,16},{14,20},{16,18},{2... | collective-permute-start | bytes 6291464 | tf_op jit(solution)/shard_map/ppermute | solution.py:32
  15.1 4.8 %collective-permute-start.6 = (bf16[2048,512]{1,0:T(8,128)(2,1)S(1)}, bf16[2048,512]{1,0:T(8,128)(2,1)}, u32[]{:S(2)}, u32[]{:S(2)}) collective-permute-start(bf16[2048,512]{1,0:T(8,128)(2,1)S(1)} %multiply_convert_fusion), channel_id=1, source_target_pairs={{2,4},{0,6},{10,12},{8,14},{18,20},{16,22},{26,28},{24,30},{3,5},{... | collective-permute-start | bytes 6291464 | tf_op jit(solution)/shard_map/ppermute | solution.py:32
  19.9 0.0 collective-permute-done.3
  19.9 2.0 %collective-permute-start.4 = (bf16[2048,512]{1,0:T(8,128)(2,1)}, bf16[2048,512]{1,0:T(8,128)(2,1)}, u32[]{:S(2)}, u32[]{:S(2)}) collective-permute-start(bf16[2048,512]{1,0:T(8,128)(2,1)} %collective-permute-done.3), channel_id=1, source_target_pairs={{2,8},{10,16},{18,24},{3,9},{11,17},{19,25}} | collective-permute-start | bytes 6291464 | tf_op jit(solution)/shard_map/ppermute | solution.py:32
  21.9 0.0 collective-permute-done.1
  21.9 2.0 %collective-permute-start.5 = (bf16[2048,512]{1,0:T(8,128)(2,1)}, bf16[2048,512]{1,0:T(8,128)(2,1)}, u32[]{:S(2)}, u32[]{:S(2)}) collective-permute-start(bf16[2048,512]{1,0:T(8,128)(2,1)} %collective-permute-done.1), channel_id=1, source_target_pairs={{4,2},{12,10},{20,18},{28,26},{5,3},{13,11},{21,19},{29,27}} | collective-permute-start | bytes 6291464 | tf_op jit(solution)/shard_map/ppermute | solution.py:32
  24.6 1.3 %convolution_convert_fusion.3 = bf16[512,512]{1,0:T(8,128)(2,1)S(1)} fusion(bf16[2048,512]{1,0:T(8,128)(2,1)S(1)} %multiply_convert_fusion), kind=kOutput, calls=%fused_computation.9 | convolution fusion | flops 1074003968 | bytes 2621440 | tf_op jit(solution)/shard_map/dot_general | solution.py:50
  25.9 2.9 %convolution_convert_fusion.2 = bf16[512,512]{1,0:T(8,128)(2,1)S(1)} fusion(bf16[2048,512]{1,0:T(8,128)(2,1)S(1)} %multiply_convert_fusion, bf16[2048,512]{1,0:T(8,128)(2,1)} %collective-permute-done.1), kind=kOutput, calls=%fused_computation.8 | convolution fusion | flops 1074003968 | bytes 4718592 | tf_op jit(solution)/shard_map/dot_general | solution.py:50
  28.8 0.1 fusion.1
  28.8 1.6 %collective-permute-start.2 = (bf16[2,256,512]{2,1,0:T(8,128)(2,1)S(1)}, bf16[2,256,512]{2,1,0:T(8,128)(2,1)S(1)}, u32[]{:S(2)}, u32[]{:S(2)}) collective-permute-start(bf16[2,256,512]{2,1,0:T(8,128)(2,1)S(1)} %fusion.1), channel_id=1, source_target_pairs={{0,1},{1,0},{2,3},{3,2},{4,5},{5,4},{6,7},{7,6},{8,9},{9,8},{10,11... | collective-permute-start | bytes 1572872 | tf_op jit(solution)/shard_map/ppermute | solution.py:17
  30.4 1.8 %broadcast_select_fusion = bf16[2048,512]{1,0:T(8,128)(2,1)S(1)} fusion(bf16[2048,512]{1,0:T(8,128)(2,1)} %collective-permute-done.3, bf16[2048,512]{1,0:T(8,128)(2,1)} %collective-permute-done.1, pred[]{:T(512)S(6)} %eq.22), kind=kLoop, calls=%fused_computation.5 | loop fusion | flops 1048576 | bytes 6291457 | tf_op jit(solution)/shard_map/jit(_where)/select_n | solution.py:41
  32.2 31.2 %collective-permute-done.6 = bf16[2048,512]{1,0:T(8,128)(2,1)} collective-permute-done((bf16[2048,512]{1,0:T(8,128)(2,1)S(1)}, bf16[2048,512]{1,0:T(8,128)(2,1)}, u32[]{:S(2)}, u32[]{:S(2)}) %collective-permute-start.6) | collective-permute-done | bytes 2097184 | tf_op jit(solution)/shard_map/ppermute | solution.py:32
  63.4 0.0 collective-permute-done.4
  63.4 0.0 collective-permute-done.5
  63.4 3.2 %add_add_fusion = bf16[2048,512]{1,0:T(8,128)(2,1)S(1)} fusion(bf16[2048,512]{1,0:T(8,128)(2,1)} %collective-permute-done.6, bf16[2048,512]{1,0:T(8,128)(2,1)} %collective-permute-done.4, bf16[2048,512]{1,0:T(8,128)(2,1)} %collective-permute-done.5), kind=kLoop, calls=%fused_computation.4 | loop fusion | flops 2097152 | bytes 8388608 | tf_op jit(solution)/shard_map/add | solution.py:42
  66.6 1.3 %convolution_convert_fusion.1 = bf16[512,512]{1,0:T(8,128)(2,1)S(1)} fusion(bf16[2048,512]{1,0:T(8,128)(2,1)S(1)} %broadcast_select_fusion, bf16[2048,512]{1,0:T(8,128)(2,1)S(1)} %add_add_fusion), kind=kOutput, calls=%fused_computation.7 | convolution fusion | flops 1074003968 | bytes 4718592 | tf_op jit(solution)/shard_map/dot_general | solution.py:50
  67.9 4.4 %collective-permute-start.7 = (bf16[512,512]{1,0:T(8,128)(2,1)S(1)}, bf16[512,512]{1,0:T(8,128)(2,1)S(1)}, u32[]{:S(2)}, u32[]{:S(2)}) collective-permute-start(bf16[512,512]{1,0:T(8,128)(2,1)S(1)} %convolution_convert_fusion.1), channel_id=1, source_target_pairs={{0,2},{2,0},{4,6},{6,4},{8,10},{10,8},{12,14},{14,12},{16,18},{18,... | collective-permute-start | bytes 1572872 | tf_op jit(solution)/shard_map/ppermute | solution.py:32
  72.2 1.3 %convolution_convert_fusion = bf16[512,512]{1,0:T(8,128)(2,1)S(1)} fusion(bf16[2048,512]{1,0:T(8,128)(2,1)S(1)} %multiply_convert_fusion, bf16[2048,512]{1,0:T(8,128)(2,1)S(1)} %add_add_fusion), kind=kOutput, calls=%fused_computation.6 | convolution fusion | flops 1074003968 | bytes 4718592 | tf_op jit(solution)/shard_map/dot_general | solution.py:50
  73.6 1.6 %collective-permute-start.9 = (bf16[256,512]{1,0:T(8,128)(2,1)S(1)}, bf16[256,512]{1,0:T(8,128)(2,1)S(1)}, u32[]{:S(2)}, u32[]{:S(2)}) collective-permute-start(bf16[256,512]{1,0:T(8,128)(2,1)S(1)} %dynamic-slice_bitcast_fusion), channel_id=1, source_target_pairs={{0,1},{1,0},{2,3},{3,2},{4,5},{5,4},{6,7},{7,6},{8,9},{9,8},{10,11... | collective-permute-start | bytes 786440 | tf_op jit(solution)/shard_map/ppermute | solution.py:17
  75.2 0.0 collective-permute-done.7
  75.2 0.6 collective-permute-start.8
  75.8 0.0 collective-permute-done.2
  75.8 0.2 convert_add_fusion
  75.9 0.1 fusion.5
  76.0 6.8 %collective-permute-done.9 = bf16[256,512]{1,0:T(8,128)(2,1)S(1)} collective-permute-done((bf16[256,512]{1,0:T(8,128)(2,1)S(1)}, bf16[256,512]{1,0:T(8,128)(2,1)S(1)}, u32[]{:S(2)}, u32[]{:S(2)}) %collective-permute-start.9) | collective-permute-done | bytes 262176 | tf_op jit(solution)/shard_map/ppermute | solution.py:17
  82.8 4.7 %collective-permute-done.8 = bf16[256,512]{1,0:T(8,128)(2,1)S(1)} collective-permute-done((bf16[256,512]{1,0:T(8,128)(2,1)S(1)}, bf16[256,512]{1,0:T(8,128)(2,1)S(1)}, u32[]{:S(2)}, u32[]{:S(2)}) %collective-permute-start.8) | collective-permute-done | bytes 262176 | tf_op jit(solution)/shard_map/ppermute | solution.py:17
  87.5 0.3 multiply_select_fusion.2
  87.8 1.5 %pad_maximum_fusion = f32[256,2048]{1,0:T(8,128)} fusion(f32[256,512]{1,0:T(8,128)S(1)} %get-tuple-element.8, f32[256,512]{1,0:T(8,128)S(1)} %get-tuple-element.9, f32[256,512]{1,0:T(8,128)S(1)} %get-tuple-element.7, f32[256,512]{1,0:T(8,128)S(1)} %fusion.5), kind=kLoop, calls=%fused_computation.3 | loop fusion | flops 1572864 | bytes 4194304 | tf_op jit(solution)/shard_map/concatenate | solution.py:113
  (5 shorter events, 0.1 us)
Async XLA Ops:
  0.7 3.4 %copy-start = (f32[2048,512]{1,0:T(8,128)S(1)}, f32[2048,512]{1,0:T(8,128)}, u32[]{:S(2)}) copy-start(f32[2048,512]{1,0:T(8,128)} %param.2) | copy-start | bytes 12582916
  4.2 4.6 %collective-permute-start = (f32[2,512]{1,0:T(2,128)S(1)}, f32[2,512]{1,0:T(2,128)S(1)}, u32[]{:S(2)}, u32[]{:S(2)}) collective-permute-start(f32[2,512]{1,0:T(2,128)S(1)} %pad_maximum_fusion.1), channel_id=1, source_target_pairs={{0,1},{1,0},{2,3},{3,2},{4,5},{5,4},{6,7},{7,6},{8,9},{9,8},{10,11... | collective-permute-start | bytes 12296 | tf_op jit(solution)/shard_map/ppermute | solution.py:17
  9.4 10.5 %collective-permute-start.3 = (bf16[2048,512]{1,0:T(8,128)(2,1)S(1)}, bf16[2048,512]{1,0:T(8,128)(2,1)}, u32[]{:S(2)}, u32[]{:S(2)}) collective-permute-start(bf16[2048,512]{1,0:T(8,128)(2,1)S(1)} %multiply_convert_fusion), channel_id=1, source_target_pairs={{4,2},{6,4},{2,0},{12,10},{14,12},{10,8},{20,18},{22,20},{18,16},{... | collective-permute-start | bytes 6291464 | tf_op jit(solution)/shard_map/ppermute | solution.py:32
  10.7 11.2 %collective-permute-start.1 = (bf16[2048,512]{1,0:T(8,128)(2,1)S(1)}, bf16[2048,512]{1,0:T(8,128)(2,1)}, u32[]{:S(2)}, u32[]{:S(2)}) collective-permute-start(bf16[2048,512]{1,0:T(8,128)(2,1)S(1)} %multiply_convert_fusion), channel_id=1, source_target_pairs={{0,2},{4,6},{2,8},{6,12},{8,10},{12,14},{10,16},{14,20},{16,18},{2... | collective-permute-start | bytes 6291464 | tf_op jit(solution)/shard_map/ppermute | solution.py:32
  15.1 48.3 %collective-permute-start.6 = (bf16[2048,512]{1,0:T(8,128)(2,1)S(1)}, bf16[2048,512]{1,0:T(8,128)(2,1)}, u32[]{:S(2)}, u32[]{:S(2)}) collective-permute-start(bf16[2048,512]{1,0:T(8,128)(2,1)S(1)} %multiply_convert_fusion), channel_id=1, source_target_pairs={{2,4},{0,6},{10,12},{8,14},{18,20},{16,22},{26,28},{24,30},{3,5},{... | collective-permute-start | bytes 6291464 | tf_op jit(solution)/shard_map/ppermute | solution.py:32
  19.9 43.5 %collective-permute-start.4 = (bf16[2048,512]{1,0:T(8,128)(2,1)}, bf16[2048,512]{1,0:T(8,128)(2,1)}, u32[]{:S(2)}, u32[]{:S(2)}) collective-permute-start(bf16[2048,512]{1,0:T(8,128)(2,1)} %collective-permute-done.3), channel_id=1, source_target_pairs={{2,8},{10,16},{18,24},{3,9},{11,17},{19,25}} | collective-permute-start | bytes 6291464 | tf_op jit(solution)/shard_map/ppermute | solution.py:32
  21.9 41.5 %collective-permute-start.5 = (bf16[2048,512]{1,0:T(8,128)(2,1)}, bf16[2048,512]{1,0:T(8,128)(2,1)}, u32[]{:S(2)}, u32[]{:S(2)}) collective-permute-start(bf16[2048,512]{1,0:T(8,128)(2,1)} %collective-permute-done.1), channel_id=1, source_target_pairs={{4,2},{12,10},{20,18},{28,26},{5,3},{13,11},{21,19},{29,27}} | collective-permute-start | bytes 6291464 | tf_op jit(solution)/shard_map/ppermute | solution.py:32
  28.8 46.9 %collective-permute-start.2 = (bf16[2,256,512]{2,1,0:T(8,128)(2,1)S(1)}, bf16[2,256,512]{2,1,0:T(8,128)(2,1)S(1)}, u32[]{:S(2)}, u32[]{:S(2)}) collective-permute-start(bf16[2,256,512]{2,1,0:T(8,128)(2,1)S(1)} %fusion.1), channel_id=1, source_target_pairs={{0,1},{1,0},{2,3},{3,2},{4,5},{5,4},{6,7},{7,6},{8,9},{9,8},{10,11... | collective-permute-start | bytes 1572872 | tf_op jit(solution)/shard_map/ppermute | solution.py:17
  67.9 7.3 %collective-permute-start.7 = (bf16[512,512]{1,0:T(8,128)(2,1)S(1)}, bf16[512,512]{1,0:T(8,128)(2,1)S(1)}, u32[]{:S(2)}, u32[]{:S(2)}) collective-permute-start(bf16[512,512]{1,0:T(8,128)(2,1)S(1)} %convolution_convert_fusion.1), channel_id=1, source_target_pairs={{0,2},{2,0},{4,6},{6,4},{8,10},{10,8},{12,14},{14,12},{16,18},{18,... | collective-permute-start | bytes 1572872 | tf_op jit(solution)/shard_map/ppermute | solution.py:32
  73.6 9.2 %collective-permute-start.9 = (bf16[256,512]{1,0:T(8,128)(2,1)S(1)}, bf16[256,512]{1,0:T(8,128)(2,1)S(1)}, u32[]{:S(2)}, u32[]{:S(2)}) collective-permute-start(bf16[256,512]{1,0:T(8,128)(2,1)S(1)} %dynamic-slice_bitcast_fusion), channel_id=1, source_target_pairs={{0,1},{1,0},{2,3},{3,2},{4,5},{5,4},{6,7},{7,6},{8,9},{9,8},{10,11... | collective-permute-start | bytes 786440 | tf_op jit(solution)/shard_map/ppermute | solution.py:17
  75.2 12.3 %collective-permute-start.8 = (bf16[256,512]{1,0:T(8,128)(2,1)S(1)}, bf16[256,512]{1,0:T(8,128)(2,1)S(1)}, u32[]{:S(2)}, u32[]{:S(2)}) collective-permute-start(bf16[256,512]{1,0:T(8,128)(2,1)S(1)} %dynamic-slice_bitcast_fusion.1), channel_id=1, source_target_pairs={{0,1},{1,0},{2,3},{3,2},{4,5},{5,4},{6,7},{7,6},{8,9},{9,8},{10,11... | collective-permute-start | bytes 786440 | tf_op jit(solution)/shard_map/ppermute | solution.py:17

commit v11 on v10

--- a/solution.py
+++ b/solution.py
@@ -26,7 +26,7 @@
     return out
 
 
-def relayed(standard, count, place):
+def relayed(standard, count, place, early_of):
     def send(value, pairs):
         pairs = [(s, t) for s, t in pairs if 0 <= s < count and 0 <= t < count]
         return lax.ppermute(value, "snp", pairs)
@@ -38,12 +38,16 @@
     fast_a = send(standard, pairs_of((0, 1), (2, 3), (1, 4), (3, 6)))
     fast_b = send(standard, pairs_of((2, 1), (3, 2), (1, 0)))
     relay = send(fast_b, pairs_of((1, 4))) + send(fast_a, pairs_of((2, 1)))
-    lhs = lax.optimization_barrier(jnp.where(place % 2 == 0, fast_b, fast_a))
+    width = standard.shape[1]
+    early = early_of(tile_term(standard, fast_a).astype(jnp.bfloat16))
+    both, early = lax.optimization_barrier(
+        (jnp.concatenate([standard, jnp.where(place % 2 == 0, fast_b, fast_a)], axis=1), early)
+    )
     rhs = lax.optimization_barrier(relay + cross)
-    handed = send(tile_term(lhs, rhs).astype(jnp.bfloat16), pairs_of((0, 1), (1, 0), (2, 3), (3, 2)))
-    own_late = tile_term(standard, rhs).astype(jnp.bfloat16)
-    with_a = tile_term(standard, fast_a).astype(jnp.bfloat16)
-    return with_a, own_late, handed
+    product = tile_term(both, rhs).astype(jnp.bfloat16)
+    own_late = product[:width]
+    handed = send(product[width:], pairs_of((0, 1), (1, 0), (2, 3), (3, 2)))
+    return early, own_late, handed
 
 
 def tile_term(standard, neighbour):
@@ -94,8 +98,9 @@
 
     if count % 4 == 0:
         place = lax.axis_index("snp") % 4
-        with_a, own_late, handed = relayed(standard, count, place)
-        early = exchanged(jnp.stack([first, with_a]))
+        early, own_late, handed = relayed(
+            standard, count, place, lambda with_a: exchanged(jnp.stack([first, with_a]))
+        )
         late = [exchanged(own_late), exchanged(handed)]
         totals = [
             early[0],

time: 89.6 us -> 86.3 us (0.963)
  starting transfers between devices: 25.6 us -> 21.4 us
  waiting for transfers between devices: 44.3 us -> 46.5 us
  other arithmetic: 10.6 us -> 9.42 us
    ppermute x6, starting transfers between devices: 18.9 us -> 13.7 us  [send(): return lax.ppermute(value, 'snp', pairs)]
    ppermute x4, waiting for transfers between devices: 13.1 us -> 17 us  [rotated(): lax.ppermute(value, axis, [(source, (source + steps) % count) for source...]
    add x1, other arithmetic: 3.16 us -> 0.3 us  [relayed(): rhs = lax.optimization_barrier(relay + cross)]
    ppermute x6, waiting for transfers between devices: 31.2 us -> 29.5 us  [send(): return lax.ppermute(value, 'snp', pairs)]
    select_n x2, other arithmetic: 0.37 us -> 1.38 us  [local(): kept.append(jnp.where(dist <= own_reach, tile, jnp.zeros_like(tile)))]
    ppermute x4, starting transfers between devices: 6.78 us -> 7.71 us  [rotated(): lax.ppermute(value, axis, [(source, (source + steps) % count) for source...]
    dot_general x4 -> x3, matrix products: 6.68 us -> 6.52 us  [tile_term(): lax.dot_general(standard, neighbour, (((0,), (0,)), ((), ())), preferred_...]
  transfers between devices with their start and end apart: 10 -> 10, of which waited for: 4 -> 5; matrix products, arithmetic and copies ran while one was open for 13% -> 8% of each run, Pallas kernels for 0% -> 0%
where the time goes in v11:
time: 86.3 us; the launch traced here: 86 us
  waiting for transfers between devices  46.5 us (54%)
  starting transfers between devices  21.4 us (25%)
  other arithmetic  9.42 us (11%)
  matrix products  6.52 us (8%)
  local copies, waits for them, and re-layouts  1.33 us (2%)
    ppermute x6, waiting for transfers between devices, send(): return lax.ppermute(value, 'snp', pairs)  29.5 us
    ppermute x4, waiting for transfers between devices, rotated(): lax.ppermute(value, axis, [(source, (source + steps) % count) for source...  17 us
    ppermute x6, starting transfers between devices, send(): return lax.ppermute(value, 'snp', pairs)  13.7 us
    ppermute x4, starting transfers between devices, rotated(): lax.ppermute(value, axis, [(source, (source + steps) % count) for source...  7.71 us
    dot_general x3, matrix products, tile_term(): lax.dot_general(standard, neighbour, (((0,), (0,)), ((), ())), preferred_...  6.52 us
    reduce_sum x1, other arithmetic, local(): part_square = jnp.sum(shifted_dosage * shifted_dosage, axis=0)  2.94 us
    select_n x1, other arithmetic, relayed(): jnp.where(place % 2 == 0, fast_b, fast_a)  1.81 us
  transfers between devices with their start and end apart: 10, of which 5 were waited for; matrix products, arithmetic and copies ran while one was open for 8% of the time, Pallas kernels for 0%

profile of v11, /device:TPU:0, one launch (start us, length us, event | category | flops | bytes accessed | tf_op | source)
XLA Modules:
  0.0 86.0 jit_solution(1178880294855263021)
XLA Ops:
  0.0 0.7 slice.23
  0.7 0.0 copy-start
  0.7 2.9 %multiply_reduce_fusion = (f32[512]{0:T(512)S(1)}, f32[512]{0:T(512)S(1)}) fusion(f32[2048,512]{1,0:T(8,128)} %param.2, f32[512]{0:T(512)S(1)} %bitcast.71), kind=kLoop, calls=%fused_computation.2 | loop fusion | flops 4193280 | bytes 4200448 | tf_op jit(solution)/shard_map/reduce_sum | solution.py:68
  3.7 0.5 copy-done
  4.2 3.0 %collective-permute-start = (f32[2,512]{1,0:T(2,128)S(1)}, f32[2,512]{1,0:T(2,128)S(1)}, u32[]{:S(2)}, u32[]{:S(2)}) collective-permute-start(f32[2,512]{1,0:T(2,128)S(1)} %pad_maximum_fusion.2), channel_id=1, source_target_pairs={{0,1},{1,0},{2,3},{3,2},{4,5},{5,4},{6,7},{7,6},{8,9},{9,8},{10,11... | collective-permute-start | bytes 12296 | tf_op jit(solution)/shard_map/ppermute | solution.py:17
  7.2 1.6 %collective-permute-done = f32[2,512]{1,0:T(2,128)S(1)} collective-permute-done((f32[2,512]{1,0:T(2,128)S(1)}, f32[2,512]{1,0:T(2,128)S(1)}, u32[]{:S(2)}, u32[]{:S(2)}) %collective-permute-start) | collective-permute-done | bytes 4128 | tf_op jit(solution)/shard_map/ppermute | solution.py:17
  8.8 0.6 multiply_convert_fusion
  9.4 1.3 %collective-permute-start.1 = (bf16[2048,512]{1,0:T(8,128)(2,1)S(1)}, bf16[2048,512]{1,0:T(8,128)(2,1)}, u32[]{:S(2)}, u32[]{:S(2)}) collective-permute-start(bf16[2048,512]{1,0:T(8,128)(2,1)S(1)} %multiply_convert_fusion), channel_id=1, source_target_pairs={{4,2},{6,4},{2,0},{12,10},{14,12},{10,8},{20,18},{22,20},{18,16},{... | collective-permute-start | bytes 6291464 | tf_op jit(solution)/shard_map/ppermute | solution.py:32
  10.7 4.4 %collective-permute-start.2 = (bf16[2048,512]{1,0:T(8,128)(2,1)S(1)}, bf16[2048,512]{1,0:T(8,128)(2,1)}, u32[]{:S(2)}, u32[]{:S(2)}) collective-permute-start(bf16[2048,512]{1,0:T(8,128)(2,1)S(1)} %multiply_convert_fusion), channel_id=1, source_target_pairs={{0,2},{4,6},{2,8},{6,12},{8,10},{12,14},{10,16},{14,20},{16,18},{2... | collective-permute-start | bytes 6291464 | tf_op jit(solution)/shard_map/ppermute | solution.py:32
  15.1 3.7 %collective-permute-start.6 = (bf16[2048,512]{1,0:T(8,128)(2,1)S(1)}, bf16[2048,512]{1,0:T(8,128)(2,1)S(1)}, u32[]{:S(2)}, u32[]{:S(2)}) collective-permute-start(bf16[2048,512]{1,0:T(8,128)(2,1)S(1)} %multiply_convert_fusion), channel_id=1, source_target_pairs={{2,4},{0,6},{10,12},{8,14},{18,20},{16,22},{26,28},{24,30},{3,5},{... | collective-permute-start | bytes 6291464 | tf_op jit(solution)/shard_map/ppermute | solution.py:32
  18.8 0.0 collective-permute-done.1
  18.8 0.8 collective-permute-start.4
  19.6 0.0 collective-permute-done.2
  19.6 0.8 collective-permute-start.5
  20.4 1.3 %convolution_convert_fusion.2 = bf16[512,512]{1,0:T(8,128)(2,1)S(1)} fusion(bf16[2048,512]{1,0:T(8,128)(2,1)S(1)} %multiply_convert_fusion), kind=kOutput, calls=%fused_computation.9 | convolution fusion | flops 1074003968 | bytes 2621440 | tf_op jit(solution)/shard_map/dot_general | solution.py:54
  21.7 2.9 %convolution_convert_fusion.1 = bf16[512,512]{1,0:T(8,128)(2,1)S(1)} fusion(bf16[2048,512]{1,0:T(8,128)(2,1)S(1)} %multiply_convert_fusion, bf16[2048,512]{1,0:T(8,128)(2,1)} %collective-permute-done.2), kind=kOutput, calls=%fused_computation.8 | convolution fusion | flops 1074003968 | bytes 4718592 | tf_op jit(solution)/shard_map/dot_general | solution.py:54
  24.5 0.1 fusion.1
  24.6 1.6 %collective-permute-start.3 = (bf16[2,256,512]{2,1,0:T(8,128)(2,1)S(1)}, bf16[2,256,512]{2,1,0:T(8,128)(2,1)S(1)}, u32[]{:S(2)}, u32[]{:S(2)}) collective-permute-start(bf16[2,256,512]{2,1,0:T(8,128)(2,1)S(1)} %fusion.1), channel_id=1, source_target_pairs={{0,1},{1,0},{2,3},{3,2},{4,5},{5,4},{6,7},{7,6},{8,9},{9,8},{10,11... | collective-permute-start | bytes 1572872 | tf_op jit(solution)/shard_map/ppermute | solution.py:17
  26.2 1.8 %broadcast_select_fusion = bf16[2048,512]{1,0:T(8,128)(2,1)S(1)} fusion(bf16[2048,512]{1,0:T(8,128)(2,1)} %collective-permute-done.1, bf16[2048,512]{1,0:T(8,128)(2,1)} %collective-permute-done.2, pred[]{:T(512)S(6)} %eq.21), kind=kLoop, calls=%fused_computation.6 | loop fusion | flops 1048576 | bytes 6291457 | tf_op jit(solution)/shard_map/jit(_where)/select_n | solution.py:44
  28.0 0.6 pad_maximum_fusion
  28.7 5.2 %collective-permute-done.3 = bf16[2,256,512]{2,1,0:T(8,128)(2,1)S(1)} collective-permute-done((bf16[2,256,512]{2,1,0:T(8,128)(2,1)S(1)}, bf16[2,256,512]{2,1,0:T(8,128)(2,1)S(1)}, u32[]{:S(2)}, u32[]{:S(2)}) %collective-permute-start.3) | collective-permute-done | bytes 524320 | tf_op jit(solution)/shard_map/ppermute | solution.py:17
  33.9 0.2 convert_add_fusion
  34.0 29.5 %collective-permute-done.6 = bf16[2048,512]{1,0:T(8,128)(2,1)S(1)} collective-permute-done((bf16[2048,512]{1,0:T(8,128)(2,1)S(1)}, bf16[2048,512]{1,0:T(8,128)(2,1)S(1)}, u32[]{:S(2)}, u32[]{:S(2)}) %collective-permute-start.6) | collective-permute-done | bytes 2097184 | tf_op jit(solution)/shard_map/ppermute | solution.py:32
  63.5 0.0 collective-permute-done.4
  63.5 0.0 collective-permute-done.5
  63.6 0.3 add_add_fusion
  63.9 2.4 %convolution_convert_fusion = bf16[1024,512]{1,0:T(8,128)(2,1)S(1)} fusion(bf16[2048,1024]{1,0:T(8,128)(2,1)S(1)} %pad_maximum_fusion, bf16[2048,512]{1,0:T(8,128)(2,1)S(1)} %add_add_fusion), kind=kOutput, calls=%fused_computation.7 | convolution fusion | flops 2148007936 | bytes 7340032 | tf_op jit(solution)/shard_map/dot_general | solution.py:54
  66.2 0.1 fusion.12
  66.3 2.8 %collective-permute-start.7 = (bf16[512,512]{1,0:T(8,128)(2,1)S(1)}, bf16[512,512]{1,0:T(8,128)(2,1)S(1)}, u32[]{:S(2)}, u32[]{:S(2)}) collective-permute-start(bf16[512,512]{1,0:T(8,128)(2,1)S(1)} %get-tuple-element.15), channel_id=1, source_target_pairs={{0,2},{2,0},{4,6},{6,4},{8,10},{10,8},{12,14},{14,12},{16,18},{18,... | collective-permute-start | bytes 1572872 | tf_op jit(solution)/shard_map/ppermute | solution.py:32
  69.1 1.6 %collective-permute-start.9 = (bf16[256,512]{1,0:T(8,128)(2,1)S(1)}, bf16[256,512]{1,0:T(8,128)(2,1)S(1)}, u32[]{:S(2)}, u32[]{:S(2)}) collective-permute-start(bf16[256,512]{1,0:T(8,128)(2,1)S(1)} %dynamic-slice_bitcast_fusion), channel_id=1, source_target_pairs={{0,1},{1,0},{2,3},{3,2},{4,5},{5,4},{6,7},{7,6},{8,9},{9,8},{10,11... | collective-permute-start | bytes 786440 | tf_op jit(solution)/shard_map/ppermute | solution.py:17
  70.7 0.0 collective-permute-done.7
  70.7 0.0 copy-start.1
  70.7 1.5 %collective-permute-start.8 = (bf16[256,512]{1,0:T(8,128)(2,1)S(1)}, bf16[256,512]{1,0:T(8,128)(2,1)}, u32[]{:S(2)}, u32[]{:S(2)}) collective-permute-start(bf16[256,512]{1,0:T(8,128)(2,1)S(1)} %dynamic-slice_bitcast_fusion.1), channel_id=1, source_target_pairs={{0,1},{1,0},{2,3},{3,2},{4,5},{5,4},{6,7},{7,6},{8,9},{9,8},{10,11... | collective-permute-start | bytes 786440 | tf_op jit(solution)/shard_map/ppermute | solution.py:17
  72.9 0.1 select_bitcast_fusion
  73.0 5.4 %collective-permute-done.9 = bf16[256,512]{1,0:T(8,128)(2,1)S(1)} collective-permute-done((bf16[256,512]{1,0:T(8,128)(2,1)S(1)}, bf16[256,512]{1,0:T(8,128)(2,1)S(1)}, u32[]{:S(2)}, u32[]{:S(2)}) %collective-permute-start.9) | collective-permute-done | bytes 262176 | tf_op jit(solution)/shard_map/ppermute | solution.py:17
  78.4 4.8 %collective-permute-done.8 = bf16[256,512]{1,0:T(8,128)(2,1)} collective-permute-done((bf16[256,512]{1,0:T(8,128)(2,1)S(1)}, bf16[256,512]{1,0:T(8,128)(2,1)}, u32[]{:S(2)}, u32[]{:S(2)}) %collective-permute-start.8) | collective-permute-done | bytes 262176 | tf_op jit(solution)/shard_map/ppermute | solution.py:17
  83.1 0.0 copy-done.1
  83.1 1.3 %fusion.6 = (f32[256,512]{1,0:T(8,128)S(1)}, f32[256,512]{1,0:T(8,128)S(1)}, f32[256,512]{1,0:T(8,128)S(1)}) fusion(f32[2,256,512]{2,1,0:T(8,128)S(1)} %convert_add_fusion, bf16[256,512]{1,0:T(8,128)(2,1)} %collective-permute-done.8, bf16[256,512]{1,0:T(8,128)(2,1)S(1)} %collective-permute-done.9, pred[]{:T(512)S(6)} %eq.23, pred[]{:T(512)S(6)} %eq.22, ...), kind=kLoop, calls=%fused_computation.25 | loop fusion | flops 2228224 | bytes 3145740 | tf_op jit(solution)/shard_map/jit(_where)/select_n | solution.py:117
  84.5 1.5 %pad_maximum_fusion.1 = f32[256,2048]{1,0:T(8,128)} fusion(f32[256,512]{1,0:T(8,128)S(1)} %get-tuple-element.12, f32[256,512]{1,0:T(8,128)S(1)} %get-tuple-element.13, f32[256,512]{1,0:T(8,128)S(1)} %get-tuple-element.11, f32[256,512]{1,0:T(8,128)S(1)} %select_bitcast_fusion), kind=kLoop, calls=%fused_computation.4 | loop fusion | flops 1572864 | bytes 4194304 | tf_op jit(solution)/shard_map/concatenate | solution.py:118
  (5 shorter events, 0.1 us)
Async XLA Ops:
  0.7 3.4 %copy-start = (f32[2048,512]{1,0:T(8,128)S(1)}, f32[2048,512]{1,0:T(8,128)}, u32[]{:S(2)}) copy-start(f32[2048,512]{1,0:T(8,128)} %param.2) | copy-start | bytes 12582916
  4.2 4.6 %collective-permute-start = (f32[2,512]{1,0:T(2,128)S(1)}, f32[2,512]{1,0:T(2,128)S(1)}, u32[]{:S(2)}, u32[]{:S(2)}) collective-permute-start(f32[2,512]{1,0:T(2,128)S(1)} %pad_maximum_fusion.2), channel_id=1, source_target_pairs={{0,1},{1,0},{2,3},{3,2},{4,5},{5,4},{6,7},{7,6},{8,9},{9,8},{10,11... | collective-permute-start | bytes 12296 | tf_op jit(solution)/shard_map/ppermute | solution.py:17
  9.4 9.3 %collective-permute-start.1 = (bf16[2048,512]{1,0:T(8,128)(2,1)S(1)}, bf16[2048,512]{1,0:T(8,128)(2,1)}, u32[]{:S(2)}, u32[]{:S(2)}) collective-permute-start(bf16[2048,512]{1,0:T(8,128)(2,1)S(1)} %multiply_convert_fusion), channel_id=1, source_target_pairs={{4,2},{6,4},{2,0},{12,10},{14,12},{10,8},{20,18},{22,20},{18,16},{... | collective-permute-start | bytes 6291464 | tf_op jit(solution)/shard_map/ppermute | solution.py:32
  10.7 8.9 %collective-permute-start.2 = (bf16[2048,512]{1,0:T(8,128)(2,1)S(1)}, bf16[2048,512]{1,0:T(8,128)(2,1)}, u32[]{:S(2)}, u32[]{:S(2)}) collective-permute-start(bf16[2048,512]{1,0:T(8,128)(2,1)S(1)} %multiply_convert_fusion), channel_id=1, source_target_pairs={{0,2},{4,6},{2,8},{6,12},{8,10},{12,14},{10,16},{14,20},{16,18},{2... | collective-permute-start | bytes 6291464 | tf_op jit(solution)/shard_map/ppermute | solution.py:32
  15.1 48.5 %collective-permute-start.6 = (bf16[2048,512]{1,0:T(8,128)(2,1)S(1)}, bf16[2048,512]{1,0:T(8,128)(2,1)S(1)}, u32[]{:S(2)}, u32[]{:S(2)}) collective-permute-start(bf16[2048,512]{1,0:T(8,128)(2,1)S(1)} %multiply_convert_fusion), channel_id=1, source_target_pairs={{2,4},{0,6},{10,12},{8,14},{18,20},{16,22},{26,28},{24,30},{3,5},{... | collective-permute-start | bytes 6291464 | tf_op jit(solution)/shard_map/ppermute | solution.py:32
  18.8 44.8 %collective-permute-start.4 = (bf16[2048,512]{1,0:T(8,128)(2,1)}, bf16[2048,512]{1,0:T(8,128)(2,1)S(1)}, u32[]{:S(2)}, u32[]{:S(2)}) collective-permute-start(bf16[2048,512]{1,0:T(8,128)(2,1)} %collective-permute-done.1), channel_id=1, source_target_pairs={{2,8},{10,16},{18,24},{3,9},{11,17},{19,25}} | collective-permute-start | bytes 6291464 | tf_op jit(solution)/shard_map/ppermute | solution.py:32
  19.6 44.0 %collective-permute-start.5 = (bf16[2048,512]{1,0:T(8,128)(2,1)}, bf16[2048,512]{1,0:T(8,128)(2,1)S(1)}, u32[]{:S(2)}, u32[]{:S(2)}) collective-permute-start(bf16[2048,512]{1,0:T(8,128)(2,1)} %collective-permute-done.2), channel_id=1, source_target_pairs={{4,2},{12,10},{20,18},{28,26},{5,3},{13,11},{21,19},{29,27}} | collective-permute-start | bytes 6291464 | tf_op jit(solution)/shard_map/ppermute | solution.py:32
  24.6 9.2 %collective-permute-start.3 = (bf16[2,256,512]{2,1,0:T(8,128)(2,1)S(1)}, bf16[2,256,512]{2,1,0:T(8,128)(2,1)S(1)}, u32[]{:S(2)}, u32[]{:S(2)}) collective-permute-start(bf16[2,256,512]{2,1,0:T(8,128)(2,1)S(1)} %fusion.1), channel_id=1, source_target_pairs={{0,1},{1,0},{2,3},{3,2},{4,5},{5,4},{6,7},{7,6},{8,9},{9,8},{10,11... | collective-permute-start | bytes 1572872 | tf_op jit(solution)/shard_map/ppermute | solution.py:17
  66.3 4.4 %collective-permute-start.7 = (bf16[512,512]{1,0:T(8,128)(2,1)S(1)}, bf16[512,512]{1,0:T(8,128)(2,1)S(1)}, u32[]{:S(2)}, u32[]{:S(2)}) collective-permute-start(bf16[512,512]{1,0:T(8,128)(2,1)S(1)} %get-tuple-element.15), channel_id=1, source_target_pairs={{0,2},{2,0},{4,6},{6,4},{8,10},{10,8},{12,14},{14,12},{16,18},{18,... | collective-permute-start | bytes 1572872 | tf_op jit(solution)/shard_map/ppermute | solution.py:32
  69.1 9.2 %collective-permute-start.9 = (bf16[256,512]{1,0:T(8,128)(2,1)S(1)}, bf16[256,512]{1,0:T(8,128)(2,1)S(1)}, u32[]{:S(2)}, u32[]{:S(2)}) collective-permute-start(bf16[256,512]{1,0:T(8,128)(2,1)S(1)} %dynamic-slice_bitcast_fusion), channel_id=1, source_target_pairs={{0,1},{1,0},{2,3},{3,2},{4,5},{5,4},{6,7},{7,6},{8,9},{9,8},{10,11... | collective-permute-start | bytes 786440 | tf_op jit(solution)/shard_map/ppermute | solution.py:17
  70.7 12.4 %copy-start.1 = (bf16[512,512]{1,0:T(8,128)(2,1)}, bf16[512,512]{1,0:T(8,128)(2,1)S(1)}, u32[]{:S(2)}) copy-start(bf16[512,512]{1,0:T(8,128)(2,1)S(1)} %collective-permute-done.7) | copy-start | bytes 1572868
  70.7 12.4 %collective-permute-start.8 = (bf16[256,512]{1,0:T(8,128)(2,1)S(1)}, bf16[256,512]{1,0:T(8,128)(2,1)}, u32[]{:S(2)}, u32[]{:S(2)}) collective-permute-start(bf16[256,512]{1,0:T(8,128)(2,1)S(1)} %dynamic-slice_bitcast_fusion.1), channel_id=1, source_target_pairs={{0,1},{1,0},{2,3},{3,2},{4,5},{5,4},{6,7},{7,6},{8,9},{9,8},{10,11... | collective-permute-start | bytes 786440 | tf_op jit(solution)/shard_map/ppermute | solution.py:17

commit v12 on v11

--- a/solution.py
+++ b/solution.py
@@ -46,8 +46,28 @@
     rhs = lax.optimization_barrier(relay + cross)
     product = tile_term(both, rhs).astype(jnp.bfloat16)
     own_late = product[:width]
-    handed = send(product[width:], pairs_of((0, 1), (1, 0), (2, 3), (3, 2)))
+    handed = to_partner(product[width:], count)
     return early, own_late, handed
+
+
+def to_partner(partial, count):
+    n_smp = lax.axis_size("smp")
+    me = lax.axis_index("smp")
+    width = partial.shape[1]
+    share = width // n_smp
+    pieces = partial.reshape(n_smp, share, width)
+    partners = [(b + s, b + t) for b in range(0, count, 4) for s, t in ((0, 1), (1, 0), (2, 3), (3, 2))]
+    partners = [(s, t) for s, t in partners if t < count]
+    total = lax.ppermute(
+        lax.dynamic_index_in_dim(pieces, me, 0, keepdims=False), "snp", partners
+    ).astype(jnp.float32)
+    for step in range(1, n_smp):
+        outgoing = lax.dynamic_index_in_dim(pieces, (me + step) % n_smp, 0, keepdims=False)
+        pairs = [
+            (s * n_smp + k, t * n_smp + (k + step) % n_smp) for s, t in partners for k in range(n_smp)
+        ]
+        total = total + lax.ppermute(outgoing, ("snp", "smp"), pairs).astype(jnp.float32)
+    return total
 
 
 def tile_term(standard, neighbour):
@@ -101,7 +121,7 @@
         early, own_late, handed = relayed(
             standard, count, place, lambda with_a: exchanged(jnp.stack([first, with_a]))
         )
-        late = [exchanged(own_late), exchanged(handed)]
+        late = [exchanged(own_late), handed]
         totals = [
             early[0],
             jnp.where(place == 0, late[1], jnp.where(place == 2, late[0], early[1])),

time: 86.3 us -> 85.9 us (level)
  starting transfers between devices: 21.4 us -> 20 us
  waiting for transfers between devices: 46.5 us -> 47.6 us
    ppermute x0 -> x2, waiting for transfers between devices: none -> 5.43 us  [the longest x1 5.43 us: to_partner(): lax.ppermute(outgoing, ('snp', 'smp'), pairs).astype(jnp.float32)]
    ppermute x4 -> x3, waiting for transfers between devices: 17 us -> 12.6 us  [rotated(): lax.ppermute(value, axis, [(source, (source + steps) % count) for source...]
    ppermute x0 -> x2, starting transfers between devices: none -> 3.89 us  [the longest x1 3.88 us: to_partner(): lax.ppermute(outgoing, ('snp', 'smp'), pairs).astype(jnp.float32)]
    ppermute x6 -> x5, starting transfers between devices: 13.7 us -> 10.9 us  [send(): return lax.ppermute(value, 'snp', pairs)]
    ppermute x4 -> x3, starting transfers between devices: 7.71 us -> 5.19 us  [rotated(): lax.ppermute(value, axis, [(source, (source + steps) % count) for source...]
    ppermute x6 -> x5, waiting for transfers between devices: 29.5 us -> 29.5 us  [send(): return lax.ppermute(value, 'snp', pairs)]
where the time goes in v12:
time: 85.9 us; the launch traced here: 85.6 us
  waiting for transfers between devices  47.6 us (55%)
  starting transfers between devices  20 us (23%)
  other arithmetic  9.34 us (11%)
  matrix products  6.52 us (8%)
  local copies, waits for them, and re-layouts  1.36 us (2%)
    ppermute x5, waiting for transfers between devices, send(): return lax.ppermute(value, 'snp', pairs)  29.5 us
    ppermute x3, waiting for transfers between devices, rotated(): lax.ppermute(value, axis, [(source, (source + steps) % count) for source...  12.6 us
    ppermute x5, starting transfers between devices, send(): return lax.ppermute(value, 'snp', pairs)  10.9 us
    dot_general x3, matrix products, tile_term(): lax.dot_general(standard, neighbour, (((0,), (0,)), ((), ())), preferred_...  6.52 us
    ppermute x1, waiting for transfers between devices, to_partner(): lax.ppermute(outgoing, ('snp', 'smp'), pairs).astype(jnp.float32)  5.43 us
    ppermute x3, starting transfers between devices, rotated(): lax.ppermute(value, axis, [(source, (source + steps) % count) for source...  5.19 us
    ppermute x1, starting transfers between devices, to_partner(): lax.ppermute(outgoing, ('snp', 'smp'), pairs).astype(jnp.float32)  3.88 us
    reduce_sum x1, other arithmetic, local(): part_square = jnp.sum(shifted_dosage * shifted_dosage, axis=0)  2.94 us
  transfers between devices with their start and end apart: 10, of which 5 were waited for; matrix products, arithmetic and copies ran while one was open for 8% of the time, Pallas kernels for 0%

profile of v12, /device:TPU:0, one launch (start us, length us, event | category | flops | bytes accessed | tf_op | source)
XLA Modules:
  0.0 85.6 jit_solution(5757217633034656047)
XLA Ops:
  0.0 0.7 slice.23
  0.7 0.0 copy-start
  0.7 2.9 %multiply_reduce_fusion = (f32[512]{0:T(512)S(1)}, f32[512]{0:T(512)S(1)}) fusion(f32[2048,512]{1,0:T(8,128)} %param.2, f32[512]{0:T(512)S(1)} %bitcast.67), kind=kLoop, calls=%fused_computation.2 | loop fusion | flops 4193280 | bytes 4200448 | tf_op jit(solution)/shard_map/reduce_sum | solution.py:88
  3.7 0.5 copy-done
  4.2 3.0 %collective-permute-start = (f32[2,512]{1,0:T(2,128)S(1)}, f32[2,512]{1,0:T(2,128)S(1)}, u32[]{:S(2)}, u32[]{:S(2)}) collective-permute-start(f32[2,512]{1,0:T(2,128)S(1)} %pad_maximum_fusion.2), channel_id=1, source_target_pairs={{0,1},{1,0},{2,3},{3,2},{4,5},{5,4},{6,7},{7,6},{8,9},{9,8},{10,11... | collective-permute-start | bytes 12296 | tf_op jit(solution)/shard_map/ppermute | solution.py:17
  7.2 1.6 %collective-permute-done = f32[2,512]{1,0:T(2,128)S(1)} collective-permute-done((f32[2,512]{1,0:T(2,128)S(1)}, f32[2,512]{1,0:T(2,128)S(1)}, u32[]{:S(2)}, u32[]{:S(2)}) %collective-permute-start) | collective-permute-done | bytes 4128 | tf_op jit(solution)/shard_map/ppermute | solution.py:17
  8.8 0.6 multiply_convert_fusion
  9.4 1.3 %collective-permute-start.1 = (bf16[2048,512]{1,0:T(8,128)(2,1)S(1)}, bf16[2048,512]{1,0:T(8,128)(2,1)}, u32[]{:S(2)}, u32[]{:S(2)}) collective-permute-start(bf16[2048,512]{1,0:T(8,128)(2,1)S(1)} %multiply_convert_fusion), channel_id=1, source_target_pairs={{4,2},{6,4},{2,0},{12,10},{14,12},{10,8},{20,18},{22,20},{18,16},{... | collective-permute-start | bytes 6291464 | tf_op jit(solution)/shard_map/ppermute | solution.py:32
  10.7 4.4 %collective-permute-start.2 = (bf16[2048,512]{1,0:T(8,128)(2,1)S(1)}, bf16[2048,512]{1,0:T(8,128)(2,1)}, u32[]{:S(2)}, u32[]{:S(2)}) collective-permute-start(bf16[2048,512]{1,0:T(8,128)(2,1)S(1)} %multiply_convert_fusion), channel_id=1, source_target_pairs={{0,2},{4,6},{2,8},{6,12},{8,10},{12,14},{10,16},{14,20},{16,18},{2... | collective-permute-start | bytes 6291464 | tf_op jit(solution)/shard_map/ppermute | solution.py:32
  15.1 3.7 %collective-permute-start.6 = (bf16[2048,512]{1,0:T(8,128)(2,1)S(1)}, bf16[2048,512]{1,0:T(8,128)(2,1)S(1)}, u32[]{:S(2)}, u32[]{:S(2)}) collective-permute-start(bf16[2048,512]{1,0:T(8,128)(2,1)S(1)} %multiply_convert_fusion), channel_id=1, source_target_pairs={{2,4},{0,6},{10,12},{8,14},{18,20},{16,22},{26,28},{24,30},{3,5},{... | collective-permute-start | bytes 6291464 | tf_op jit(solution)/shard_map/ppermute | solution.py:32
  18.8 0.0 collective-permute-done.1
  18.8 0.8 collective-permute-start.4
  19.6 0.0 collective-permute-done.2
  19.6 0.8 collective-permute-start.5
  20.4 1.3 %convolution_convert_fusion.2 = bf16[512,512]{1,0:T(8,128)(2,1)S(1)} fusion(bf16[2048,512]{1,0:T(8,128)(2,1)S(1)} %multiply_convert_fusion), kind=kOutput, calls=%fused_computation.9 | convolution fusion | flops 1074003968 | bytes 2621440 | tf_op jit(solution)/shard_map/dot_general | solution.py:74
  21.7 2.9 %convolution_convert_fusion.1 = bf16[512,512]{1,0:T(8,128)(2,1)S(1)} fusion(bf16[2048,512]{1,0:T(8,128)(2,1)S(1)} %multiply_convert_fusion, bf16[2048,512]{1,0:T(8,128)(2,1)} %collective-permute-done.2), kind=kOutput, calls=%fused_computation.8 | convolution fusion | flops 1074003968 | bytes 4718592 | tf_op jit(solution)/shard_map/dot_general | solution.py:74
  24.5 0.1 fusion.1
  24.6 1.6 %collective-permute-start.3 = (bf16[2,256,512]{2,1,0:T(8,128)(2,1)S(1)}, bf16[2,256,512]{2,1,0:T(8,128)(2,1)S(1)}, u32[]{:S(2)}, u32[]{:S(2)}) collective-permute-start(bf16[2,256,512]{2,1,0:T(8,128)(2,1)S(1)} %fusion.1), channel_id=1, source_target_pairs={{0,1},{1,0},{2,3},{3,2},{4,5},{5,4},{6,7},{7,6},{8,9},{9,8},{10,11... | collective-permute-start | bytes 1572872 | tf_op jit(solution)/shard_map/ppermute | solution.py:17
  26.2 1.8 %broadcast_select_fusion = bf16[2048,512]{1,0:T(8,128)(2,1)S(1)} fusion(bf16[2048,512]{1,0:T(8,128)(2,1)} %collective-permute-done.1, bf16[2048,512]{1,0:T(8,128)(2,1)} %collective-permute-done.2, pred[]{:T(512)S(6)} %eq.21), kind=kLoop, calls=%fused_computation.6 | loop fusion | flops 1048576 | bytes 6291457 | tf_op jit(solution)/shard_map/jit(_where)/select_n | solution.py:44
  28.0 0.6 pad_maximum_fusion
  28.7 5.2 %collective-permute-done.3 = bf16[2,256,512]{2,1,0:T(8,128)(2,1)S(1)} collective-permute-done((bf16[2,256,512]{2,1,0:T(8,128)(2,1)S(1)}, bf16[2,256,512]{2,1,0:T(8,128)(2,1)S(1)}, u32[]{:S(2)}, u32[]{:S(2)}) %collective-permute-start.3) | collective-permute-done | bytes 524320 | tf_op jit(solution)/shard_map/ppermute | solution.py:17
  33.9 0.2 convert_add_fusion
  34.0 29.5 %collective-permute-done.6 = bf16[2048,512]{1,0:T(8,128)(2,1)S(1)} collective-permute-done((bf16[2048,512]{1,0:T(8,128)(2,1)S(1)}, bf16[2048,512]{1,0:T(8,128)(2,1)S(1)}, u32[]{:S(2)}, u32[]{:S(2)}) %collective-permute-start.6) | collective-permute-done | bytes 2097184 | tf_op jit(solution)/shard_map/ppermute | solution.py:32
  63.5 0.0 collective-permute-done.4
  63.5 0.0 collective-permute-done.5
  63.6 0.3 add_add_fusion
  63.9 2.4 %convolution_convert_fusion = bf16[1024,512]{1,0:T(8,128)(2,1)S(1)} fusion(bf16[2048,1024]{1,0:T(8,128)(2,1)S(1)} %pad_maximum_fusion, bf16[2048,512]{1,0:T(8,128)(2,1)S(1)} %add_add_fusion), kind=kOutput, calls=%fused_computation.7 | convolution fusion | flops 2148007936 | bytes 7340032 | tf_op jit(solution)/shard_map/dot_general | solution.py:74
  66.2 0.1 fusion.12
  66.4 3.9 %collective-permute-start.8 = (bf16[256,512]{1,0:T(8,128)(2,1)S(1)}, bf16[256,512]{1,0:T(8,128)(2,1)S(1)}, u32[]{:S(2)}, u32[]{:S(2)}) collective-permute-start(bf16[256,512]{1,0:T(8,128)(2,1)S(1)} %get-tuple-element.17), channel_id=1, source_target_pairs={{0,3},{1,2},{2,1},{3,0},{4,7},{5,6},{6,5},{7,4},{8,11},{9,10},{10,... | collective-permute-start | bytes 786440 | tf_op jit(solution)/shard_map/ppermute | solution.py:69
  70.3 0.0 collective-permute-start.7
  70.3 0.6 collective-permute-start.9
  71.5 0.1 select_bitcast_fusion
  71.6 5.4 %collective-permute-done.8 = bf16[256,512]{1,0:T(8,128)(2,1)S(1)} collective-permute-done((bf16[256,512]{1,0:T(8,128)(2,1)S(1)}, bf16[256,512]{1,0:T(8,128)(2,1)S(1)}, u32[]{:S(2)}, u32[]{:S(2)}) %collective-permute-start.8) | collective-permute-done | bytes 262176 | tf_op jit(solution)/shard_map/ppermute | solution.py:69
  77.0 0.0 collective-permute-done.7
  77.0 5.8 %collective-permute-done.9 = bf16[256,512]{1,0:T(8,128)(2,1)} collective-permute-done((bf16[256,512]{1,0:T(8,128)(2,1)S(1)}, bf16[256,512]{1,0:T(8,128)(2,1)}, u32[]{:S(2)}, u32[]{:S(2)}) %collective-permute-start.9) | collective-permute-done | bytes 262176 | tf_op jit(solution)/shard_map/ppermute | solution.py:17
  82.9 1.2 %fusion.6 = (f32[256,512]{1,0:T(8,128)S(1)}, f32[256,512]{1,0:T(8,128)S(1)}, f32[256,512]{1,0:T(8,128)S(1)}) fusion(f32[2,256,512]{2,1,0:T(8,128)S(1)} %convert_add_fusion, bf16[256,512]{1,0:T(8,128)(2,1)S(1)} %collective-permute-done.8, bf16[256,512]{1,0:T(8,128)(2,1)S(1)} %collective-permute-done.7, bf16[256,512]{1,0:T(8,128)(2,1)} %collective-permute-done.9, ...), kind=kLoop, calls=%fused_computation.24 | loop fusion | flops 2228224 | bytes 3145740 | tf_op jit(solution)/shard_map/jit(_where)/select_n | solution.py:137
  84.1 1.5 %pad_maximum_fusion.1 = f32[256,2048]{1,0:T(8,128)} fusion(f32[256,512]{1,0:T(8,128)S(1)} %get-tuple-element.12, f32[256,512]{1,0:T(8,128)S(1)} %get-tuple-element.13, f32[256,512]{1,0:T(8,128)S(1)} %get-tuple-element.11, f32[256,512]{1,0:T(8,128)S(1)} %select_bitcast_fusion), kind=kLoop, calls=%fused_computation.4 | loop fusion | flops 1572864 | bytes 4194304 | tf_op jit(solution)/shard_map/concatenate | solution.py:138
  (5 shorter events, 0.1 us)
Async XLA Ops:
  0.7 3.4 %copy-start = (f32[2048,512]{1,0:T(8,128)S(1)}, f32[2048,512]{1,0:T(8,128)}, u32[]{:S(2)}) copy-start(f32[2048,512]{1,0:T(8,128)} %param.2) | copy-start | bytes 12582916
  4.2 4.6 %collective-permute-start = (f32[2,512]{1,0:T(2,128)S(1)}, f32[2,512]{1,0:T(2,128)S(1)}, u32[]{:S(2)}, u32[]{:S(2)}) collective-permute-start(f32[2,512]{1,0:T(2,128)S(1)} %pad_maximum_fusion.2), channel_id=1, source_target_pairs={{0,1},{1,0},{2,3},{3,2},{4,5},{5,4},{6,7},{7,6},{8,9},{9,8},{10,11... | collective-permute-start | bytes 12296 | tf_op jit(solution)/shard_map/ppermute | solution.py:17
  9.4 9.3 %collective-permute-start.1 = (bf16[2048,512]{1,0:T(8,128)(2,1)S(1)}, bf16[2048,512]{1,0:T(8,128)(2,1)}, u32[]{:S(2)}, u32[]{:S(2)}) collective-permute-start(bf16[2048,512]{1,0:T(8,128)(2,1)S(1)} %multiply_convert_fusion), channel_id=1, source_target_pairs={{4,2},{6,4},{2,0},{12,10},{14,12},{10,8},{20,18},{22,20},{18,16},{... | collective-permute-start | bytes 6291464 | tf_op jit(solution)/shard_map/ppermute | solution.py:32
  10.7 8.9 %collective-permute-start.2 = (bf16[2048,512]{1,0:T(8,128)(2,1)S(1)}, bf16[2048,512]{1,0:T(8,128)(2,1)}, u32[]{:S(2)}, u32[]{:S(2)}) collective-permute-start(bf16[2048,512]{1,0:T(8,128)(2,1)S(1)} %multiply_convert_fusion), channel_id=1, source_target_pairs={{0,2},{4,6},{2,8},{6,12},{8,10},{12,14},{10,16},{14,20},{16,18},{2... | collective-permute-start | bytes 6291464 | tf_op jit(solution)/shard_map/ppermute | solution.py:32
  15.1 48.5 %collective-permute-start.6 = (bf16[2048,512]{1,0:T(8,128)(2,1)S(1)}, bf16[2048,512]{1,0:T(8,128)(2,1)S(1)}, u32[]{:S(2)}, u32[]{:S(2)}) collective-permute-start(bf16[2048,512]{1,0:T(8,128)(2,1)S(1)} %multiply_convert_fusion), channel_id=1, source_target_pairs={{2,4},{0,6},{10,12},{8,14},{18,20},{16,22},{26,28},{24,30},{3,5},{... | collective-permute-start | bytes 6291464 | tf_op jit(solution)/shard_map/ppermute | solution.py:32
  18.8 44.8 %collective-permute-start.4 = (bf16[2048,512]{1,0:T(8,128)(2,1)}, bf16[2048,512]{1,0:T(8,128)(2,1)S(1)}, u32[]{:S(2)}, u32[]{:S(2)}) collective-permute-start(bf16[2048,512]{1,0:T(8,128)(2,1)} %collective-permute-done.1), channel_id=1, source_target_pairs={{2,8},{10,16},{18,24},{3,9},{11,17},{19,25}} | collective-permute-start | bytes 6291464 | tf_op jit(solution)/shard_map/ppermute | solution.py:32
  19.6 44.0 %collective-permute-start.5 = (bf16[2048,512]{1,0:T(8,128)(2,1)}, bf16[2048,512]{1,0:T(8,128)(2,1)S(1)}, u32[]{:S(2)}, u32[]{:S(2)}) collective-permute-start(bf16[2048,512]{1,0:T(8,128)(2,1)} %collective-permute-done.2), channel_id=1, source_target_pairs={{4,2},{12,10},{20,18},{28,26},{5,3},{13,11},{21,19},{29,27}} | collective-permute-start | bytes 6291464 | tf_op jit(solution)/shard_map/ppermute | solution.py:32
  24.6 9.2 %collective-permute-start.3 = (bf16[2,256,512]{2,1,0:T(8,128)(2,1)S(1)}, bf16[2,256,512]{2,1,0:T(8,128)(2,1)S(1)}, u32[]{:S(2)}, u32[]{:S(2)}) collective-permute-start(bf16[2,256,512]{2,1,0:T(8,128)(2,1)S(1)} %fusion.1), channel_id=1, source_target_pairs={{0,1},{1,0},{2,3},{3,2},{4,5},{5,4},{6,7},{7,6},{8,9},{9,8},{10,11... | collective-permute-start | bytes 1572872 | tf_op jit(solution)/shard_map/ppermute | solution.py:17
  66.4 10.6 %collective-permute-start.8 = (bf16[256,512]{1,0:T(8,128)(2,1)S(1)}, bf16[256,512]{1,0:T(8,128)(2,1)S(1)}, u32[]{:S(2)}, u32[]{:S(2)}) collective-permute-start(bf16[256,512]{1,0:T(8,128)(2,1)S(1)} %get-tuple-element.17), channel_id=1, source_target_pairs={{0,3},{1,2},{2,1},{3,0},{4,7},{5,6},{6,5},{7,4},{8,11},{9,10},{10,... | collective-permute-start | bytes 786440 | tf_op jit(solution)/shard_map/ppermute | solution.py:69
  70.3 6.8 %collective-permute-start.7 = (bf16[256,512]{1,0:T(8,128)(2,1)S(1)}, bf16[256,512]{1,0:T(8,128)(2,1)S(1)}, u32[]{:S(2)}, u32[]{:S(2)}) collective-permute-start(bf16[256,512]{1,0:T(8,128)(2,1)S(1)} %get-tuple-element.16), channel_id=1, source_target_pairs={{0,2},{2,0},{4,6},{6,4},{8,10},{10,8},{12,14},{14,12},{16,18},{18,... | collective-permute-start | bytes 786440 | tf_op jit(solution)/shard_map/ppermute | solution.py:61
  70.3 12.6 %collective-permute-start.9 = (bf16[256,512]{1,0:T(8,128)(2,1)S(1)}, bf16[256,512]{1,0:T(8,128)(2,1)}, u32[]{:S(2)}, u32[]{:S(2)}) collective-permute-start(bf16[256,512]{1,0:T(8,128)(2,1)S(1)} %dynamic-slice_bitcast_fusion), channel_id=1, source_target_pairs={{0,1},{1,0},{2,3},{3,2},{4,5},{5,4},{6,7},{7,6},{8,9},{9,8},{10,11... | collective-permute-start | bytes 786440 | tf_op jit(solution)/shard_map/ppermute | solution.py:17

commit v13 on v12

--- a/solution.py
+++ b/solution.py
@@ -121,13 +121,26 @@
         early, own_late, handed = relayed(
             standard, count, place, lambda with_a: exchanged(jnp.stack([first, with_a]))
         )
-        late = [exchanged(own_late), handed]
-        totals = [
-            early[0],
-            jnp.where(place == 0, late[1], jnp.where(place == 2, late[0], early[1])),
-            jnp.where(place < 2, late[0], late[1]),
-            jnp.where(place == 1, late[1], jnp.where(place == 3, late[0], early[1])),
-        ]
+        late_own = exchanged(own_late)
+
+        def scaled(tile, dist):
+            return jnp.where(dist <= own_reach, tile / samples, jnp.zeros_like(tile))
+
+        odd = place % 2 == 1
+        blank = jnp.zeros_like(early[0])
+        out = jnp.concatenate(
+            [
+                scaled(early[0], 0),
+                jnp.where(odd, scaled(early[1], 1), blank),
+                blank,
+                jnp.where(odd, blank, scaled(early[1], 3)),
+            ],
+            axis=1,
+        )
+        own_tap = jnp.where(place < 2, 2, jnp.where(place == 2, 1, 3))
+        hand_tap = jnp.where(place == 0, 1, jnp.where(place == 1, 3, 2))
+        out = lax.dynamic_update_slice(out, scaled(late_own, own_tap), (0, own_tap * width))
+        return lax.dynamic_update_slice(out, scaled(handed, hand_tap), (0, hand_tap * width))
     else:
         rest = [tile_term(standard, nb).astype(jnp.bfloat16) for nb in chained(standard)]
         totals = list(exchanged(jnp.stack([first] + rest)))

time: 85.9 us -> 83 us (0.966)
  starting transfers between devices: 20 us -> 18.4 us
  other arithmetic: 9.34 us -> 7.88 us
    ppermute x1, starting transfers between devices: 3.88 us -> 0.47 us  [to_partner(): lax.ppermute(outgoing, ('snp', 'smp'), pairs).astype(jnp.float32)]
    concatenate x1, other arithmetic: 1.5 us -> 0.15 us  [local(): jnp.concatenate([scaled(early[0], 0), jnp.where(odd, scaled(early[1], 1),...]
    select_n x2 -> x1, other arithmetic: 1.3 us -> 0.21 us  [scaled(): return jnp.where(dist <= own_reach, tile / samples, jnp.zeros_like(tile))]
    ppermute x3, starting transfers between devices: 5.19 us -> 6.2 us  [rotated(): lax.ppermute(value, axis, [(source, (source + steps) % count) for source...]
    dynamic_update_slice x0 -> x2, other arithmetic: none -> 0.98 us  [the longest x1 0.88 us: local(): lax.dynamic_update_slice(out, scaled(handed, hand_tap), (0, hand_tap * wi...]
    ppermute x1, waiting for transfers between devices: 5.43 us -> 4.55 us  [to_partner(): lax.ppermute(outgoing, ('snp', 'smp'), pairs).astype(jnp.float32)]
  transfers between devices with their start and end apart: 10 -> 10, of which waited for: 5 -> 5; matrix products, arithmetic and copies ran while one was open for 8% -> 9% of each run, Pallas kernels for 0% -> 0%
where the time goes in v13:
time: 83 us; the launch traced here: 82.7 us
  waiting for transfers between devices  47.6 us (57%)
  starting transfers between devices  18.4 us (22%)
  other arithmetic  7.88 us (9%)
  matrix products  6.52 us (8%)
  local copies, waits for them, and re-layouts  1.41 us (2%)
  between operations  0.9 us (1%)
    ppermute x5, waiting for transfers between devices, send(): return lax.ppermute(value, 'snp', pairs)  29.6 us
    ppermute x3, waiting for transfers between devices, rotated(): lax.ppermute(value, axis, [(source, (source + steps) % count) for source...  13.4 us
    ppermute x5, starting transfers between devices, send(): return lax.ppermute(value, 'snp', pairs)  11.5 us
    dot_general x3, matrix products, tile_term(): lax.dot_general(standard, neighbour, (((0,), (0,)), ((), ())), preferred_...  6.52 us
    ppermute x3, starting transfers between devices, rotated(): lax.ppermute(value, axis, [(source, (source + steps) % count) for source...  6.2 us
    ppermute x1, waiting for transfers between devices, to_partner(): lax.ppermute(outgoing, ('snp', 'smp'), pairs).astype(jnp.float32)  4.55 us
    reduce_sum x1, other arithmetic, local(): part_square = jnp.sum(shifted_dosage * shifted_dosage, axis=0)  2.94 us
    select_n x1, other arithmetic, relayed(): jnp.where(place % 2 == 0, fast_b, fast_a)  1.81 us
  transfers between devices with their start and end apart: 10, of which 5 were waited for; matrix products, arithmetic and copies ran while one was open for 9% of the time, Pallas kernels for 0%

profile of v13, /device:TPU:0, one launch (start us, length us, event | category | flops | bytes accessed | tf_op | source)
XLA Modules:
  0.0 82.7 jit_solution(1741676914390548818)
XLA Ops:
  0.0 0.7 slice.23
  0.7 0.0 copy-start
  0.7 2.9 %multiply_reduce_fusion = (f32[512]{0:T(512)S(1)}, f32[512]{0:T(512)S(1)}) fusion(f32[2048,512]{1,0:T(8,128)} %param.2, f32[512]{0:T(512)S(1)} %bitcast.56), kind=kLoop, calls=%fused_computation.2 | loop fusion | flops 4193280 | bytes 4200448 | tf_op jit(solution)/shard_map/reduce_sum | solution.py:88
  3.7 0.5 copy-done
  4.2 3.0 %collective-permute-start = (f32[2,512]{1,0:T(2,128)S(1)}, f32[2,512]{1,0:T(2,128)S(1)}, u32[]{:S(2)}, u32[]{:S(2)}) collective-permute-start(f32[2,512]{1,0:T(2,128)S(1)} %pad_maximum_fusion.2), channel_id=1, source_target_pairs={{0,1},{1,0},{2,3},{3,2},{4,5},{5,4},{6,7},{7,6},{8,9},{9,8},{10,11... | collective-permute-start | bytes 12296 | tf_op jit(solution)/shard_map/ppermute | solution.py:17
  7.2 1.6 %collective-permute-done = f32[2,512]{1,0:T(2,128)S(1)} collective-permute-done((f32[2,512]{1,0:T(2,128)S(1)}, f32[2,512]{1,0:T(2,128)S(1)}, u32[]{:S(2)}, u32[]{:S(2)}) %collective-permute-start) | collective-permute-done | bytes 4128 | tf_op jit(solution)/shard_map/ppermute | solution.py:17
  8.8 0.6 multiply_convert_fusion
  9.4 2.6 %collective-permute-start.2 = (bf16[2048,512]{1,0:T(8,128)(2,1)S(1)}, bf16[2048,512]{1,0:T(8,128)(2,1)}, u32[]{:S(2)}, u32[]{:S(2)}) collective-permute-start(bf16[2048,512]{1,0:T(8,128)(2,1)S(1)} %multiply_convert_fusion), channel_id=1, source_target_pairs={{0,2},{4,6},{2,8},{6,12},{8,10},{12,14},{10,16},{14,20},{16,18},{2... | collective-permute-start | bytes 6291464 | tf_op jit(solution)/shard_map/ppermute | solution.py:32
  12.1 1.3 %collective-permute-start.1 = (bf16[2048,512]{1,0:T(8,128)(2,1)S(1)}, bf16[2048,512]{1,0:T(8,128)(2,1)}, u32[]{:S(2)}, u32[]{:S(2)}) collective-permute-start(bf16[2048,512]{1,0:T(8,128)(2,1)S(1)} %multiply_convert_fusion), channel_id=1, source_target_pairs={{4,2},{6,4},{2,0},{12,10},{14,12},{10,8},{20,18},{22,20},{18,16},{... | collective-permute-start | bytes 6291464 | tf_op jit(solution)/shard_map/ppermute | solution.py:32
  14.1 6.0 %collective-permute-start.6 = (bf16[2048,512]{1,0:T(8,128)(2,1)S(1)}, bf16[2048,512]{1,0:T(8,128)(2,1)S(1)}, u32[]{:S(2)}, u32[]{:S(2)}) collective-permute-start(bf16[2048,512]{1,0:T(8,128)(2,1)S(1)} %multiply_convert_fusion), channel_id=1, source_target_pairs={{2,4},{0,6},{10,12},{8,14},{18,20},{16,22},{26,28},{24,30},{3,5},{... | collective-permute-start | bytes 6291464 | tf_op jit(solution)/shard_map/ppermute | solution.py:32
  20.1 0.0 collective-permute-done.2
  20.1 0.8 collective-permute-start.5
  20.9 0.0 collective-permute-done.1
  20.9 0.8 collective-permute-start.4
  21.7 1.3 %convolution_convert_fusion.2 = bf16[512,512]{1,0:T(8,128)(2,1)S(1)} fusion(bf16[2048,512]{1,0:T(8,128)(2,1)S(1)} %multiply_convert_fusion), kind=kOutput, calls=%fused_computation.9 | convolution fusion | flops 1074003968 | bytes 2621440 | tf_op jit(solution)/shard_map/dot_general | solution.py:74
  23.0 2.9 %convolution_convert_fusion.1 = bf16[512,512]{1,0:T(8,128)(2,1)S(1)} fusion(bf16[2048,512]{1,0:T(8,128)(2,1)S(1)} %multiply_convert_fusion, bf16[2048,512]{1,0:T(8,128)(2,1)} %collective-permute-done.2), kind=kOutput, calls=%fused_computation.8 | convolution fusion | flops 1074003968 | bytes 4718592 | tf_op jit(solution)/shard_map/dot_general | solution.py:74
  25.9 0.1 fusion.1
  25.9 1.6 %collective-permute-start.3 = (bf16[2,256,512]{2,1,0:T(8,128)(2,1)S(1)}, bf16[2,256,512]{2,1,0:T(8,128)(2,1)S(1)}, u32[]{:S(2)}, u32[]{:S(2)}) collective-permute-start(bf16[2,256,512]{2,1,0:T(8,128)(2,1)S(1)} %fusion.1), channel_id=1, source_target_pairs={{0,1},{1,0},{2,3},{3,2},{4,5},{5,4},{6,7},{7,6},{8,9},{9,8},{10,11... | collective-permute-start | bytes 1572872 | tf_op jit(solution)/shard_map/ppermute | solution.py:17
  27.5 1.8 %broadcast_select_fusion = bf16[2048,512]{1,0:T(8,128)(2,1)S(1)} fusion(bf16[2048,512]{1,0:T(8,128)(2,1)} %collective-permute-done.1, bf16[2048,512]{1,0:T(8,128)(2,1)} %collective-permute-done.2, pred[]{:T(512)S(6)} %eq.22), kind=kLoop, calls=%fused_computation.6 | loop fusion | flops 1048576 | bytes 6291457 | tf_op jit(solution)/shard_map/jit(_where)/select_n | solution.py:44
  29.3 0.6 pad_maximum_fusion
  30.0 5.2 %collective-permute-done.3 = bf16[2,256,512]{2,1,0:T(8,128)(2,1)S(1)} collective-permute-done((bf16[2,256,512]{2,1,0:T(8,128)(2,1)S(1)}, bf16[2,256,512]{2,1,0:T(8,128)(2,1)S(1)}, u32[]{:S(2)}, u32[]{:S(2)}) %collective-permute-start.3) | collective-permute-done | bytes 524320 | tf_op jit(solution)/shard_map/ppermute | solution.py:17
  35.2 0.2 convert_add_fusion
  35.3 0.2 select_bitcast_fusion.2
  35.6 29.6 %collective-permute-done.6 = bf16[2048,512]{1,0:T(8,128)(2,1)S(1)} collective-permute-done((bf16[2048,512]{1,0:T(8,128)(2,1)S(1)}, bf16[2048,512]{1,0:T(8,128)(2,1)S(1)}, u32[]{:S(2)}, u32[]{:S(2)}) %collective-permute-start.6) | collective-permute-done | bytes 2097184 | tf_op jit(solution)/shard_map/ppermute | solution.py:32
  65.1 0.0 collective-permute-done.5
  65.1 0.0 collective-permute-done.4
  65.1 0.3 add_add_fusion
  65.5 2.4 %convolution_convert_fusion = bf16[1024,512]{1,0:T(8,128)(2,1)S(1)} fusion(bf16[2048,1024]{1,0:T(8,128)(2,1)S(1)} %pad_maximum_fusion, bf16[2048,512]{1,0:T(8,128)(2,1)S(1)} %add_add_fusion), kind=kOutput, calls=%fused_computation.7 | convolution fusion | flops 2148007936 | bytes 7340032 | tf_op jit(solution)/shard_map/dot_general | solution.py:74
  67.8 0.1 fusion.9
  68.0 1.6 %collective-permute-start.7 = (bf16[256,512]{1,0:T(8,128)(2,1)S(1)}, bf16[256,512]{1,0:T(8,128)(2,1)S(1)}, u32[]{:S(2)}, u32[]{:S(2)}) collective-permute-start(bf16[256,512]{1,0:T(8,128)(2,1)S(1)} %dynamic-slice_bitcast_fusion.2), channel_id=1, source_target_pairs={{0,1},{1,0},{2,3},{3,2},{4,5},{5,4},{6,7},{7,6},{8,9},{9,8},{10,11... | collective-permute-start | bytes 786440 | tf_op jit(solution)/shard_map/ppermute | solution.py:17
  69.6 0.2 collective-permute-start.8
  69.8 0.5 collective-permute-start.9
  70.3 0.2 pad_maximum_fusion.1
  70.5 6.7 %collective-permute-done.7 = bf16[256,512]{1,0:T(8,128)(2,1)S(1)} collective-permute-done((bf16[256,512]{1,0:T(8,128)(2,1)S(1)}, bf16[256,512]{1,0:T(8,128)(2,1)S(1)}, u32[]{:S(2)}, u32[]{:S(2)}) %collective-permute-start.7) | collective-permute-done | bytes 262176 | tf_op jit(solution)/shard_map/ppermute | solution.py:17
  77.1 0.1 fusion.6
  77.2 0.0 copy-start.1
  77.2 0.0 collective-permute-done.8
  77.3 4.5 %collective-permute-done.9 = bf16[256,512]{1,0:T(8,128)(2,1)S(1)} collective-permute-done((bf16[256,512]{1,0:T(8,128)(2,1)S(1)}, bf16[256,512]{1,0:T(8,128)(2,1)S(1)}, u32[]{:S(2)}, u32[]{:S(2)}) %collective-permute-start.9) | collective-permute-done | bytes 262176 | tf_op jit(solution)/shard_map/ppermute | solution.py:69
  81.8 0.0 copy-done.1
  81.8 0.9 %select_dynamic-update-slice_fusion = f32[256,2048]{1,0:T(8,128)} fusion(f32[256,2048]{1,0:T(8,128)} %copy-done.1, s32[]{:T(128)S(6)} %select_n.142, bf16[256,512]{1,0:T(8,128)(2,1)S(1)} %collective-permute-done.9, bf16[256,512]{1,0:T(8,128)(2,1)S(1)} %collective-permute-done.8, pred[]{:T(512)S(6)} %le.7), kind=kLoop, calls=%fused_computation.23 | loop fusion | flops 655360 | bytes 1048581 | tf_op jit(solution)/shard_map/dynamic_update_slice | solution.py:143
  (6 shorter events, 0.1 us)
Async XLA Ops:
  0.7 3.4 %copy-start = (f32[2048,512]{1,0:T(8,128)S(1)}, f32[2048,512]{1,0:T(8,128)}, u32[]{:S(2)}) copy-start(f32[2048,512]{1,0:T(8,128)} %param.2) | copy-start | bytes 12582916
  4.2 4.6 %collective-permute-start = (f32[2,512]{1,0:T(2,128)S(1)}, f32[2,512]{1,0:T(2,128)S(1)}, u32[]{:S(2)}, u32[]{:S(2)}) collective-permute-start(f32[2,512]{1,0:T(2,128)S(1)} %pad_maximum_fusion.2), channel_id=1, source_target_pairs={{0,1},{1,0},{2,3},{3,2},{4,5},{5,4},{6,7},{7,6},{8,9},{9,8},{10,11... | collective-permute-start | bytes 12296 | tf_op jit(solution)/shard_map/ppermute | solution.py:17
  9.4 10.7 %collective-permute-start.2 = (bf16[2048,512]{1,0:T(8,128)(2,1)S(1)}, bf16[2048,512]{1,0:T(8,128)(2,1)}, u32[]{:S(2)}, u32[]{:S(2)}) collective-permute-start(bf16[2048,512]{1,0:T(8,128)(2,1)S(1)} %multiply_convert_fusion), channel_id=1, source_target_pairs={{0,2},{4,6},{2,8},{6,12},{8,10},{12,14},{10,16},{14,20},{16,18},{2... | collective-permute-start | bytes 6291464 | tf_op jit(solution)/shard_map/ppermute | solution.py:32
  12.1 8.8 %collective-permute-start.1 = (bf16[2048,512]{1,0:T(8,128)(2,1)S(1)}, bf16[2048,512]{1,0:T(8,128)(2,1)}, u32[]{:S(2)}, u32[]{:S(2)}) collective-permute-start(bf16[2048,512]{1,0:T(8,128)(2,1)S(1)} %multiply_convert_fusion), channel_id=1, source_target_pairs={{4,2},{6,4},{2,0},{12,10},{14,12},{10,8},{20,18},{22,20},{18,16},{... | collective-permute-start | bytes 6291464 | tf_op jit(solution)/shard_map/ppermute | solution.py:32
  14.1 51.1 %collective-permute-start.6 = (bf16[2048,512]{1,0:T(8,128)(2,1)S(1)}, bf16[2048,512]{1,0:T(8,128)(2,1)S(1)}, u32[]{:S(2)}, u32[]{:S(2)}) collective-permute-start(bf16[2048,512]{1,0:T(8,128)(2,1)S(1)} %multiply_convert_fusion), channel_id=1, source_target_pairs={{2,4},{0,6},{10,12},{8,14},{18,20},{16,22},{26,28},{24,30},{3,5},{... | collective-permute-start | bytes 6291464 | tf_op jit(solution)/shard_map/ppermute | solution.py:32
  20.1 45.0 %collective-permute-start.5 = (bf16[2048,512]{1,0:T(8,128)(2,1)}, bf16[2048,512]{1,0:T(8,128)(2,1)S(1)}, u32[]{:S(2)}, u32[]{:S(2)}) collective-permute-start(bf16[2048,512]{1,0:T(8,128)(2,1)} %collective-permute-done.2), channel_id=1, source_target_pairs={{4,2},{12,10},{20,18},{28,26},{5,3},{13,11},{21,19},{29,27}} | collective-permute-start | bytes 6291464 | tf_op jit(solution)/shard_map/ppermute | solution.py:32
  20.9 44.2 %collective-permute-start.4 = (bf16[2048,512]{1,0:T(8,128)(2,1)}, bf16[2048,512]{1,0:T(8,128)(2,1)S(1)}, u32[]{:S(2)}, u32[]{:S(2)}) collective-permute-start(bf16[2048,512]{1,0:T(8,128)(2,1)} %collective-permute-done.1), channel_id=1, source_target_pairs={{2,8},{10,16},{18,24},{3,9},{11,17},{19,25}} | collective-permute-start | bytes 6291464 | tf_op jit(solution)/shard_map/ppermute | solution.py:32
  25.9 9.2 %collective-permute-start.3 = (bf16[2,256,512]{2,1,0:T(8,128)(2,1)S(1)}, bf16[2,256,512]{2,1,0:T(8,128)(2,1)S(1)}, u32[]{:S(2)}, u32[]{:S(2)}) collective-permute-start(bf16[2,256,512]{2,1,0:T(8,128)(2,1)S(1)} %fusion.1), channel_id=1, source_target_pairs={{0,1},{1,0},{2,3},{3,2},{4,5},{5,4},{6,7},{7,6},{8,9},{9,8},{10,11... | collective-permute-start | bytes 1572872 | tf_op jit(solution)/shard_map/ppermute | solution.py:17
  68.0 9.2 %collective-permute-start.7 = (bf16[256,512]{1,0:T(8,128)(2,1)S(1)}, bf16[256,512]{1,0:T(8,128)(2,1)S(1)}, u32[]{:S(2)}, u32[]{:S(2)}) collective-permute-start(bf16[256,512]{1,0:T(8,128)(2,1)S(1)} %dynamic-slice_bitcast_fusion.2), channel_id=1, source_target_pairs={{0,1},{1,0},{2,3},{3,2},{4,5},{5,4},{6,7},{7,6},{8,9},{9,8},{10,11... | collective-permute-start | bytes 786440 | tf_op jit(solution)/shard_map/ppermute | solution.py:17
  69.6 7.7 %collective-permute-start.8 = (bf16[256,512]{1,0:T(8,128)(2,1)S(1)}, bf16[256,512]{1,0:T(8,128)(2,1)S(1)}, u32[]{:S(2)}, u32[]{:S(2)}) collective-permute-start(bf16[256,512]{1,0:T(8,128)(2,1)S(1)} %get-tuple-element.16), channel_id=1, source_target_pairs={{0,2},{2,0},{4,6},{6,4},{8,10},{10,8},{12,14},{14,12},{16,18},{18,... | collective-permute-start | bytes 786440 | tf_op jit(solution)/shard_map/ppermute | solution.py:61
  69.8 12.0 %collective-permute-start.9 = (bf16[256,512]{1,0:T(8,128)(2,1)S(1)}, bf16[256,512]{1,0:T(8,128)(2,1)S(1)}, u32[]{:S(2)}, u32[]{:S(2)}) collective-permute-start(bf16[256,512]{1,0:T(8,128)(2,1)S(1)} %get-tuple-element.17), channel_id=1, source_target_pairs={{0,3},{1,2},{2,1},{3,0},{4,7},{5,6},{6,5},{7,4},{8,11},{9,10},{10,... | collective-permute-start | bytes 786440 | tf_op jit(solution)/shard_map/ppermute | solution.py:69
  77.2 4.6 %copy-start.1 = (f32[256,2048]{1,0:T(8,128)}, f32[256,2048]{1,0:T(8,128)S(1)}, u32[]{:S(2)}) copy-start(f32[256,2048]{1,0:T(8,128)S(1)} %fusion.6) | copy-start | bytes 6291460

commit v14 on v13

--- a/solution.py
+++ b/solution.py
@@ -34,28 +34,36 @@
     def pairs_of(*steps):
         return [(b + s, b + t) for b in range(0, count, 4) for s, t in steps]
 
-    cross = send(standard, pairs_of((1, 2), (0, 3)))
     fast_a = send(standard, pairs_of((0, 1), (2, 3), (1, 4), (3, 6)))
     fast_b = send(standard, pairs_of((2, 1), (3, 2), (1, 0)))
-    relay = send(fast_b, pairs_of((1, 4))) + send(fast_a, pairs_of((2, 1)))
     width = standard.shape[1]
+    half = width // 2
+
+    def in_turn(value, pairs):
+        first_half = send(value[:, :half], pairs)
+        second_half = send(lax.optimization_barrier((value[:, half:], first_half))[0], pairs)
+        return [first_half, second_half]
+
+    cross = in_turn(standard, pairs_of((1, 2), (0, 3)))
+    relay_b = in_turn(fast_b, pairs_of((1, 4)))
+    relay_a = in_turn(fast_a, pairs_of((2, 1)))
     early = early_of(tile_term(standard, fast_a).astype(jnp.bfloat16))
     both, early = lax.optimization_barrier(
         (jnp.concatenate([standard, jnp.where(place % 2 == 0, fast_b, fast_a)], axis=1), early)
     )
-    rhs = lax.optimization_barrier(relay + cross)
-    product = tile_term(both, rhs).astype(jnp.bfloat16)
-    own_late = product[:width]
-    handed = to_partner(product[width:], count)
-    return early, own_late, handed
+    parts = []
+    for piece in range(2):
+        rhs = lax.optimization_barrier(relay_a[piece] + relay_b[piece] + cross[piece])
+        product = tile_term(both, rhs).astype(jnp.bfloat16)
+        parts.append((piece * half, product[:width], to_partner(product[width:], count)))
+    return early, parts
 
 
 def to_partner(partial, count):
     n_smp = lax.axis_size("smp")
     me = lax.axis_index("smp")
-    width = partial.shape[1]
-    share = width // n_smp
-    pieces = partial.reshape(n_smp, share, width)
+    share = partial.shape[0] // n_smp
+    pieces = partial.reshape(n_smp, share, partial.shape[1])
     partners = [(b + s, b + t) for b in range(0, count, 4) for s, t in ((0, 1), (1, 0), (2, 3), (3, 2))]
     partners = [(s, t) for s, t in partners if t < count]
     total = lax.ppermute(
@@ -108,7 +116,7 @@
     first = tile_term(standard, standard).astype(jnp.bfloat16)
 
     def exchanged(partial):
-        pieces = partial.reshape(partial.shape[:-2] + (n_smp, share, width))
+        pieces = partial.reshape(partial.shape[:-2] + (n_smp, share, partial.shape[-1]))
         axis = pieces.ndim - 3
         total = lax.dynamic_index_in_dim(pieces, me, axis, keepdims=False).astype(jnp.float32)
         for s in range(1, n_smp):
@@ -118,11 +126,9 @@
 
     if count % 4 == 0:
         place = lax.axis_index("snp") % 4
-        early, own_late, handed = relayed(
+        early, parts = relayed(
             standard, count, place, lambda with_a: exchanged(jnp.stack([first, with_a]))
         )
-        late_own = exchanged(own_late)
-
         def scaled(tile, dist):
             return jnp.where(dist <= own_reach, tile / samples, jnp.zeros_like(tile))
 
@@ -139,8 +145,11 @@
         )
         own_tap = jnp.where(place < 2, 2, jnp.where(place == 2, 1, 3))
         hand_tap = jnp.where(place == 0, 1, jnp.where(place == 1, 3, 2))
-        out = lax.dynamic_update_slice(out, scaled(late_own, own_tap), (0, own_tap * width))
-        return lax.dynamic_update_slice(out, scaled(handed, hand_tap), (0, hand_tap * width))
+        for offset, own_late, handed in parts:
+            late_own = exchanged(own_late)
+            out = lax.dynamic_update_slice(out, scaled(late_own, own_tap), (0, own_tap * width + offset))
+            out = lax.dynamic_update_slice(out, scaled(handed, hand_tap), (0, hand_tap * width + offset))
+        return out
     else:
         rest = [tile_term(standard, nb).astype(jnp.bfloat16) for nb in chained(standard)]
         totals = list(exchanged(jnp.stack([first] + rest)))

time: 83 us -> 96.5 us (1.16)
  starting transfers between devices: 18.4 us -> 36.1 us
  waiting for transfers between devices: 47.6 us -> 37 us
  local copies, waits for them, and re-layouts: 1.41 us -> 5.86 us
  other arithmetic: 7.88 us -> 9.13 us
    ppermute x5 -> x8, waiting for transfers between devices: 29.6 us -> 20.1 us  [send(): return lax.ppermute(value, 'snp', pairs)]
    ppermute x1 -> x2, starting transfers between devices: 0.21 us -> 8.39 us  [to_partner(): lax.ppermute(lax.dynamic_index_in_dim(pieces, me, 0, keepdims=False), 'sn...]
    ppermute x5 -> x8, starting transfers between devices: 11.5 us -> 17.6 us  [send(): return lax.ppermute(value, 'snp', pairs)]
    slice x1 -> x5, local copies, waits for them, and re-layouts: 0.07 us -> 4.54 us  [the longest x3 4.46 us: in_turn(): value[:, half:]]
    ppermute x3 -> x4, waiting for transfers between devices: 13.4 us -> 10.4 us  [rotated(): lax.ppermute(value, axis, [(source, (source + steps) % count) for source...]
    ppermute x1 -> x2, starting transfers between devices: 0.47 us -> 3.35 us  [to_partner(): lax.ppermute(outgoing, ('snp', 'smp'), pairs).astype(jnp.float32)]
    add x1 -> x2, other arithmetic: 0.3 us -> 1.53 us  [relayed(): relay_a[piece] + relay_b[piece] + cross[piece]]
    ppermute x1 -> x2, waiting for transfers between devices: 4.55 us -> 5.63 us  [to_partner(): lax.ppermute(outgoing, ('snp', 'smp'), pairs).astype(jnp.float32)]
  transfers between devices with their start and end apart: 10 -> 16, of which waited for: 5 -> 6; matrix products, arithmetic and copies ran while one was open for 9% -> 17% of each run, Pallas kernels for 0% -> 0%
where the time goes in v14:
time: 96.5 us; the launch traced here: 95.8 us
  waiting for transfers between devices  37 us (38%)
  starting transfers between devices  36.1 us (37%)
  other arithmetic  9.13 us (9%)
  matrix products  6.77 us (7%)
  local copies, waits for them, and re-layouts  5.86 us (6%)
    ppermute x8, waiting for transfers between devices, send(): return lax.ppermute(value, 'snp', pairs)  20.1 us
    ppermute x8, starting transfers between devices, send(): return lax.ppermute(value, 'snp', pairs)  17.6 us
    ppermute x4, waiting for transfers between devices, rotated(): lax.ppermute(value, axis, [(source, (source + steps) % count) for source...  10.4 us
    ppermute x2, starting transfers between devices, to_partner(): lax.ppermute(lax.dynamic_index_in_dim(pieces, me, 0, keepdims=False), 'sn...  8.39 us
    ppermute x4, starting transfers between devices, rotated(): lax.ppermute(value, axis, [(source, (source + steps) % count) for source...  6.78 us
    dot_general x4, matrix products, tile_term(): lax.dot_general(standard, neighbour, (((0,), (0,)), ((), ())), preferred_...  6.77 us
    ppermute x2, waiting for transfers between devices, to_partner(): lax.ppermute(outgoing, ('snp', 'smp'), pairs).astype(jnp.float32)  5.63 us
    slice x3, local copies, waits for them, and re-layouts, in_turn(): value[:, half:]  4.46 us
  transfers between devices with their start and end apart: 16, of which 6 were waited for; matrix products, arithmetic and copies ran while one was open for 17% of the time, Pallas kernels for 0%

profile of v14, /device:TPU:0, one launch (start us, length us, event | category | flops | bytes accessed | tf_op | source)
XLA Modules:
  0.0 95.8 jit_solution(18395026226184343487)
XLA Ops:
  0.0 0.7 slice.47
  0.7 2.9 %multiply_reduce_fusion = (f32[512]{0:T(512)S(1)}, f32[512]{0:T(512)S(1)}) fusion(f32[2048,512]{1,0:T(8,128)} %param.2, f32[512]{0:T(512)S(1)} %bitcast.72), kind=kLoop, calls=%fused_computation.2 | loop fusion | flops 4193280 | bytes 4200448 | tf_op jit(solution)/shard_map/reduce_sum | solution.py:96
  3.7 0.5 copy-done
  4.2 3.0 %collective-permute-start = (f32[2,512]{1,0:T(2,128)S(1)}, f32[2,512]{1,0:T(2,128)S(1)}, u32[]{:S(2)}, u32[]{:S(2)}) collective-permute-start(f32[2,512]{1,0:T(2,128)S(1)} %pad_maximum_fusion.2), channel_id=1, source_target_pairs={{0,1},{1,0},{2,3},{3,2},{4,5},{5,4},{6,7},{7,6},{8,9},{9,8},{10,11... | collective-permute-start | bytes 12296 | tf_op jit(solution)/shard_map/ppermute | solution.py:17
  7.2 1.6 %collective-permute-done = f32[2,512]{1,0:T(2,128)S(1)} collective-permute-done((f32[2,512]{1,0:T(2,128)S(1)}, f32[2,512]{1,0:T(2,128)S(1)}, u32[]{:S(2)}, u32[]{:S(2)}) %collective-permute-start) | collective-permute-done | bytes 4128 | tf_op jit(solution)/shard_map/ppermute | solution.py:17
  8.8 0.6 multiply_convert_fusion
  9.4 2.6 %collective-permute-start.2 = (bf16[2048,512]{1,0:T(8,128)(2,1)S(1)}, bf16[2048,512]{1,0:T(8,128)(2,1)}, u32[]{:S(2)}, u32[]{:S(2)}) collective-permute-start(bf16[2048,512]{1,0:T(8,128)(2,1)S(1)} %multiply_convert_fusion), channel_id=1, source_target_pairs={{0,2},{4,6},{2,8},{6,12},{8,10},{12,14},{10,16},{14,20},{16,18},{2... | collective-permute-start | bytes 6291464 | tf_op jit(solution)/shard_map/ppermute | solution.py:32
  12.0 1.3 %collective-permute-start.1 = (bf16[2048,512]{1,0:T(8,128)(2,1)S(1)}, bf16[2048,512]{1,0:T(8,128)(2,1)}, u32[]{:S(2)}, u32[]{:S(2)}) collective-permute-start(bf16[2048,512]{1,0:T(8,128)(2,1)S(1)} %multiply_convert_fusion), channel_id=1, source_target_pairs={{4,2},{6,4},{2,0},{12,10},{14,12},{10,8},{20,18},{22,20},{18,16},{... | collective-permute-start | bytes 6291464 | tf_op jit(solution)/shard_map/ppermute | solution.py:32
  13.3 1.1 %fusion.14 = (bf16[2048,256]{1,0:T(8,128)(2,1)S(1)}, bf16[2048,256]{1,0:T(8,128)(2,1)}) fusion(bf16[2048,512]{1,0:T(8,128)(2,1)S(1)} %multiply_convert_fusion), kind=kLoop, calls=%fused_computation.51 | loop fusion | bytes 4194304 | tf_op jit(solution)/shard_map/slice | solution.py:44
  14.4 6.9 %collective-permute-start.6 = (bf16[2048,256]{1,0:T(8,128)(2,1)}, bf16[2048,256]{1,0:T(8,128)(2,1)}, u32[]{:S(2)}, u32[]{:S(2)}) collective-permute-start(bf16[2048,256]{1,0:T(8,128)(2,1)} %get-tuple-element.22), channel_id=1, source_target_pairs={{2,4},{0,6},{10,12},{8,14},{18,20},{16,22},{26,28},{24,30},{3,5},{... | collective-permute-start | bytes 3145736 | tf_op jit(solution)/shard_map/ppermute | solution.py:32
  22.0 1.3 %convolution_convert_fusion.1 = bf16[512,512]{1,0:T(8,128)(2,1)S(1)} fusion(bf16[2048,512]{1,0:T(8,128)(2,1)S(1)} %multiply_convert_fusion), kind=kOutput, calls=%fused_computation.7 | convolution fusion | flops 1074003968 | bytes 2621440 | tf_op jit(solution)/shard_map/dot_general | solution.py:82
  23.3 20.1 %collective-permute-done.6 = bf16[2048,256]{1,0:T(8,128)(2,1)} collective-permute-done((bf16[2048,256]{1,0:T(8,128)(2,1)}, bf16[2048,256]{1,0:T(8,128)(2,1)}, u32[]{:S(2)}, u32[]{:S(2)}) %collective-permute-start.6) | collective-permute-done | bytes 1048608 | tf_op jit(solution)/shard_map/ppermute | solution.py:32
  43.4 3.9 %collective-permute-start.12 = (bf16[2048,256]{1,0:T(8,128)(2,1)S(1)}, bf16[2048,256]{1,0:T(8,128)(2,1)S(1)}, u32[]{:S(2)}, u32[]{:S(2)}) collective-permute-start(bf16[2048,256]{1,0:T(8,128)(2,1)S(1)} %get-tuple-element.14), channel_id=1, source_target_pairs={{2,4},{0,6},{10,12},{8,14},{18,20},{16,22},{26,28},{24,30},{3,5},{... | collective-permute-start | bytes 3145736 | tf_op jit(solution)/shard_map/ppermute | solution.py:32
  47.2 1.7 %fusion.13 = (bf16[2048,256]{1,0:T(8,128)(2,1)S(1)}, bf16[2048,256]{1,0:T(8,128)(2,1)S(1)}) fusion(bf16[2048,512]{1,0:T(8,128)(2,1)} %collective-permute-done.2), kind=kLoop, calls=%fused_computation.50 | loop fusion | bytes 4194304 | tf_op jit(solution)/shard_map/slice | solution.py:44
  48.9 0.7 collective-permute-start.4
  49.7 1.7 %fusion.12 = (bf16[2048,256]{1,0:T(8,128)(2,1)S(1)}, bf16[2048,256]{1,0:T(8,128)(2,1)S(1)}) fusion(bf16[2048,512]{1,0:T(8,128)(2,1)} %collective-permute-done.1), kind=kLoop, calls=%fused_computation.49 | loop fusion | bytes 4194304 | tf_op jit(solution)/shard_map/slice | solution.py:44
  51.4 0.7 collective-permute-start.5
  52.1 2.9 %convolution_convert_fusion = bf16[512,512]{1,0:T(8,128)(2,1)S(1)} fusion(bf16[2048,512]{1,0:T(8,128)(2,1)S(1)} %multiply_convert_fusion, bf16[2048,512]{1,0:T(8,128)(2,1)} %collective-permute-done.2), kind=kOutput, calls=%fused_computation.6 | convolution fusion | flops 1074003968 | bytes 4718592 | tf_op jit(solution)/shard_map/dot_general | solution.py:82
  55.0 0.1 fusion.1
  55.0 1.6 %collective-permute-start.3 = (bf16[2,256,512]{2,1,0:T(8,128)(2,1)S(1)}, bf16[2,256,512]{2,1,0:T(8,128)(2,1)S(1)}, u32[]{:S(2)}, u32[]{:S(2)}) collective-permute-start(bf16[2,256,512]{2,1,0:T(8,128)(2,1)S(1)} %fusion.1), channel_id=1, source_target_pairs={{0,1},{1,0},{2,3},{3,2},{4,5},{5,4},{6,7},{7,6},{8,9},{9,8},{10,11... | collective-permute-start | bytes 1572872 | tf_op jit(solution)/shard_map/ppermute | solution.py:17
  56.6 1.8 %broadcast_select_fusion = bf16[2048,512]{1,0:T(8,128)(2,1)S(1)} fusion(bf16[2048,512]{1,0:T(8,128)(2,1)} %collective-permute-done.1, bf16[2048,512]{1,0:T(8,128)(2,1)} %collective-permute-done.2, pred[]{:T(512)S(6)} %eq.24), kind=kLoop, calls=%fused_computation.5 | loop fusion | flops 1048576 | bytes 6291457 | tf_op jit(solution)/shard_map/jit(_where)/select_n | solution.py:52
  58.4 0.6 pad_maximum_fusion
  59.1 8.8 %collective-permute-done.3 = bf16[2,256,512]{2,1,0:T(8,128)(2,1)S(1)} collective-permute-done((bf16[2,256,512]{2,1,0:T(8,128)(2,1)S(1)}, bf16[2,256,512]{2,1,0:T(8,128)(2,1)S(1)}, u32[]{:S(2)}, u32[]{:S(2)}) %collective-permute-start.3) | collective-permute-done | bytes 524320 | tf_op jit(solution)/shard_map/ppermute | solution.py:17
  67.9 0.2 convert_add_fusion
  68.0 0.2 select_bitcast_fusion.2
  68.2 0.0 collective-permute-done.4
  68.3 0.7 collective-permute-start.10
  69.0 0.0 collective-permute-done.5
  69.0 0.7 collective-permute-start.11
  69.7 1.4 %add_add_fusion.1 = bf16[2048,256]{1,0:T(8,128)(2,1)S(1)} fusion(bf16[2048,256]{1,0:T(8,128)(2,1)} %collective-permute-done.6, bf16[2048,256]{1,0:T(8,128)(2,1)S(1)} %collective-permute-done.4, bf16[2048,256]{1,0:T(8,128)(2,1)S(1)} %collective-permute-done.5), kind=kLoop, calls=%fused_computation.16 | loop fusion | flops 1048576 | bytes 4194304 | tf_op jit(solution)/shard_map/add | solution.py:56
  71.1 1.3 %convolution_convert_fusion.3 = bf16[1024,256]{1,0:T(8,128)(2,1)S(1)} fusion(bf16[2048,1024]{1,0:T(8,128)(2,1)S(1)} %pad_maximum_fusion, bf16[2048,256]{1,0:T(8,128)(2,1)S(1)} %add_add_fusion.1), kind=kOutput, calls=%fused_computation.9 | convolution fusion | flops 1074003968 | bytes 5767168 | tf_op jit(solution)/shard_map/dot_general | solution.py:82
  72.5 1.6 %collective-permute-start.7 = (bf16[256,256]{1,0:T(8,128)(2,1)S(1)}, bf16[256,256]{1,0:T(8,128)(2,1)S(1)}, u32[]{:S(2)}, u32[]{:S(2)}) collective-permute-start(bf16[256,256]{1,0:T(8,128)(2,1)S(1)} %dynamic-slice_bitcast_fusion.5), channel_id=1, source_target_pairs={{0,1},{1,0},{2,3},{3,2},{4,5},{5,4},{6,7},{7,6},{8,9},{9,8},{10,11... | collective-permute-start | bytes 393224 | tf_op jit(solution)/shard_map/ppermute | solution.py:17
  74.1 0.2 pad_maximum_fusion.1
  74.4 3.8 %collective-permute-start.8 = (bf16[256,256]{1,0:T(8,128)(2,1)S(1)}, bf16[256,256]{1,0:T(8,128)(2,1)S(1)}, u32[]{:S(2)}, u32[]{:S(2)}) collective-permute-start(bf16[256,256]{1,0:T(8,128)(2,1)S(1)} %get-tuple-element.32), channel_id=1, source_target_pairs={{0,2},{2,0},{4,6},{6,4},{8,10},{10,8},{12,14},{14,12},{16,18},{18,... | collective-permute-start | bytes 393224 | tf_op jit(solution)/shard_map/ppermute | solution.py:69
  78.3 3.3 %collective-permute-start.9 = (bf16[256,256]{1,0:T(8,128)(2,1)S(1)}, bf16[256,256]{1,0:T(8,128)(2,1)S(1)}, u32[]{:S(2)}, u32[]{:S(2)}) collective-permute-start(bf16[256,256]{1,0:T(8,128)(2,1)S(1)} %get-tuple-element.33), channel_id=1, source_target_pairs={{0,3},{1,2},{2,1},{3,0},{4,7},{5,6},{6,5},{7,4},{8,11},{9,10},{10,... | collective-permute-start | bytes 393224 | tf_op jit(solution)/shard_map/ppermute | solution.py:77
  81.7 0.0 collective-permute-done.11
  81.7 0.2 add_add_fusion
  81.9 1.3 %convolution_convert_fusion.2 = bf16[1024,256]{1,0:T(8,128)(2,1)S(1)} fusion(bf16[2048,1024]{1,0:T(8,128)(2,1)S(1)} %pad_maximum_fusion, bf16[2048,256]{1,0:T(8,128)(2,1)S(1)} %add_add_fusion), kind=kOutput, calls=%fused_computation.8 | convolution fusion | flops 1074003968 | bytes 5767168 | tf_op jit(solution)/shard_map/dot_general | solution.py:82
  83.2 0.6 collective-permute-start.13
  83.8 0.0 collective-permute-done.8
  83.8 1.1 %collective-permute-done.9 = bf16[256,256]{1,0:T(8,128)(2,1)S(1)} collective-permute-done((bf16[256,256]{1,0:T(8,128)(2,1)S(1)}, bf16[256,256]{1,0:T(8,128)(2,1)S(1)}, u32[]{:S(2)}, u32[]{:S(2)}) %collective-permute-start.9) | collective-permute-done | bytes 131104 | tf_op jit(solution)/shard_map/ppermute | solution.py:77
  85.0 4.5 %collective-permute-start.14 = (bf16[256,256]{1,0:T(8,128)(2,1)S(1)}, bf16[256,256]{1,0:T(8,128)(2,1)S(1)}, u32[]{:S(2)}, u32[]{:S(2)}) collective-permute-start(bf16[256,256]{1,0:T(8,128)(2,1)S(1)} %get-tuple-element.30), channel_id=1, source_target_pairs={{0,2},{2,0},{4,6},{6,4},{8,10},{10,8},{12,14},{14,12},{16,18},{18,... | collective-permute-start | bytes 393224 | tf_op jit(solution)/shard_map/ppermute | solution.py:69
  89.5 0.0 collective-permute-start.15
  89.5 0.0 collective-permute-done.13
  89.6 0.0 copy-start.1
  89.6 0.9 collective-permute-done.14
  90.5 4.5 %collective-permute-done.15 = bf16[256,256]{1,0:T(8,128)(2,1)S(1)} collective-permute-done((bf16[256,256]{1,0:T(8,128)(2,1)S(1)}, bf16[256,256]{1,0:T(8,128)(2,1)S(1)}, u32[]{:S(2)}, u32[]{:S(2)}) %collective-permute-start.15) | collective-permute-done | bytes 131104 | tf_op jit(solution)/shard_map/ppermute | solution.py:77
  95.1 0.7 select_dynamic-update-slice_fusion
  (21 shorter events, 0.4 us)
Async XLA Ops:
  0.7 3.4 %copy-start = (f32[2048,512]{1,0:T(8,128)S(1)}, f32[2048,512]{1,0:T(8,128)}, u32[]{:S(2)}) copy-start(f32[2048,512]{1,0:T(8,128)} %param.2) | copy-start | bytes 12582916
  4.2 4.6 %collective-permute-start = (f32[2,512]{1,0:T(2,128)S(1)}, f32[2,512]{1,0:T(2,128)S(1)}, u32[]{:S(2)}, u32[]{:S(2)}) collective-permute-start(f32[2,512]{1,0:T(2,128)S(1)} %pad_maximum_fusion.2), channel_id=1, source_target_pairs={{0,1},{1,0},{2,3},{3,2},{4,5},{5,4},{6,7},{7,6},{8,9},{9,8},{10,11... | collective-permute-start | bytes 12296 | tf_op jit(solution)/shard_map/ppermute | solution.py:17
  9.4 37.8 %collective-permute-start.2 = (bf16[2048,512]{1,0:T(8,128)(2,1)S(1)}, bf16[2048,512]{1,0:T(8,128)(2,1)}, u32[]{:S(2)}, u32[]{:S(2)}) collective-permute-start(bf16[2048,512]{1,0:T(8,128)(2,1)S(1)} %multiply_convert_fusion), channel_id=1, source_target_pairs={{0,2},{4,6},{2,8},{6,12},{8,10},{12,14},{10,16},{14,20},{16,18},{2... | collective-permute-start | bytes 6291464 | tf_op jit(solution)/shard_map/ppermute | solution.py:32
  12.0 37.6 %collective-permute-start.1 = (bf16[2048,512]{1,0:T(8,128)(2,1)S(1)}, bf16[2048,512]{1,0:T(8,128)(2,1)}, u32[]{:S(2)}, u32[]{:S(2)}) collective-permute-start(bf16[2048,512]{1,0:T(8,128)(2,1)S(1)} %multiply_convert_fusion), channel_id=1, source_target_pairs={{4,2},{6,4},{2,0},{12,10},{14,12},{10,8},{20,18},{22,20},{18,16},{... | collective-permute-start | bytes 6291464 | tf_op jit(solution)/shard_map/ppermute | solution.py:32
  14.4 28.9 %collective-permute-start.6 = (bf16[2048,256]{1,0:T(8,128)(2,1)}, bf16[2048,256]{1,0:T(8,128)(2,1)}, u32[]{:S(2)}, u32[]{:S(2)}) collective-permute-start(bf16[2048,256]{1,0:T(8,128)(2,1)} %get-tuple-element.22), channel_id=1, source_target_pairs={{2,4},{0,6},{10,12},{8,14},{18,20},{16,22},{26,28},{24,30},{3,5},{... | collective-permute-start | bytes 3145736 | tf_op jit(solution)/shard_map/ppermute | solution.py:32
  43.4 38.3 %collective-permute-start.12 = (bf16[2048,256]{1,0:T(8,128)(2,1)S(1)}, bf16[2048,256]{1,0:T(8,128)(2,1)S(1)}, u32[]{:S(2)}, u32[]{:S(2)}) collective-permute-start(bf16[2048,256]{1,0:T(8,128)(2,1)S(1)} %get-tuple-element.14), channel_id=1, source_target_pairs={{2,4},{0,6},{10,12},{8,14},{18,20},{16,22},{26,28},{24,30},{3,5},{... | collective-permute-start | bytes 3145736 | tf_op jit(solution)/shard_map/ppermute | solution.py:32
  48.9 19.3 %collective-permute-start.4 = (bf16[2048,256]{1,0:T(8,128)(2,1)S(1)}, bf16[2048,256]{1,0:T(8,128)(2,1)S(1)}, u32[]{:S(2)}, u32[]{:S(2)}) collective-permute-start(bf16[2048,256]{1,0:T(8,128)(2,1)S(1)} %get-tuple-element.20), channel_id=1, source_target_pairs={{4,2},{12,10},{20,18},{28,26},{5,3},{13,11},{21,19},{29,27}} | collective-permute-start | bytes 3145736 | tf_op jit(solution)/shard_map/ppermute | solution.py:32
  51.4 17.6 %collective-permute-start.5 = (bf16[2048,256]{1,0:T(8,128)(2,1)S(1)}, bf16[2048,256]{1,0:T(8,128)(2,1)S(1)}, u32[]{:S(2)}, u32[]{:S(2)}) collective-permute-start(bf16[2048,256]{1,0:T(8,128)(2,1)S(1)} %get-tuple-element.18), channel_id=1, source_target_pairs={{2,8},{10,16},{18,24},{3,9},{11,17},{19,25}} | collective-permute-start | bytes 3145736 | tf_op jit(solution)/shard_map/ppermute | solution.py:32
  55.0 12.8 %collective-permute-start.3 = (bf16[2,256,512]{2,1,0:T(8,128)(2,1)S(1)}, bf16[2,256,512]{2,1,0:T(8,128)(2,1)S(1)}, u32[]{:S(2)}, u32[]{:S(2)}) collective-permute-start(bf16[2,256,512]{2,1,0:T(8,128)(2,1)S(1)} %fusion.1), channel_id=1, source_target_pairs={{0,1},{1,0},{2,3},{3,2},{4,5},{5,4},{6,7},{7,6},{8,9},{9,8},{10,11... | collective-permute-start | bytes 1572872 | tf_op jit(solution)/shard_map/ppermute | solution.py:17
  68.3 13.4 %collective-permute-start.10 = (bf16[2048,256]{1,0:T(8,128)(2,1)S(1)}, bf16[2048,256]{1,0:T(8,128)(2,1)S(1)}, u32[]{:S(2)}, u32[]{:S(2)}) collective-permute-start(bf16[2048,256]{1,0:T(8,128)(2,1)S(1)} %get-tuple-element.12), channel_id=1, source_target_pairs={{4,2},{12,10},{20,18},{28,26},{5,3},{13,11},{21,19},{29,27}} | collective-permute-start | bytes 3145736 | tf_op jit(solution)/shard_map/ppermute | solution.py:32
  69.0 12.7 %collective-permute-start.11 = (bf16[2048,256]{1,0:T(8,128)(2,1)S(1)}, bf16[2048,256]{1,0:T(8,128)(2,1)S(1)}, u32[]{:S(2)}, u32[]{:S(2)}) collective-permute-start(bf16[2048,256]{1,0:T(8,128)(2,1)S(1)} %get-tuple-element.13), channel_id=1, source_target_pairs={{2,8},{10,16},{18,24},{3,9},{11,17},{19,25}} | collective-permute-start | bytes 3145736 | tf_op jit(solution)/shard_map/ppermute | solution.py:32
  72.5 5.7 %collective-permute-start.7 = (bf16[256,256]{1,0:T(8,128)(2,1)S(1)}, bf16[256,256]{1,0:T(8,128)(2,1)S(1)}, u32[]{:S(2)}, u32[]{:S(2)}) collective-permute-start(bf16[256,256]{1,0:T(8,128)(2,1)S(1)} %dynamic-slice_bitcast_fusion.5), channel_id=1, source_target_pairs={{0,1},{1,0},{2,3},{3,2},{4,5},{5,4},{6,7},{7,6},{8,9},{9,8},{10,11... | collective-permute-start | bytes 393224 | tf_op jit(solution)/shard_map/ppermute | solution.py:17
  74.4 9.4 %collective-permute-start.8 = (bf16[256,256]{1,0:T(8,128)(2,1)S(1)}, bf16[256,256]{1,0:T(8,128)(2,1)S(1)}, u32[]{:S(2)}, u32[]{:S(2)}) collective-permute-start(bf16[256,256]{1,0:T(8,128)(2,1)S(1)} %get-tuple-element.32), channel_id=1, source_target_pairs={{0,2},{2,0},{4,6},{6,4},{8,10},{10,8},{12,14},{14,12},{16,18},{18,... | collective-permute-start | bytes 393224 | tf_op jit(solution)/shard_map/ppermute | solution.py:69
  78.3 6.6 %collective-permute-start.9 = (bf16[256,256]{1,0:T(8,128)(2,1)S(1)}, bf16[256,256]{1,0:T(8,128)(2,1)S(1)}, u32[]{:S(2)}, u32[]{:S(2)}) collective-permute-start(bf16[256,256]{1,0:T(8,128)(2,1)S(1)} %get-tuple-element.33), channel_id=1, source_target_pairs={{0,3},{1,2},{2,1},{3,0},{4,7},{5,6},{6,5},{7,4},{8,11},{9,10},{10,... | collective-permute-start | bytes 393224 | tf_op jit(solution)/shard_map/ppermute | solution.py:77
  83.2 6.3 %collective-permute-start.13 = (bf16[256,256]{1,0:T(8,128)(2,1)S(1)}, bf16[256,256]{1,0:T(8,128)(2,1)S(1)}, u32[]{:S(2)}, u32[]{:S(2)}) collective-permute-start(bf16[256,256]{1,0:T(8,128)(2,1)S(1)} %dynamic-slice_bitcast_fusion.2), channel_id=1, source_target_pairs={{0,1},{1,0},{2,3},{3,2},{4,5},{5,4},{6,7},{7,6},{8,9},{9,8},{10,11... | collective-permute-start | bytes 393224 | tf_op jit(solution)/shard_map/ppermute | solution.py:17
  85.0 5.5 %collective-permute-start.14 = (bf16[256,256]{1,0:T(8,128)(2,1)S(1)}, bf16[256,256]{1,0:T(8,128)(2,1)S(1)}, u32[]{:S(2)}, u32[]{:S(2)}) collective-permute-start(bf16[256,256]{1,0:T(8,128)(2,1)S(1)} %get-tuple-element.30), channel_id=1, source_target_pairs={{0,2},{2,0},{4,6},{6,4},{8,10},{10,8},{12,14},{14,12},{16,18},{18,... | collective-permute-start | bytes 393224 | tf_op jit(solution)/shard_map/ppermute | solution.py:69
  89.5 5.5 %collective-permute-start.15 = (bf16[256,256]{1,0:T(8,128)(2,1)S(1)}, bf16[256,256]{1,0:T(8,128)(2,1)S(1)}, u32[]{:S(2)}, u32[]{:S(2)}) collective-permute-start(bf16[256,256]{1,0:T(8,128)(2,1)S(1)} %get-tuple-element.31), channel_id=1, source_target_pairs={{0,3},{1,2},{2,1},{3,0},{4,7},{5,6},{6,5},{7,4},{8,11},{9,10},{10,... | collective-permute-start | bytes 393224 | tf_op jit(solution)/shard_map/ppermute | solution.py:77
  89.6 5.5 %copy-start.1 = (f32[256,2048]{1,0:T(8,128)}, f32[256,2048]{1,0:T(8,128)S(1)}, u32[]{:S(2)}) copy-start(f32[256,2048]{1,0:T(8,128)S(1)} %fusion.6) | copy-start | bytes 6291460

commit v15 on v14

--- a/solution.py
+++ b/solution.py
@@ -41,8 +41,8 @@
 
     def in_turn(value, pairs):
         first_half = send(value[:, :half], pairs)
-        second_half = send(lax.optimization_barrier((value[:, half:], first_half))[0], pairs)
-        return [first_half, second_half]
+        held = lax.optimization_barrier((value[:, half:], first_half, fast_a, fast_b))[0]
+        return [first_half, send(held, pairs)]
 
     cross = in_turn(standard, pairs_of((1, 2), (0, 3)))
     relay_b = in_turn(fast_b, pairs_of((1, 4)))

time: 96.5 us -> 90 us (0.933)
  waiting for transfers between devices: 37 us -> 34.5 us
  starting transfers between devices: 36.1 us -> 34.3 us
  other arithmetic: 9.13 us -> 7.93 us
    ppermute x8, waiting for transfers between devices: 20.1 us -> 16.6 us  [send(): return lax.ppermute(value, 'snp', pairs)]
    ppermute x4, waiting for transfers between devices: 10.4 us -> 11.7 us  [rotated(): lax.ppermute(value, axis, [(source, (source + steps) % count) for source...]
    add x2, other arithmetic: 1.53 us -> 0.34 us  [relayed(): relay_a[piece] + relay_b[piece] + cross[piece]]
    ppermute x8, starting transfers between devices: 17.6 us -> 16.6 us  [send(): return lax.ppermute(value, 'snp', pairs)]
    slice x3, local copies, waits for them, and re-layouts: 4.46 us -> 3.5 us  [in_turn(): value[:, half:]]
  transfers between devices with their start and end apart: 16 -> 16, of which waited for: 6 -> 7; matrix products, arithmetic and copies ran while one was open for 17% -> 16% of each run, Pallas kernels for 0% -> 0%
where the time goes in v15:
time: 90 us; the launch traced here: 89.4 us
  waiting for transfers between devices  34.5 us (38%)
  starting transfers between devices  34.3 us (38%)
  other arithmetic  7.93 us (9%)
  matrix products  6.81 us (8%)
  local copies, waits for them, and re-layouts  4.9 us (5%)
  between operations  1.03 us (1%)
    ppermute x8, starting transfers between devices, send(): return lax.ppermute(value, 'snp', pairs)  16.6 us
    ppermute x8, waiting for transfers between devices, send(): return lax.ppermute(value, 'snp', pairs)  16.6 us
    ppermute x4, waiting for transfers between devices, rotated(): lax.ppermute(value, axis, [(source, (source + steps) % count) for source...  11.7 us
    ppermute x2, starting transfers between devices, to_partner(): lax.ppermute(lax.dynamic_index_in_dim(pieces, me, 0, keepdims=False), 'sn...  7.63 us
    dot_general x4, matrix products, tile_term(): lax.dot_general(standard, neighbour, (((0,), (0,)), ((), ())), preferred_...  6.81 us
    ppermute x4, starting transfers between devices, rotated(): lax.ppermute(value, axis, [(source, (source + steps) % count) for source...  6.77 us
    ppermute x2, waiting for transfers between devices, to_partner(): lax.ppermute(outgoing, ('snp', 'smp'), pairs).astype(jnp.float32)  5.57 us
    slice x3, local copies, waits for them, and re-layouts, in_turn(): value[:, half:]  3.5 us
  transfers between devices with their start and end apart: 16, of which 7 were waited for; matrix products, arithmetic and copies ran while one was open for 16% of the time, Pallas kernels for 0%

profile of v15, /device:TPU:0, one launch (start us, length us, event | category | flops | bytes accessed | tf_op | source)
XLA Modules:
  0.0 89.4 jit_solution(18236222808618945335)
XLA Ops:
  0.0 0.7 slice.47
  0.7 2.9 %multiply_reduce_fusion = (f32[512]{0:T(512)S(1)}, f32[512]{0:T(512)S(1)}) fusion(f32[2048,512]{1,0:T(8,128)} %param.2, f32[512]{0:T(512)S(1)} %bitcast.72), kind=kLoop, calls=%fused_computation.2 | loop fusion | flops 4193280 | bytes 4200448 | tf_op jit(solution)/shard_map/reduce_sum | solution.py:96
  3.7 0.5 copy-done
  4.2 3.0 %collective-permute-start = (f32[2,512]{1,0:T(2,128)S(1)}, f32[2,512]{1,0:T(2,128)S(1)}, u32[]{:S(2)}, u32[]{:S(2)}) collective-permute-start(f32[2,512]{1,0:T(2,128)S(1)} %pad_maximum_fusion.2), channel_id=1, source_target_pairs={{0,1},{1,0},{2,3},{3,2},{4,5},{5,4},{6,7},{7,6},{8,9},{9,8},{10,11... | collective-permute-start | bytes 12296 | tf_op jit(solution)/shard_map/ppermute | solution.py:17
  7.2 1.6 %collective-permute-done = f32[2,512]{1,0:T(2,128)S(1)} collective-permute-done((f32[2,512]{1,0:T(2,128)S(1)}, f32[2,512]{1,0:T(2,128)S(1)}, u32[]{:S(2)}, u32[]{:S(2)}) %collective-permute-start) | collective-permute-done | bytes 4128 | tf_op jit(solution)/shard_map/ppermute | solution.py:17
  8.8 0.6 multiply_convert_fusion
  9.4 2.6 %collective-permute-start.2 = (bf16[2048,512]{1,0:T(8,128)(2,1)S(1)}, bf16[2048,512]{1,0:T(8,128)(2,1)}, u32[]{:S(2)}, u32[]{:S(2)}) collective-permute-start(bf16[2048,512]{1,0:T(8,128)(2,1)S(1)} %multiply_convert_fusion), channel_id=1, source_target_pairs={{0,2},{4,6},{2,8},{6,12},{8,10},{12,14},{10,16},{14,20},{16,18},{2... | collective-permute-start | bytes 6291464 | tf_op jit(solution)/shard_map/ppermute | solution.py:32
  12.0 1.3 %collective-permute-start.1 = (bf16[2048,512]{1,0:T(8,128)(2,1)S(1)}, bf16[2048,512]{1,0:T(8,128)(2,1)}, u32[]{:S(2)}, u32[]{:S(2)}) collective-permute-start(bf16[2048,512]{1,0:T(8,128)(2,1)S(1)} %multiply_convert_fusion), channel_id=1, source_target_pairs={{4,2},{6,4},{2,0},{12,10},{14,12},{10,8},{20,18},{22,20},{18,16},{... | collective-permute-start | bytes 6291464 | tf_op jit(solution)/shard_map/ppermute | solution.py:32
  14.1 0.1 fusion.14
  14.2 5.9 %collective-permute-start.6 = (bf16[2048,256]{1,0:T(8,128)(2,1)S(1)}, bf16[2048,256]{1,0:T(8,128)(2,1)S(1)}, u32[]{:S(2)}, u32[]{:S(2)}) collective-permute-start(bf16[2048,256]{1,0:T(8,128)(2,1)S(1)} %get-tuple-element.22), channel_id=1, source_target_pairs={{2,4},{0,6},{10,12},{8,14},{18,20},{16,22},{26,28},{24,30},{3,5},{... | collective-permute-start | bytes 3145736 | tf_op jit(solution)/shard_map/ppermute | solution.py:32
  20.2 1.3 %convolution_convert_fusion.1 = bf16[512,512]{1,0:T(8,128)(2,1)S(1)} fusion(bf16[2048,512]{1,0:T(8,128)(2,1)S(1)} %multiply_convert_fusion), kind=kOutput, calls=%fused_computation.7 | convolution fusion | flops 1074003968 | bytes 2621440 | tf_op jit(solution)/shard_map/dot_general | solution.py:82
  21.4 0.0 collective-permute-done.2
  21.5 1.7 %fusion.13 = (bf16[2048,256]{1,0:T(8,128)(2,1)S(1)}, bf16[2048,256]{1,0:T(8,128)(2,1)S(1)}) fusion(bf16[2048,512]{1,0:T(8,128)(2,1)} %collective-permute-done.2), kind=kLoop, calls=%fused_computation.50 | loop fusion | bytes 4194304 | tf_op jit(solution)/shard_map/slice | solution.py:44
  23.1 0.7 collective-permute-start.4
  23.9 0.0 collective-permute-done.1
  23.9 1.7 %fusion.12 = (bf16[2048,256]{1,0:T(8,128)(2,1)S(1)}, bf16[2048,256]{1,0:T(8,128)(2,1)S(1)}) fusion(bf16[2048,512]{1,0:T(8,128)(2,1)} %collective-permute-done.1), kind=kLoop, calls=%fused_computation.49 | loop fusion | bytes 4194304 | tf_op jit(solution)/shard_map/slice | solution.py:44
  25.6 0.7 collective-permute-start.5
  26.3 16.5 %collective-permute-done.6 = bf16[2048,256]{1,0:T(8,128)(2,1)S(1)} collective-permute-done((bf16[2048,256]{1,0:T(8,128)(2,1)S(1)}, bf16[2048,256]{1,0:T(8,128)(2,1)S(1)}, u32[]{:S(2)}, u32[]{:S(2)}) %collective-permute-start.6) | collective-permute-done | bytes 1048608 | tf_op jit(solution)/shard_map/ppermute | solution.py:32
  42.8 3.9 %collective-permute-start.12 = (bf16[2048,256]{1,0:T(8,128)(2,1)S(1)}, bf16[2048,256]{1,0:T(8,128)(2,1)S(1)}, u32[]{:S(2)}, u32[]{:S(2)}) collective-permute-start(bf16[2048,256]{1,0:T(8,128)(2,1)S(1)} %get-tuple-element.14), channel_id=1, source_target_pairs={{2,4},{0,6},{10,12},{8,14},{18,20},{16,22},{26,28},{24,30},{3,5},{... | collective-permute-start | bytes 3145736 | tf_op jit(solution)/shard_map/ppermute | solution.py:32
  46.7 2.9 %convolution_convert_fusion = bf16[512,512]{1,0:T(8,128)(2,1)S(1)} fusion(bf16[2048,512]{1,0:T(8,128)(2,1)S(1)} %multiply_convert_fusion, bf16[2048,512]{1,0:T(8,128)(2,1)} %collective-permute-done.2), kind=kOutput, calls=%fused_computation.6 | convolution fusion | flops 1074003968 | bytes 4718592 | tf_op jit(solution)/shard_map/dot_general | solution.py:82
  49.6 0.1 fusion.1
  49.6 1.6 %collective-permute-start.3 = (bf16[2,256,512]{2,1,0:T(8,128)(2,1)S(1)}, bf16[2,256,512]{2,1,0:T(8,128)(2,1)S(1)}, u32[]{:S(2)}, u32[]{:S(2)}) collective-permute-start(bf16[2,256,512]{2,1,0:T(8,128)(2,1)S(1)} %fusion.1), channel_id=1, source_target_pairs={{0,1},{1,0},{2,3},{3,2},{4,5},{5,4},{6,7},{7,6},{8,9},{9,8},{10,11... | collective-permute-start | bytes 1572872 | tf_op jit(solution)/shard_map/ppermute | solution.py:17
  51.2 1.8 %broadcast_select_fusion = bf16[2048,512]{1,0:T(8,128)(2,1)S(1)} fusion(bf16[2048,512]{1,0:T(8,128)(2,1)} %collective-permute-done.1, bf16[2048,512]{1,0:T(8,128)(2,1)} %collective-permute-done.2, pred[]{:T(512)S(6)} %eq.24), kind=kLoop, calls=%fused_computation.5 | loop fusion | flops 1048576 | bytes 6291457 | tf_op jit(solution)/shard_map/jit(_where)/select_n | solution.py:52
  53.0 0.6 pad_maximum_fusion
  53.7 9.8 %collective-permute-done.3 = bf16[2,256,512]{2,1,0:T(8,128)(2,1)S(1)} collective-permute-done((bf16[2,256,512]{2,1,0:T(8,128)(2,1)S(1)}, bf16[2,256,512]{2,1,0:T(8,128)(2,1)S(1)}, u32[]{:S(2)}, u32[]{:S(2)}) %collective-permute-start.3) | collective-permute-done | bytes 524320 | tf_op jit(solution)/shard_map/ppermute | solution.py:17
  63.5 0.2 convert_add_fusion
  63.6 0.2 select_bitcast_fusion.2
  63.9 0.7 collective-permute-start.10
  64.6 0.7 collective-permute-start.11
  65.4 0.2 add_add_fusion.1
  65.5 1.3 %convolution_convert_fusion.3 = bf16[1024,256]{1,0:T(8,128)(2,1)S(1)} fusion(bf16[2048,1024]{1,0:T(8,128)(2,1)S(1)} %pad_maximum_fusion, bf16[2048,256]{1,0:T(8,128)(2,1)S(1)} %add_add_fusion.1), kind=kOutput, calls=%fused_computation.9 | convolution fusion | flops 1074003968 | bytes 5767168 | tf_op jit(solution)/shard_map/dot_general | solution.py:82
  66.9 1.6 %collective-permute-start.7 = (bf16[256,256]{1,0:T(8,128)(2,1)S(1)}, bf16[256,256]{1,0:T(8,128)(2,1)S(1)}, u32[]{:S(2)}, u32[]{:S(2)}) collective-permute-start(bf16[256,256]{1,0:T(8,128)(2,1)S(1)} %dynamic-slice_bitcast_fusion.5), channel_id=1, source_target_pairs={{0,1},{1,0},{2,3},{3,2},{4,5},{5,4},{6,7},{7,6},{8,9},{9,8},{10,11... | collective-permute-start | bytes 393224 | tf_op jit(solution)/shard_map/ppermute | solution.py:17
  68.5 0.2 pad_maximum_fusion.1
  68.8 2.9 %collective-permute-start.8 = (bf16[256,256]{1,0:T(8,128)(2,1)S(1)}, bf16[256,256]{1,0:T(8,128)(2,1)S(1)}, u32[]{:S(2)}, u32[]{:S(2)}) collective-permute-start(bf16[256,256]{1,0:T(8,128)(2,1)S(1)} %get-tuple-element.32), channel_id=1, source_target_pairs={{0,2},{2,0},{4,6},{6,4},{8,10},{10,8},{12,14},{14,12},{16,18},{18,... | collective-permute-start | bytes 393224 | tf_op jit(solution)/shard_map/ppermute | solution.py:69
  71.7 0.3 collective-permute-done.7
  72.0 3.1 %collective-permute-start.9 = (bf16[256,256]{1,0:T(8,128)(2,1)S(1)}, bf16[256,256]{1,0:T(8,128)(2,1)S(1)}, u32[]{:S(2)}, u32[]{:S(2)}) collective-permute-start(bf16[256,256]{1,0:T(8,128)(2,1)S(1)} %get-tuple-element.33), channel_id=1, source_target_pairs={{0,3},{1,2},{2,1},{3,0},{4,7},{5,6},{6,5},{7,4},{8,11},{9,10},{10,... | collective-permute-start | bytes 393224 | tf_op jit(solution)/shard_map/ppermute | solution.py:77
  75.1 0.0 collective-permute-done.10
  75.1 0.0 collective-permute-done.11
  75.1 0.2 add_add_fusion
  75.3 1.3 %convolution_convert_fusion.2 = bf16[1024,256]{1,0:T(8,128)(2,1)S(1)} fusion(bf16[2048,1024]{1,0:T(8,128)(2,1)S(1)} %pad_maximum_fusion, bf16[2048,256]{1,0:T(8,128)(2,1)S(1)} %add_add_fusion), kind=kOutput, calls=%fused_computation.8 | convolution fusion | flops 1074003968 | bytes 5767168 | tf_op jit(solution)/shard_map/dot_general | solution.py:82
  76.7 0.6 collective-permute-start.13
  77.3 1.0 %collective-permute-done.9 = bf16[256,256]{1,0:T(8,128)(2,1)S(1)} collective-permute-done((bf16[256,256]{1,0:T(8,128)(2,1)S(1)}, bf16[256,256]{1,0:T(8,128)(2,1)S(1)}, u32[]{:S(2)}, u32[]{:S(2)}) %collective-permute-start.9) | collective-permute-done | bytes 131104 | tf_op jit(solution)/shard_map/ppermute | solution.py:77
  78.4 4.8 %collective-permute-start.14 = (bf16[256,256]{1,0:T(8,128)(2,1)S(1)}, bf16[256,256]{1,0:T(8,128)(2,1)S(1)}, u32[]{:S(2)}, u32[]{:S(2)}) collective-permute-start(bf16[256,256]{1,0:T(8,128)(2,1)S(1)} %get-tuple-element.30), channel_id=1, source_target_pairs={{0,2},{2,0},{4,6},{6,4},{8,10},{10,8},{12,14},{14,12},{16,18},{18,... | collective-permute-start | bytes 393224 | tf_op jit(solution)/shard_map/ppermute | solution.py:69
  83.2 0.2 collective-permute-start.15
  83.4 0.0 copy-start.1
  83.4 0.7 collective-permute-done.14
  84.1 4.5 %collective-permute-done.15 = bf16[256,256]{1,0:T(8,128)(2,1)S(1)} collective-permute-done((bf16[256,256]{1,0:T(8,128)(2,1)S(1)}, bf16[256,256]{1,0:T(8,128)(2,1)S(1)}, u32[]{:S(2)}, u32[]{:S(2)}) %collective-permute-start.15) | collective-permute-done | bytes 131104 | tf_op jit(solution)/shard_map/ppermute | solution.py:77
  88.7 0.7 select_dynamic-update-slice_fusion
  (21 shorter events, 0.4 us)
Async XLA Ops:
  0.7 3.4 %copy-start = (f32[2048,512]{1,0:T(8,128)S(1)}, f32[2048,512]{1,0:T(8,128)}, u32[]{:S(2)}) copy-start(f32[2048,512]{1,0:T(8,128)} %param.2) | copy-start | bytes 12582916
  4.2 4.6 %collective-permute-start = (f32[2,512]{1,0:T(2,128)S(1)}, f32[2,512]{1,0:T(2,128)S(1)}, u32[]{:S(2)}, u32[]{:S(2)}) collective-permute-start(f32[2,512]{1,0:T(2,128)S(1)} %pad_maximum_fusion.2), channel_id=1, source_target_pairs={{0,1},{1,0},{2,3},{3,2},{4,5},{5,4},{6,7},{7,6},{8,9},{9,8},{10,11... | collective-permute-start | bytes 12296 | tf_op jit(solution)/shard_map/ppermute | solution.py:17
  9.4 12.0 %collective-permute-start.2 = (bf16[2048,512]{1,0:T(8,128)(2,1)S(1)}, bf16[2048,512]{1,0:T(8,128)(2,1)}, u32[]{:S(2)}, u32[]{:S(2)}) collective-permute-start(bf16[2048,512]{1,0:T(8,128)(2,1)S(1)} %multiply_convert_fusion), channel_id=1, source_target_pairs={{0,2},{4,6},{2,8},{6,12},{8,10},{12,14},{10,16},{14,20},{16,18},{2... | collective-permute-start | bytes 6291464 | tf_op jit(solution)/shard_map/ppermute | solution.py:32
  12.0 11.8 %collective-permute-start.1 = (bf16[2048,512]{1,0:T(8,128)(2,1)S(1)}, bf16[2048,512]{1,0:T(8,128)(2,1)}, u32[]{:S(2)}, u32[]{:S(2)}) collective-permute-start(bf16[2048,512]{1,0:T(8,128)(2,1)S(1)} %multiply_convert_fusion), channel_id=1, source_target_pairs={{4,2},{6,4},{2,0},{12,10},{14,12},{10,8},{20,18},{22,20},{18,16},{... | collective-permute-start | bytes 6291464 | tf_op jit(solution)/shard_map/ppermute | solution.py:32
  14.2 28.6 %collective-permute-start.6 = (bf16[2048,256]{1,0:T(8,128)(2,1)S(1)}, bf16[2048,256]{1,0:T(8,128)(2,1)S(1)}, u32[]{:S(2)}, u32[]{:S(2)}) collective-permute-start(bf16[2048,256]{1,0:T(8,128)(2,1)S(1)} %get-tuple-element.22), channel_id=1, source_target_pairs={{2,4},{0,6},{10,12},{8,14},{18,20},{16,22},{26,28},{24,30},{3,5},{... | collective-permute-start | bytes 3145736 | tf_op jit(solution)/shard_map/ppermute | solution.py:32
  23.1 40.7 %collective-permute-start.4 = (bf16[2048,256]{1,0:T(8,128)(2,1)S(1)}, bf16[2048,256]{1,0:T(8,128)(2,1)S(1)}, u32[]{:S(2)}, u32[]{:S(2)}) collective-permute-start(bf16[2048,256]{1,0:T(8,128)(2,1)S(1)} %get-tuple-element.20), channel_id=1, source_target_pairs={{4,2},{12,10},{20,18},{28,26},{5,3},{13,11},{21,19},{29,27}} | collective-permute-start | bytes 3145736 | tf_op jit(solution)/shard_map/ppermute | solution.py:32
  25.6 39.0 %collective-permute-start.5 = (bf16[2048,256]{1,0:T(8,128)(2,1)S(1)}, bf16[2048,256]{1,0:T(8,128)(2,1)S(1)}, u32[]{:S(2)}, u32[]{:S(2)}) collective-permute-start(bf16[2048,256]{1,0:T(8,128)(2,1)S(1)} %get-tuple-element.18), channel_id=1, source_target_pairs={{2,8},{10,16},{18,24},{3,9},{11,17},{19,25}} | collective-permute-start | bytes 3145736 | tf_op jit(solution)/shard_map/ppermute | solution.py:32
  42.8 32.2 %collective-permute-start.12 = (bf16[2048,256]{1,0:T(8,128)(2,1)S(1)}, bf16[2048,256]{1,0:T(8,128)(2,1)S(1)}, u32[]{:S(2)}, u32[]{:S(2)}) collective-permute-start(bf16[2048,256]{1,0:T(8,128)(2,1)S(1)} %get-tuple-element.14), channel_id=1, source_target_pairs={{2,4},{0,6},{10,12},{8,14},{18,20},{16,22},{26,28},{24,30},{3,5},{... | collective-permute-start | bytes 3145736 | tf_op jit(solution)/shard_map/ppermute | solution.py:32
  49.6 13.8 %collective-permute-start.3 = (bf16[2,256,512]{2,1,0:T(8,128)(2,1)S(1)}, bf16[2,256,512]{2,1,0:T(8,128)(2,1)S(1)}, u32[]{:S(2)}, u32[]{:S(2)}) collective-permute-start(bf16[2,256,512]{2,1,0:T(8,128)(2,1)S(1)} %fusion.1), channel_id=1, source_target_pairs={{0,1},{1,0},{2,3},{3,2},{4,5},{5,4},{6,7},{7,6},{8,9},{9,8},{10,11... | collective-permute-start | bytes 1572872 | tf_op jit(solution)/shard_map/ppermute | solution.py:17
  63.9 11.2 %collective-permute-start.10 = (bf16[2048,256]{1,0:T(8,128)(2,1)S(1)}, bf16[2048,256]{1,0:T(8,128)(2,1)S(1)}, u32[]{:S(2)}, u32[]{:S(2)}) collective-permute-start(bf16[2048,256]{1,0:T(8,128)(2,1)S(1)} %get-tuple-element.12), channel_id=1, source_target_pairs={{4,2},{12,10},{20,18},{28,26},{5,3},{13,11},{21,19},{29,27}} | collective-permute-start | bytes 3145736 | tf_op jit(solution)/shard_map/ppermute | solution.py:32
  64.6 10.5 %collective-permute-start.11 = (bf16[2048,256]{1,0:T(8,128)(2,1)S(1)}, bf16[2048,256]{1,0:T(8,128)(2,1)S(1)}, u32[]{:S(2)}, u32[]{:S(2)}) collective-permute-start(bf16[2048,256]{1,0:T(8,128)(2,1)S(1)} %get-tuple-element.13), channel_id=1, source_target_pairs={{2,8},{10,16},{18,24},{3,9},{11,17},{19,25}} | collective-permute-start | bytes 3145736 | tf_op jit(solution)/shard_map/ppermute | solution.py:32
  66.9 5.0 %collective-permute-start.7 = (bf16[256,256]{1,0:T(8,128)(2,1)S(1)}, bf16[256,256]{1,0:T(8,128)(2,1)S(1)}, u32[]{:S(2)}, u32[]{:S(2)}) collective-permute-start(bf16[256,256]{1,0:T(8,128)(2,1)S(1)} %dynamic-slice_bitcast_fusion.5), channel_id=1, source_target_pairs={{0,1},{1,0},{2,3},{3,2},{4,5},{5,4},{6,7},{7,6},{8,9},{9,8},{10,11... | collective-permute-start | bytes 393224 | tf_op jit(solution)/shard_map/ppermute | solution.py:17
  68.8 8.5 %collective-permute-start.8 = (bf16[256,256]{1,0:T(8,128)(2,1)S(1)}, bf16[256,256]{1,0:T(8,128)(2,1)S(1)}, u32[]{:S(2)}, u32[]{:S(2)}) collective-permute-start(bf16[256,256]{1,0:T(8,128)(2,1)S(1)} %get-tuple-element.32), channel_id=1, source_target_pairs={{0,2},{2,0},{4,6},{6,4},{8,10},{10,8},{12,14},{14,12},{16,18},{18,... | collective-permute-start | bytes 393224 | tf_op jit(solution)/shard_map/ppermute | solution.py:69
  72.0 6.3 %collective-permute-start.9 = (bf16[256,256]{1,0:T(8,128)(2,1)S(1)}, bf16[256,256]{1,0:T(8,128)(2,1)S(1)}, u32[]{:S(2)}, u32[]{:S(2)}) collective-permute-start(bf16[256,256]{1,0:T(8,128)(2,1)S(1)} %get-tuple-element.33), channel_id=1, source_target_pairs={{0,3},{1,2},{2,1},{3,0},{4,7},{5,6},{6,5},{7,4},{8,11},{9,10},{10,... | collective-permute-start | bytes 393224 | tf_op jit(solution)/shard_map/ppermute | solution.py:77
  76.7 6.6 %collective-permute-start.13 = (bf16[256,256]{1,0:T(8,128)(2,1)S(1)}, bf16[256,256]{1,0:T(8,128)(2,1)S(1)}, u32[]{:S(2)}, u32[]{:S(2)}) collective-permute-start(bf16[256,256]{1,0:T(8,128)(2,1)S(1)} %dynamic-slice_bitcast_fusion.2), channel_id=1, source_target_pairs={{0,1},{1,0},{2,3},{3,2},{4,5},{5,4},{6,7},{7,6},{8,9},{9,8},{10,11... | collective-permute-start | bytes 393224 | tf_op jit(solution)/shard_map/ppermute | solution.py:17
  78.4 5.8 %collective-permute-start.14 = (bf16[256,256]{1,0:T(8,128)(2,1)S(1)}, bf16[256,256]{1,0:T(8,128)(2,1)S(1)}, u32[]{:S(2)}, u32[]{:S(2)}) collective-permute-start(bf16[256,256]{1,0:T(8,128)(2,1)S(1)} %get-tuple-element.30), channel_id=1, source_target_pairs={{0,2},{2,0},{4,6},{6,4},{8,10},{10,8},{12,14},{14,12},{16,18},{18,... | collective-permute-start | bytes 393224 | tf_op jit(solution)/shard_map/ppermute | solution.py:69
  83.2 5.5 %collective-permute-start.15 = (bf16[256,256]{1,0:T(8,128)(2,1)S(1)}, bf16[256,256]{1,0:T(8,128)(2,1)S(1)}, u32[]{:S(2)}, u32[]{:S(2)}) collective-permute-start(bf16[256,256]{1,0:T(8,128)(2,1)S(1)} %get-tuple-element.31), channel_id=1, source_target_pairs={{0,3},{1,2},{2,1},{3,0},{4,7},{5,6},{6,5},{7,4},{8,11},{9,10},{10,... | collective-permute-start | bytes 393224 | tf_op jit(solution)/shard_map/ppermute | solution.py:77
  83.4 5.3 %copy-start.1 = (f32[256,2048]{1,0:T(8,128)}, f32[256,2048]{1,0:T(8,128)S(1)}, u32[]{:S(2)}) copy-start(f32[256,2048]{1,0:T(8,128)S(1)} %fusion.6) | copy-start | bytes 6291460

commit v16 on v13

--- a/solution.py
+++ b/solution.py
@@ -34,10 +34,10 @@
     def pairs_of(*steps):
         return [(b + s, b + t) for b in range(0, count, 4) for s, t in steps]
 
-    cross = send(standard, pairs_of((1, 2), (0, 3)))
+    cross = send(standard, pairs_of((1, 2), (0, 3), (3, 5)))
     fast_a = send(standard, pairs_of((0, 1), (2, 3), (1, 4), (3, 6)))
     fast_b = send(standard, pairs_of((2, 1), (3, 2), (1, 0)))
-    relay = send(fast_b, pairs_of((1, 4))) + send(fast_a, pairs_of((2, 1)))
+    relay = send(fast_b, pairs_of((1, 4)))
     width = standard.shape[1]
     early = early_of(tile_term(standard, fast_a).astype(jnp.bfloat16))
     both, early = lax.optimization_barrier(

time: 83 us -> 83.4 us (level)
  waiting for transfers between devices: 47.6 us -> 48.6 us
  starting transfers between devices: 18.4 us -> 17.5 us
    ppermute x5 -> x4, starting transfers between devices: 11.5 us -> 10.1 us  [send(): return lax.ppermute(value, 'snp', pairs)]
    ppermute x1, waiting for transfers between devices: 4.55 us -> 5.72 us  [to_partner(): lax.ppermute(outgoing, ('snp', 'smp'), pairs).astype(jnp.float32)]
    ppermute x5 -> x4, waiting for transfers between devices: 29.6 us -> 30.1 us  [send(): return lax.ppermute(value, 'snp', pairs)]
  transfers between devices with their start and end apart: 10 -> 9, of which waited for: 5 -> 5; matrix products, arithmetic and copies ran while one was open for 9% -> 9% of each run, Pallas kernels for 0% -> 0%
where the time goes in v16:
time: 83.4 us; the launch traced here: 83.1 us
  waiting for transfers between devices  48.6 us (58%)
  starting transfers between devices  17.5 us (21%)
  other arithmetic  8.21 us (10%)
  matrix products  6.49 us (8%)
  local copies, waits for them, and re-layouts  1.41 us (2%)
  between operations  0.84 us (1%)
    ppermute x4, waiting for transfers between devices, send(): return lax.ppermute(value, 'snp', pairs)  30.1 us
    ppermute x3, waiting for transfers between devices, rotated(): lax.ppermute(value, axis, [(source, (source + steps) % count) for source...  12.8 us
    ppermute x4, starting transfers between devices, send(): return lax.ppermute(value, 'snp', pairs)  10.1 us
    dot_general x3, matrix products, tile_term(): lax.dot_general(standard, neighbour, (((0,), (0,)), ((), ())), preferred_...  6.49 us
    ppermute x3, starting transfers between devices, rotated(): lax.ppermute(value, axis, [(source, (source + steps) % count) for source...  6.21 us
    ppermute x1, waiting for transfers between devices, to_partner(): lax.ppermute(outgoing, ('snp', 'smp'), pairs).astype(jnp.float32)  5.72 us
    reduce_sum x1, other arithmetic, local(): part_square = jnp.sum(shifted_dosage * shifted_dosage, axis=0)  2.94 us
    select_n x1, other arithmetic, relayed(): jnp.where(place % 2 == 0, fast_b, fast_a)  1.81 us
  transfers between devices with their start and end apart: 9, of which 5 were waited for; matrix products, arithmetic and copies ran while one was open for 9% of the time, Pallas kernels for 0%

profile of v16, /device:TPU:0, one launch (start us, length us, event | category | flops | bytes accessed | tf_op | source)
XLA Modules:
  0.0 83.1 jit_solution(13423654361672878442)
XLA Ops:
  0.0 0.7 slice.23
  0.7 0.0 copy-start
  0.7 2.9 %multiply_reduce_fusion = (f32[512]{0:T(512)S(1)}, f32[512]{0:T(512)S(1)}) fusion(f32[2048,512]{1,0:T(8,128)} %param.2, f32[512]{0:T(512)S(1)} %bitcast.56), kind=kLoop, calls=%fused_computation.2 | loop fusion | flops 4193280 | bytes 4200448 | tf_op jit(solution)/shard_map/reduce_sum | solution.py:88
  3.7 0.5 copy-done
  4.2 3.0 %collective-permute-start = (f32[2,512]{1,0:T(2,128)S(1)}, f32[2,512]{1,0:T(2,128)S(1)}, u32[]{:S(2)}, u32[]{:S(2)}) collective-permute-start(f32[2,512]{1,0:T(2,128)S(1)} %pad_maximum_fusion.2), channel_id=1, source_target_pairs={{0,1},{1,0},{2,3},{3,2},{4,5},{5,4},{6,7},{7,6},{8,9},{9,8},{10,11... | collective-permute-start | bytes 12296 | tf_op jit(solution)/shard_map/ppermute | solution.py:17
  7.2 1.6 %collective-permute-done = f32[2,512]{1,0:T(2,128)S(1)} collective-permute-done((f32[2,512]{1,0:T(2,128)S(1)}, f32[2,512]{1,0:T(2,128)S(1)}, u32[]{:S(2)}, u32[]{:S(2)}) %collective-permute-start) | collective-permute-done | bytes 4128 | tf_op jit(solution)/shard_map/ppermute | solution.py:17
  8.8 0.6 multiply_convert_fusion
  9.4 1.3 %collective-permute-start.1 = (bf16[2048,512]{1,0:T(8,128)(2,1)S(1)}, bf16[2048,512]{1,0:T(8,128)(2,1)}, u32[]{:S(2)}, u32[]{:S(2)}) collective-permute-start(bf16[2048,512]{1,0:T(8,128)(2,1)S(1)} %multiply_convert_fusion), channel_id=1, source_target_pairs={{4,2},{6,4},{2,0},{12,10},{14,12},{10,8},{20,18},{22,20},{18,16},{... | collective-permute-start | bytes 6291464 | tf_op jit(solution)/shard_map/ppermute | solution.py:32
  10.7 4.4 %collective-permute-start.2 = (bf16[2048,512]{1,0:T(8,128)(2,1)S(1)}, bf16[2048,512]{1,0:T(8,128)(2,1)}, u32[]{:S(2)}, u32[]{:S(2)}) collective-permute-start(bf16[2048,512]{1,0:T(8,128)(2,1)S(1)} %multiply_convert_fusion), channel_id=1, source_target_pairs={{0,2},{4,6},{2,8},{6,12},{8,10},{12,14},{10,16},{14,20},{16,18},{2... | collective-permute-start | bytes 6291464 | tf_op jit(solution)/shard_map/ppermute | solution.py:32
  15.7 3.7 %collective-permute-start.5 = (bf16[2048,512]{1,0:T(8,128)(2,1)S(1)}, bf16[2048,512]{1,0:T(8,128)(2,1)S(1)}, u32[]{:S(2)}, u32[]{:S(2)}) collective-permute-start(bf16[2048,512]{1,0:T(8,128)(2,1)S(1)} %multiply_convert_fusion), channel_id=1, source_target_pairs={{2,4},{0,6},{6,10},{10,12},{8,14},{14,18},{18,20},{16,22},{22,26},... | collective-permute-start | bytes 6291464 | tf_op jit(solution)/shard_map/ppermute | solution.py:32
  19.5 0.0 collective-permute-done.1
  19.5 0.8 collective-permute-start.4
  20.3 1.3 %convolution_convert_fusion.2 = bf16[512,512]{1,0:T(8,128)(2,1)S(1)} fusion(bf16[2048,512]{1,0:T(8,128)(2,1)S(1)} %multiply_convert_fusion), kind=kOutput, calls=%fused_computation.8 | convolution fusion | flops 1074003968 | bytes 2621440 | tf_op jit(solution)/shard_map/dot_general | solution.py:74
  21.6 0.0 collective-permute-done.2
  21.6 2.9 %convolution_convert_fusion.1 = bf16[512,512]{1,0:T(8,128)(2,1)S(1)} fusion(bf16[2048,512]{1,0:T(8,128)(2,1)S(1)} %multiply_convert_fusion, bf16[2048,512]{1,0:T(8,128)(2,1)} %collective-permute-done.2), kind=kOutput, calls=%fused_computation.7 | convolution fusion | flops 1074003968 | bytes 4718592 | tf_op jit(solution)/shard_map/dot_general | solution.py:74
  24.4 0.1 fusion.1
  24.5 1.6 %collective-permute-start.3 = (bf16[2,256,512]{2,1,0:T(8,128)(2,1)S(1)}, bf16[2,256,512]{2,1,0:T(8,128)(2,1)S(1)}, u32[]{:S(2)}, u32[]{:S(2)}) collective-permute-start(bf16[2,256,512]{2,1,0:T(8,128)(2,1)S(1)} %fusion.1), channel_id=1, source_target_pairs={{0,1},{1,0},{2,3},{3,2},{4,5},{5,4},{6,7},{7,6},{8,9},{9,8},{10,11... | collective-permute-start | bytes 1572872 | tf_op jit(solution)/shard_map/ppermute | solution.py:17
  26.1 1.8 %broadcast_select_fusion = bf16[2048,512]{1,0:T(8,128)(2,1)S(1)} fusion(bf16[2048,512]{1,0:T(8,128)(2,1)} %collective-permute-done.1, bf16[2048,512]{1,0:T(8,128)(2,1)} %collective-permute-done.2, pred[]{:T(512)S(6)} %eq.22), kind=kLoop, calls=%fused_computation.5 | loop fusion | flops 1048576 | bytes 6291457 | tf_op jit(solution)/shard_map/jit(_where)/select_n | solution.py:44
  27.9 0.6 pad_maximum_fusion
  28.5 5.2 %collective-permute-done.3 = bf16[2,256,512]{2,1,0:T(8,128)(2,1)S(1)} collective-permute-done((bf16[2,256,512]{2,1,0:T(8,128)(2,1)S(1)}, bf16[2,256,512]{2,1,0:T(8,128)(2,1)S(1)}, u32[]{:S(2)}, u32[]{:S(2)}) %collective-permute-start.3) | collective-permute-done | bytes 524320 | tf_op jit(solution)/shard_map/ppermute | solution.py:17
  33.7 0.2 convert_add_fusion
  33.9 0.2 select_bitcast_fusion.2
  34.1 30.1 %collective-permute-done.5 = bf16[2048,512]{1,0:T(8,128)(2,1)S(1)} collective-permute-done((bf16[2048,512]{1,0:T(8,128)(2,1)S(1)}, bf16[2048,512]{1,0:T(8,128)(2,1)S(1)}, u32[]{:S(2)}, u32[]{:S(2)}) %collective-permute-start.5) | collective-permute-done | bytes 2097184 | tf_op jit(solution)/shard_map/ppermute | solution.py:32
  64.2 0.0 collective-permute-done.4
  64.3 0.6 add.92
  64.8 2.4 %convolution_convert_fusion = bf16[1024,512]{1,0:T(8,128)(2,1)S(1)} fusion(bf16[2048,1024]{1,0:T(8,128)(2,1)S(1)} %pad_maximum_fusion, bf16[2048,512]{1,0:T(8,128)(2,1)S(1)} %add.92), kind=kOutput, calls=%fused_computation.6 | convolution fusion | flops 2148007936 | bytes 7340032 | tf_op jit(solution)/shard_map/dot_general | solution.py:74
  67.2 0.1 fusion.9
  67.3 1.6 %collective-permute-start.6 = (bf16[256,512]{1,0:T(8,128)(2,1)S(1)}, bf16[256,512]{1,0:T(8,128)(2,1)S(1)}, u32[]{:S(2)}, u32[]{:S(2)}) collective-permute-start(bf16[256,512]{1,0:T(8,128)(2,1)S(1)} %dynamic-slice_bitcast_fusion.2), channel_id=1, source_target_pairs={{0,1},{1,0},{2,3},{3,2},{4,5},{5,4},{6,7},{7,6},{8,9},{9,8},{10,11... | collective-permute-start | bytes 786440 | tf_op jit(solution)/shard_map/ppermute | solution.py:17
  68.9 1.0 %collective-permute-start.7 = (bf16[256,512]{1,0:T(8,128)(2,1)S(1)}, bf16[256,512]{1,0:T(8,128)(2,1)S(1)}, u32[]{:S(2)}, u32[]{:S(2)}) collective-permute-start(bf16[256,512]{1,0:T(8,128)(2,1)S(1)} %get-tuple-element.16), channel_id=1, source_target_pairs={{0,2},{2,0},{4,6},{6,4},{8,10},{10,8},{12,14},{14,12},{16,18},{18,... | collective-permute-start | bytes 786440 | tf_op jit(solution)/shard_map/ppermute | solution.py:61
  69.9 0.2 collective-permute-start.8
  70.2 0.2 pad_maximum_fusion.1
  70.3 6.0 %collective-permute-done.6 = bf16[256,512]{1,0:T(8,128)(2,1)S(1)} collective-permute-done((bf16[256,512]{1,0:T(8,128)(2,1)S(1)}, bf16[256,512]{1,0:T(8,128)(2,1)S(1)}, u32[]{:S(2)}, u32[]{:S(2)}) %collective-permute-start.6) | collective-permute-done | bytes 262176 | tf_op jit(solution)/shard_map/ppermute | solution.py:17
  76.3 0.1 fusion.6
  76.4 0.0 copy-start.1
  76.5 0.0 collective-permute-done.7
  76.5 5.7 %collective-permute-done.8 = bf16[256,512]{1,0:T(8,128)(2,1)S(1)} collective-permute-done((bf16[256,512]{1,0:T(8,128)(2,1)S(1)}, bf16[256,512]{1,0:T(8,128)(2,1)S(1)}, u32[]{:S(2)}, u32[]{:S(2)}) %collective-permute-start.8) | collective-permute-done | bytes 262176 | tf_op jit(solution)/shard_map/ppermute | solution.py:69
  82.2 0.0 copy-done.1
  82.2 0.9 %select_dynamic-update-slice_fusion = f32[256,2048]{1,0:T(8,128)} fusion(f32[256,2048]{1,0:T(8,128)} %copy-done.1, s32[]{:T(128)S(6)} %select_n.142, bf16[256,512]{1,0:T(8,128)(2,1)S(1)} %collective-permute-done.8, bf16[256,512]{1,0:T(8,128)(2,1)S(1)} %collective-permute-done.7, pred[]{:T(512)S(6)} %le.7), kind=kLoop, calls=%fused_computation.22 | loop fusion | flops 655360 | bytes 1048581 | tf_op jit(solution)/shard_map/dynamic_update_slice | solution.py:143
  (6 shorter events, 0.1 us)
Async XLA Ops:
  0.7 3.4 %copy-start = (f32[2048,512]{1,0:T(8,128)S(1)}, f32[2048,512]{1,0:T(8,128)}, u32[]{:S(2)}) copy-start(f32[2048,512]{1,0:T(8,128)} %param.2) | copy-start | bytes 12582916
  4.2 4.6 %collective-permute-start = (f32[2,512]{1,0:T(2,128)S(1)}, f32[2,512]{1,0:T(2,128)S(1)}, u32[]{:S(2)}, u32[]{:S(2)}) collective-permute-start(f32[2,512]{1,0:T(2,128)S(1)} %pad_maximum_fusion.2), channel_id=1, source_target_pairs={{0,1},{1,0},{2,3},{3,2},{4,5},{5,4},{6,7},{7,6},{8,9},{9,8},{10,11... | collective-permute-start | bytes 12296 | tf_op jit(solution)/shard_map/ppermute | solution.py:17
  9.4 10.0 %collective-permute-start.1 = (bf16[2048,512]{1,0:T(8,128)(2,1)S(1)}, bf16[2048,512]{1,0:T(8,128)(2,1)}, u32[]{:S(2)}, u32[]{:S(2)}) collective-permute-start(bf16[2048,512]{1,0:T(8,128)(2,1)S(1)} %multiply_convert_fusion), channel_id=1, source_target_pairs={{4,2},{6,4},{2,0},{12,10},{14,12},{10,8},{20,18},{22,20},{18,16},{... | collective-permute-start | bytes 6291464 | tf_op jit(solution)/shard_map/ppermute | solution.py:32
  10.7 10.8 %collective-permute-start.2 = (bf16[2048,512]{1,0:T(8,128)(2,1)S(1)}, bf16[2048,512]{1,0:T(8,128)(2,1)}, u32[]{:S(2)}, u32[]{:S(2)}) collective-permute-start(bf16[2048,512]{1,0:T(8,128)(2,1)S(1)} %multiply_convert_fusion), channel_id=1, source_target_pairs={{0,2},{4,6},{2,8},{6,12},{8,10},{12,14},{10,16},{14,20},{16,18},{2... | collective-permute-start | bytes 6291464 | tf_op jit(solution)/shard_map/ppermute | solution.py:32
  15.7 48.5 %collective-permute-start.5 = (bf16[2048,512]{1,0:T(8,128)(2,1)S(1)}, bf16[2048,512]{1,0:T(8,128)(2,1)S(1)}, u32[]{:S(2)}, u32[]{:S(2)}) collective-permute-start(bf16[2048,512]{1,0:T(8,128)(2,1)S(1)} %multiply_convert_fusion), channel_id=1, source_target_pairs={{2,4},{0,6},{6,10},{10,12},{8,14},{14,18},{18,20},{16,22},{22,26},... | collective-permute-start | bytes 6291464 | tf_op jit(solution)/shard_map/ppermute | solution.py:32
  19.5 44.8 %collective-permute-start.4 = (bf16[2048,512]{1,0:T(8,128)(2,1)}, bf16[2048,512]{1,0:T(8,128)(2,1)S(1)}, u32[]{:S(2)}, u32[]{:S(2)}) collective-permute-start(bf16[2048,512]{1,0:T(8,128)(2,1)} %collective-permute-done.1), channel_id=1, source_target_pairs={{2,8},{10,16},{18,24},{3,9},{11,17},{19,25}} | collective-permute-start | bytes 6291464 | tf_op jit(solution)/shard_map/ppermute | solution.py:32
  24.5 9.2 %collective-permute-start.3 = (bf16[2,256,512]{2,1,0:T(8,128)(2,1)S(1)}, bf16[2,256,512]{2,1,0:T(8,128)(2,1)S(1)}, u32[]{:S(2)}, u32[]{:S(2)}) collective-permute-start(bf16[2,256,512]{2,1,0:T(8,128)(2,1)S(1)} %fusion.1), channel_id=1, source_target_pairs={{0,1},{1,0},{2,3},{3,2},{4,5},{5,4},{6,7},{7,6},{8,9},{9,8},{10,11... | collective-permute-start | bytes 1572872 | tf_op jit(solution)/shard_map/ppermute | solution.py:17
  67.3 9.0 %collective-permute-start.6 = (bf16[256,512]{1,0:T(8,128)(2,1)S(1)}, bf16[256,512]{1,0:T(8,128)(2,1)S(1)}, u32[]{:S(2)}, u32[]{:S(2)}) collective-permute-start(bf16[256,512]{1,0:T(8,128)(2,1)S(1)} %dynamic-slice_bitcast_fusion.2), channel_id=1, source_target_pairs={{0,1},{1,0},{2,3},{3,2},{4,5},{5,4},{6,7},{7,6},{8,9},{9,8},{10,11... | collective-permute-start | bytes 786440 | tf_op jit(solution)/shard_map/ppermute | solution.py:17
  68.9 7.5 %collective-permute-start.7 = (bf16[256,512]{1,0:T(8,128)(2,1)S(1)}, bf16[256,512]{1,0:T(8,128)(2,1)S(1)}, u32[]{:S(2)}, u32[]{:S(2)}) collective-permute-start(bf16[256,512]{1,0:T(8,128)(2,1)S(1)} %get-tuple-element.16), channel_id=1, source_target_pairs={{0,2},{2,0},{4,6},{6,4},{8,10},{10,8},{12,14},{14,12},{16,18},{18,... | collective-permute-start | bytes 786440 | tf_op jit(solution)/shard_map/ppermute | solution.py:61
  69.9 12.3 %collective-permute-start.8 = (bf16[256,512]{1,0:T(8,128)(2,1)S(1)}, bf16[256,512]{1,0:T(8,128)(2,1)S(1)}, u32[]{:S(2)}, u32[]{:S(2)}) collective-permute-start(bf16[256,512]{1,0:T(8,128)(2,1)S(1)} %get-tuple-element.17), channel_id=1, source_target_pairs={{0,3},{1,2},{2,1},{3,0},{4,7},{5,6},{6,5},{7,4},{8,11},{9,10},{10,... | collective-permute-start | bytes 786440 | tf_op jit(solution)/shard_map/ppermute | solution.py:69
  76.4 5.7 %copy-start.1 = (f32[256,2048]{1,0:T(8,128)}, f32[256,2048]{1,0:T(8,128)S(1)}, u32[]{:S(2)}) copy-start(f32[256,2048]{1,0:T(8,128)S(1)} %fusion.6) | copy-start | bytes 6291460

commit v17 on v13

--- a/solution.py
+++ b/solution.py
@@ -84,8 +84,13 @@
 
     origin = dosage[0]
     shifted_dosage = dosage - origin
-    part_sum = jnp.sum(shifted_dosage, axis=0)
-    part_square = jnp.sum(shifted_dosage * shifted_dosage, axis=0)
+    groups = 16 if rows % 128 == 0 else 1
+    grouped = shifted_dosage.reshape(groups, rows // groups, width)
+    part_sum, part_square = lax.optimization_barrier(
+        (jnp.sum(grouped, axis=1), jnp.sum(grouped * grouped, axis=1))
+    )
+    part_sum = jnp.sum(part_sum, axis=0)
+    part_square = jnp.sum(part_square, axis=0)
     part_mean = origin + part_sum / rows
     part_m2 = part_square - part_sum * (part_sum / rows)
     stats = jnp.stack([part_mean, part_m2])

time: 83 us -> 85.4 us (1.029)
  other arithmetic: 7.88 us -> 10.8 us
    convert_element_type x1, other arithmetic: 0.59 us -> 2.78 us  [local(): standard = ((dosage - mean) * lax.rsqrt(var + 1e-05)).astype(jnp.bfloat16)]
    reduce_sum x1 -> x3, other arithmetic: 2.94 us -> 2.89 us  [the longest x1 2.85 us: local(): jnp.sum(grouped * grouped, axis=1)]
where the time goes in v17:
time: 85.4 us; the launch traced here: 85 us
  waiting for transfers between devices  47.5 us (56%)
  starting transfers between devices  18.4 us (22%)
  other arithmetic  10.8 us (13%)
  matrix products  6.49 us (8%)
  local copies, waits for them, and re-layouts  0.9 us (1%)
  between operations  0.9 us (1%)
    ppermute x5, waiting for transfers between devices, send(): return lax.ppermute(value, 'snp', pairs)  29.6 us
    ppermute x3, waiting for transfers between devices, rotated(): lax.ppermute(value, axis, [(source, (source + steps) % count) for source...  13.4 us
    ppermute x5, starting transfers between devices, send(): return lax.ppermute(value, 'snp', pairs)  11.5 us
    dot_general x3, matrix products, tile_term(): lax.dot_general(standard, neighbour, (((0,), (0,)), ((), ())), preferred_...  6.49 us
    ppermute x3, starting transfers between devices, rotated(): lax.ppermute(value, axis, [(source, (source + steps) % count) for source...  6.22 us
    ppermute x1, waiting for transfers between devices, to_partner(): lax.ppermute(outgoing, ('snp', 'smp'), pairs).astype(jnp.float32)  4.54 us
    reduce_sum x1, other arithmetic, local(): jnp.sum(grouped * grouped, axis=1)  2.85 us
    convert_element_type x1, other arithmetic, local(): standard = ((dosage - mean) * lax.rsqrt(var + 1e-05)).astype(jnp.bfloat16)  2.78 us
  transfers between devices with their start and end apart: 10, of which 5 were waited for; matrix products, arithmetic and copies ran while one was open for 9% of the time, Pallas kernels for 0%

profile of v17, /device:TPU:0, one launch (start us, length us, event | category | flops | bytes accessed | tf_op | source)
XLA Modules:
  0.0 85.0 jit_solution(3972309850853641326)
XLA Ops:
  0.0 0.7 slice.23
  0.7 2.8 %fusion = (f32[16,512]{1,0:T(8,128)S(1)}, f32[16,512]{1,0:T(8,128)S(1)}) fusion(f32[2048,512]{1,0:T(8,128)} %param.2, f32[512]{0:T(512)S(1)} %bitcast.59), kind=kLoop, calls=%fused_computation.3 | loop fusion | flops 4177920 | bytes 4261888 | tf_op jit(solution)/shard_map/reduce_sum | solution.py:90
  3.6 0.7 fusion.8
  4.3 3.0 %collective-permute-start = (f32[2,512]{1,0:T(2,128)S(1)}, f32[2,512]{1,0:T(2,128)S(1)}, u32[]{:S(2)}, u32[]{:S(2)}) collective-permute-start(f32[2,512]{1,0:T(2,128)S(1)} %pad_maximum_fusion.2), channel_id=1, source_target_pairs={{0,1},{1,0},{2,3},{3,2},{4,5},{5,4},{6,7},{7,6},{8,9},{9,8},{10,11... | collective-permute-start | bytes 12296 | tf_op jit(solution)/shard_map/ppermute | solution.py:17
  7.4 1.6 %collective-permute-done = f32[2,512]{1,0:T(2,128)S(1)} collective-permute-done((f32[2,512]{1,0:T(2,128)S(1)}, f32[2,512]{1,0:T(2,128)S(1)}, u32[]{:S(2)}, u32[]{:S(2)}) %collective-permute-start) | collective-permute-done | bytes 4128 | tf_op jit(solution)/shard_map/ppermute | solution.py:17
  9.0 2.8 %multiply_convert_fusion = bf16[2048,512]{1,0:T(8,128)(2,1)S(1)} fusion(f32[2048,512]{1,0:T(8,128)} %param.2, f32[512]{0:T(512)S(1)} %bitcast.61, f32[512]{0:T(512)S(1)} %bitcast.60), kind=kLoop, calls=%fused_computation.4 | loop fusion | flops 3145728 | bytes 6295552 | tf_op jit(solution)/shard_map/convert_element_type | solution.py:108
  11.8 2.6 %collective-permute-start.2 = (bf16[2048,512]{1,0:T(8,128)(2,1)S(1)}, bf16[2048,512]{1,0:T(8,128)(2,1)}, u32[]{:S(2)}, u32[]{:S(2)}) collective-permute-start(bf16[2048,512]{1,0:T(8,128)(2,1)S(1)} %multiply_convert_fusion), channel_id=1, source_target_pairs={{0,2},{4,6},{2,8},{6,12},{8,10},{12,14},{10,16},{14,20},{16,18},{2... | collective-permute-start | bytes 6291464 | tf_op jit(solution)/shard_map/ppermute | solution.py:32
  14.4 1.3 %collective-permute-start.1 = (bf16[2048,512]{1,0:T(8,128)(2,1)S(1)}, bf16[2048,512]{1,0:T(8,128)(2,1)}, u32[]{:S(2)}, u32[]{:S(2)}) collective-permute-start(bf16[2048,512]{1,0:T(8,128)(2,1)S(1)} %multiply_convert_fusion), channel_id=1, source_target_pairs={{4,2},{6,4},{2,0},{12,10},{14,12},{10,8},{20,18},{22,20},{18,16},{... | collective-permute-start | bytes 6291464 | tf_op jit(solution)/shard_map/ppermute | solution.py:32
  16.4 6.0 %collective-permute-start.6 = (bf16[2048,512]{1,0:T(8,128)(2,1)S(1)}, bf16[2048,512]{1,0:T(8,128)(2,1)S(1)}, u32[]{:S(2)}, u32[]{:S(2)}) collective-permute-start(bf16[2048,512]{1,0:T(8,128)(2,1)S(1)} %multiply_convert_fusion), channel_id=1, source_target_pairs={{2,4},{0,6},{10,12},{8,14},{18,20},{16,22},{26,28},{24,30},{3,5},{... | collective-permute-start | bytes 6291464 | tf_op jit(solution)/shard_map/ppermute | solution.py:32
  22.4 0.0 collective-permute-done.2
  22.4 0.8 collective-permute-start.5
  23.2 0.0 collective-permute-done.1
  23.2 0.8 collective-permute-start.4
  24.1 1.3 %convolution_convert_fusion.2 = bf16[512,512]{1,0:T(8,128)(2,1)S(1)} fusion(bf16[2048,512]{1,0:T(8,128)(2,1)S(1)} %multiply_convert_fusion), kind=kOutput, calls=%fused_computation.10 | convolution fusion | flops 1074003968 | bytes 2621440 | tf_op jit(solution)/shard_map/dot_general | solution.py:74
  25.3 2.9 %convolution_convert_fusion.1 = bf16[512,512]{1,0:T(8,128)(2,1)S(1)} fusion(bf16[2048,512]{1,0:T(8,128)(2,1)S(1)} %multiply_convert_fusion, bf16[2048,512]{1,0:T(8,128)(2,1)} %collective-permute-done.2), kind=kOutput, calls=%fused_computation.9 | convolution fusion | flops 1074003968 | bytes 4718592 | tf_op jit(solution)/shard_map/dot_general | solution.py:74
  28.2 0.1 fusion.2
  28.3 1.6 %collective-permute-start.3 = (bf16[2,256,512]{2,1,0:T(8,128)(2,1)S(1)}, bf16[2,256,512]{2,1,0:T(8,128)(2,1)S(1)}, u32[]{:S(2)}, u32[]{:S(2)}) collective-permute-start(bf16[2,256,512]{2,1,0:T(8,128)(2,1)S(1)} %fusion.2), channel_id=1, source_target_pairs={{0,1},{1,0},{2,3},{3,2},{4,5},{5,4},{6,7},{7,6},{8,9},{9,8},{10,11... | collective-permute-start | bytes 1572872 | tf_op jit(solution)/shard_map/ppermute | solution.py:17
  29.9 1.8 %broadcast_select_fusion = bf16[2048,512]{1,0:T(8,128)(2,1)S(1)} fusion(bf16[2048,512]{1,0:T(8,128)(2,1)} %collective-permute-done.1, bf16[2048,512]{1,0:T(8,128)(2,1)} %collective-permute-done.2, pred[]{:T(512)S(6)} %eq.22), kind=kLoop, calls=%fused_computation.7 | loop fusion | flops 1048576 | bytes 6291457 | tf_op jit(solution)/shard_map/jit(_where)/select_n | solution.py:44
  31.7 0.6 pad_maximum_fusion
  32.3 5.2 %collective-permute-done.3 = bf16[2,256,512]{2,1,0:T(8,128)(2,1)S(1)} collective-permute-done((bf16[2,256,512]{2,1,0:T(8,128)(2,1)S(1)}, bf16[2,256,512]{2,1,0:T(8,128)(2,1)S(1)}, u32[]{:S(2)}, u32[]{:S(2)}) %collective-permute-start.3) | collective-permute-done | bytes 524320 | tf_op jit(solution)/shard_map/ppermute | solution.py:17
  37.5 0.2 convert_add_fusion
  37.7 0.2 select_bitcast_fusion.2
  37.9 29.6 %collective-permute-done.6 = bf16[2048,512]{1,0:T(8,128)(2,1)S(1)} collective-permute-done((bf16[2048,512]{1,0:T(8,128)(2,1)S(1)}, bf16[2048,512]{1,0:T(8,128)(2,1)S(1)}, u32[]{:S(2)}, u32[]{:S(2)}) %collective-permute-start.6) | collective-permute-done | bytes 2097184 | tf_op jit(solution)/shard_map/ppermute | solution.py:32
  67.5 0.0 collective-permute-done.5
  67.5 0.0 collective-permute-done.4
  67.5 0.3 add_add_fusion
  67.8 2.4 %convolution_convert_fusion = bf16[1024,512]{1,0:T(8,128)(2,1)S(1)} fusion(bf16[2048,1024]{1,0:T(8,128)(2,1)S(1)} %pad_maximum_fusion, bf16[2048,512]{1,0:T(8,128)(2,1)S(1)} %add_add_fusion), kind=kOutput, calls=%fused_computation.8 | convolution fusion | flops 2148007936 | bytes 7340032 | tf_op jit(solution)/shard_map/dot_general | solution.py:74
  70.2 0.1 fusion.10
  70.3 1.6 %collective-permute-start.7 = (bf16[256,512]{1,0:T(8,128)(2,1)S(1)}, bf16[256,512]{1,0:T(8,128)(2,1)S(1)}, u32[]{:S(2)}, u32[]{:S(2)}) collective-permute-start(bf16[256,512]{1,0:T(8,128)(2,1)S(1)} %dynamic-slice_bitcast_fusion.2), channel_id=1, source_target_pairs={{0,1},{1,0},{2,3},{3,2},{4,5},{5,4},{6,7},{7,6},{8,9},{9,8},{10,11... | collective-permute-start | bytes 786440 | tf_op jit(solution)/shard_map/ppermute | solution.py:17
  71.9 0.2 collective-permute-start.8
  72.1 0.5 collective-permute-start.9
  72.6 0.2 pad_maximum_fusion.1
  72.8 6.6 %collective-permute-done.7 = bf16[256,512]{1,0:T(8,128)(2,1)S(1)} collective-permute-done((bf16[256,512]{1,0:T(8,128)(2,1)S(1)}, bf16[256,512]{1,0:T(8,128)(2,1)S(1)}, u32[]{:S(2)}, u32[]{:S(2)}) %collective-permute-start.7) | collective-permute-done | bytes 262176 | tf_op jit(solution)/shard_map/ppermute | solution.py:17
  79.5 0.1 fusion.7
  79.6 0.0 copy-start
  79.6 0.0 collective-permute-done.8
  79.6 4.5 %collective-permute-done.9 = bf16[256,512]{1,0:T(8,128)(2,1)S(1)} collective-permute-done((bf16[256,512]{1,0:T(8,128)(2,1)S(1)}, bf16[256,512]{1,0:T(8,128)(2,1)S(1)}, u32[]{:S(2)}, u32[]{:S(2)}) %collective-permute-start.9) | collective-permute-done | bytes 262176 | tf_op jit(solution)/shard_map/ppermute | solution.py:69
  84.1 0.0 copy-done
  84.1 0.9 %select_dynamic-update-slice_fusion = f32[256,2048]{1,0:T(8,128)} fusion(f32[256,2048]{1,0:T(8,128)} %copy-done, s32[]{:T(128)S(6)} %select_n.142, bf16[256,512]{1,0:T(8,128)(2,1)S(1)} %collective-permute-done.9, bf16[256,512]{1,0:T(8,128)(2,1)S(1)} %collective-permute-done.8, pred[]{:T(512)S(6)} %le.7), kind=kLoop, calls=%fused_computation.24 | loop fusion | flops 655360 | bytes 1048581 | tf_op jit(solution)/shard_map/dynamic_update_slice | solution.py:148
  (7 shorter events, 0.2 us)
Async XLA Ops:
  4.3 4.6 %collective-permute-start = (f32[2,512]{1,0:T(2,128)S(1)}, f32[2,512]{1,0:T(2,128)S(1)}, u32[]{:S(2)}, u32[]{:S(2)}) collective-permute-start(f32[2,512]{1,0:T(2,128)S(1)} %pad_maximum_fusion.2), channel_id=1, source_target_pairs={{0,1},{1,0},{2,3},{3,2},{4,5},{5,4},{6,7},{7,6},{8,9},{9,8},{10,11... | collective-permute-start | bytes 12296 | tf_op jit(solution)/shard_map/ppermute | solution.py:17
  11.8 10.7 %collective-permute-start.2 = (bf16[2048,512]{1,0:T(8,128)(2,1)S(1)}, bf16[2048,512]{1,0:T(8,128)(2,1)}, u32[]{:S(2)}, u32[]{:S(2)}) collective-permute-start(bf16[2048,512]{1,0:T(8,128)(2,1)S(1)} %multiply_convert_fusion), channel_id=1, source_target_pairs={{0,2},{4,6},{2,8},{6,12},{8,10},{12,14},{10,16},{14,20},{16,18},{2... | collective-permute-start | bytes 6291464 | tf_op jit(solution)/shard_map/ppermute | solution.py:32
  14.4 8.8 %collective-permute-start.1 = (bf16[2048,512]{1,0:T(8,128)(2,1)S(1)}, bf16[2048,512]{1,0:T(8,128)(2,1)}, u32[]{:S(2)}, u32[]{:S(2)}) collective-permute-start(bf16[2048,512]{1,0:T(8,128)(2,1)S(1)} %multiply_convert_fusion), channel_id=1, source_target_pairs={{4,2},{6,4},{2,0},{12,10},{14,12},{10,8},{20,18},{22,20},{18,16},{... | collective-permute-start | bytes 6291464 | tf_op jit(solution)/shard_map/ppermute | solution.py:32
  16.4 51.1 %collective-permute-start.6 = (bf16[2048,512]{1,0:T(8,128)(2,1)S(1)}, bf16[2048,512]{1,0:T(8,128)(2,1)S(1)}, u32[]{:S(2)}, u32[]{:S(2)}) collective-permute-start(bf16[2048,512]{1,0:T(8,128)(2,1)S(1)} %multiply_convert_fusion), channel_id=1, source_target_pairs={{2,4},{0,6},{10,12},{8,14},{18,20},{16,22},{26,28},{24,30},{3,5},{... | collective-permute-start | bytes 6291464 | tf_op jit(solution)/shard_map/ppermute | solution.py:32
  22.4 45.1 %collective-permute-start.5 = (bf16[2048,512]{1,0:T(8,128)(2,1)}, bf16[2048,512]{1,0:T(8,128)(2,1)S(1)}, u32[]{:S(2)}, u32[]{:S(2)}) collective-permute-start(bf16[2048,512]{1,0:T(8,128)(2,1)} %collective-permute-done.2), channel_id=1, source_target_pairs={{4,2},{12,10},{20,18},{28,26},{5,3},{13,11},{21,19},{29,27}} | collective-permute-start | bytes 6291464 | tf_op jit(solution)/shard_map/ppermute | solution.py:32
  23.2 44.2 %collective-permute-start.4 = (bf16[2048,512]{1,0:T(8,128)(2,1)}, bf16[2048,512]{1,0:T(8,128)(2,1)S(1)}, u32[]{:S(2)}, u32[]{:S(2)}) collective-permute-start(bf16[2048,512]{1,0:T(8,128)(2,1)} %collective-permute-done.1), channel_id=1, source_target_pairs={{2,8},{10,16},{18,24},{3,9},{11,17},{19,25}} | collective-permute-start | bytes 6291464 | tf_op jit(solution)/shard_map/ppermute | solution.py:32
  28.3 9.2 %collective-permute-start.3 = (bf16[2,256,512]{2,1,0:T(8,128)(2,1)S(1)}, bf16[2,256,512]{2,1,0:T(8,128)(2,1)S(1)}, u32[]{:S(2)}, u32[]{:S(2)}) collective-permute-start(bf16[2,256,512]{2,1,0:T(8,128)(2,1)S(1)} %fusion.2), channel_id=1, source_target_pairs={{0,1},{1,0},{2,3},{3,2},{4,5},{5,4},{6,7},{7,6},{8,9},{9,8},{10,11... | collective-permute-start | bytes 1572872 | tf_op jit(solution)/shard_map/ppermute | solution.py:17
  70.3 9.2 %collective-permute-start.7 = (bf16[256,512]{1,0:T(8,128)(2,1)S(1)}, bf16[256,512]{1,0:T(8,128)(2,1)S(1)}, u32[]{:S(2)}, u32[]{:S(2)}) collective-permute-start(bf16[256,512]{1,0:T(8,128)(2,1)S(1)} %dynamic-slice_bitcast_fusion.2), channel_id=1, source_target_pairs={{0,1},{1,0},{2,3},{3,2},{4,5},{5,4},{6,7},{7,6},{8,9},{9,8},{10,11... | collective-permute-start | bytes 786440 | tf_op jit(solution)/shard_map/ppermute | solution.py:17
  71.9 7.7 %collective-permute-start.8 = (bf16[256,512]{1,0:T(8,128)(2,1)S(1)}, bf16[256,512]{1,0:T(8,128)(2,1)S(1)}, u32[]{:S(2)}, u32[]{:S(2)}) collective-permute-start(bf16[256,512]{1,0:T(8,128)(2,1)S(1)} %get-tuple-element.20), channel_id=1, source_target_pairs={{0,2},{2,0},{4,6},{6,4},{8,10},{10,8},{12,14},{14,12},{16,18},{18,... | collective-permute-start | bytes 786440 | tf_op jit(solution)/shard_map/ppermute | solution.py:61
  72.1 12.0 %collective-permute-start.9 = (bf16[256,512]{1,0:T(8,128)(2,1)S(1)}, bf16[256,512]{1,0:T(8,128)(2,1)S(1)}, u32[]{:S(2)}, u32[]{:S(2)}) collective-permute-start(bf16[256,512]{1,0:T(8,128)(2,1)S(1)} %get-tuple-element.21), channel_id=1, source_target_pairs={{0,3},{1,2},{2,1},{3,0},{4,7},{5,6},{6,5},{7,4},{8,11},{9,10},{10,... | collective-permute-start | bytes 786440 | tf_op jit(solution)/shard_map/ppermute | solution.py:69
  79.6 4.6 %copy-start = (f32[256,2048]{1,0:T(8,128)}, f32[256,2048]{1,0:T(8,128)S(1)}, u32[]{:S(2)}) copy-start(f32[256,2048]{1,0:T(8,128)S(1)} %fusion.7) | copy-start | bytes 6291460

commit v18 on v16

--- a/solution.py
+++ b/solution.py
@@ -34,16 +34,15 @@
     def pairs_of(*steps):
         return [(b + s, b + t) for b in range(0, count, 4) for s, t in steps]
 
-    cross = send(standard, pairs_of((1, 2), (0, 3), (3, 5)))
+    cross = send(standard, pairs_of((1, 2), (0, 3), (2, 4), (3, 5)))
     fast_a = send(standard, pairs_of((0, 1), (2, 3), (1, 4), (3, 6)))
-    fast_b = send(standard, pairs_of((2, 1), (3, 2), (1, 0)))
-    relay = send(fast_b, pairs_of((1, 4)))
+    fast_b = send(standard, pairs_of((3, 2), (1, 0)))
     width = standard.shape[1]
     early = early_of(tile_term(standard, fast_a).astype(jnp.bfloat16))
     both, early = lax.optimization_barrier(
         (jnp.concatenate([standard, jnp.where(place % 2 == 0, fast_b, fast_a)], axis=1), early)
     )
-    rhs = lax.optimization_barrier(relay + cross)
+    rhs = lax.optimization_barrier(cross)
     product = tile_term(both, rhs).astype(jnp.bfloat16)
     own_late = product[:width]
     handed = to_partner(product[width:], count)

time: 83.4 us -> 98.8 us (1.18)
  the two profiles are of different devices: /device:TPU:0 before, /device:TPU:16 now
where the time goes in v18:
time: 98.8 us; the launch traced here: 98.5 us
  waiting for transfers between devices  48.1 us (49%)
  starting transfers between devices  32.4 us (33%)
  matrix products  8.09 us (8%)
  other arithmetic  7.61 us (8%)
  local copies, waits for them, and re-layouts  1.41 us (1%)
    ppermute x3, waiting for transfers between devices, send(): return lax.ppermute(value, 'snp', pairs)  37.1 us
    ppermute x1, starting transfers between devices, to_partner(): lax.ppermute(lax.dynamic_index_in_dim(pieces, me, 0, keepdims=False), 'sn...  18.2 us
    ppermute x3, starting transfers between devices, send(): return lax.ppermute(value, 'snp', pairs)  9.21 us
    ppermute x1, waiting for transfers between devices, to_partner(): lax.ppermute(outgoing, ('snp', 'smp'), pairs).astype(jnp.float32)  8.51 us
    dot_general x3, matrix products, tile_term(): lax.dot_general(standard, neighbour, (((0,), (0,)), ((), ())), preferred_...  8.09 us
    ppermute x3, starting transfers between devices, rotated(): lax.ppermute(value, axis, [(source, (source + steps) % count) for source...  4.76 us
    reduce_sum x1, other arithmetic, local(): part_square = jnp.sum(shifted_dosage * shifted_dosage, axis=0)  2.94 us
    ppermute x3, waiting for transfers between devices, rotated(): lax.ppermute(value, axis, [(source, (source + steps) % count) for source...  2.09 us
  transfers between devices with their start and end apart: 8, of which 5 were waited for; matrix products, arithmetic and copies ran while one was open for 7% of the time, Pallas kernels for 0%

profile of v18, /device:TPU:16, one launch (start us, length us, event | category | flops | bytes accessed | tf_op | source)
XLA Modules:
  0.0 98.5 jit_solution(11983587637768298371)
XLA Ops:
  0.0 0.7 slice.23
  0.7 0.0 copy-start
  0.7 2.9 %multiply_reduce_fusion = (f32[512]{0:T(512)S(1)}, f32[512]{0:T(512)S(1)}) fusion(f32[2048,512]{1,0:T(8,128)} %param.2, f32[512]{0:T(512)S(1)} %bitcast.56), kind=kLoop, calls=%fused_computation.2 | loop fusion | flops 4193280 | bytes 4200448 | tf_op jit(solution)/shard_map/reduce_sum | solution.py:87
  3.7 0.5 copy-done
  4.2 1.6 %collective-permute-start = (f32[2,512]{1,0:T(2,128)S(1)}, f32[2,512]{1,0:T(2,128)S(1)}, u32[]{:S(2)}, u32[]{:S(2)}) collective-permute-start(f32[2,512]{1,0:T(2,128)S(1)} %pad_maximum_fusion.2), channel_id=1, source_target_pairs={{0,1},{1,0},{2,3},{3,2},{4,5},{5,4},{6,7},{7,6},{8,9},{9,8},{10,11... | collective-permute-start | bytes 12296 | tf_op jit(solution)/shard_map/ppermute | solution.py:17
  5.8 2.1 %collective-permute-done = f32[2,512]{1,0:T(2,128)S(1)} collective-permute-done((f32[2,512]{1,0:T(2,128)S(1)}, f32[2,512]{1,0:T(2,128)S(1)}, u32[]{:S(2)}, u32[]{:S(2)}) %collective-permute-start) | collective-permute-done | bytes 4128 | tf_op jit(solution)/shard_map/ppermute | solution.py:17
  7.9 0.6 multiply_convert_fusion
  8.5 1.9 %collective-permute-start.2 = (bf16[2048,512]{1,0:T(8,128)(2,1)S(1)}, bf16[2048,512]{1,0:T(8,128)(2,1)}, u32[]{:S(2)}, u32[]{:S(2)}) collective-permute-start(bf16[2048,512]{1,0:T(8,128)(2,1)S(1)} %multiply_convert_fusion), channel_id=1, source_target_pairs={{0,2},{4,6},{2,8},{6,12},{8,10},{12,14},{10,16},{14,20},{16,18},{2... | collective-permute-start | bytes 6291464 | tf_op jit(solution)/shard_map/ppermute | solution.py:32
  10.4 1.3 %collective-permute-start.1 = (bf16[2048,512]{1,0:T(8,128)(2,1)S(1)}, bf16[2048,512]{1,0:T(8,128)(2,1)}, u32[]{:S(2)}, u32[]{:S(2)}) collective-permute-start(bf16[2048,512]{1,0:T(8,128)(2,1)S(1)} %multiply_convert_fusion), channel_id=1, source_target_pairs={{6,4},{2,0},{14,12},{10,8},{22,20},{18,16},{30,28},{26,24},{7,5},{... | collective-permute-start | bytes 6291464 | tf_op jit(solution)/shard_map/ppermute | solution.py:32
  11.7 6.0 %collective-permute-start.4 = (bf16[2048,512]{1,0:T(8,128)(2,1)S(1)}, bf16[2048,512]{1,0:T(8,128)(2,1)}, u32[]{:S(2)}, u32[]{:S(2)}) collective-permute-start(bf16[2048,512]{1,0:T(8,128)(2,1)S(1)} %multiply_convert_fusion), channel_id=1, source_target_pairs={{2,4},{0,6},{4,8},{6,10},{10,12},{8,14},{12,16},{14,18},{18,20},{1... | collective-permute-start | bytes 6291464 | tf_op jit(solution)/shard_map/ppermute | solution.py:32
  18.4 1.3 %convolution_convert_fusion.2 = bf16[512,512]{1,0:T(8,128)(2,1)S(1)} fusion(bf16[2048,512]{1,0:T(8,128)(2,1)S(1)} %multiply_convert_fusion), kind=kOutput, calls=%fused_computation.8 | convolution fusion | flops 1074003968 | bytes 2621440 | tf_op jit(solution)/shard_map/dot_general | solution.py:73
  19.7 16.2 %collective-permute-done.2 = bf16[2048,512]{1,0:T(8,128)(2,1)} collective-permute-done((bf16[2048,512]{1,0:T(8,128)(2,1)S(1)}, bf16[2048,512]{1,0:T(8,128)(2,1)}, u32[]{:S(2)}, u32[]{:S(2)}) %collective-permute-start.2) | collective-permute-done | bytes 2097184 | tf_op jit(solution)/shard_map/ppermute | solution.py:32
  35.9 2.9 %convolution_convert_fusion.1 = bf16[512,512]{1,0:T(8,128)(2,1)S(1)} fusion(bf16[2048,512]{1,0:T(8,128)(2,1)S(1)} %multiply_convert_fusion, bf16[2048,512]{1,0:T(8,128)(2,1)} %collective-permute-done.2), kind=kOutput, calls=%fused_computation.7 | convolution fusion | flops 1074003968 | bytes 4718592 | tf_op jit(solution)/shard_map/dot_general | solution.py:73
  38.8 0.1 fusion.1
  38.9 1.6 %collective-permute-start.3 = (bf16[2,256,512]{2,1,0:T(8,128)(2,1)S(1)}, bf16[2,256,512]{2,1,0:T(8,128)(2,1)S(1)}, u32[]{:S(2)}, u32[]{:S(2)}) collective-permute-start(bf16[2,256,512]{2,1,0:T(8,128)(2,1)S(1)} %fusion.1), channel_id=1, source_target_pairs={{0,1},{1,0},{2,3},{3,2},{4,5},{5,4},{6,7},{7,6},{8,9},{9,8},{10,11... | collective-permute-start | bytes 1572872 | tf_op jit(solution)/shard_map/ppermute | solution.py:17
  40.5 0.0 collective-permute-done.1
  40.5 1.8 %broadcast_select_fusion = bf16[2048,512]{1,0:T(8,128)(2,1)S(1)} fusion(bf16[2048,512]{1,0:T(8,128)(2,1)} %collective-permute-done.1, bf16[2048,512]{1,0:T(8,128)(2,1)} %collective-permute-done.2, pred[]{:T(512)S(6)} %eq.22), kind=kLoop, calls=%fused_computation.5 | loop fusion | flops 1048576 | bytes 6291457 | tf_op jit(solution)/shard_map/jit(_where)/select_n | solution.py:43
  42.3 20.9 %collective-permute-done.4 = bf16[2048,512]{1,0:T(8,128)(2,1)} collective-permute-done((bf16[2048,512]{1,0:T(8,128)(2,1)S(1)}, bf16[2048,512]{1,0:T(8,128)(2,1)}, u32[]{:S(2)}, u32[]{:S(2)}) %collective-permute-start.4) | collective-permute-done | bytes 2097184 | tf_op jit(solution)/shard_map/ppermute | solution.py:32
  63.2 0.6 pad_maximum_fusion
  63.8 0.0 collective-permute-done.3
  63.8 0.2 convert_add_fusion
  64.0 3.9 %convolution_convert_fusion = bf16[1024,512]{1,0:T(8,128)(2,1)S(1)} fusion(bf16[2048,1024]{1,0:T(8,128)(2,1)S(1)} %pad_maximum_fusion, bf16[2048,512]{1,0:T(8,128)(2,1)} %collective-permute-done.4), kind=kOutput, calls=%fused_computation.6 | convolution fusion | flops 2148007936 | bytes 7340032 | tf_op jit(solution)/shard_map/dot_general | solution.py:73
  68.0 0.1 fusion.9
  68.1 1.6 %collective-permute-start.5 = (bf16[256,512]{1,0:T(8,128)(2,1)S(1)}, bf16[256,512]{1,0:T(8,128)(2,1)S(1)}, u32[]{:S(2)}, u32[]{:S(2)}) collective-permute-start(bf16[256,512]{1,0:T(8,128)(2,1)S(1)} %dynamic-slice_bitcast_fusion.2), channel_id=1, source_target_pairs={{0,1},{1,0},{2,3},{3,2},{4,5},{5,4},{6,7},{7,6},{8,9},{9,8},{10,11... | collective-permute-start | bytes 786440 | tf_op jit(solution)/shard_map/ppermute | solution.py:17
  69.7 18.2 %collective-permute-start.6 = (bf16[256,512]{1,0:T(8,128)(2,1)S(1)}, bf16[256,512]{1,0:T(8,128)(2,1)S(1)}, u32[]{:S(2)}, u32[]{:S(2)}) collective-permute-start(bf16[256,512]{1,0:T(8,128)(2,1)S(1)} %get-tuple-element.16), channel_id=1, source_target_pairs={{0,2},{2,0},{4,6},{6,4},{8,10},{10,8},{12,14},{14,12},{16,18},{18,... | collective-permute-start | bytes 786440 | tf_op jit(solution)/shard_map/ppermute | solution.py:60
  87.9 0.2 collective-permute-start.7
  88.1 0.2 select_bitcast_fusion.2
  88.3 0.1 broadcast.66
  88.4 0.2 pad_maximum_fusion.1
  88.6 0.0 collective-permute-done.5
  88.6 0.1 fusion.6
  88.7 0.0 copy-start.1
  88.7 0.4 collective-permute-done.6
  89.1 8.5 %collective-permute-done.7 = bf16[256,512]{1,0:T(8,128)(2,1)S(1)} collective-permute-done((bf16[256,512]{1,0:T(8,128)(2,1)S(1)}, bf16[256,512]{1,0:T(8,128)(2,1)S(1)}, u32[]{:S(2)}, u32[]{:S(2)}) %collective-permute-start.7) | collective-permute-done | bytes 262176 | tf_op jit(solution)/shard_map/ppermute | solution.py:68
  97.6 0.0 copy-done.1
  97.6 0.9 select_dynamic-update-slice_fusion
  (5 shorter events, 0.1 us)
Async XLA Ops:
  0.7 3.4 %copy-start = (f32[2048,512]{1,0:T(8,128)S(1)}, f32[2048,512]{1,0:T(8,128)}, u32[]{:S(2)}) copy-start(f32[2048,512]{1,0:T(8,128)} %param.2) | copy-start | bytes 12582916
  4.2 3.7 %collective-permute-start = (f32[2,512]{1,0:T(2,128)S(1)}, f32[2,512]{1,0:T(2,128)S(1)}, u32[]{:S(2)}, u32[]{:S(2)}) collective-permute-start(f32[2,512]{1,0:T(2,128)S(1)} %pad_maximum_fusion.2), channel_id=1, source_target_pairs={{0,1},{1,0},{2,3},{3,2},{4,5},{5,4},{6,7},{7,6},{8,9},{9,8},{10,11... | collective-permute-start | bytes 12296 | tf_op jit(solution)/shard_map/ppermute | solution.py:17
  8.5 27.5 %collective-permute-start.2 = (bf16[2048,512]{1,0:T(8,128)(2,1)S(1)}, bf16[2048,512]{1,0:T(8,128)(2,1)}, u32[]{:S(2)}, u32[]{:S(2)}) collective-permute-start(bf16[2048,512]{1,0:T(8,128)(2,1)S(1)} %multiply_convert_fusion), channel_id=1, source_target_pairs={{0,2},{4,6},{2,8},{6,12},{8,10},{12,14},{10,16},{14,20},{16,18},{2... | collective-permute-start | bytes 6291464 | tf_op jit(solution)/shard_map/ppermute | solution.py:32
  10.4 30.1 %collective-permute-start.1 = (bf16[2048,512]{1,0:T(8,128)(2,1)S(1)}, bf16[2048,512]{1,0:T(8,128)(2,1)}, u32[]{:S(2)}, u32[]{:S(2)}) collective-permute-start(bf16[2048,512]{1,0:T(8,128)(2,1)S(1)} %multiply_convert_fusion), channel_id=1, source_target_pairs={{6,4},{2,0},{14,12},{10,8},{22,20},{18,16},{30,28},{26,24},{7,5},{... | collective-permute-start | bytes 6291464 | tf_op jit(solution)/shard_map/ppermute | solution.py:32
  11.7 51.5 %collective-permute-start.4 = (bf16[2048,512]{1,0:T(8,128)(2,1)S(1)}, bf16[2048,512]{1,0:T(8,128)(2,1)}, u32[]{:S(2)}, u32[]{:S(2)}) collective-permute-start(bf16[2048,512]{1,0:T(8,128)(2,1)S(1)} %multiply_convert_fusion), channel_id=1, source_target_pairs={{2,4},{0,6},{4,8},{6,10},{10,12},{8,14},{12,16},{14,18},{18,20},{1... | collective-permute-start | bytes 6291464 | tf_op jit(solution)/shard_map/ppermute | solution.py:32
  38.9 25.0 %collective-permute-start.3 = (bf16[2,256,512]{2,1,0:T(8,128)(2,1)S(1)}, bf16[2,256,512]{2,1,0:T(8,128)(2,1)S(1)}, u32[]{:S(2)}, u32[]{:S(2)}) collective-permute-start(bf16[2,256,512]{2,1,0:T(8,128)(2,1)S(1)} %fusion.1), channel_id=1, source_target_pairs={{0,1},{1,0},{2,3},{3,2},{4,5},{5,4},{6,7},{7,6},{8,9},{9,8},{10,11... | collective-permute-start | bytes 1572872 | tf_op jit(solution)/shard_map/ppermute | solution.py:17
  68.1 20.5 %collective-permute-start.5 = (bf16[256,512]{1,0:T(8,128)(2,1)S(1)}, bf16[256,512]{1,0:T(8,128)(2,1)S(1)}, u32[]{:S(2)}, u32[]{:S(2)}) collective-permute-start(bf16[256,512]{1,0:T(8,128)(2,1)S(1)} %dynamic-slice_bitcast_fusion.2), channel_id=1, source_target_pairs={{0,1},{1,0},{2,3},{3,2},{4,5},{5,4},{6,7},{7,6},{8,9},{9,8},{10,11... | collective-permute-start | bytes 786440 | tf_op jit(solution)/shard_map/ppermute | solution.py:17
  69.7 19.4 %collective-permute-start.6 = (bf16[256,512]{1,0:T(8,128)(2,1)S(1)}, bf16[256,512]{1,0:T(8,128)(2,1)S(1)}, u32[]{:S(2)}, u32[]{:S(2)}) collective-permute-start(bf16[256,512]{1,0:T(8,128)(2,1)S(1)} %get-tuple-element.16), channel_id=1, source_target_pairs={{0,2},{2,0},{4,6},{6,4},{8,10},{10,8},{12,14},{14,12},{16,18},{18,... | collective-permute-start | bytes 786440 | tf_op jit(solution)/shard_map/ppermute | solution.py:60
  87.9 9.7 %collective-permute-start.7 = (bf16[256,512]{1,0:T(8,128)(2,1)S(1)}, bf16[256,512]{1,0:T(8,128)(2,1)S(1)}, u32[]{:S(2)}, u32[]{:S(2)}) collective-permute-start(bf16[256,512]{1,0:T(8,128)(2,1)S(1)} %get-tuple-element.17), channel_id=1, source_target_pairs={{0,3},{1,2},{2,1},{3,0},{4,7},{5,6},{6,5},{7,4},{8,11},{9,10},{10,... | collective-permute-start | bytes 786440 | tf_op jit(solution)/shard_map/ppermute | solution.py:68
  88.7 8.9 %copy-start.1 = (f32[256,2048]{1,0:T(8,128)}, f32[256,2048]{1,0:T(8,128)S(1)}, u32[]{:S(2)}) copy-start(f32[256,2048]{1,0:T(8,128)S(1)} %fusion.6) | copy-start | bytes 6291460
